TPU v7x, 512 devices: a whole 4x4x16 slice. The times are simulated.
512 devices in a mesh: sub: 128 (over z, x, core), crow: 4 (over y).
Axes of the slice: x: 4, y: 4, z: 16, core: 2. Of those that a mesh axis runs over, the one named last changes fastest.
Arguments:
- deflation: bfloat16 [128, 12288, 128], P('sub', 'crow'), as said below
- diag_op: bfloat16 [128, 96, 128, 128], P('sub', 'crow'), as said below
- upper_op: bfloat16 [128, 96, 128, 128], P('sub', 'crow'), may hold values from -0.022094727 to 0.022094727
- tile_blocks: int32 [128, 4, 16], P('sub', 'crow'), may hold values from 0 to 23
- pair_counts: int32 [128, 8], P('sub'), may hold values from 0 to 8, as said below
- pivot_owner: int32 [128], P('sub'), may hold values from 0 to 3
Outputs:
- schur_self: float32 [16384, 128], P(('sub', 'crow'))
- schur_coupling: float32 [16384, 1024], P(('sub', 'crow'))
- panel: float32 [16384, 32], P(('sub', 'crow'))
Inputs may be any that keep to these rules, and one draw needn't show every extreme that they name: deflation has independent columns of different scales. Each diag_op block is symmetric with a positive diagonal, and every A_s is symmetric positive definite. pair_counts[s, j] equals pair_counts[s + o[j], 7 - j], is 0 where s + o[j] lies outside 0 to 127, and the pair of subdomains 0 and 1 shares 8 tiles.
All inputs are finite; a program needn't handle non-finite values.
Results may differ from a plain program's by a relative error of at most 0.0029.
Values may be sent and summed in bfloat16 or wider, within the bound.
No kernel may reach another device: no remote copies, remote signals or barrier semaphores. Data moves between devices by JAX's collectives and lax.ppermute only.
A program may use at most 64 MiB of HBM per device.

v0:
```python
import jax
import jax.numpy as jnp
from jax import lax
from jax.sharding import PartitionSpec as P


def padded_2(block, sides, width):
    for axis, dim in sides:
        count = lax.axis_size(axis)
        forward = [(i, i + 1) for i in range(count - 1)]
        backward = [(target, source) for source, target in forward]
        low = lax.ppermute(
            lax.slice_in_dim(block, block.shape[dim] - width, None, axis=dim), axis, forward
        )
        high = lax.ppermute(lax.slice_in_dim(block, 0, width, axis=dim), axis, backward)
        block = jnp.concatenate([low, block, high], axis=dim)
    return block


def shifted(value, axis, steps):
    count = lax.axis_size(axis)
    initial, last = (max(0, -steps), min(count, count - steps))
    return lax.ppermute(value, axis, [(source, source + steps) for source in range(initial, last)])


def broadcast(shard, axis, root):
    mine = lax.axis_index(axis) == root
    return lax.psum(jnp.where(mine, shard, jnp.zeros_like(shard)), axis)


def neighbour_offsets(across):
    return [-across - 1, -across, -across + 1, -1, 1, across - 1, across, across + 1]


def per_device(deflation, diag_op, upper_op, tile_blocks, pair_counts, pivot_owner):
    crow_count = lax.axis_size("crow")
    crow_place = lax.axis_index("crow")
    sub_count = lax.axis_size("sub")
    across = min(16, sub_count // 2)
    offsets = neighbour_offsets(across)
    local_rows = deflation[0]
    blocks_here, tile_rows = (diag_op.shape[1], diag_op.shape[2])
    coarse_width = local_rows.shape[1]
    slot_count = pair_counts.shape[1]
    per_slot = tile_blocks.shape[2] // slot_count
    padded = padded_2(local_rows, (("crow", 0),), tile_rows)
    stacked = padded.reshape(blocks_here + 2, tile_rows, coarse_width)
    centre = stacked[1:-1]
    previous_upper = shifted(upper_op[0, blocks_here - 1], "crow", 1)
    lower_blocks = jnp.concatenate([previous_upper[None], upper_op[0, :-1]], 0)
    product = (
        jnp.einsum("bij,bjk->bik", diag_op[0], centre, preferred_element_type=jnp.float32)
        + jnp.einsum("bij,bjk->bik", upper_op[0], stacked[2:], preferred_element_type=jnp.float32)
        + jnp.einsum("bji,bjk->bik", lower_blocks, stacked[:-2], preferred_element_type=jnp.float32)
    )
    applied = product.astype(jnp.bfloat16)
    chosen = tile_blocks[0, 0]
    own_tiles = centre[chosen].reshape(slot_count, per_slot, tile_rows, coarse_width)
    outgoing = applied[chosen].reshape(slot_count, per_slot, tile_rows, coarse_width)
    position = crow_place * per_slot + jnp.arange(per_slot, dtype=jnp.int32)
    live_mask = (position[None, :] < pair_counts[0][:, None]).astype(jnp.bfloat16)
    own_masked = own_tiles * live_mask[:, :, None, None]
    arrived = [None] * slot_count
    for slot_index in range(slot_count):
        arrived[slot_index] = shifted(
            outgoing[slot_count - 1 - slot_index], "sub", -offsets[slot_index]
        )
    received = jnp.stack(arrived)
    flat_vectors = centre.reshape(blocks_here * tile_rows, coarse_width)
    flat_applied = applied.reshape(blocks_here * tile_rows, coarse_width)
    row_share = coarse_width // crow_count
    owner_index = pivot_owner[0]
    gram_part = jnp.einsum(
        "nr,nk->rk", flat_vectors, flat_applied, preferred_element_type=jnp.float32
    )
    coupling = jnp.einsum(
        "jutr,jutk->rjk", own_masked, received, preferred_element_type=jnp.float32
    )
    own_rows = lax.psum_scatter(
        jnp.concatenate([gram_part[:, None, :], coupling], 1).reshape(
            row_share * lax.axis_size("crow"), (slot_count + 1) * coarse_width
        ),
        "crow",
        scatter_dimension=0,
        tiled=True,
    )
    leading = broadcast(own_rows, "crow", owner_index)
    pivot_block = lax.dynamic_slice_in_dim(leading, owner_index * row_share, row_share, 1)
    factor = jnp.linalg.cholesky(pivot_block)
    solved = jax.scipy.linalg.solve_triangular(factor, leading, lower=True)
    columns = lax.dynamic_slice_in_dim(own_rows, owner_index * row_share, row_share, 1)
    panel_rows = jax.scipy.linalg.solve_triangular(factor, columns.T, lower=True).T
    updated = own_rows - jnp.dot(panel_rows, solved, precision=lax.Precision.HIGHEST)
    return (updated[:, :coarse_width], updated[:, coarse_width:], panel_rows)


def solution(mesh):
    placed = (
        P("sub", "crow", None),
        P("sub", "crow", None, None),
        P("sub", "crow", None, None),
        P("sub", "crow", None),
        P("sub", None),
        P("sub"),
    )
    return jax.shard_map(
        per_device,
        mesh=mesh,
        in_specs=placed,
        out_specs=(P(("sub", "crow"), None), P(("sub", "crow"), None), P(("sub", "crow"), None)),
        check_vma=False,
    )
```

profile of v0, /device:TPU:4, one launch (start us, length us, event | category | flops | bytes accessed | tf_op | source)
XLA Modules:
  0.0 182.8 jit_solution(14846364270615309179)
XLA Ops:
  7.2 0.8 slice_bitcast_fusion
  8.1 1.3 collective-permute-start
  9.4 4.5 %collective-permute-start.2 = (bf16[128,128]{1,0:T(8,128)(2,1)S(1)}, bf16[128,128]{1,0:T(8,128)(2,1)S(1)}, u32[]{:S(2)}, u32[]{:S(2)}) collective-permute-start(bf16[128,128]{1,0:T(8,128)(2,1)S(1)} %get-tuple-element.11), channel_id=1, source_target_pairs={{0,1},{1,2},{2,3},{4,5},{5,6},{6,7},{8,9},{9,10},{10,11},{12,13},{... | collective-permute-start | bytes 98312 | tf_op jit(solution)/shard_map/ppermute | solution.py:12
  13.9 0.8 slice.97
  14.8 3.5 %collective-permute-start.1 = (bf16[128,128]{0,1:T(8,128)(2,1)S(1)}, bf16[128,128]{0,1:T(8,128)(2,1)S(1)}, u32[]{:S(2)}, u32[]{:S(2)}) collective-permute-start(bf16[128,128]{0,1:T(8,128)(2,1)S(1)} %bitcast.93), channel_id=1, source_target_pairs={{0,1},{1,2},{2,3},{4,5},{5,6},{6,7},{8,9},{9,10},{10,11},{12,13},{... | collective-permute-start | bytes 98312 | tf_op jit(solution)/shard_map/ppermute | solution.py:23
  19.0 1.6 fusion.7
  20.7 1.0 slice.98
  21.6 2.3 %copy.28 = bf16[1,23,128,128]{2,3,1,0:T(8,128)(2,1)} copy(bf16[1,23,128,128]{3,2,1,0:T(8,128)(2,1)} %slice.98) | data formatting | bytes 1507328
  23.9 1.4 gather_fusion.1
  25.5 1.0 copy-done.4
  26.9 0.7 copy-done.5
  27.6 1.4 fusion.1
  29.0 1.9 %gather_fusion = bf16[16,128,128]{2,1,0:T(8,128)(2,1)S(1)} fusion(bf16[24,128,128]{2,1,0:T(8,128)(2,1)} %fusion.1, s32[1024]{0:T(1024)S(1)} %pad_clamp_fusion), kind=kCustom, calls=%fused_computation | custom fusion | bytes 1048640 | tf_op jit(solution)/shard_map/gather | solution.py:59
  30.9 3.9 %collective-permute-start.3 = (bf16[2,128,128]{2,1,0:T(8,128)(2,1)S(1)}, bf16[2,128,128]{2,1,0:T(8,128)(2,1)S(1)}, u32[]{:S(2)}, u32[]{:S(2)}) collective-permute-start(bf16[2,128,128]{2,1,0:T(8,128)(2,1)S(1)} %get-tuple-element.20), channel_id=1, source_target_pairs={{0,68},{4,72},{8,76},{12,80},{16,84},{20,88},{24,92},{28,96},{32,1... | collective-permute-start | bytes 196616 | tf_op jit(solution)/shard_map/ppermute | solution.py:23
  34.8 6.4 %collective-permute-start.4 = (bf16[2,128,128]{2,1,0:T(8,128)(2,1)S(1)}, bf16[2,128,128]{2,1,0:T(8,128)(2,1)S(1)}, u32[]{:S(2)}, u32[]{:S(2)}) collective-permute-start(bf16[2,128,128]{2,1,0:T(8,128)(2,1)S(1)} %get-tuple-element.19), channel_id=1, source_target_pairs={{0,64},{4,68},{8,72},{12,76},{16,80},{20,84},{24,88},{28,92},{32,9... | collective-permute-start | bytes 196616 | tf_op jit(solution)/shard_map/ppermute | solution.py:23
  41.2 6.9 %collective-permute-start.5 = (bf16[2,128,128]{2,1,0:T(8,128)(2,1)S(1)}, bf16[2,128,128]{2,1,0:T(8,128)(2,1)S(1)}, u32[]{:S(2)}, u32[]{:S(2)}) collective-permute-start(bf16[2,128,128]{2,1,0:T(8,128)(2,1)S(1)} %get-tuple-element.18), channel_id=1, source_target_pairs={{0,60},{4,64},{8,68},{12,72},{16,76},{20,80},{24,84},{28,88},{32,9... | collective-permute-start | bytes 196616 | tf_op jit(solution)/shard_map/ppermute | solution.py:23
  48.1 1.9 %collective-permute-start.6 = (bf16[2,128,128]{2,1,0:T(8,128)(2,1)S(1)}, bf16[2,128,128]{2,1,0:T(8,128)(2,1)S(1)}, u32[]{:S(2)}, u32[]{:S(2)}) collective-permute-start(bf16[2,128,128]{2,1,0:T(8,128)(2,1)S(1)} %get-tuple-element.17), channel_id=1, source_target_pairs={{0,4},{4,8},{8,12},{12,16},{16,20},{20,24},{24,28},{28,32},{32,36}... | collective-permute-start | bytes 196616 | tf_op jit(solution)/shard_map/ppermute | solution.py:23
  50.1 3.6 %collective-permute-start.7 = (bf16[2,128,128]{2,1,0:T(8,128)(2,1)S(1)}, bf16[2,128,128]{2,1,0:T(8,128)(2,1)S(1)}, u32[]{:S(2)}, u32[]{:S(2)}) collective-permute-start(bf16[2,128,128]{2,1,0:T(8,128)(2,1)S(1)} %get-tuple-element.16), channel_id=1, source_target_pairs={{4,0},{8,4},{12,8},{16,12},{20,16},{24,20},{28,24},{32,28},{36,32}... | collective-permute-start | bytes 196616 | tf_op jit(solution)/shard_map/ppermute | solution.py:23
  54.2 1.3 collective-permute-start.8
  55.5 1.3 collective-permute-start.9
  56.8 1.3 collective-permute-start.10
  58.2 3.8 %collective-permute-done.8 = bf16[2,128,128]{2,1,0:T(8,128)(2,1)S(1)} collective-permute-done((bf16[2,128,128]{2,1,0:T(8,128)(2,1)S(1)}, bf16[2,128,128]{2,1,0:T(8,128)(2,1)S(1)}, u32[]{:S(2)}, u32[]{:S(2)}) %collective-permute-start.8) | collective-permute-done | bytes 65568 | tf_op jit(solution)/shard_map/ppermute | solution.py:23
  62.0 6.9 %collective-permute-done.9 = bf16[2,128,128]{2,1,0:T(8,128)(2,1)S(1)} collective-permute-done((bf16[2,128,128]{2,1,0:T(8,128)(2,1)S(1)}, bf16[2,128,128]{2,1,0:T(8,128)(2,1)S(1)}, u32[]{:S(2)}, u32[]{:S(2)}) %collective-permute-start.9) | collective-permute-done | bytes 65568 | tf_op jit(solution)/shard_map/ppermute | solution.py:23
  69.5 1.1 copy.25
  71.3 31.2 %reduce-scatter.4.cloned.1.call-done = f32[32,1152]{1,0:T(8,128)} async-done(((f32[128,1152]{1,0:T(8,128)}), f32[32,1152]{1,0:T(8,128)}) %reduce-scatter.4.cloned.1.call-update) | async-done | bytes 147472 | tf_op jit(solution)/shard_map/reduce_scatter | solution.py:79
  102.4 1.2 copy.26
  103.6 0.9 broadcast_select_fusion
  104.5 58.9 %all-reduce.2.cloned.1.call-done = f32[32,1152]{0,1:T(8,128)} async-done(((f32[32,1152]{0,1:T(8,128)}), f32[32,1152]{0,1:T(8,128)}) %all-reduce.2.cloned.1.call-update) | async-done | bytes 147472 | tf_op jit(solution)/shard_map/psum | solution.py:28
  164.2 0.7 fusion.16
  164.9 2.9 %cholesky.16 = f32[32,32]{1,0:T(8,128)S(1)} custom-call(f32[32,32]{1,0:T(8,128)S(1)} %fusion.16), custom_call_target="Cholesky" | custom-call | tf_op jit(solution)/shard_map/jit(cholesky)/cholesky | solution.py:89
  169.2 2.4 %custom-call.10 = f32[1,32,32]{1,2,0:T(8,128)S(1)} custom-call(f32[1,32,32]{2,1,0:T(8,128)S(1)} %fusion.11), custom_call_target="InvertDiagBlocksLowerTriangular" | custom-call | tf_op jit(solution)/shard_map/jit(_solve_triangular)/triangular_solve | solution.py:92
  171.8 1.8 fusion.12
  (58 shorter events, 7.2 us)
Async XLA Ops:
  7.2 11.8 %copy-start = (bf16[1,24,128,128]{3,2,1,0:T(8,128)(2,1)S(1)}, bf16[1,24,128,128]{3,2,1,0:T(8,128)(2,1)}, u32[]{:S(2)}) copy-start(bf16[1,24,128,128]{3,2,1,0:T(8,128)(2,1)} %param.7) | copy-start | bytes 2359300
  7.2 95.2 %reduce-scatter.4.cloned.1.call-start = ((), (), s32[]{:S(2)}) async-start(), calls=%async_computation.2 | async-start | bytes 737280 | tf_op jit(solution)/shard_map/reduce_scatter | solution.py:79
  8.1 17.3 %collective-permute-start = (bf16[128,128]{1,0:T(8,128)(2,1)S(1)}, bf16[128,128]{1,0:T(8,128)(2,1)S(1)}, u32[]{:S(2)}, u32[]{:S(2)}) collective-permute-start(bf16[128,128]{1,0:T(8,128)(2,1)S(1)} %get-tuple-element.12), channel_id=1, source_target_pairs={{1,0},{2,1},{3,2},{5,4},{6,5},{7,6},{9,8},{10,9},{11,10},{13,12},{... | collective-permute-start | bytes 98312 | tf_op jit(solution)/shard_map/ppermute | solution.py:15
  9.4 16.0 %collective-permute-start.2 = (bf16[128,128]{1,0:T(8,128)(2,1)S(1)}, bf16[128,128]{1,0:T(8,128)(2,1)S(1)}, u32[]{:S(2)}, u32[]{:S(2)}) collective-permute-start(bf16[128,128]{1,0:T(8,128)(2,1)S(1)} %get-tuple-element.11), channel_id=1, source_target_pairs={{0,1},{1,2},{2,3},{4,5},{5,6},{6,7},{8,9},{9,10},{10,11},{12,13},{... | collective-permute-start | bytes 98312 | tf_op jit(solution)/shard_map/ppermute | solution.py:12
  14.8 12.1 %collective-permute-start.1 = (bf16[128,128]{0,1:T(8,128)(2,1)S(1)}, bf16[128,128]{0,1:T(8,128)(2,1)S(1)}, u32[]{:S(2)}, u32[]{:S(2)}) collective-permute-start(bf16[128,128]{0,1:T(8,128)(2,1)S(1)} %bitcast.93), channel_id=1, source_target_pairs={{0,1},{1,2},{2,3},{4,5},{5,6},{6,7},{8,9},{9,10},{10,11},{12,13},{... | collective-permute-start | bytes 98312 | tf_op jit(solution)/shard_map/ppermute | solution.py:23
  19.0 1.6 copy-start.8
  19.0 1.7 copy-start.3
  20.5 3.4 %copy-start.1 = (bf16[1,3072,128]{2,1,0:T(8,128)(2,1)S(1)}, bf16[1,3072,128]{2,1,0:T(8,128)(2,1)}, u32[]{:S(2)}) copy-start(bf16[1,3072,128]{2,1,0:T(8,128)(2,1)} %param.6) | copy-start | bytes 2359300
  25.4 1.1 copy-start.4
  26.5 1.1 copy-start.5
  29.0 24.7 %copy-start.2 = (bf16[24,128,128]{2,1,0:T(8,128)(2,1)S(1)}, bf16[24,128,128]{2,1,0:T(8,128)(2,1)}, u32[]{:S(2)}) copy-start(bf16[24,128,128]{2,1,0:T(8,128)(2,1)} %fusion.1) | copy-start | bytes 2359300
  30.9 38.1 %copy-start.6 = (bf16[16,128,128]{2,1,0:T(8,128)(2,1)S(1)}, bf16[16,128,128]{2,1,0:T(8,128)(2,1)}, u32[]{:S(2)}) copy-start(bf16[16,128,128]{2,1,0:T(8,128)(2,1)} %gather_fusion.1) | copy-start | bytes 1572868
  30.9 23.2 %collective-permute-start.3 = (bf16[2,128,128]{2,1,0:T(8,128)(2,1)S(1)}, bf16[2,128,128]{2,1,0:T(8,128)(2,1)S(1)}, u32[]{:S(2)}, u32[]{:S(2)}) collective-permute-start(bf16[2,128,128]{2,1,0:T(8,128)(2,1)S(1)} %get-tuple-element.20), channel_id=1, source_target_pairs={{0,68},{4,72},{8,76},{12,80},{16,84},{20,88},{24,92},{28,96},{32,1... | collective-permute-start | bytes 196616 | tf_op jit(solution)/shard_map/ppermute | solution.py:23
  34.8 20.6 %collective-permute-start.4 = (bf16[2,128,128]{2,1,0:T(8,128)(2,1)S(1)}, bf16[2,128,128]{2,1,0:T(8,128)(2,1)S(1)}, u32[]{:S(2)}, u32[]{:S(2)}) collective-permute-start(bf16[2,128,128]{2,1,0:T(8,128)(2,1)S(1)} %get-tuple-element.19), channel_id=1, source_target_pairs={{0,64},{4,68},{8,72},{12,76},{16,80},{20,84},{24,88},{28,92},{32,9... | collective-permute-start | bytes 196616 | tf_op jit(solution)/shard_map/ppermute | solution.py:23
  41.2 15.6 %collective-permute-start.5 = (bf16[2,128,128]{2,1,0:T(8,128)(2,1)S(1)}, bf16[2,128,128]{2,1,0:T(8,128)(2,1)S(1)}, u32[]{:S(2)}, u32[]{:S(2)}) collective-permute-start(bf16[2,128,128]{2,1,0:T(8,128)(2,1)S(1)} %get-tuple-element.18), channel_id=1, source_target_pairs={{0,60},{4,64},{8,68},{12,72},{16,76},{20,80},{24,84},{28,88},{32,9... | collective-permute-start | bytes 196616 | tf_op jit(solution)/shard_map/ppermute | solution.py:23
  48.1 10.0 %collective-permute-start.6 = (bf16[2,128,128]{2,1,0:T(8,128)(2,1)S(1)}, bf16[2,128,128]{2,1,0:T(8,128)(2,1)S(1)}, u32[]{:S(2)}, u32[]{:S(2)}) collective-permute-start(bf16[2,128,128]{2,1,0:T(8,128)(2,1)S(1)} %get-tuple-element.17), channel_id=1, source_target_pairs={{0,4},{4,8},{8,12},{12,16},{16,20},{20,24},{24,28},{28,32},{32,36}... | collective-permute-start | bytes 196616 | tf_op jit(solution)/shard_map/ppermute | solution.py:23
  50.1 8.1 %collective-permute-start.7 = (bf16[2,128,128]{2,1,0:T(8,128)(2,1)S(1)}, bf16[2,128,128]{2,1,0:T(8,128)(2,1)S(1)}, u32[]{:S(2)}, u32[]{:S(2)}) collective-permute-start(bf16[2,128,128]{2,1,0:T(8,128)(2,1)S(1)} %get-tuple-element.16), channel_id=1, source_target_pairs={{4,0},{8,4},{12,8},{16,12},{20,16},{24,20},{28,24},{32,28},{36,32}... | collective-permute-start | bytes 196616 | tf_op jit(solution)/shard_map/ppermute | solution.py:23
  54.2 7.8 %collective-permute-start.8 = (bf16[2,128,128]{2,1,0:T(8,128)(2,1)S(1)}, bf16[2,128,128]{2,1,0:T(8,128)(2,1)S(1)}, u32[]{:S(2)}, u32[]{:S(2)}) collective-permute-start(bf16[2,128,128]{2,1,0:T(8,128)(2,1)S(1)} %get-tuple-element.15), channel_id=1, source_target_pairs={{60,0},{64,4},{68,8},{72,12},{76,16},{80,20},{84,24},{88,28},{92,3... | collective-permute-start | bytes 196616 | tf_op jit(solution)/shard_map/ppermute | solution.py:23
  55.5 13.4 %collective-permute-start.9 = (bf16[2,128,128]{2,1,0:T(8,128)(2,1)S(1)}, bf16[2,128,128]{2,1,0:T(8,128)(2,1)S(1)}, u32[]{:S(2)}, u32[]{:S(2)}) collective-permute-start(bf16[2,128,128]{2,1,0:T(8,128)(2,1)S(1)} %get-tuple-element.14), channel_id=1, source_target_pairs={{64,0},{68,4},{72,8},{76,12},{80,16},{84,20},{88,24},{92,28},{96,3... | collective-permute-start | bytes 196616 | tf_op jit(solution)/shard_map/ppermute | solution.py:23
  56.8 12.2 %collective-permute-start.10 = (bf16[2,128,128]{2,1,0:T(8,128)(2,1)S(1)}, bf16[2,128,128]{2,1,0:T(8,128)(2,1)S(1)}, u32[]{:S(2)}, u32[]{:S(2)}) collective-permute-start(bf16[2,128,128]{2,1,0:T(8,128)(2,1)S(1)} %get-tuple-element.13), channel_id=1, source_target_pairs={{68,0},{72,4},{76,8},{80,12},{84,16},{88,20},{92,24},{96,28},{100,... | collective-permute-start | bytes 196616 | tf_op jit(solution)/shard_map/ppermute | solution.py:23
  70.6 92.8 %all-reduce.2.cloned.1.call-start = ((), (), s32[]{:S(2)}) async-start(), calls=%async_computation.1 | async-start | bytes 1179648 | tf_op jit(solution)/shard_map/psum | solution.py:28
  102.4 71.2 %copy-start.7 = (f32[32,1152]{1,0:T(8,128)S(1)}, f32[32,1152]{1,0:T(8,128)}, u32[]{:S(2)}) copy-start(f32[32,1152]{1,0:T(8,128)} %reduce-scatter.4.cloned.1.call-done) | copy-start | bytes 442372
Sparse Core Ops, SparseCore 0:
  70.7 31.6 reduce-scatter.3
  104.8 58.5 all-reduce.1
where the time goes:
time: 184 us; the launch traced here: 183 us
  waiting for transfers between devices  101 us (55%)
  starting transfers between devices  36 us (20%)
  local copies, waits for them, and re-layouts  15.2 us (8%)
  between operations  15 us (8%)
  other arithmetic  9.15 us (5%)
  matrix products  6.46 us (4%)
    psum x1, waiting for transfers between devices, broadcast(): return lax.psum(jnp.where(mine, shard, jnp.zeros_like(shard)), axis)  58.9 us
    reduce_scatter x1, waiting for transfers between devices, per_device(): lax.psum_scatter(jnp.concatenate([gram_part[:, None, :], coupling], 1).re...  31.2 us
    ppermute x9, starting transfers between devices, shifted(): lax.ppermute(value, axis, [(source, source + steps) for source in range(i...  30.1 us
    ppermute x9, waiting for transfers between devices, shifted(): lax.ppermute(value, axis, [(source, source + steps) for source in range(i...  10.8 us
    unnamed x30, local copies, waits for them, and re-layouts  7.24 us
    ppermute x1, starting transfers between devices, padded_2(): lax.ppermute(lax.slice_in_dim(block, block.shape[dim] - width, None, axis...  4.55 us
  transfers between devices with their start and end apart: 13, of which 5 were waited for; matrix products, arithmetic and copies ran while one was open for 5% of the time, Pallas kernels for 0%

commit v1 on v0

--- a/solution.py
+++ b/solution.py
@@ -76,15 +76,26 @@
     coupling = jnp.einsum(
         "jutr,jutk->rjk", own_masked, received, preferred_element_type=jnp.float32
     )
-    own_rows = lax.psum_scatter(
-        jnp.concatenate([gram_part[:, None, :], coupling], 1).reshape(
-            row_share * lax.axis_size("crow"), (slot_count + 1) * coarse_width
-        ),
-        "crow",
-        scatter_dimension=0,
-        tiled=True,
+    whole = jnp.concatenate([gram_part[:, None, :], coupling], 1).reshape(
+        coarse_width, (slot_count + 1) * coarse_width
     )
-    leading = broadcast(own_rows, "crow", owner_index)
+    pivot_partial = lax.dynamic_slice_in_dim(whole, owner_index * row_share, row_share, 0)
+
+    def payload(target):
+        rows = lax.dynamic_slice_in_dim(whole, target * row_share, row_share, 0)
+        return jnp.concatenate([rows, pivot_partial], 0)
+
+    pieces = [payload(crow_place)]
+    for step in range(1, crow_count):
+        target = (crow_place + step) % crow_count
+        pairs = [(i, (i + step) % crow_count) for i in range(crow_count)]
+        pieces.append(lax.ppermute(payload(target), "crow", pairs))
+    if crow_count == 4:
+        total = (pieces[0] + pieces[2]) + (pieces[1] + pieces[3])
+    else:
+        total = sum(pieces[1:], pieces[0])
+    own_rows = total[:row_share]
+    leading = total[row_share:]
     pivot_block = lax.dynamic_slice_in_dim(leading, owner_index * row_share, row_share, 1)
     factor = jnp.linalg.cholesky(pivot_block)
     solved = jax.scipy.linalg.solve_triangular(factor, leading, lower=True)

time: 184 us -> 102 us (0.55)
  the two profiles are of different devices: /device:TPU:4 before, /device:TPU:95 now
where the time goes in v1:
time: 102 us
  starting transfers between devices  49.8 us (49%)
  waiting for transfers between devices  18.9 us (19%)
  local copies, waits for them, and re-layouts  17.1 us (17%)
  other arithmetic  7.77 us (8%)
  matrix products  6.31 us (6%)
  between operations  1.7 us (2%)
    ppermute x9, starting transfers between devices, shifted(): lax.ppermute(value, axis, [(source, source + steps) for source in range(i...  34 us
    ppermute x3, starting transfers between devices, per_device(): pieces.append(lax.ppermute(payload(target), 'crow', pairs))  10.5 us
    ppermute x3, waiting for transfers between devices, per_device(): pieces.append(lax.ppermute(payload(target), 'crow', pairs))  9.69 us
    ppermute x9, waiting for transfers between devices, shifted(): lax.ppermute(value, axis, [(source, source + steps) for source in range(i...  9.24 us
    unnamed x33, local copies, waits for them, and re-layouts  8.54 us
    ppermute x1, starting transfers between devices, padded_2(): lax.ppermute(lax.slice_in_dim(block, 0, width, axis=dim), axis, backward)  3.99 us
    another operation x3, other arithmetic, per_device(): factor = jnp.linalg.cholesky(pivot_block)  3.59 us
    another operation x2, other arithmetic, per_device(): jax.scipy.linalg.solve_triangular(factor, columns.T, lower=True)  3.09 us
  transfers between devices with their start and end apart: 14, of which 6 were waited for; matrix products, arithmetic and copies ran while one was open for 9% of the time, Pallas kernels for 0%

profile of v1, /device:TPU:95, one launch (start us, length us, event | category | flops | bytes accessed | tf_op | source)
XLA Modules:
  0.0 101.6 jit_solution(1080671127000866767)
XLA Ops:
  1.5 1.3 %collective-permute-start.2 = (bf16[128,128]{1,0:T(8,128)(2,1)S(1)}, bf16[128,128]{1,0:T(8,128)(2,1)S(1)}, u32[]{:S(2)}, u32[]{:S(2)}) collective-permute-start(bf16[128,128]{1,0:T(8,128)(2,1)S(1)} %get-tuple-element.17), channel_id=1, source_target_pairs={{0,1},{1,2},{2,3},{4,5},{5,6},{6,7},{8,9},{9,10},{10,11},{12,13},{... | collective-permute-start | bytes 98312 | tf_op jit(solution)/shard_map/ppermute | solution.py:12
  2.8 4.0 %collective-permute-start = (bf16[128,128]{1,0:T(8,128)(2,1)S(1)}, bf16[128,128]{1,0:T(8,128)(2,1)S(1)}, u32[]{:S(2)}, u32[]{:S(2)}) collective-permute-start(bf16[128,128]{1,0:T(8,128)(2,1)S(1)} %get-tuple-element.18), channel_id=1, source_target_pairs={{1,0},{2,1},{3,2},{5,4},{6,5},{7,6},{9,8},{10,9},{11,10},{13,12},{... | collective-permute-start | bytes 98312 | tf_op jit(solution)/shard_map/ppermute | solution.py:15
  7.7 1.3 %collective-permute-start.1 = (bf16[128,128]{0,1:T(8,128)(2,1)S(1)}, bf16[128,128]{0,1:T(8,128)(2,1)S(1)}, u32[]{:S(2)}, u32[]{:S(2)}) collective-permute-start(bf16[128,128]{0,1:T(8,128)(2,1)S(1)} %bitcast.89), channel_id=1, source_target_pairs={{0,1},{1,2},{2,3},{4,5},{5,6},{6,7},{8,9},{9,10},{10,11},{12,13},{... | collective-permute-start | bytes 98312 | tf_op jit(solution)/shard_map/ppermute | solution.py:23
  9.7 1.6 %fusion.7 = f32[24,128,128]{2,1,0:T(8,128)S(1)} fusion(bf16[24,128,128]{2,1,0:T(8,128)(2,1)} %bitcast.79, bf16[1,24,128,128]{3,2,1,0:T(8,128)(2,1)S(1)} %copy-done), kind=kOutput, calls=%fused_computation.15 | convolution fusion | flops 100663296 | bytes 3145728 | tf_op jit(solution)/shard_map/bij,bjk->bik/dot_general | solution.py:52
  11.3 1.0 slice.105
  13.0 2.3 %copy.63 = bf16[1,23,128,128]{2,3,1,0:T(8,128)(2,1)} copy(bf16[1,23,128,128]{3,2,1,0:T(8,128)(2,1)} %slice.105) | data formatting | bytes 1507328
  15.2 1.4 %gather_fusion.1 = bf16[16,128,128]{2,1,0:T(8,128)(2,1)} fusion(bf16[24,128,128]{2,1,0:T(8,128)(2,1)S(1)} %bitcast.80, s32[1024]{0:T(1024)S(1)} %pad_clamp_fusion), kind=kCustom, calls=%fused_computation.1 | custom fusion | bytes 1048640 | tf_op jit(solution)/shard_map/gather | solution.py:58
  16.8 1.0 copy-done.4
  18.9 1.4 %fusion.1 = bf16[24,128,128]{2,1,0:T(8,128)(2,1)} fusion(f32[24,128,128]{2,1,0:T(8,128)S(1)} %fusion.7, f32[24,128,128]{1,2,0:T(8,128)S(1)} %fusion.5, bf16[24,128,128]{2,1,0:T(8,128)(2,1)S(1)} %bitcast.84, bf16[23,128,128]{1,2,0:T(8,128)(2,1)S(1)} %bitcast.85, bf16[1,128,128]{1,2,0:T(8,128)(2,1)S(1)} %bitcast.88), kind=kOutput, calls=%fused_computation.5 | convolution fusion | flops 102236160 | bytes 5505024 | tf_op jit(solution)/shard_map/bji,bjk->bik/dot_general | solution.py:54
  20.3 1.9 %gather_fusion = bf16[16,128,128]{2,1,0:T(8,128)(2,1)S(1)} fusion(bf16[24,128,128]{2,1,0:T(8,128)(2,1)} %fusion.1, s32[1024]{0:T(1024)S(1)} %pad_clamp_fusion), kind=kCustom, calls=%fused_computation | custom fusion | bytes 1048640 | tf_op jit(solution)/shard_map/gather | solution.py:59
  22.2 8.6 %collective-permute-start.3 = (bf16[2,128,128]{2,1,0:T(8,128)(2,1)S(1)}, bf16[2,128,128]{2,1,0:T(8,128)(2,1)S(1)}, u32[]{:S(2)}, u32[]{:S(2)}) collective-permute-start(bf16[2,128,128]{2,1,0:T(8,128)(2,1)S(1)} %get-tuple-element.33), channel_id=1, source_target_pairs={{0,68},{4,72},{8,76},{12,80},{16,84},{20,88},{24,92},{28,96},{32,1... | collective-permute-start | bytes 196616 | tf_op jit(solution)/shard_map/ppermute | solution.py:23
  30.8 4.9 %collective-permute-start.4 = (bf16[2,128,128]{2,1,0:T(8,128)(2,1)S(1)}, bf16[2,128,128]{2,1,0:T(8,128)(2,1)S(1)}, u32[]{:S(2)}, u32[]{:S(2)}) collective-permute-start(bf16[2,128,128]{2,1,0:T(8,128)(2,1)S(1)} %get-tuple-element.32), channel_id=1, source_target_pairs={{0,64},{4,68},{8,72},{12,76},{16,80},{20,84},{24,88},{28,92},{32,9... | collective-permute-start | bytes 196616 | tf_op jit(solution)/shard_map/ppermute | solution.py:23
  35.7 4.3 %collective-permute-start.5 = (bf16[2,128,128]{2,1,0:T(8,128)(2,1)S(1)}, bf16[2,128,128]{2,1,0:T(8,128)(2,1)S(1)}, u32[]{:S(2)}, u32[]{:S(2)}) collective-permute-start(bf16[2,128,128]{2,1,0:T(8,128)(2,1)S(1)} %get-tuple-element.31), channel_id=1, source_target_pairs={{0,60},{4,64},{8,68},{12,72},{16,76},{20,80},{24,84},{28,88},{32,9... | collective-permute-start | bytes 196616 | tf_op jit(solution)/shard_map/ppermute | solution.py:23
  40.0 5.5 %collective-permute-start.6 = (bf16[2,128,128]{2,1,0:T(8,128)(2,1)S(1)}, bf16[2,128,128]{2,1,0:T(8,128)(2,1)S(1)}, u32[]{:S(2)}, u32[]{:S(2)}) collective-permute-start(bf16[2,128,128]{2,1,0:T(8,128)(2,1)S(1)} %get-tuple-element.30), channel_id=1, source_target_pairs={{0,4},{4,8},{8,12},{12,16},{16,20},{20,24},{24,28},{28,32},{32,36}... | collective-permute-start | bytes 196616 | tf_op jit(solution)/shard_map/ppermute | solution.py:23
  45.5 1.9 %collective-permute-start.7 = (bf16[2,128,128]{2,1,0:T(8,128)(2,1)S(1)}, bf16[2,128,128]{2,1,0:T(8,128)(2,1)S(1)}, u32[]{:S(2)}, u32[]{:S(2)}) collective-permute-start(bf16[2,128,128]{2,1,0:T(8,128)(2,1)S(1)} %get-tuple-element.29), channel_id=1, source_target_pairs={{4,0},{8,4},{12,8},{16,12},{20,16},{24,20},{28,24},{32,28},{36,32}... | collective-permute-start | bytes 196616 | tf_op jit(solution)/shard_map/ppermute | solution.py:23
  47.9 3.6 %collective-permute-start.8 = (bf16[2,128,128]{2,1,0:T(8,128)(2,1)S(1)}, bf16[2,128,128]{2,1,0:T(8,128)(2,1)S(1)}, u32[]{:S(2)}, u32[]{:S(2)}) collective-permute-start(bf16[2,128,128]{2,1,0:T(8,128)(2,1)S(1)} %get-tuple-element.28), channel_id=1, source_target_pairs={{60,0},{64,4},{68,8},{72,12},{76,16},{80,20},{84,24},{88,28},{92,3... | collective-permute-start | bytes 196616 | tf_op jit(solution)/shard_map/ppermute | solution.py:23
  51.6 1.9 %collective-permute-start.9 = (bf16[2,128,128]{2,1,0:T(8,128)(2,1)S(1)}, bf16[2,128,128]{2,1,0:T(8,128)(2,1)S(1)}, u32[]{:S(2)}, u32[]{:S(2)}) collective-permute-start(bf16[2,128,128]{2,1,0:T(8,128)(2,1)S(1)} %get-tuple-element.27), channel_id=1, source_target_pairs={{64,0},{68,4},{72,8},{76,12},{80,16},{84,20},{88,24},{92,28},{96,3... | collective-permute-start | bytes 196616 | tf_op jit(solution)/shard_map/ppermute | solution.py:23
  53.5 1.9 %collective-permute-start.10 = (bf16[2,128,128]{2,1,0:T(8,128)(2,1)S(1)}, bf16[2,128,128]{2,1,0:T(8,128)(2,1)S(1)}, u32[]{:S(2)}, u32[]{:S(2)}) collective-permute-start(bf16[2,128,128]{2,1,0:T(8,128)(2,1)S(1)} %get-tuple-element.26), channel_id=1, source_target_pairs={{68,0},{72,4},{76,8},{80,12},{84,16},{88,20},{92,24},{96,28},{100,... | collective-permute-start | bytes 196616 | tf_op jit(solution)/shard_map/ppermute | solution.py:23
  55.5 1.1 %collective-permute-done.8 = bf16[2,128,128]{2,1,0:T(8,128)(2,1)S(1)} collective-permute-done((bf16[2,128,128]{2,1,0:T(8,128)(2,1)S(1)}, bf16[2,128,128]{2,1,0:T(8,128)(2,1)S(1)}, u32[]{:S(2)}, u32[]{:S(2)}) %collective-permute-start.8) | collective-permute-done | bytes 65568 | tf_op jit(solution)/shard_map/ppermute | solution.py:23
  56.6 4.8 %collective-permute-done.9 = bf16[2,128,128]{2,1,0:T(8,128)(2,1)S(1)} collective-permute-done((bf16[2,128,128]{2,1,0:T(8,128)(2,1)S(1)}, bf16[2,128,128]{2,1,0:T(8,128)(2,1)S(1)}, u32[]{:S(2)}, u32[]{:S(2)}) %collective-permute-start.9) | collective-permute-done | bytes 65568 | tf_op jit(solution)/shard_map/ppermute | solution.py:23
  61.4 3.4 %collective-permute-done.10 = bf16[2,128,128]{2,1,0:T(8,128)(2,1)S(1)} collective-permute-done((bf16[2,128,128]{2,1,0:T(8,128)(2,1)S(1)}, bf16[2,128,128]{2,1,0:T(8,128)(2,1)S(1)}, u32[]{:S(2)}, u32[]{:S(2)}) %collective-permute-start.10) | collective-permute-done | bytes 65568 | tf_op jit(solution)/shard_map/ppermute | solution.py:23
  65.2 1.6 %constant_dynamic-slice_fusion.1 = (f32[32,1152]{0,1:T(8,128)S(1)}, f32[32,1152]{0,1:T(8,128)S(1)}, f32[32,1152]{0,1:T(8,128)S(1)}, f32[32,1152]{0,1:T(8,128)}, f32[32,1152]{0,1:T(8,128)S(1)}) fusion(f32[128,1152]{0,1:T(8,128)S(1)} %bitcast.78, s32[]{:T(128)S(6)} %select_n.57, s32[]{:T(128)S(6)} %select_n.55, s32[]{:T(128)S(6)} %select_n.53, ...), kind=kLoop, calls=%fused_computation.54 | loop fusion | bytes 1474580 | tf_op jit(solution)/shard_map/dynamic_slice | solution.py:85
  66.9 1.3 %copy.65 = f32[32,1152]{1,0:T(8,128)S(1)} copy(f32[32,1152]{0,1:T(8,128)} %get-tuple-element.24) | data formatting | bytes 294912
  68.8 5.1 %collective-permute-start.11 = (f32[64,1152]{1,0:T(8,128)S(1)}, f32[64,1152]{1,0:T(8,128)S(1)}, u32[]{:S(2)}, u32[]{:S(2)}) collective-permute-start(f32[64,1152]{1,0:T(8,128)S(1)} %get-tuple-element.35), channel_id=1, source_target_pairs={{0,2},{1,3},{2,0},{3,1},{4,6},{5,7},{6,4},{7,5},{8,10},{9,11},{10,... | collective-permute-start | bytes 884744 | tf_op jit(solution)/shard_map/ppermute | solution.py:92
  74.1 3.5 %collective-permute-start.12 = (f32[64,1152]{1,0:T(8,128)S(1)}, f32[64,1152]{1,0:T(8,128)S(1)}, u32[]{:S(2)}, u32[]{:S(2)}) collective-permute-start(f32[64,1152]{1,0:T(8,128)S(1)} %get-tuple-element.36), channel_id=1, source_target_pairs={{0,1},{1,2},{2,3},{3,0},{4,5},{5,6},{6,7},{7,4},{8,9},{9,10},{10,1... | collective-permute-start | bytes 884744 | tf_op jit(solution)/shard_map/ppermute | solution.py:92
  77.6 1.9 %collective-permute-start.13 = (f32[64,1152]{1,0:T(8,128)S(1)}, f32[64,1152]{1,0:T(8,128)S(1)}, u32[]{:S(2)}, u32[]{:S(2)}) collective-permute-start(f32[64,1152]{1,0:T(8,128)S(1)} %get-tuple-element.34), channel_id=1, source_target_pairs={{0,3},{1,0},{2,1},{3,2},{4,7},{5,4},{6,5},{7,6},{8,11},{9,8},{10,9... | collective-permute-start | bytes 884744 | tf_op jit(solution)/shard_map/ppermute | solution.py:92
  80.7 6.1 %collective-permute-done.12 = f32[64,1152]{1,0:T(8,128)S(1)} collective-permute-done((f32[64,1152]{1,0:T(8,128)S(1)}, f32[64,1152]{1,0:T(8,128)S(1)}, u32[]{:S(2)}, u32[]{:S(2)}) %collective-permute-start.12) | collective-permute-done | bytes 294944 | tf_op jit(solution)/shard_map/ppermute | solution.py:92
  87.0 2.8 %collective-permute-done.13 = f32[64,1152]{1,0:T(8,128)S(1)} collective-permute-done((f32[64,1152]{1,0:T(8,128)S(1)}, f32[64,1152]{1,0:T(8,128)S(1)}, u32[]{:S(2)}, u32[]{:S(2)}) %collective-permute-start.13) | collective-permute-done | bytes 294944 | tf_op jit(solution)/shard_map/ppermute | solution.py:92
  90.4 2.9 %cholesky.16 = f32[32,32]{1,0:T(8,128)S(1)} custom-call(f32[32,32]{1,0:T(8,128)S(1)} %fusion.17), custom_call_target="Cholesky" | custom-call | tf_op jit(solution)/shard_map/jit(cholesky)/cholesky | solution.py:100
  94.7 2.4 %custom-call.10 = f32[1,32,32]{1,2,0:T(8,128)S(1)} custom-call(f32[1,32,32]{2,1,0:T(8,128)S(1)} %fusion.12), custom_call_target="InvertDiagBlocksLowerTriangular" | custom-call | tf_op jit(solution)/shard_map/jit(_solve_triangular)/triangular_solve | solution.py:103
  97.1 0.9 fusion.13
  98.2 1.1 %convolution_subtract_fusion = f32[32,1152]{0,1:T(8,128)S(1)} fusion(f32[32,32]{1,0:T(8,128)S(1)} %fusion.15, f32[32,1152]{1,0:T(8,128)S(1)} %fusion.13, f32[64,1152]{0,1:T(8,128)S(1)} %add_add_fusion), kind=kOutput, calls=%fused_computation.2 | convolution fusion | flops 14192640 | bytes 446464 | tf_op jit(solution)/shard_map/dot_general | solution.py:104
  (68 shorter events, 11.3 us)
Async XLA Ops:
  0.6 9.0 %copy-start = (bf16[1,24,128,128]{3,2,1,0:T(8,128)(2,1)S(1)}, bf16[1,24,128,128]{3,2,1,0:T(8,128)(2,1)}, u32[]{:S(2)}) copy-start(bf16[1,24,128,128]{3,2,1,0:T(8,128)(2,1)} %param.7) | copy-start | bytes 2359300
  1.5 15.2 %collective-permute-start.2 = (bf16[128,128]{1,0:T(8,128)(2,1)S(1)}, bf16[128,128]{1,0:T(8,128)(2,1)S(1)}, u32[]{:S(2)}, u32[]{:S(2)}) collective-permute-start(bf16[128,128]{1,0:T(8,128)(2,1)S(1)} %get-tuple-element.17), channel_id=1, source_target_pairs={{0,1},{1,2},{2,3},{4,5},{5,6},{6,7},{8,9},{9,10},{10,11},{12,13},{... | collective-permute-start | bytes 98312 | tf_op jit(solution)/shard_map/ppermute | solution.py:12
  2.8 13.9 %collective-permute-start = (bf16[128,128]{1,0:T(8,128)(2,1)S(1)}, bf16[128,128]{1,0:T(8,128)(2,1)S(1)}, u32[]{:S(2)}, u32[]{:S(2)}) collective-permute-start(bf16[128,128]{1,0:T(8,128)(2,1)S(1)} %get-tuple-element.18), channel_id=1, source_target_pairs={{1,0},{2,1},{3,2},{5,4},{6,5},{7,6},{9,8},{10,9},{11,10},{13,12},{... | collective-permute-start | bytes 98312 | tf_op jit(solution)/shard_map/ppermute | solution.py:15
  7.7 10.5 %collective-permute-start.1 = (bf16[128,128]{0,1:T(8,128)(2,1)S(1)}, bf16[128,128]{0,1:T(8,128)(2,1)S(1)}, u32[]{:S(2)}, u32[]{:S(2)}) collective-permute-start(bf16[128,128]{0,1:T(8,128)(2,1)S(1)} %bitcast.89), channel_id=1, source_target_pairs={{0,1},{1,2},{2,3},{4,5},{5,6},{6,7},{8,9},{9,10},{10,11},{12,13},{... | collective-permute-start | bytes 98312 | tf_op jit(solution)/shard_map/ppermute | solution.py:23
  9.6 1.6 %copy-start.7 = (s32[1,8]{1,0:T(1,128)S(1)}, s32[1,8]{1,0:T(1,128)}, u32[]{:S(2)}) copy-start(s32[1,8]{1,0:T(1,128)} %param.10) | copy-start | bytes 100
  9.6 1.7 %copy-start.3 = (bf16[1,24,128,128]{3,2,1,0:T(8,128)(2,1)S(1)}, bf16[1,24,128,128]{3,2,1,0:T(8,128)(2,1)}, u32[]{:S(2)}) copy-start(bf16[1,24,128,128]{3,2,1,0:T(8,128)(2,1)} %param.8) | copy-start | bytes 2359300
  11.2 4.0 %copy-start.1 = (bf16[1,3072,128]{2,1,0:T(8,128)(2,1)S(1)}, bf16[1,3072,128]{2,1,0:T(8,128)(2,1)}, u32[]{:S(2)}) copy-start(bf16[1,3072,128]{2,1,0:T(8,128)(2,1)} %param.6) | copy-start | bytes 2359300
  16.6 1.1 %copy-start.4 = (bf16[1,24,128,128]{3,2,1,0:T(8,128)(2,1)S(1)}, bf16[1,24,128,128]{3,2,1,0:T(8,128)(2,1)}, u32[]{:S(2)}) copy-start(bf16[1,24,128,128]{3,2,1,0:T(8,128)(2,1)} %param.8) | copy-start | bytes 2359300
  17.8 1.1 %copy-start.5 = (bf16[1,23,128,128]{2,3,1,0:T(8,128)(2,1)S(1)}, bf16[1,23,128,128]{2,3,1,0:T(8,128)(2,1)}, u32[]{:S(2)}) copy-start(bf16[1,23,128,128]{2,3,1,0:T(8,128)(2,1)} %copy.63) | copy-start | bytes 2260996
  20.3 27.2 %copy-start.2 = (bf16[24,128,128]{2,1,0:T(8,128)(2,1)S(1)}, bf16[24,128,128]{2,1,0:T(8,128)(2,1)}, u32[]{:S(2)}) copy-start(bf16[24,128,128]{2,1,0:T(8,128)(2,1)} %fusion.1) | copy-start | bytes 2359300
  22.2 42.6 %copy-start.6 = (bf16[16,128,128]{2,1,0:T(8,128)(2,1)S(1)}, bf16[16,128,128]{2,1,0:T(8,128)(2,1)}, u32[]{:S(2)}) copy-start(bf16[16,128,128]{2,1,0:T(8,128)(2,1)} %gather_fusion.1) | copy-start | bytes 1572868
  22.2 25.7 %collective-permute-start.3 = (bf16[2,128,128]{2,1,0:T(8,128)(2,1)S(1)}, bf16[2,128,128]{2,1,0:T(8,128)(2,1)S(1)}, u32[]{:S(2)}, u32[]{:S(2)}) collective-permute-start(bf16[2,128,128]{2,1,0:T(8,128)(2,1)S(1)} %get-tuple-element.33), channel_id=1, source_target_pairs={{0,68},{4,72},{8,76},{12,80},{16,84},{20,88},{24,92},{28,96},{32,1... | collective-permute-start | bytes 196616 | tf_op jit(solution)/shard_map/ppermute | solution.py:23
  30.8 20.7 %collective-permute-start.4 = (bf16[2,128,128]{2,1,0:T(8,128)(2,1)S(1)}, bf16[2,128,128]{2,1,0:T(8,128)(2,1)S(1)}, u32[]{:S(2)}, u32[]{:S(2)}) collective-permute-start(bf16[2,128,128]{2,1,0:T(8,128)(2,1)S(1)} %get-tuple-element.32), channel_id=1, source_target_pairs={{0,64},{4,68},{8,72},{12,76},{16,80},{20,84},{24,88},{28,92},{32,9... | collective-permute-start | bytes 196616 | tf_op jit(solution)/shard_map/ppermute | solution.py:23
  35.7 17.8 %collective-permute-start.5 = (bf16[2,128,128]{2,1,0:T(8,128)(2,1)S(1)}, bf16[2,128,128]{2,1,0:T(8,128)(2,1)S(1)}, u32[]{:S(2)}, u32[]{:S(2)}) collective-permute-start(bf16[2,128,128]{2,1,0:T(8,128)(2,1)S(1)} %get-tuple-element.31), channel_id=1, source_target_pairs={{0,60},{4,64},{8,68},{12,72},{16,76},{20,80},{24,84},{28,88},{32,9... | collective-permute-start | bytes 196616 | tf_op jit(solution)/shard_map/ppermute | solution.py:23
  40.0 15.5 %collective-permute-start.6 = (bf16[2,128,128]{2,1,0:T(8,128)(2,1)S(1)}, bf16[2,128,128]{2,1,0:T(8,128)(2,1)S(1)}, u32[]{:S(2)}, u32[]{:S(2)}) collective-permute-start(bf16[2,128,128]{2,1,0:T(8,128)(2,1)S(1)} %get-tuple-element.30), channel_id=1, source_target_pairs={{0,4},{4,8},{8,12},{12,16},{16,20},{20,24},{24,28},{28,32},{32,36}... | collective-permute-start | bytes 196616 | tf_op jit(solution)/shard_map/ppermute | solution.py:23
  45.5 10.0 %collective-permute-start.7 = (bf16[2,128,128]{2,1,0:T(8,128)(2,1)S(1)}, bf16[2,128,128]{2,1,0:T(8,128)(2,1)S(1)}, u32[]{:S(2)}, u32[]{:S(2)}) collective-permute-start(bf16[2,128,128]{2,1,0:T(8,128)(2,1)S(1)} %get-tuple-element.29), channel_id=1, source_target_pairs={{4,0},{8,4},{12,8},{16,12},{20,16},{24,20},{28,24},{32,28},{36,32}... | collective-permute-start | bytes 196616 | tf_op jit(solution)/shard_map/ppermute | solution.py:23
  47.9 8.7 %collective-permute-start.8 = (bf16[2,128,128]{2,1,0:T(8,128)(2,1)S(1)}, bf16[2,128,128]{2,1,0:T(8,128)(2,1)S(1)}, u32[]{:S(2)}, u32[]{:S(2)}) collective-permute-start(bf16[2,128,128]{2,1,0:T(8,128)(2,1)S(1)} %get-tuple-element.28), channel_id=1, source_target_pairs={{60,0},{64,4},{68,8},{72,12},{76,16},{80,20},{84,24},{88,28},{92,3... | collective-permute-start | bytes 196616 | tf_op jit(solution)/shard_map/ppermute | solution.py:23
  51.6 9.8 %collective-permute-start.9 = (bf16[2,128,128]{2,1,0:T(8,128)(2,1)S(1)}, bf16[2,128,128]{2,1,0:T(8,128)(2,1)S(1)}, u32[]{:S(2)}, u32[]{:S(2)}) collective-permute-start(bf16[2,128,128]{2,1,0:T(8,128)(2,1)S(1)} %get-tuple-element.27), channel_id=1, source_target_pairs={{64,0},{68,4},{72,8},{76,12},{80,16},{84,20},{88,24},{92,28},{96,3... | collective-permute-start | bytes 196616 | tf_op jit(solution)/shard_map/ppermute | solution.py:23
  53.5 11.3 %collective-permute-start.10 = (bf16[2,128,128]{2,1,0:T(8,128)(2,1)S(1)}, bf16[2,128,128]{2,1,0:T(8,128)(2,1)S(1)}, u32[]{:S(2)}, u32[]{:S(2)}) collective-permute-start(bf16[2,128,128]{2,1,0:T(8,128)(2,1)S(1)} %get-tuple-element.26), channel_id=1, source_target_pairs={{68,0},{72,4},{76,8},{80,12},{84,16},{88,20},{92,24},{96,28},{100,... | collective-permute-start | bytes 196616 | tf_op jit(solution)/shard_map/ppermute | solution.py:23
  68.8 11.6 %collective-permute-start.11 = (f32[64,1152]{1,0:T(8,128)S(1)}, f32[64,1152]{1,0:T(8,128)S(1)}, u32[]{:S(2)}, u32[]{:S(2)}) collective-permute-start(f32[64,1152]{1,0:T(8,128)S(1)} %get-tuple-element.35), channel_id=1, source_target_pairs={{0,2},{1,3},{2,0},{3,1},{4,6},{5,7},{6,4},{7,5},{8,10},{9,11},{10,... | collective-permute-start | bytes 884744 | tf_op jit(solution)/shard_map/ppermute | solution.py:92
  74.1 12.7 %collective-permute-start.12 = (f32[64,1152]{1,0:T(8,128)S(1)}, f32[64,1152]{1,0:T(8,128)S(1)}, u32[]{:S(2)}, u32[]{:S(2)}) collective-permute-start(f32[64,1152]{1,0:T(8,128)S(1)} %get-tuple-element.36), channel_id=1, source_target_pairs={{0,1},{1,2},{2,3},{3,0},{4,5},{5,6},{6,7},{7,4},{8,9},{9,10},{10,1... | collective-permute-start | bytes 884744 | tf_op jit(solution)/shard_map/ppermute | solution.py:92
  77.6 12.1 %collective-permute-start.13 = (f32[64,1152]{1,0:T(8,128)S(1)}, f32[64,1152]{1,0:T(8,128)S(1)}, u32[]{:S(2)}, u32[]{:S(2)}) collective-permute-start(f32[64,1152]{1,0:T(8,128)S(1)} %get-tuple-element.34), channel_id=1, source_target_pairs={{0,3},{1,0},{2,1},{3,2},{4,7},{5,4},{6,5},{7,6},{8,11},{9,8},{10,9... | collective-permute-start | bytes 884744 | tf_op jit(solution)/shard_map/ppermute | solution.py:92

commit v2 on v1

--- a/solution.py
+++ b/solution.py
@@ -43,10 +43,13 @@
     coarse_width = local_rows.shape[1]
     slot_count = pair_counts.shape[1]
     per_slot = tile_blocks.shape[2] // slot_count
-    padded = padded_2(local_rows, (("crow", 0),), tile_rows)
-    stacked = padded.reshape(blocks_here + 2, tile_rows, coarse_width)
-    centre = stacked[1:-1]
-    previous_upper = shifted(upper_op[0, blocks_here - 1], "crow", 1)
+    forward_pair = shifted(
+        jnp.stack([local_rows[-tile_rows:], upper_op[0, blocks_here - 1]]), "crow", 1
+    )
+    next_rows = shifted(local_rows[:tile_rows], "crow", -1)
+    centre = local_rows.reshape(blocks_here, tile_rows, coarse_width)
+    stacked = jnp.concatenate([forward_pair[:1], centre, next_rows[None]], 0)
+    previous_upper = forward_pair[1]
     lower_blocks = jnp.concatenate([previous_upper[None], upper_op[0, :-1]], 0)
     product = (
         jnp.einsum("bij,bjk->bik", diag_op[0], centre, preferred_element_type=jnp.float32)
@@ -80,20 +83,20 @@
         coarse_width, (slot_count + 1) * coarse_width
     )
     pivot_partial = lax.dynamic_slice_in_dim(whole, owner_index * row_share, row_share, 0)
-
-    def payload(target):
-        rows = lax.dynamic_slice_in_dim(whole, target * row_share, row_share, 0)
-        return jnp.concatenate([rows, pivot_partial], 0)
-
-    pieces = [payload(crow_place)]
-    for step in range(1, crow_count):
-        target = (crow_place + step) % crow_count
-        pairs = [(i, (i + step) % crow_count) for i in range(crow_count)]
-        pieces.append(lax.ppermute(payload(target), "crow", pairs))
+    outgoing_rows = jnp.concatenate(
+        [
+            whole.reshape(crow_count, row_share, whole.shape[1]),
+            jnp.broadcast_to(pivot_partial[None], (crow_count,) + pivot_partial.shape),
+        ],
+        1,
+    )
+    pieces = lax.all_to_all(outgoing_rows, "crow", 0, 0, tiled=True).reshape(
+        crow_count, 2 * row_share, whole.shape[1]
+    )
     if crow_count == 4:
-        total = (pieces[0] + pieces[2]) + (pieces[1] + pieces[3])
+        total = (pieces[0] + pieces[1]) + (pieces[2] + pieces[3])
     else:
-        total = sum(pieces[1:], pieces[0])
+        total = pieces.sum(0)
     own_rows = total[:row_share]
     leading = total[row_share:]
     pivot_block = lax.dynamic_slice_in_dim(leading, owner_index * row_share, row_share, 1)

time: 102 us -> 99.5 us (0.975)
  the two profiles are of different devices: /device:TPU:95 before, /device:TPU:71 now
where the time goes in v2:
time: 99.5 us; the launch traced here: 98.8 us
  starting transfers between devices  42.2 us (42%)
  waiting for transfers between devices  25.7 us (26%)
  local copies, waits for them, and re-layouts  11.6 us (12%)
  matrix products  8.95 us (9%)
  other arithmetic  8.72 us (9%)
  between operations  1.64 us (2%)
    ppermute x10, starting transfers between devices, shifted(): lax.ppermute(value, axis, [(source, source + steps) for source in range(i...  38 us
    all_to_all x1, waiting for transfers between devices, per_device(): lax.all_to_all(outgoing_rows, 'crow', 0, 0, tiled=True)  16.5 us
    ppermute x10, waiting for transfers between devices, shifted(): lax.ppermute(value, axis, [(source, source + steps) for source in range(i...  9.23 us
    all_to_all x1, starting transfers between devices, per_device(): lax.all_to_all(outgoing_rows, 'crow', 0, 0, tiled=True)  4.19 us
    another operation x3, other arithmetic, per_device(): factor = jnp.linalg.cholesky(pivot_block)  3.6 us
    another operation x2, other arithmetic, per_device(): jax.scipy.linalg.solve_triangular(factor, columns.T, lower=True)  3.09 us
    unnamed x21, local copies, waits for them, and re-layouts  3.08 us
    dot_general x1, matrix products, per_device(): jnp.einsum('bji,bjk->bik', lower_blocks, stacked[:-2], preferred_element_...  3.01 us
  transfers between devices with their start and end apart: 11, of which 4 were waited for; matrix products, arithmetic and copies ran while one was open for 11% of the time, Pallas kernels for 0%

profile of v2, /device:TPU:71, one launch (start us, length us, event | category | flops | bytes accessed | tf_op | source)
XLA Modules:
  0.0 98.8 jit_solution(9496606911328515033)
XLA Ops:
  0.6 0.9 fusion.29
  1.5 1.3 %collective-permute-start = (bf16[128,128]{1,0:T(8,128)(2,1)S(1)}, bf16[128,128]{1,0:T(8,128)(2,1)S(1)}, u32[]{:S(2)}, u32[]{:S(2)}) collective-permute-start(bf16[128,128]{1,0:T(8,128)(2,1)S(1)} %get-tuple-element.10), channel_id=1, source_target_pairs={{1,0},{2,1},{3,2},{5,4},{6,5},{7,6},{9,8},{10,9},{11,10},{13,12},{... | collective-permute-start | bytes 98312 | tf_op jit(solution)/shard_map/ppermute | solution.py:23
  2.8 0.8 slice_bitcast_fusion
  3.6 4.0 %collective-permute-start.1 = (bf16[2,128,128]{2,1,0:T(8,128)(2,1)S(1)}, bf16[2,128,128]{2,1,0:T(8,128)(2,1)S(1)}, u32[]{:S(2)}, u32[]{:S(2)}) collective-permute-start(bf16[2,128,128]{2,1,0:T(8,128)(2,1)S(1)} %pad_maximum_fusion.6), channel_id=1, source_target_pairs={{0,1},{1,2},{2,3},{4,5},{5,6},{6,7},{8,9},{9,10},{10,11},{12,13},{... | collective-permute-start | bytes 196616 | tf_op jit(solution)/shard_map/ppermute | solution.py:23
  7.6 0.7 fusion.25
  8.3 1.6 %fusion.10 = f32[24,128,128]{2,1,0:T(8,128)S(1)} fusion(bf16[24,128,128]{2,1,0:T(8,128)(2,1)} %bitcast.85, bf16[1,24,128,128]{3,2,1,0:T(8,128)(2,1)S(1)} %copy-done), kind=kOutput, calls=%fused_computation.19 | convolution fusion | flops 100663296 | bytes 3145728 | tf_op jit(solution)/shard_map/bij,bjk->bik/dot_general | solution.py:55
  9.9 1.0 slice.117
  10.9 2.3 %copy.28 = bf16[1,23,128,128]{2,3,1,0:T(8,128)(2,1)} copy(bf16[1,23,128,128]{3,2,1,0:T(8,128)(2,1)} %slice.117) | data formatting | bytes 1507328
  13.2 1.4 %gather_fusion.1 = bf16[16,128,128]{2,1,0:T(8,128)(2,1)} fusion(bf16[24,128,128]{2,1,0:T(8,128)(2,1)S(1)} %bitcast.86, s32[1024]{0:T(1024)S(1)} %pad_clamp_fusion), kind=kCustom, calls=%fused_computation.1 | custom fusion | bytes 1048640 | tf_op jit(solution)/shard_map/gather | solution.py:61
  15.3 2.7 %fusion.3 = f32[24,128,128]{1,2,0:T(8,128)} fusion(bf16[1,128,128]{2,1,0:T(8,128)(2,1)S(1)} %bitcast.94, bf16[24,128,128]{2,1,0:T(8,128)(2,1)S(1)} %bitcast.87, bf16[1,24,128,128]{3,2,1,0:T(8,128)(2,1)} %param.8), kind=kOutput, calls=%fused_computation.12 | convolution fusion | flops 102236160 | bytes 3178496 | tf_op jit(solution)/shard_map/bij,bjk->bik/dot_general | solution.py:56
  18.1 3.0 %fusion.1 = bf16[24,128,128]{2,1,0:T(8,128)(2,1)} fusion(f32[24,128,128]{2,1,0:T(8,128)S(1)} %fusion.10, f32[24,128,128]{1,2,0:T(8,128)} %fusion.3, bf16[24,128,128]{2,1,0:T(8,128)(2,1)S(1)} %bitcast.88, bf16[1,128,128]{2,1,0:T(8,128)(2,1)S(1)} %get-tuple-element.22, bf16[23,128,128]{1,2,0:T(8,128)(2,1)} %bitcast.91, bf16[1,128,128]{1,2,0:T(8,128)(2,1)S(1)} %copy.18), kind=kOutput, calls=%fused_computation.5 | convolution fusion | flops 102629376 | bytes 5537792 | tf_op jit(solution)/shard_map/bji,bjk->bik/dot_general | solution.py:57
  21.1 1.9 %gather_fusion = bf16[16,128,128]{2,1,0:T(8,128)(2,1)S(1)} fusion(bf16[24,128,128]{2,1,0:T(8,128)(2,1)} %fusion.1, s32[1024]{0:T(1024)S(1)} %pad_clamp_fusion), kind=kCustom, calls=%fused_computation | custom fusion | bytes 1048640 | tf_op jit(solution)/shard_map/gather | solution.py:62
  23.0 8.6 %collective-permute-start.2 = (bf16[2,128,128]{2,1,0:T(8,128)(2,1)S(1)}, bf16[2,128,128]{2,1,0:T(8,128)(2,1)S(1)}, u32[]{:S(2)}, u32[]{:S(2)}) collective-permute-start(bf16[2,128,128]{2,1,0:T(8,128)(2,1)S(1)} %get-tuple-element.18), channel_id=1, source_target_pairs={{0,68},{4,72},{8,76},{12,80},{16,84},{20,88},{24,92},{28,96},{32,1... | collective-permute-start | bytes 196616 | tf_op jit(solution)/shard_map/ppermute | solution.py:23
  31.6 4.9 %collective-permute-start.3 = (bf16[2,128,128]{2,1,0:T(8,128)(2,1)S(1)}, bf16[2,128,128]{2,1,0:T(8,128)(2,1)S(1)}, u32[]{:S(2)}, u32[]{:S(2)}) collective-permute-start(bf16[2,128,128]{2,1,0:T(8,128)(2,1)S(1)} %get-tuple-element.17), channel_id=1, source_target_pairs={{0,64},{4,68},{8,72},{12,76},{16,80},{20,84},{24,88},{28,92},{32,9... | collective-permute-start | bytes 196616 | tf_op jit(solution)/shard_map/ppermute | solution.py:23
  36.5 4.3 %collective-permute-start.4 = (bf16[2,128,128]{2,1,0:T(8,128)(2,1)S(1)}, bf16[2,128,128]{2,1,0:T(8,128)(2,1)S(1)}, u32[]{:S(2)}, u32[]{:S(2)}) collective-permute-start(bf16[2,128,128]{2,1,0:T(8,128)(2,1)S(1)} %get-tuple-element.16), channel_id=1, source_target_pairs={{0,60},{4,64},{8,68},{12,72},{16,76},{20,80},{24,84},{28,88},{32,9... | collective-permute-start | bytes 196616 | tf_op jit(solution)/shard_map/ppermute | solution.py:23
  40.8 5.5 %collective-permute-start.5 = (bf16[2,128,128]{2,1,0:T(8,128)(2,1)S(1)}, bf16[2,128,128]{2,1,0:T(8,128)(2,1)S(1)}, u32[]{:S(2)}, u32[]{:S(2)}) collective-permute-start(bf16[2,128,128]{2,1,0:T(8,128)(2,1)S(1)} %get-tuple-element.15), channel_id=1, source_target_pairs={{0,4},{4,8},{8,12},{12,16},{16,20},{20,24},{24,28},{28,32},{32,36}... | collective-permute-start | bytes 196616 | tf_op jit(solution)/shard_map/ppermute | solution.py:23
  46.3 1.9 %collective-permute-start.6 = (bf16[2,128,128]{2,1,0:T(8,128)(2,1)S(1)}, bf16[2,128,128]{2,1,0:T(8,128)(2,1)S(1)}, u32[]{:S(2)}, u32[]{:S(2)}) collective-permute-start(bf16[2,128,128]{2,1,0:T(8,128)(2,1)S(1)} %get-tuple-element.14), channel_id=1, source_target_pairs={{4,0},{8,4},{12,8},{16,12},{20,16},{24,20},{28,24},{32,28},{36,32}... | collective-permute-start | bytes 196616 | tf_op jit(solution)/shard_map/ppermute | solution.py:23
  48.7 3.6 %collective-permute-start.7 = (bf16[2,128,128]{2,1,0:T(8,128)(2,1)S(1)}, bf16[2,128,128]{2,1,0:T(8,128)(2,1)S(1)}, u32[]{:S(2)}, u32[]{:S(2)}) collective-permute-start(bf16[2,128,128]{2,1,0:T(8,128)(2,1)S(1)} %get-tuple-element.13), channel_id=1, source_target_pairs={{60,0},{64,4},{68,8},{72,12},{76,16},{80,20},{84,24},{88,28},{92,3... | collective-permute-start | bytes 196616 | tf_op jit(solution)/shard_map/ppermute | solution.py:23
  52.4 1.9 %collective-permute-start.8 = (bf16[2,128,128]{2,1,0:T(8,128)(2,1)S(1)}, bf16[2,128,128]{2,1,0:T(8,128)(2,1)S(1)}, u32[]{:S(2)}, u32[]{:S(2)}) collective-permute-start(bf16[2,128,128]{2,1,0:T(8,128)(2,1)S(1)} %get-tuple-element.12), channel_id=1, source_target_pairs={{64,0},{68,4},{72,8},{76,12},{80,16},{84,20},{88,24},{92,28},{96,3... | collective-permute-start | bytes 196616 | tf_op jit(solution)/shard_map/ppermute | solution.py:23
  54.3 1.9 %collective-permute-start.9 = (bf16[2,128,128]{2,1,0:T(8,128)(2,1)S(1)}, bf16[2,128,128]{2,1,0:T(8,128)(2,1)S(1)}, u32[]{:S(2)}, u32[]{:S(2)}) collective-permute-start(bf16[2,128,128]{2,1,0:T(8,128)(2,1)S(1)} %get-tuple-element.11), channel_id=1, source_target_pairs={{68,0},{72,4},{76,8},{80,12},{84,16},{88,20},{92,24},{96,28},{100,... | collective-permute-start | bytes 196616 | tf_op jit(solution)/shard_map/ppermute | solution.py:23
  56.3 1.1 %collective-permute-done.7 = bf16[2,128,128]{2,1,0:T(8,128)(2,1)S(1)} collective-permute-done((bf16[2,128,128]{2,1,0:T(8,128)(2,1)S(1)}, bf16[2,128,128]{2,1,0:T(8,128)(2,1)S(1)}, u32[]{:S(2)}, u32[]{:S(2)}) %collective-permute-start.7) | collective-permute-done | bytes 65568 | tf_op jit(solution)/shard_map/ppermute | solution.py:23
  57.4 4.8 %collective-permute-done.8 = bf16[2,128,128]{2,1,0:T(8,128)(2,1)S(1)} collective-permute-done((bf16[2,128,128]{2,1,0:T(8,128)(2,1)S(1)}, bf16[2,128,128]{2,1,0:T(8,128)(2,1)S(1)}, u32[]{:S(2)}, u32[]{:S(2)}) %collective-permute-start.8) | collective-permute-done | bytes 65568 | tf_op jit(solution)/shard_map/ppermute | solution.py:23
  62.2 3.4 %collective-permute-done.9 = bf16[2,128,128]{2,1,0:T(8,128)(2,1)S(1)} collective-permute-done((bf16[2,128,128]{2,1,0:T(8,128)(2,1)S(1)}, bf16[2,128,128]{2,1,0:T(8,128)(2,1)S(1)}, u32[]{:S(2)}, u32[]{:S(2)}) %collective-permute-start.9) | collective-permute-done | bytes 65568 | tf_op jit(solution)/shard_map/ppermute | solution.py:23
  67.1 1.1 %pad_maximum_fusion = f32[4,64,1152]{2,1,0:T(8,128)} fusion(f32[4,32,1152]{2,1,0:T(8,128)S(1)} %broadcast_in_dim.9, f32[4,32,1152]{2,1,0:T(8,128)S(1)} %reshape_reshape.3), kind=kLoop, calls=%fused_computation.7 | loop fusion | flops 294912 | bytes 2359296 | tf_op jit(solution)/shard_map/concatenate | solution.py:86
  68.2 4.2 %all-to-all-start = ((f32[4,64,1152]{2,1,0:T(8,128)}), f32[4,64,1152]{2,1,0:T(8,128)S(1)}, u32[]{:S(2)}, u32[]{:S(2)}) async-start(f32[4,64,1152]{2,1,0:T(8,128)} %pad_maximum_fusion), calls=%async_computation | async-start | bytes 2359296 | tf_op jit(solution)/shard_map/all_to_all | solution.py:93
  72.4 16.5 %all-to-all-done = f32[4,64,1152]{2,1,0:T(8,128)S(1)} async-done(((f32[4,64,1152]{2,1,0:T(8,128)}), f32[4,64,1152]{2,1,0:T(8,128)S(1)}, u32[]{:S(2)}, u32[]{:S(2)}) %all-to-all-start) | async-done | bytes 1179680 | tf_op jit(solution)/shard_map/all_to_all | solution.py:93
  89.2 2.9 %cholesky.16 = f32[32,32]{1,0:T(8,128)S(1)} custom-call(f32[32,32]{1,0:T(8,128)S(1)} %fusion.18), custom_call_target="Cholesky" | custom-call | tf_op jit(solution)/shard_map/jit(cholesky)/cholesky | solution.py:103
  92.2 0.6 compare_reduce_fusion
  92.8 0.7 fusion.17
  93.5 2.4 %custom-call.10 = f32[1,32,32]{1,2,0:T(8,128)S(1)} custom-call(f32[1,32,32]{2,1,0:T(8,128)S(1)} %fusion.17), custom_call_target="InvertDiagBlocksLowerTriangular" | custom-call | tf_op jit(solution)/shard_map/jit(_solve_triangular)/triangular_solve | solution.py:106
  96.9 0.7 slice.159
  98.2 0.7 copy.24
  (52 shorter events, 4.2 us)
Async XLA Ops:
  0.6 7.6 %copy-start = (bf16[1,24,128,128]{3,2,1,0:T(8,128)(2,1)S(1)}, bf16[1,24,128,128]{3,2,1,0:T(8,128)(2,1)}, u32[]{:S(2)}) copy-start(bf16[1,24,128,128]{3,2,1,0:T(8,128)(2,1)} %param.7) | copy-start | bytes 2359300
  1.5 13.8 %collective-permute-start = (bf16[128,128]{1,0:T(8,128)(2,1)S(1)}, bf16[128,128]{1,0:T(8,128)(2,1)S(1)}, u32[]{:S(2)}, u32[]{:S(2)}) collective-permute-start(bf16[128,128]{1,0:T(8,128)(2,1)S(1)} %get-tuple-element.10), channel_id=1, source_target_pairs={{1,0},{2,1},{3,2},{5,4},{6,5},{7,6},{9,8},{10,9},{11,10},{13,12},{... | collective-permute-start | bytes 98312 | tf_op jit(solution)/shard_map/ppermute | solution.py:23
  3.6 14.4 %collective-permute-start.1 = (bf16[2,128,128]{2,1,0:T(8,128)(2,1)S(1)}, bf16[2,128,128]{2,1,0:T(8,128)(2,1)S(1)}, u32[]{:S(2)}, u32[]{:S(2)}) collective-permute-start(bf16[2,128,128]{2,1,0:T(8,128)(2,1)S(1)} %pad_maximum_fusion.6), channel_id=1, source_target_pairs={{0,1},{1,2},{2,3},{4,5},{5,6},{6,7},{8,9},{9,10},{10,11},{12,13},{... | collective-permute-start | bytes 196616 | tf_op jit(solution)/shard_map/ppermute | solution.py:23
  8.2 1.6 %copy-start.5 = (s32[1,8]{1,0:T(1,128)S(1)}, s32[1,8]{1,0:T(1,128)}, u32[]{:S(2)}) copy-start(s32[1,8]{1,0:T(1,128)} %param.10) | copy-start | bytes 100
  8.2 1.7 %copy-start.3 = (bf16[1,24,128,128]{3,2,1,0:T(8,128)(2,1)S(1)}, bf16[1,24,128,128]{3,2,1,0:T(8,128)(2,1)}, u32[]{:S(2)}) copy-start(bf16[1,24,128,128]{3,2,1,0:T(8,128)(2,1)} %param.8) | copy-start | bytes 2359300
  9.8 3.4 %copy-start.1 = (bf16[1,3072,128]{2,1,0:T(8,128)(2,1)S(1)}, bf16[1,3072,128]{2,1,0:T(8,128)(2,1)}, u32[]{:S(2)}) copy-start(bf16[1,3072,128]{2,1,0:T(8,128)(2,1)} %param.6) | copy-start | bytes 2359300
  21.1 27.2 %copy-start.2 = (bf16[24,128,128]{2,1,0:T(8,128)(2,1)S(1)}, bf16[24,128,128]{2,1,0:T(8,128)(2,1)}, u32[]{:S(2)}) copy-start(bf16[24,128,128]{2,1,0:T(8,128)(2,1)} %fusion.1) | copy-start | bytes 2359300
  23.0 42.6 %copy-start.4 = (bf16[16,128,128]{2,1,0:T(8,128)(2,1)S(1)}, bf16[16,128,128]{2,1,0:T(8,128)(2,1)}, u32[]{:S(2)}) copy-start(bf16[16,128,128]{2,1,0:T(8,128)(2,1)} %gather_fusion.1) | copy-start | bytes 1572868
  23.0 25.7 %collective-permute-start.2 = (bf16[2,128,128]{2,1,0:T(8,128)(2,1)S(1)}, bf16[2,128,128]{2,1,0:T(8,128)(2,1)S(1)}, u32[]{:S(2)}, u32[]{:S(2)}) collective-permute-start(bf16[2,128,128]{2,1,0:T(8,128)(2,1)S(1)} %get-tuple-element.18), channel_id=1, source_target_pairs={{0,68},{4,72},{8,76},{12,80},{16,84},{20,88},{24,92},{28,96},{32,1... | collective-permute-start | bytes 196616 | tf_op jit(solution)/shard_map/ppermute | solution.py:23
  31.6 20.7 %collective-permute-start.3 = (bf16[2,128,128]{2,1,0:T(8,128)(2,1)S(1)}, bf16[2,128,128]{2,1,0:T(8,128)(2,1)S(1)}, u32[]{:S(2)}, u32[]{:S(2)}) collective-permute-start(bf16[2,128,128]{2,1,0:T(8,128)(2,1)S(1)} %get-tuple-element.17), channel_id=1, source_target_pairs={{0,64},{4,68},{8,72},{12,76},{16,80},{20,84},{24,88},{28,92},{32,9... | collective-permute-start | bytes 196616 | tf_op jit(solution)/shard_map/ppermute | solution.py:23
  36.5 17.8 %collective-permute-start.4 = (bf16[2,128,128]{2,1,0:T(8,128)(2,1)S(1)}, bf16[2,128,128]{2,1,0:T(8,128)(2,1)S(1)}, u32[]{:S(2)}, u32[]{:S(2)}) collective-permute-start(bf16[2,128,128]{2,1,0:T(8,128)(2,1)S(1)} %get-tuple-element.16), channel_id=1, source_target_pairs={{0,60},{4,64},{8,68},{12,72},{16,76},{20,80},{24,84},{28,88},{32,9... | collective-permute-start | bytes 196616 | tf_op jit(solution)/shard_map/ppermute | solution.py:23
  40.8 15.5 %collective-permute-start.5 = (bf16[2,128,128]{2,1,0:T(8,128)(2,1)S(1)}, bf16[2,128,128]{2,1,0:T(8,128)(2,1)S(1)}, u32[]{:S(2)}, u32[]{:S(2)}) collective-permute-start(bf16[2,128,128]{2,1,0:T(8,128)(2,1)S(1)} %get-tuple-element.15), channel_id=1, source_target_pairs={{0,4},{4,8},{8,12},{12,16},{16,20},{20,24},{24,28},{28,32},{32,36}... | collective-permute-start | bytes 196616 | tf_op jit(solution)/shard_map/ppermute | solution.py:23
  46.3 10.0 %collective-permute-start.6 = (bf16[2,128,128]{2,1,0:T(8,128)(2,1)S(1)}, bf16[2,128,128]{2,1,0:T(8,128)(2,1)S(1)}, u32[]{:S(2)}, u32[]{:S(2)}) collective-permute-start(bf16[2,128,128]{2,1,0:T(8,128)(2,1)S(1)} %get-tuple-element.14), channel_id=1, source_target_pairs={{4,0},{8,4},{12,8},{16,12},{20,16},{24,20},{28,24},{32,28},{36,32}... | collective-permute-start | bytes 196616 | tf_op jit(solution)/shard_map/ppermute | solution.py:23
  48.7 8.7 %collective-permute-start.7 = (bf16[2,128,128]{2,1,0:T(8,128)(2,1)S(1)}, bf16[2,128,128]{2,1,0:T(8,128)(2,1)S(1)}, u32[]{:S(2)}, u32[]{:S(2)}) collective-permute-start(bf16[2,128,128]{2,1,0:T(8,128)(2,1)S(1)} %get-tuple-element.13), channel_id=1, source_target_pairs={{60,0},{64,4},{68,8},{72,12},{76,16},{80,20},{84,24},{88,28},{92,3... | collective-permute-start | bytes 196616 | tf_op jit(solution)/shard_map/ppermute | solution.py:23
  52.4 9.8 %collective-permute-start.8 = (bf16[2,128,128]{2,1,0:T(8,128)(2,1)S(1)}, bf16[2,128,128]{2,1,0:T(8,128)(2,1)S(1)}, u32[]{:S(2)}, u32[]{:S(2)}) collective-permute-start(bf16[2,128,128]{2,1,0:T(8,128)(2,1)S(1)} %get-tuple-element.12), channel_id=1, source_target_pairs={{64,0},{68,4},{72,8},{76,12},{80,16},{84,20},{88,24},{92,28},{96,3... | collective-permute-start | bytes 196616 | tf_op jit(solution)/shard_map/ppermute | solution.py:23
  54.3 11.3 %collective-permute-start.9 = (bf16[2,128,128]{2,1,0:T(8,128)(2,1)S(1)}, bf16[2,128,128]{2,1,0:T(8,128)(2,1)S(1)}, u32[]{:S(2)}, u32[]{:S(2)}) collective-permute-start(bf16[2,128,128]{2,1,0:T(8,128)(2,1)S(1)} %get-tuple-element.11), channel_id=1, source_target_pairs={{68,0},{72,4},{76,8},{80,12},{84,16},{88,20},{92,24},{96,28},{100,... | collective-permute-start | bytes 196616 | tf_op jit(solution)/shard_map/ppermute | solution.py:23
  68.2 20.7 %all-to-all-start = ((f32[4,64,1152]{2,1,0:T(8,128)}), f32[4,64,1152]{2,1,0:T(8,128)S(1)}, u32[]{:S(2)}, u32[]{:S(2)}) async-start(f32[4,64,1152]{2,1,0:T(8,128)} %pad_maximum_fusion), calls=%async_computation | async-start | bytes 2359296 | tf_op jit(solution)/shard_map/all_to_all | solution.py:93

commit v3 on v2

--- a/solution.py
+++ b/solution.py
@@ -2,6 +2,8 @@
 import jax.numpy as jnp
 from jax import lax
 from jax.sharding import PartitionSpec as P
+from jax.experimental import pallas as pl
+from jax.experimental.pallas import tpu as pltpu
 
 
 def padded_2(block, sides, width):
@@ -32,6 +34,64 @@
     return [-across - 1, -across, -across + 1, -1, 1, across - 1, across, across + 1]
 
 
+def _ab(a, b):
+    return lax.dot_general(a, b, (((1,), (0,)), ((), ())), preferred_element_type=jnp.float32)
+
+
+def _atb(a, b):
+    return lax.dot_general(a, b, (((0,), (0,)), ((), ())), preferred_element_type=jnp.float32)
+
+
+def local_apply_kernel(
+    chosen_ref, live_ref, z_ref, zp_ref, zn_ref, d_ref, u_ref, up_ref,
+    gram_ref, out_ref, own_ref, app_ref,
+):
+    count = z_ref.shape[0]
+
+    def store(b, total, gram):
+        app = total.astype(jnp.bfloat16)
+        app_ref[b] = app
+        return gram + _atb(z_ref[b], app)
+
+    first = (_ab(d_ref[0], z_ref[0]) + _ab(u_ref[0], z_ref[1])) + _atb(up_ref[...], zp_ref[...])
+    gram = store(0, first, jnp.zeros(gram_ref.shape, jnp.float32))
+
+    def body(b, gram):
+        total = (_ab(d_ref[b], z_ref[b]) + _ab(u_ref[b], z_ref[b + 1])) + _atb(
+            u_ref[b - 1], z_ref[b - 1]
+        )
+        return store(b, total, gram)
+
+    gram = lax.fori_loop(1, count - 1, body, gram)
+    last = count - 1
+    final = (_ab(d_ref[last], z_ref[last]) + _ab(u_ref[last], zn_ref[...])) + _atb(
+        u_ref[last - 1], z_ref[last - 1]
+    )
+    gram_ref[...] = store(last, final, gram)
+    for i in range(out_ref.shape[0]):
+        block = chosen_ref[i]
+        out_ref[i] = app_ref[block]
+        own_ref[i] = jnp.where(live_ref[i] > 0, z_ref[block], jnp.zeros_like(z_ref[block]))
+
+
+def local_apply(chosen, live, centre, prev_rows, next_rows, diagonal, upper, prev_upper):
+    tiles = chosen.shape[0]
+    blocks, rows, width = centre.shape
+    vmem = pl.BlockSpec(memory_space=pltpu.VMEM)
+    smem = pl.BlockSpec(memory_space=pltpu.SMEM)
+    return pl.pallas_call(
+        local_apply_kernel,
+        out_shape=(
+            jax.ShapeDtypeStruct((width, width), jnp.float32),
+            jax.ShapeDtypeStruct((tiles, rows, width), centre.dtype),
+            jax.ShapeDtypeStruct((tiles, rows, width), centre.dtype),
+        ),
+        in_specs=[smem, smem] + [vmem] * 6,
+        out_specs=(vmem, vmem, vmem),
+        scratch_shapes=[pltpu.VMEM((blocks, rows, width), centre.dtype)],
+    )(chosen, live, centre, prev_rows, next_rows, diagonal, upper, prev_upper)
+
+
 def per_device(deflation, diag_op, upper_op, tile_blocks, pair_counts, pivot_owner):
     crow_count = lax.axis_size("crow")
     crow_place = lax.axis_index("crow")
@@ -48,34 +108,22 @@
     )
     next_rows = shifted(local_rows[:tile_rows], "crow", -1)
     centre = local_rows.reshape(blocks_here, tile_rows, coarse_width)
-    stacked = jnp.concatenate([forward_pair[:1], centre, next_rows[None]], 0)
-    previous_upper = forward_pair[1]
-    lower_blocks = jnp.concatenate([previous_upper[None], upper_op[0, :-1]], 0)
-    product = (
-        jnp.einsum("bij,bjk->bik", diag_op[0], centre, preferred_element_type=jnp.float32)
-        + jnp.einsum("bij,bjk->bik", upper_op[0], stacked[2:], preferred_element_type=jnp.float32)
-        + jnp.einsum("bji,bjk->bik", lower_blocks, stacked[:-2], preferred_element_type=jnp.float32)
+    chosen = tile_blocks[0, 0]
+    position = crow_place * per_slot + jnp.arange(per_slot, dtype=jnp.int32)
+    live = (position[None, :] < pair_counts[0][:, None]).astype(jnp.int32).reshape(-1)
+    gram_part, outgoing, own_masked = local_apply(
+        chosen, live, centre, forward_pair[0], next_rows, diag_op[0], upper_op[0], forward_pair[1]
     )
-    applied = product.astype(jnp.bfloat16)
-    chosen = tile_blocks[0, 0]
-    own_tiles = centre[chosen].reshape(slot_count, per_slot, tile_rows, coarse_width)
-    outgoing = applied[chosen].reshape(slot_count, per_slot, tile_rows, coarse_width)
-    position = crow_place * per_slot + jnp.arange(per_slot, dtype=jnp.int32)
-    live_mask = (position[None, :] < pair_counts[0][:, None]).astype(jnp.bfloat16)
-    own_masked = own_tiles * live_mask[:, :, None, None]
+    outgoing = outgoing.reshape(slot_count, per_slot, tile_rows, coarse_width)
+    own_masked = own_masked.reshape(slot_count, per_slot, tile_rows, coarse_width)
     arrived = [None] * slot_count
     for slot_index in range(slot_count):
         arrived[slot_index] = shifted(
             outgoing[slot_count - 1 - slot_index], "sub", -offsets[slot_index]
         )
     received = jnp.stack(arrived)
-    flat_vectors = centre.reshape(blocks_here * tile_rows, coarse_width)
-    flat_applied = applied.reshape(blocks_here * tile_rows, coarse_width)
     row_share = coarse_width // crow_count
     owner_index = pivot_owner[0]
-    gram_part = jnp.einsum(
-        "nr,nk->rk", flat_vectors, flat_applied, preferred_element_type=jnp.float32
-    )
     coupling = jnp.einsum(
         "jutr,jutk->rjk", own_masked, received, preferred_element_type=jnp.float32
     )

time: 99.5 us -> 103 us (1.035)
  the two profiles are of different devices: /device:TPU:71 before, /device:TPU:416 now
where the time goes in v3:
time: 103 us; the launch traced here: 102 us
  starting transfers between devices  40.1 us (39%)
  waiting for transfers between devices  31.5 us (31%)
  Pallas kernels  10.2 us (10%)
  local copies, waits for them, and re-layouts  8.76 us (9%)
  other arithmetic  8.7 us (8%)
  between operations  1.57 us (2%)
  matrix products  1.27 us (1%)
    ppermute x10, starting transfers between devices, shifted(): lax.ppermute(value, axis, [(source, source + steps) for source in range(i...  34.7 us
    ppermute x10, waiting for transfers between devices, shifted(): lax.ppermute(value, axis, [(source, source + steps) for source in range(i...  19.4 us
    all_to_all x1, waiting for transfers between devices, per_device(): lax.all_to_all(outgoing_rows, 'crow', 0, 0, tiled=True)  12.1 us
    pallas_call x1, Pallas kernels, local_apply(): pl.pallas_call(local_apply_kernel, out_shape=(jax.ShapeDtypeStruct((width...  10.2 us
    all_to_all x1, starting transfers between devices, per_device(): lax.all_to_all(outgoing_rows, 'crow', 0, 0, tiled=True)  5.37 us
    another operation x3, other arithmetic, per_device(): factor = jnp.linalg.cholesky(pivot_block)  3.6 us
    another operation x2, other arithmetic, per_device(): jax.scipy.linalg.solve_triangular(factor, columns.T, lower=True)  3.09 us
  transfers between devices with their start and end apart: 11, of which 5 were waited for; matrix products, arithmetic and copies ran while one was open for 4% of the time, Pallas kernels for 0%

profile of v3, /device:TPU:416, one launch (start us, length us, event | category | flops | bytes accessed | tf_op | source)
XLA Modules:
  0.0 102.1 jit_solution(8081990863582488643)
XLA Ops:
  0.6 0.8 slice_bitcast_fusion.2
  1.4 1.3 %collective-permute-start.1 = (bf16[128,128]{1,0:T(8,128)(2,1)S(1)}, bf16[128,128]{1,0:T(8,128)(2,1)S(1)}, u32[]{:S(2)}, u32[]{:S(2)}) collective-permute-start(bf16[128,128]{1,0:T(8,128)(2,1)S(1)} %get-tuple-element.15), channel_id=1, source_target_pairs={{1,0},{2,1},{3,2},{5,4},{6,5},{7,6},{9,8},{10,9},{11,10},{13,12},{... | collective-permute-start | bytes 98312 | tf_op jit(solution)/shard_map/ppermute | solution.py:25
  2.7 0.8 slice_bitcast_fusion.3
  3.5 4.5 %collective-permute-start = (bf16[2,128,128]{2,1,0:T(8,128)(2,1)S(1)}, bf16[2,128,128]{2,1,0:T(8,128)(2,1)S(1)}, u32[]{:S(2)}, u32[]{:S(2)}) collective-permute-start(bf16[2,128,128]{2,1,0:T(8,128)(2,1)S(1)} %pad_maximum_fusion.2), channel_id=1, source_target_pairs={{0,1},{1,2},{2,3},{4,5},{5,6},{6,7},{8,9},{9,10},{10,11},{12,13},{... | collective-permute-start | bytes 196616 | tf_op jit(solution)/shard_map/ppermute | solution.py:25
  8.0 0.7 compare_convert_fusion
  8.8 0.6 reshape.68.live_ref
  9.9 0.6 slice_bitcast_fusion
  10.6 0.6 copy-done.1
  11.2 10.2 %shard_map.85 = (f32[128,128]{1,0:T(8,128)}, bf16[16,128,128]{2,1,0:T(8,128)(2,1)}, bf16[16,128,128]{2,1,0:T(8,128)(2,1)}) custom-call(s32[16]{0:T(128)} %bitcast.73, s32[16]{0:T(128)} %reshape.68.live_ref, bf16[24,128,128]{2,1,0:T(8,128)(2,1)} %bitcast.67, bf16[128,128]{1,0:T(8,128)(2,1)} %get-tuple-element.28.zp_ref, bf16[128,128]{1,0:T(8,128)(2,1)} %copy-done.1, ...), custom_call_target="tpu_custom_call" | custom-call | tf_op jit(solution)/shard_map/pallas_call | solution.py:82
  21.4 1.2 %fusion.12 = (bf16[2,128,128]{2,1,0:T(8,128)(2,1)S(1)}, bf16[2,128,128]{2,1,0:T(8,128)(2,1)S(1)}, bf16[2,128,128]{2,1,0:T(8,128)(2,1)S(1)}, bf16[2,128,128]{2,1,...) fusion(bf16[16,128,128]{2,1,0:T(8,128)(2,1)} %get-tuple-element.7), kind=kLoop, calls=%fused_computation.41 | loop fusion | bytes 1048576 | tf_op jit(solution)/shard_map/slice | solution.py:122
  22.5 1.9 %collective-permute-start.2 = (bf16[2,128,128]{2,1,0:T(8,128)(2,1)S(1)}, bf16[2,128,128]{2,1,0:T(8,128)(2,1)S(1)}, u32[]{:S(2)}, u32[]{:S(2)}) collective-permute-start(bf16[2,128,128]{2,1,0:T(8,128)(2,1)S(1)} %get-tuple-element.24), channel_id=1, source_target_pairs={{0,68},{4,72},{8,76},{12,80},{16,84},{20,88},{24,92},{28,96},{32,1... | collective-permute-start | bytes 196616 | tf_op jit(solution)/shard_map/ppermute | solution.py:25
  25.1 0.9 copy.17
  26.0 8.8 %collective-permute-start.9 = (bf16[2,128,128]{2,1,0:T(8,128)(2,1)S(1)}, bf16[2,128,128]{2,1,0:T(8,128)(2,1)S(1)}, u32[]{:S(2)}, u32[]{:S(2)}) collective-permute-start(bf16[2,128,128]{2,1,0:T(8,128)(2,1)S(1)} %get-tuple-element.17), channel_id=1, source_target_pairs={{68,0},{72,4},{76,8},{80,12},{84,16},{88,20},{92,24},{96,28},{100,... | collective-permute-start | bytes 196616 | tf_op jit(solution)/shard_map/ppermute | solution.py:25
  34.8 3.4 %collective-permute-start.8 = (bf16[2,128,128]{2,1,0:T(8,128)(2,1)S(1)}, bf16[2,128,128]{2,1,0:T(8,128)(2,1)S(1)}, u32[]{:S(2)}, u32[]{:S(2)}) collective-permute-start(bf16[2,128,128]{2,1,0:T(8,128)(2,1)S(1)} %get-tuple-element.18), channel_id=1, source_target_pairs={{64,0},{68,4},{72,8},{76,12},{80,16},{84,20},{88,24},{92,28},{96,3... | collective-permute-start | bytes 196616 | tf_op jit(solution)/shard_map/ppermute | solution.py:25
  38.2 1.9 %collective-permute-start.7 = (bf16[2,128,128]{2,1,0:T(8,128)(2,1)S(1)}, bf16[2,128,128]{2,1,0:T(8,128)(2,1)S(1)}, u32[]{:S(2)}, u32[]{:S(2)}) collective-permute-start(bf16[2,128,128]{2,1,0:T(8,128)(2,1)S(1)} %get-tuple-element.19), channel_id=1, source_target_pairs={{60,0},{64,4},{68,8},{72,12},{76,16},{80,20},{84,24},{88,28},{92,3... | collective-permute-start | bytes 196616 | tf_op jit(solution)/shard_map/ppermute | solution.py:25
  40.1 7.0 %collective-permute-start.6 = (bf16[2,128,128]{2,1,0:T(8,128)(2,1)S(1)}, bf16[2,128,128]{2,1,0:T(8,128)(2,1)S(1)}, u32[]{:S(2)}, u32[]{:S(2)}) collective-permute-start(bf16[2,128,128]{2,1,0:T(8,128)(2,1)S(1)} %get-tuple-element.20), channel_id=1, source_target_pairs={{4,0},{8,4},{12,8},{16,12},{20,16},{24,20},{28,24},{32,28},{36,32}... | collective-permute-start | bytes 196616 | tf_op jit(solution)/shard_map/ppermute | solution.py:25
  47.1 2.2 %collective-permute-start.3 = (bf16[2,128,128]{2,1,0:T(8,128)(2,1)S(1)}, bf16[2,128,128]{2,1,0:T(8,128)(2,1)S(1)}, u32[]{:S(2)}, u32[]{:S(2)}) collective-permute-start(bf16[2,128,128]{2,1,0:T(8,128)(2,1)S(1)} %get-tuple-element.23), channel_id=1, source_target_pairs={{0,64},{4,68},{8,72},{12,76},{16,80},{20,84},{24,88},{28,92},{32,9... | collective-permute-start | bytes 196616 | tf_op jit(solution)/shard_map/ppermute | solution.py:25
  49.3 6.8 %collective-permute-done.3 = bf16[2,128,128]{2,1,0:T(8,128)(2,1)S(1)} collective-permute-done((bf16[2,128,128]{2,1,0:T(8,128)(2,1)S(1)}, bf16[2,128,128]{2,1,0:T(8,128)(2,1)S(1)}, u32[]{:S(2)}, u32[]{:S(2)}) %collective-permute-start.3) | collective-permute-done | bytes 65568 | tf_op jit(solution)/shard_map/ppermute | solution.py:25
  56.1 1.9 %collective-permute-start.4 = (bf16[2,128,128]{2,1,0:T(8,128)(2,1)S(1)}, bf16[2,128,128]{2,1,0:T(8,128)(2,1)S(1)}, u32[]{:S(2)}, u32[]{:S(2)}) collective-permute-start(bf16[2,128,128]{2,1,0:T(8,128)(2,1)S(1)} %get-tuple-element.22), channel_id=1, source_target_pairs={{0,60},{4,64},{8,68},{12,72},{16,76},{20,80},{24,84},{28,88},{32,9... | collective-permute-start | bytes 196616 | tf_op jit(solution)/shard_map/ppermute | solution.py:25
  58.0 6.3 %collective-permute-done.4 = bf16[2,128,128]{2,1,0:T(8,128)(2,1)S(1)} collective-permute-done((bf16[2,128,128]{2,1,0:T(8,128)(2,1)S(1)}, bf16[2,128,128]{2,1,0:T(8,128)(2,1)S(1)}, u32[]{:S(2)}, u32[]{:S(2)}) %collective-permute-start.4) | collective-permute-done | bytes 65568 | tf_op jit(solution)/shard_map/ppermute | solution.py:25
  64.3 1.9 %collective-permute-start.5 = (bf16[2,128,128]{2,1,0:T(8,128)(2,1)S(1)}, bf16[2,128,128]{2,1,0:T(8,128)(2,1)S(1)}, u32[]{:S(2)}, u32[]{:S(2)}) collective-permute-start(bf16[2,128,128]{2,1,0:T(8,128)(2,1)S(1)} %get-tuple-element.21), channel_id=1, source_target_pairs={{0,4},{4,8},{8,12},{12,16},{16,20},{20,24},{24,28},{28,32},{32,36}... | collective-permute-start | bytes 196616 | tf_op jit(solution)/shard_map/ppermute | solution.py:25
  66.2 5.7 %collective-permute-done.5 = bf16[2,128,128]{2,1,0:T(8,128)(2,1)S(1)} collective-permute-done((bf16[2,128,128]{2,1,0:T(8,128)(2,1)S(1)}, bf16[2,128,128]{2,1,0:T(8,128)(2,1)S(1)}, u32[]{:S(2)}, u32[]{:S(2)}) %collective-permute-start.5) | collective-permute-done | bytes 65568 | tf_op jit(solution)/shard_map/ppermute | solution.py:25
  73.6 1.1 %pad_maximum_fusion = f32[4,64,1152]{2,1,0:T(8,128)} fusion(f32[4,32,1152]{2,1,0:T(8,128)S(1)} %broadcast_in_dim.6, f32[4,32,1152]{2,1,0:T(8,128)S(1)} %reshape_reshape.3), kind=kLoop, calls=%fused_computation.2 | loop fusion | flops 294912 | bytes 2359296 | tf_op jit(solution)/shard_map/concatenate | solution.py:134
  74.7 5.4 %all-to-all-start = ((f32[4,64,1152]{2,1,0:T(8,128)}), f32[4,64,1152]{2,1,0:T(8,128)S(1)}, u32[]{:S(2)}, u32[]{:S(2)}) async-start(f32[4,64,1152]{2,1,0:T(8,128)} %pad_maximum_fusion), calls=%async_computation | async-start | bytes 2359296 | tf_op jit(solution)/shard_map/all_to_all | solution.py:141
  80.1 12.1 %all-to-all-done = f32[4,64,1152]{2,1,0:T(8,128)S(1)} async-done(((f32[4,64,1152]{2,1,0:T(8,128)}), f32[4,64,1152]{2,1,0:T(8,128)S(1)}, u32[]{:S(2)}, u32[]{:S(2)}) %all-to-all-start) | async-done | bytes 1179680 | tf_op jit(solution)/shard_map/all_to_all | solution.py:141
  92.5 2.9 %cholesky.16 = f32[32,32]{1,0:T(8,128)S(1)} custom-call(f32[32,32]{1,0:T(8,128)S(1)} %fusion.4), custom_call_target="Cholesky" | custom-call | tf_op jit(solution)/shard_map/jit(cholesky)/cholesky | solution.py:151
  95.5 0.6 compare_reduce_fusion
  96.1 0.7 fusion.3
  96.8 2.4 %custom-call.10 = f32[1,32,32]{1,2,0:T(8,128)S(1)} custom-call(f32[1,32,32]{2,1,0:T(8,128)S(1)} %fusion.3), custom_call_target="InvertDiagBlocksLowerTriangular" | custom-call | tf_op jit(solution)/shard_map/jit(_solve_triangular)/triangular_solve | solution.py:154
  100.2 0.6 slice.132
  100.8 0.7 slice.133
  101.4 0.7 copy.22
  (36 shorter events, 3.4 us)
Async XLA Ops:
  1.4 9.1 %collective-permute-start.1 = (bf16[128,128]{1,0:T(8,128)(2,1)S(1)}, bf16[128,128]{1,0:T(8,128)(2,1)S(1)}, u32[]{:S(2)}, u32[]{:S(2)}) collective-permute-start(bf16[128,128]{1,0:T(8,128)(2,1)S(1)} %get-tuple-element.15), channel_id=1, source_target_pairs={{1,0},{2,1},{3,2},{5,4},{6,5},{7,6},{9,8},{10,9},{11,10},{13,12},{... | collective-permute-start | bytes 98312 | tf_op jit(solution)/shard_map/ppermute | solution.py:25
  3.5 6.4 %collective-permute-start = (bf16[2,128,128]{2,1,0:T(8,128)(2,1)S(1)}, bf16[2,128,128]{2,1,0:T(8,128)(2,1)S(1)}, u32[]{:S(2)}, u32[]{:S(2)}) collective-permute-start(bf16[2,128,128]{2,1,0:T(8,128)(2,1)S(1)} %pad_maximum_fusion.2), channel_id=1, source_target_pairs={{0,1},{1,2},{2,3},{4,5},{5,6},{6,7},{8,9},{9,10},{10,11},{12,13},{... | collective-permute-start | bytes 196616 | tf_op jit(solution)/shard_map/ppermute | solution.py:25
  10.6 0.6 copy-start.1
  21.4 50.7 %copy-start = (bf16[16,128,128]{2,1,0:T(8,128)(2,1)S(1)}, bf16[16,128,128]{2,1,0:T(8,128)(2,1)}, u32[]{:S(2)}) copy-start(bf16[16,128,128]{2,1,0:T(8,128)(2,1)} %get-tuple-element.8) | copy-start | bytes 1572868
  22.5 24.5 %collective-permute-start.2 = (bf16[2,128,128]{2,1,0:T(8,128)(2,1)S(1)}, bf16[2,128,128]{2,1,0:T(8,128)(2,1)S(1)}, u32[]{:S(2)}, u32[]{:S(2)}) collective-permute-start(bf16[2,128,128]{2,1,0:T(8,128)(2,1)S(1)} %get-tuple-element.24), channel_id=1, source_target_pairs={{0,68},{4,72},{8,76},{12,80},{16,84},{20,88},{24,92},{28,96},{32,1... | collective-permute-start | bytes 196616 | tf_op jit(solution)/shard_map/ppermute | solution.py:25
  26.0 46.0 %collective-permute-start.9 = (bf16[2,128,128]{2,1,0:T(8,128)(2,1)S(1)}, bf16[2,128,128]{2,1,0:T(8,128)(2,1)S(1)}, u32[]{:S(2)}, u32[]{:S(2)}) collective-permute-start(bf16[2,128,128]{2,1,0:T(8,128)(2,1)S(1)} %get-tuple-element.17), channel_id=1, source_target_pairs={{68,0},{72,4},{76,8},{80,12},{84,16},{88,20},{92,24},{96,28},{100,... | collective-permute-start | bytes 196616 | tf_op jit(solution)/shard_map/ppermute | solution.py:25
  34.8 37.2 %collective-permute-start.8 = (bf16[2,128,128]{2,1,0:T(8,128)(2,1)S(1)}, bf16[2,128,128]{2,1,0:T(8,128)(2,1)S(1)}, u32[]{:S(2)}, u32[]{:S(2)}) collective-permute-start(bf16[2,128,128]{2,1,0:T(8,128)(2,1)S(1)} %get-tuple-element.18), channel_id=1, source_target_pairs={{64,0},{68,4},{72,8},{76,12},{80,16},{84,20},{88,24},{92,28},{96,3... | collective-permute-start | bytes 196616 | tf_op jit(solution)/shard_map/ppermute | solution.py:25
  38.2 33.8 %collective-permute-start.7 = (bf16[2,128,128]{2,1,0:T(8,128)(2,1)S(1)}, bf16[2,128,128]{2,1,0:T(8,128)(2,1)S(1)}, u32[]{:S(2)}, u32[]{:S(2)}) collective-permute-start(bf16[2,128,128]{2,1,0:T(8,128)(2,1)S(1)} %get-tuple-element.19), channel_id=1, source_target_pairs={{60,0},{64,4},{68,8},{72,12},{76,16},{80,20},{84,24},{88,28},{92,3... | collective-permute-start | bytes 196616 | tf_op jit(solution)/shard_map/ppermute | solution.py:25
  40.1 31.9 %collective-permute-start.6 = (bf16[2,128,128]{2,1,0:T(8,128)(2,1)S(1)}, bf16[2,128,128]{2,1,0:T(8,128)(2,1)S(1)}, u32[]{:S(2)}, u32[]{:S(2)}) collective-permute-start(bf16[2,128,128]{2,1,0:T(8,128)(2,1)S(1)} %get-tuple-element.20), channel_id=1, source_target_pairs={{4,0},{8,4},{12,8},{16,12},{20,16},{24,20},{28,24},{32,28},{36,32}... | collective-permute-start | bytes 196616 | tf_op jit(solution)/shard_map/ppermute | solution.py:25
  47.1 9.0 %collective-permute-start.3 = (bf16[2,128,128]{2,1,0:T(8,128)(2,1)S(1)}, bf16[2,128,128]{2,1,0:T(8,128)(2,1)S(1)}, u32[]{:S(2)}, u32[]{:S(2)}) collective-permute-start(bf16[2,128,128]{2,1,0:T(8,128)(2,1)S(1)} %get-tuple-element.23), channel_id=1, source_target_pairs={{0,64},{4,68},{8,72},{12,76},{16,80},{20,84},{24,88},{28,92},{32,9... | collective-permute-start | bytes 196616 | tf_op jit(solution)/shard_map/ppermute | solution.py:25
  56.1 8.2 %collective-permute-start.4 = (bf16[2,128,128]{2,1,0:T(8,128)(2,1)S(1)}, bf16[2,128,128]{2,1,0:T(8,128)(2,1)S(1)}, u32[]{:S(2)}, u32[]{:S(2)}) collective-permute-start(bf16[2,128,128]{2,1,0:T(8,128)(2,1)S(1)} %get-tuple-element.22), channel_id=1, source_target_pairs={{0,60},{4,64},{8,68},{12,72},{16,76},{20,80},{24,84},{28,88},{32,9... | collective-permute-start | bytes 196616 | tf_op jit(solution)/shard_map/ppermute | solution.py:25
  64.3 7.7 %collective-permute-start.5 = (bf16[2,128,128]{2,1,0:T(8,128)(2,1)S(1)}, bf16[2,128,128]{2,1,0:T(8,128)(2,1)S(1)}, u32[]{:S(2)}, u32[]{:S(2)}) collective-permute-start(bf16[2,128,128]{2,1,0:T(8,128)(2,1)S(1)} %get-tuple-element.21), channel_id=1, source_target_pairs={{0,4},{4,8},{8,12},{12,16},{16,20},{20,24},{24,28},{28,32},{32,36}... | collective-permute-start | bytes 196616 | tf_op jit(solution)/shard_map/ppermute | solution.py:25
  74.7 17.5 %all-to-all-start = ((f32[4,64,1152]{2,1,0:T(8,128)}), f32[4,64,1152]{2,1,0:T(8,128)S(1)}, u32[]{:S(2)}, u32[]{:S(2)}) async-start(f32[4,64,1152]{2,1,0:T(8,128)} %pad_maximum_fusion), calls=%async_computation | async-start | bytes 2359296 | tf_op jit(solution)/shard_map/all_to_all | solution.py:141

commit v4 on v3

--- a/solution.py
+++ b/solution.py
@@ -46,37 +46,29 @@
     chosen_ref, live_ref, z_ref, zp_ref, zn_ref, d_ref, u_ref, up_ref,
     gram_ref, out_ref, own_ref, app_ref,
 ):
-    count = z_ref.shape[0]
+    count, rows = d_ref.shape[0], d_ref.shape[1]
 
-    def store(b, total, gram):
-        app = total.astype(jnp.bfloat16)
-        app_ref[b] = app
-        return gram + _atb(z_ref[b], app)
+    def rows_of(b):
+        return z_ref[pl.ds(b * rows, rows), :]
 
-    first = (_ab(d_ref[0], z_ref[0]) + _ab(u_ref[0], z_ref[1])) + _atb(up_ref[...], zp_ref[...])
-    gram = store(0, first, jnp.zeros(gram_ref.shape, jnp.float32))
-
-    def body(b, gram):
-        total = (_ab(d_ref[b], z_ref[b]) + _ab(u_ref[b], z_ref[b + 1])) + _atb(
-            u_ref[b - 1], z_ref[b - 1]
-        )
-        return store(b, total, gram)
-
-    gram = lax.fori_loop(1, count - 1, body, gram)
-    last = count - 1
-    final = (_ab(d_ref[last], z_ref[last]) + _ab(u_ref[last], zn_ref[...])) + _atb(
-        u_ref[last - 1], z_ref[last - 1]
-    )
-    gram_ref[...] = store(last, final, gram)
+    for b in range(count):
+        below = zp_ref[...] if b == 0 else rows_of(b - 1)
+        lower = up_ref[...] if b == 0 else u_ref[b - 1]
+        above = zn_ref[...] if b == count - 1 else rows_of(b + 1)
+        total = (_ab(d_ref[b], rows_of(b)) + _ab(u_ref[b], above)) + _atb(lower, below)
+        app_ref[pl.ds(b * rows, rows), :] = total.astype(app_ref.dtype)
+    gram_ref[...] = _atb(z_ref[...], app_ref[...])
     for i in range(out_ref.shape[0]):
-        block = chosen_ref[i]
-        out_ref[i] = app_ref[block]
-        own_ref[i] = jnp.where(live_ref[i] > 0, z_ref[block], jnp.zeros_like(z_ref[block]))
+        start = pl.multiple_of(chosen_ref[i] * rows, rows)
+        out_ref[i] = app_ref[pl.ds(start, rows), :]
+        tile = z_ref[pl.ds(start, rows), :]
+        own_ref[i] = jnp.where(live_ref[i] > 0, tile, jnp.zeros_like(tile))
 
 
 def local_apply(chosen, live, centre, prev_rows, next_rows, diagonal, upper, prev_upper):
     tiles = chosen.shape[0]
-    blocks, rows, width = centre.shape
+    blocks, rows = diagonal.shape[0], diagonal.shape[1]
+    width = centre.shape[1]
     vmem = pl.BlockSpec(memory_space=pltpu.VMEM)
     smem = pl.BlockSpec(memory_space=pltpu.SMEM)
     return pl.pallas_call(
@@ -88,7 +80,7 @@
         ),
         in_specs=[smem, smem] + [vmem] * 6,
         out_specs=(vmem, vmem, vmem),
-        scratch_shapes=[pltpu.VMEM((blocks, rows, width), centre.dtype)],
+        scratch_shapes=[pltpu.VMEM((blocks * rows, width), centre.dtype)],
     )(chosen, live, centre, prev_rows, next_rows, diagonal, upper, prev_upper)
 
 
@@ -107,12 +99,11 @@
         jnp.stack([local_rows[-tile_rows:], upper_op[0, blocks_here - 1]]), "crow", 1
     )
     next_rows = shifted(local_rows[:tile_rows], "crow", -1)
-    centre = local_rows.reshape(blocks_here, tile_rows, coarse_width)
     chosen = tile_blocks[0, 0]
     position = crow_place * per_slot + jnp.arange(per_slot, dtype=jnp.int32)
     live = (position[None, :] < pair_counts[0][:, None]).astype(jnp.int32).reshape(-1)
     gram_part, outgoing, own_masked = local_apply(
-        chosen, live, centre, forward_pair[0], next_rows, diag_op[0], upper_op[0], forward_pair[1]
+        chosen, live, local_rows, forward_pair[0], next_rows, diag_op[0], upper_op[0], forward_pair[1]
     )
     outgoing = outgoing.reshape(slot_count, per_slot, tile_rows, coarse_width)
     own_masked = own_masked.reshape(slot_count, per_slot, tile_rows, coarse_width)

time: 103 us -> 96.2 us (0.934)
  Pallas kernels: 10.2 us -> 3.6 us
    pallas_call x1, Pallas kernels: 10.2 us -> 3.6 us  [local_apply(): pl.pallas_call(local_apply_kernel, out_shape=(jax.ShapeDtypeStruct((width...]
where the time goes in v4:
time: 96.2 us; the launch traced here: 95.5 us
  starting transfers between devices  40.1 us (42%)
  waiting for transfers between devices  31.5 us (33%)
  local copies, waits for them, and re-layouts  8.76 us (9%)
  other arithmetic  8.7 us (9%)
  Pallas kernels  3.6 us (4%)
  between operations  1.57 us (2%)
  matrix products  1.27 us (1%)
    ppermute x10, starting transfers between devices, shifted(): lax.ppermute(value, axis, [(source, source + steps) for source in range(i...  34.7 us
    ppermute x10, waiting for transfers between devices, shifted(): lax.ppermute(value, axis, [(source, source + steps) for source in range(i...  19.4 us
    all_to_all x1, waiting for transfers between devices, per_device(): lax.all_to_all(outgoing_rows, 'crow', 0, 0, tiled=True)  12.1 us
    all_to_all x1, starting transfers between devices, per_device(): lax.all_to_all(outgoing_rows, 'crow', 0, 0, tiled=True)  5.36 us
    pallas_call x1, Pallas kernels, local_apply(): pl.pallas_call(local_apply_kernel, out_shape=(jax.ShapeDtypeStruct((width...  3.6 us
    another operation x3, other arithmetic, per_device(): factor = jnp.linalg.cholesky(pivot_block)  3.6 us
    another operation x2, other arithmetic, per_device(): jax.scipy.linalg.solve_triangular(factor, columns.T, lower=True)  3.09 us
  transfers between devices with their start and end apart: 11, of which 5 were waited for; matrix products, arithmetic and copies ran while one was open for 4% of the time, Pallas kernels for 0%

profile of v4, /device:TPU:416, one launch (start us, length us, event | category | flops | bytes accessed | tf_op | source)
XLA Modules:
  0.0 95.5 jit_solution(6695613936915022425)
XLA Ops:
  0.6 0.8 slice_bitcast_fusion.2
  1.4 1.3 %collective-permute-start.1 = (bf16[128,128]{1,0:T(8,128)(2,1)S(1)}, bf16[128,128]{1,0:T(8,128)(2,1)S(1)}, u32[]{:S(2)}, u32[]{:S(2)}) collective-permute-start(bf16[128,128]{1,0:T(8,128)(2,1)S(1)} %get-tuple-element.15), channel_id=1, source_target_pairs={{1,0},{2,1},{3,2},{5,4},{6,5},{7,6},{9,8},{10,9},{11,10},{13,12},{... | collective-permute-start | bytes 98312 | tf_op jit(solution)/shard_map/ppermute | solution.py:25
  2.7 0.8 slice_bitcast_fusion.3
  3.5 4.5 %collective-permute-start = (bf16[2,128,128]{2,1,0:T(8,128)(2,1)S(1)}, bf16[2,128,128]{2,1,0:T(8,128)(2,1)S(1)}, u32[]{:S(2)}, u32[]{:S(2)}) collective-permute-start(bf16[2,128,128]{2,1,0:T(8,128)(2,1)S(1)} %pad_maximum_fusion.2), channel_id=1, source_target_pairs={{0,1},{1,2},{2,3},{4,5},{5,6},{6,7},{8,9},{9,10},{10,11},{12,13},{... | collective-permute-start | bytes 196616 | tf_op jit(solution)/shard_map/ppermute | solution.py:25
  8.0 0.7 compare_convert_fusion
  8.8 0.6 reshape.68.live_ref
  9.9 0.6 slice_bitcast_fusion
  10.6 0.6 copy-done.1
  11.2 3.6 %shard_map.85 = (f32[128,128]{1,0:T(8,128)}, bf16[16,128,128]{2,1,0:T(8,128)(2,1)}, bf16[16,128,128]{2,1,0:T(8,128)(2,1)}) custom-call(s32[16]{0:T(128)} %bitcast.73, s32[16]{0:T(128)} %reshape.68.live_ref, bf16[3072,128]{1,0:T(8,128)(2,1)} %bitcast.67, bf16[128,128]{1,0:T(8,128)(2,1)} %get-tuple-element.28.zp_ref, bf16[128,128]{1,0:T(8,128)(2,1)} %copy-done.1, ...), custom_call_target="tpu_custom_call" | custom-call | tf_op jit(solution)/shard_map/pallas_call | solution.py:74
  14.8 1.2 %fusion.12 = (bf16[2,128,128]{2,1,0:T(8,128)(2,1)S(1)}, bf16[2,128,128]{2,1,0:T(8,128)(2,1)S(1)}, bf16[2,128,128]{2,1,0:T(8,128)(2,1)S(1)}, bf16[2,128,128]{2,1,...) fusion(bf16[16,128,128]{2,1,0:T(8,128)(2,1)} %get-tuple-element.7), kind=kLoop, calls=%fused_computation.41 | loop fusion | bytes 1048576 | tf_op jit(solution)/shard_map/slice | solution.py:113
  15.9 1.9 %collective-permute-start.2 = (bf16[2,128,128]{2,1,0:T(8,128)(2,1)S(1)}, bf16[2,128,128]{2,1,0:T(8,128)(2,1)S(1)}, u32[]{:S(2)}, u32[]{:S(2)}) collective-permute-start(bf16[2,128,128]{2,1,0:T(8,128)(2,1)S(1)} %get-tuple-element.24), channel_id=1, source_target_pairs={{0,68},{4,72},{8,76},{12,80},{16,84},{20,88},{24,92},{28,96},{32,1... | collective-permute-start | bytes 196616 | tf_op jit(solution)/shard_map/ppermute | solution.py:25
  18.5 0.9 copy.17
  19.4 8.8 %collective-permute-start.9 = (bf16[2,128,128]{2,1,0:T(8,128)(2,1)S(1)}, bf16[2,128,128]{2,1,0:T(8,128)(2,1)S(1)}, u32[]{:S(2)}, u32[]{:S(2)}) collective-permute-start(bf16[2,128,128]{2,1,0:T(8,128)(2,1)S(1)} %get-tuple-element.17), channel_id=1, source_target_pairs={{68,0},{72,4},{76,8},{80,12},{84,16},{88,20},{92,24},{96,28},{100,... | collective-permute-start | bytes 196616 | tf_op jit(solution)/shard_map/ppermute | solution.py:25
  28.2 3.4 %collective-permute-start.8 = (bf16[2,128,128]{2,1,0:T(8,128)(2,1)S(1)}, bf16[2,128,128]{2,1,0:T(8,128)(2,1)S(1)}, u32[]{:S(2)}, u32[]{:S(2)}) collective-permute-start(bf16[2,128,128]{2,1,0:T(8,128)(2,1)S(1)} %get-tuple-element.18), channel_id=1, source_target_pairs={{64,0},{68,4},{72,8},{76,12},{80,16},{84,20},{88,24},{92,28},{96,3... | collective-permute-start | bytes 196616 | tf_op jit(solution)/shard_map/ppermute | solution.py:25
  31.6 1.9 %collective-permute-start.7 = (bf16[2,128,128]{2,1,0:T(8,128)(2,1)S(1)}, bf16[2,128,128]{2,1,0:T(8,128)(2,1)S(1)}, u32[]{:S(2)}, u32[]{:S(2)}) collective-permute-start(bf16[2,128,128]{2,1,0:T(8,128)(2,1)S(1)} %get-tuple-element.19), channel_id=1, source_target_pairs={{60,0},{64,4},{68,8},{72,12},{76,16},{80,20},{84,24},{88,28},{92,3... | collective-permute-start | bytes 196616 | tf_op jit(solution)/shard_map/ppermute | solution.py:25
  33.5 6.9 %collective-permute-start.6 = (bf16[2,128,128]{2,1,0:T(8,128)(2,1)S(1)}, bf16[2,128,128]{2,1,0:T(8,128)(2,1)S(1)}, u32[]{:S(2)}, u32[]{:S(2)}) collective-permute-start(bf16[2,128,128]{2,1,0:T(8,128)(2,1)S(1)} %get-tuple-element.20), channel_id=1, source_target_pairs={{4,0},{8,4},{12,8},{16,12},{20,16},{24,20},{28,24},{32,28},{36,32}... | collective-permute-start | bytes 196616 | tf_op jit(solution)/shard_map/ppermute | solution.py:25
  40.5 2.2 %collective-permute-start.3 = (bf16[2,128,128]{2,1,0:T(8,128)(2,1)S(1)}, bf16[2,128,128]{2,1,0:T(8,128)(2,1)S(1)}, u32[]{:S(2)}, u32[]{:S(2)}) collective-permute-start(bf16[2,128,128]{2,1,0:T(8,128)(2,1)S(1)} %get-tuple-element.23), channel_id=1, source_target_pairs={{0,64},{4,68},{8,72},{12,76},{16,80},{20,84},{24,88},{28,92},{32,9... | collective-permute-start | bytes 196616 | tf_op jit(solution)/shard_map/ppermute | solution.py:25
  42.7 6.8 %collective-permute-done.3 = bf16[2,128,128]{2,1,0:T(8,128)(2,1)S(1)} collective-permute-done((bf16[2,128,128]{2,1,0:T(8,128)(2,1)S(1)}, bf16[2,128,128]{2,1,0:T(8,128)(2,1)S(1)}, u32[]{:S(2)}, u32[]{:S(2)}) %collective-permute-start.3) | collective-permute-done | bytes 65568 | tf_op jit(solution)/shard_map/ppermute | solution.py:25
  49.4 1.9 %collective-permute-start.4 = (bf16[2,128,128]{2,1,0:T(8,128)(2,1)S(1)}, bf16[2,128,128]{2,1,0:T(8,128)(2,1)S(1)}, u32[]{:S(2)}, u32[]{:S(2)}) collective-permute-start(bf16[2,128,128]{2,1,0:T(8,128)(2,1)S(1)} %get-tuple-element.22), channel_id=1, source_target_pairs={{0,60},{4,64},{8,68},{12,72},{16,76},{20,80},{24,84},{28,88},{32,9... | collective-permute-start | bytes 196616 | tf_op jit(solution)/shard_map/ppermute | solution.py:25
  51.4 6.3 %collective-permute-done.4 = bf16[2,128,128]{2,1,0:T(8,128)(2,1)S(1)} collective-permute-done((bf16[2,128,128]{2,1,0:T(8,128)(2,1)S(1)}, bf16[2,128,128]{2,1,0:T(8,128)(2,1)S(1)}, u32[]{:S(2)}, u32[]{:S(2)}) %collective-permute-start.4) | collective-permute-done | bytes 65568 | tf_op jit(solution)/shard_map/ppermute | solution.py:25
  57.7 1.9 %collective-permute-start.5 = (bf16[2,128,128]{2,1,0:T(8,128)(2,1)S(1)}, bf16[2,128,128]{2,1,0:T(8,128)(2,1)S(1)}, u32[]{:S(2)}, u32[]{:S(2)}) collective-permute-start(bf16[2,128,128]{2,1,0:T(8,128)(2,1)S(1)} %get-tuple-element.21), channel_id=1, source_target_pairs={{0,4},{4,8},{8,12},{12,16},{16,20},{20,24},{24,28},{28,32},{32,36}... | collective-permute-start | bytes 196616 | tf_op jit(solution)/shard_map/ppermute | solution.py:25
  59.6 5.7 %collective-permute-done.5 = bf16[2,128,128]{2,1,0:T(8,128)(2,1)S(1)} collective-permute-done((bf16[2,128,128]{2,1,0:T(8,128)(2,1)S(1)}, bf16[2,128,128]{2,1,0:T(8,128)(2,1)S(1)}, u32[]{:S(2)}, u32[]{:S(2)}) %collective-permute-start.5) | collective-permute-done | bytes 65568 | tf_op jit(solution)/shard_map/ppermute | solution.py:25
  67.0 1.1 %pad_maximum_fusion = f32[4,64,1152]{2,1,0:T(8,128)} fusion(f32[4,32,1152]{2,1,0:T(8,128)S(1)} %broadcast_in_dim.6, f32[4,32,1152]{2,1,0:T(8,128)S(1)} %reshape_reshape.3), kind=kLoop, calls=%fused_computation.2 | loop fusion | flops 294912 | bytes 2359296 | tf_op jit(solution)/shard_map/concatenate | solution.py:125
  68.1 5.4 %all-to-all-start = ((f32[4,64,1152]{2,1,0:T(8,128)}), f32[4,64,1152]{2,1,0:T(8,128)S(1)}, u32[]{:S(2)}, u32[]{:S(2)}) async-start(f32[4,64,1152]{2,1,0:T(8,128)} %pad_maximum_fusion), calls=%async_computation | async-start | bytes 2359296 | tf_op jit(solution)/shard_map/all_to_all | solution.py:132
  73.5 12.1 %all-to-all-done = f32[4,64,1152]{2,1,0:T(8,128)S(1)} async-done(((f32[4,64,1152]{2,1,0:T(8,128)}), f32[4,64,1152]{2,1,0:T(8,128)S(1)}, u32[]{:S(2)}, u32[]{:S(2)}) %all-to-all-start) | async-done | bytes 1179680 | tf_op jit(solution)/shard_map/all_to_all | solution.py:132
  85.9 2.9 %cholesky.16 = f32[32,32]{1,0:T(8,128)S(1)} custom-call(f32[32,32]{1,0:T(8,128)S(1)} %fusion.4), custom_call_target="Cholesky" | custom-call | tf_op jit(solution)/shard_map/jit(cholesky)/cholesky | solution.py:142
  88.9 0.6 compare_reduce_fusion
  89.5 0.7 fusion.3
  90.2 2.4 %custom-call.10 = f32[1,32,32]{1,2,0:T(8,128)S(1)} custom-call(f32[1,32,32]{2,1,0:T(8,128)S(1)} %fusion.3), custom_call_target="InvertDiagBlocksLowerTriangular" | custom-call | tf_op jit(solution)/shard_map/jit(_solve_triangular)/triangular_solve | solution.py:145
  93.5 0.6 slice.132
  94.2 0.7 slice.133
  94.8 0.7 copy.22
  (36 shorter events, 3.4 us)
Async XLA Ops:
  1.4 9.1 %collective-permute-start.1 = (bf16[128,128]{1,0:T(8,128)(2,1)S(1)}, bf16[128,128]{1,0:T(8,128)(2,1)S(1)}, u32[]{:S(2)}, u32[]{:S(2)}) collective-permute-start(bf16[128,128]{1,0:T(8,128)(2,1)S(1)} %get-tuple-element.15), channel_id=1, source_target_pairs={{1,0},{2,1},{3,2},{5,4},{6,5},{7,6},{9,8},{10,9},{11,10},{13,12},{... | collective-permute-start | bytes 98312 | tf_op jit(solution)/shard_map/ppermute | solution.py:25
  3.5 6.4 %collective-permute-start = (bf16[2,128,128]{2,1,0:T(8,128)(2,1)S(1)}, bf16[2,128,128]{2,1,0:T(8,128)(2,1)S(1)}, u32[]{:S(2)}, u32[]{:S(2)}) collective-permute-start(bf16[2,128,128]{2,1,0:T(8,128)(2,1)S(1)} %pad_maximum_fusion.2), channel_id=1, source_target_pairs={{0,1},{1,2},{2,3},{4,5},{5,6},{6,7},{8,9},{9,10},{10,11},{12,13},{... | collective-permute-start | bytes 196616 | tf_op jit(solution)/shard_map/ppermute | solution.py:25
  10.6 0.6 copy-start.1
  14.8 50.7 %copy-start = (bf16[16,128,128]{2,1,0:T(8,128)(2,1)S(1)}, bf16[16,128,128]{2,1,0:T(8,128)(2,1)}, u32[]{:S(2)}) copy-start(bf16[16,128,128]{2,1,0:T(8,128)(2,1)} %get-tuple-element.8) | copy-start | bytes 1572868
  15.9 24.5 %collective-permute-start.2 = (bf16[2,128,128]{2,1,0:T(8,128)(2,1)S(1)}, bf16[2,128,128]{2,1,0:T(8,128)(2,1)S(1)}, u32[]{:S(2)}, u32[]{:S(2)}) collective-permute-start(bf16[2,128,128]{2,1,0:T(8,128)(2,1)S(1)} %get-tuple-element.24), channel_id=1, source_target_pairs={{0,68},{4,72},{8,76},{12,80},{16,84},{20,88},{24,92},{28,96},{32,1... | collective-permute-start | bytes 196616 | tf_op jit(solution)/shard_map/ppermute | solution.py:25
  19.4 46.0 %collective-permute-start.9 = (bf16[2,128,128]{2,1,0:T(8,128)(2,1)S(1)}, bf16[2,128,128]{2,1,0:T(8,128)(2,1)S(1)}, u32[]{:S(2)}, u32[]{:S(2)}) collective-permute-start(bf16[2,128,128]{2,1,0:T(8,128)(2,1)S(1)} %get-tuple-element.17), channel_id=1, source_target_pairs={{68,0},{72,4},{76,8},{80,12},{84,16},{88,20},{92,24},{96,28},{100,... | collective-permute-start | bytes 196616 | tf_op jit(solution)/shard_map/ppermute | solution.py:25
  28.2 37.2 %collective-permute-start.8 = (bf16[2,128,128]{2,1,0:T(8,128)(2,1)S(1)}, bf16[2,128,128]{2,1,0:T(8,128)(2,1)S(1)}, u32[]{:S(2)}, u32[]{:S(2)}) collective-permute-start(bf16[2,128,128]{2,1,0:T(8,128)(2,1)S(1)} %get-tuple-element.18), channel_id=1, source_target_pairs={{64,0},{68,4},{72,8},{76,12},{80,16},{84,20},{88,24},{92,28},{96,3... | collective-permute-start | bytes 196616 | tf_op jit(solution)/shard_map/ppermute | solution.py:25
  31.6 33.8 %collective-permute-start.7 = (bf16[2,128,128]{2,1,0:T(8,128)(2,1)S(1)}, bf16[2,128,128]{2,1,0:T(8,128)(2,1)S(1)}, u32[]{:S(2)}, u32[]{:S(2)}) collective-permute-start(bf16[2,128,128]{2,1,0:T(8,128)(2,1)S(1)} %get-tuple-element.19), channel_id=1, source_target_pairs={{60,0},{64,4},{68,8},{72,12},{76,16},{80,20},{84,24},{88,28},{92,3... | collective-permute-start | bytes 196616 | tf_op jit(solution)/shard_map/ppermute | solution.py:25
  33.5 31.9 %collective-permute-start.6 = (bf16[2,128,128]{2,1,0:T(8,128)(2,1)S(1)}, bf16[2,128,128]{2,1,0:T(8,128)(2,1)S(1)}, u32[]{:S(2)}, u32[]{:S(2)}) collective-permute-start(bf16[2,128,128]{2,1,0:T(8,128)(2,1)S(1)} %get-tuple-element.20), channel_id=1, source_target_pairs={{4,0},{8,4},{12,8},{16,12},{20,16},{24,20},{28,24},{32,28},{36,32}... | collective-permute-start | bytes 196616 | tf_op jit(solution)/shard_map/ppermute | solution.py:25
  40.5 9.0 %collective-permute-start.3 = (bf16[2,128,128]{2,1,0:T(8,128)(2,1)S(1)}, bf16[2,128,128]{2,1,0:T(8,128)(2,1)S(1)}, u32[]{:S(2)}, u32[]{:S(2)}) collective-permute-start(bf16[2,128,128]{2,1,0:T(8,128)(2,1)S(1)} %get-tuple-element.23), channel_id=1, source_target_pairs={{0,64},{4,68},{8,72},{12,76},{16,80},{20,84},{24,88},{28,92},{32,9... | collective-permute-start | bytes 196616 | tf_op jit(solution)/shard_map/ppermute | solution.py:25
  49.4 8.2 %collective-permute-start.4 = (bf16[2,128,128]{2,1,0:T(8,128)(2,1)S(1)}, bf16[2,128,128]{2,1,0:T(8,128)(2,1)S(1)}, u32[]{:S(2)}, u32[]{:S(2)}) collective-permute-start(bf16[2,128,128]{2,1,0:T(8,128)(2,1)S(1)} %get-tuple-element.22), channel_id=1, source_target_pairs={{0,60},{4,64},{8,68},{12,72},{16,76},{20,80},{24,84},{28,88},{32,9... | collective-permute-start | bytes 196616 | tf_op jit(solution)/shard_map/ppermute | solution.py:25
  57.7 7.7 %collective-permute-start.5 = (bf16[2,128,128]{2,1,0:T(8,128)(2,1)S(1)}, bf16[2,128,128]{2,1,0:T(8,128)(2,1)S(1)}, u32[]{:S(2)}, u32[]{:S(2)}) collective-permute-start(bf16[2,128,128]{2,1,0:T(8,128)(2,1)S(1)} %get-tuple-element.21), channel_id=1, source_target_pairs={{0,4},{4,8},{8,12},{12,16},{16,20},{20,24},{24,28},{28,32},{32,36}... | collective-permute-start | bytes 196616 | tf_op jit(solution)/shard_map/ppermute | solution.py:25
  68.1 17.5 %all-to-all-start = ((f32[4,64,1152]{2,1,0:T(8,128)}), f32[4,64,1152]{2,1,0:T(8,128)S(1)}, u32[]{:S(2)}, u32[]{:S(2)}) async-start(f32[4,64,1152]{2,1,0:T(8,128)} %pad_maximum_fusion), calls=%async_computation | async-start | bytes 2359296 | tf_op jit(solution)/shard_map/all_to_all | solution.py:132

commit v5 on v4

--- a/solution.py
+++ b/solution.py
@@ -84,6 +84,67 @@
     )(chosen, live, centre, prev_rows, next_rows, diagonal, upper, prev_upper)
 
 
+def _exact(a, b, dims):
+    return lax.dot_general(
+        a, b, (dims, ((), ())), precision=lax.Precision.HIGHEST,
+        preferred_element_type=jnp.float32,
+    )
+
+
+def panel_kernel(owner_ref, pieces_ref, self_ref, coupling_ref, panel_ref):
+    share = panel_ref.shape[0]
+    width = self_ref.shape[1]
+    total = (pieces_ref[0] + pieces_ref[1]) + (pieces_ref[2] + pieces_ref[3])
+    own = total[:share]
+    lead = total[share:]
+    owner = owner_ref[0]
+
+    def pick(rows):
+        block = jnp.zeros((share, share), jnp.float32)
+        for q in range(width // share):
+            block = jnp.where(owner == q, rows[:, q * share:(q + 1) * share], block)
+        return block
+
+    pivot = pick(lead)
+    pivot = (pivot + pivot.T) * 0.5
+    row_id = lax.broadcasted_iota(jnp.int32, (share, 2 * share), 0)
+    col_id = lax.broadcasted_iota(jnp.int32, (share, 2 * share), 1)
+    work = jnp.concatenate([pivot, jnp.eye(share, dtype=jnp.float32)], 1)
+
+    def step(k, work):
+        row = jnp.sum(jnp.where(row_id == k, work, 0.0), axis=0, keepdims=True)
+        col = jnp.sum(jnp.where(col_id == k, work, 0.0), axis=1, keepdims=True)
+        diag = jnp.sum(jnp.where(col_id[:1] == k, row, 0.0), axis=1, keepdims=True)
+        scale = 1.0 / jnp.sqrt(diag)
+        unit_row = row * scale
+        below = jnp.where(row_id[:, :1] > k, col * scale, 0.0)
+        return jnp.where(row_id == k, unit_row, work - below * unit_row)
+
+    work = lax.fori_loop(0, share, step, work)
+    inverse = work[:, share:]
+    solved = _exact(inverse, lead, ((1,), (0,)))
+    panel = _exact(pick(own), inverse, ((1,), (1,)))
+    updated = own - _exact(panel, solved, ((1,), (0,)))
+    self_ref[...] = updated[:, :width]
+    coupling_ref[...] = updated[:, width:]
+    panel_ref[...] = panel
+
+
+def eliminate_panel(owner, pieces, width):
+    share = pieces.shape[1] // 2
+    vmem = pl.BlockSpec(memory_space=pltpu.VMEM)
+    return pl.pallas_call(
+        panel_kernel,
+        out_shape=(
+            jax.ShapeDtypeStruct((share, width), jnp.float32),
+            jax.ShapeDtypeStruct((share, pieces.shape[2] - width), jnp.float32),
+            jax.ShapeDtypeStruct((share, share), jnp.float32),
+        ),
+        in_specs=[pl.BlockSpec(memory_space=pltpu.SMEM), vmem],
+        out_specs=(vmem, vmem, vmem),
+    )(owner, pieces)
+
+
 def per_device(deflation, diag_op, upper_op, tile_blocks, pair_counts, pivot_owner):
     crow_count = lax.axis_size("crow")
     crow_place = lax.axis_index("crow")
@@ -132,19 +193,7 @@
     pieces = lax.all_to_all(outgoing_rows, "crow", 0, 0, tiled=True).reshape(
         crow_count, 2 * row_share, whole.shape[1]
     )
-    if crow_count == 4:
-        total = (pieces[0] + pieces[1]) + (pieces[2] + pieces[3])
-    else:
-        total = pieces.sum(0)
-    own_rows = total[:row_share]
-    leading = total[row_share:]
-    pivot_block = lax.dynamic_slice_in_dim(leading, owner_index * row_share, row_share, 1)
-    factor = jnp.linalg.cholesky(pivot_block)
-    solved = jax.scipy.linalg.solve_triangular(factor, leading, lower=True)
-    columns = lax.dynamic_slice_in_dim(own_rows, owner_index * row_share, row_share, 1)
-    panel_rows = jax.scipy.linalg.solve_triangular(factor, columns.T, lower=True).T
-    updated = own_rows - jnp.dot(panel_rows, solved, precision=lax.Precision.HIGHEST)
-    return (updated[:, :coarse_width], updated[:, coarse_width:], panel_rows)
+    return eliminate_panel(pivot_owner, pieces, coarse_width)
 
 
 def solution(mesh):

time: 96.2 us -> 91.8 us (0.954)
  blocking collectives: 0 us -> 17.4 us
  waiting for transfers between devices: 31.5 us -> 19.4 us
  other arithmetic: 8.7 us -> 0.86 us
  Pallas kernels: 3.6 us -> 10.3 us
  starting transfers between devices: 40.1 us -> 34.7 us
  local copies, waits for them, and re-layouts: 8.76 us -> 6.62 us
    all_to_all x0 -> x1, blocking collectives: none -> 17.4 us  [per_device(): lax.all_to_all(outgoing_rows, 'crow', 0, 0, tiled=True)]
    all_to_all x1 -> x0, waiting for transfers between devices: 12.1 us -> none  [per_device(): lax.all_to_all(outgoing_rows, 'crow', 0, 0, tiled=True)]
    another operation x5 -> x0, other arithmetic: 6.68 us -> none  [the longest x3 3.6 us: per_device(): factor = jnp.linalg.cholesky(pivot_block)]
    pallas_call x0 -> x1, Pallas kernels: none -> 6.66 us  [eliminate_panel(): pl.pallas_call(panel_kernel, out_shape=(jax.ShapeDtypeStruct((share, widt...]
    all_to_all x1 -> x0, starting transfers between devices: 5.36 us -> none  [per_device(): lax.all_to_all(outgoing_rows, 'crow', 0, 0, tiled=True)]
    slice x3 -> x0, local copies, waits for them, and re-layouts: 1.29 us -> none  [the longest x2 1.27 us: per_device(): return (updated[:, :coarse_width], updated[:, coarse_width:], panel_rows)]
    concatenate x1, other arithmetic: 1.1 us -> 0.08 us  [per_device(): jnp.concatenate([whole.reshape(crow_count, row_share, whole.shape[1]), jn...]
  transfers between devices with their start and end apart: 11 -> 10, of which waited for: 5 -> 4; matrix products, arithmetic and copies ran while one was open for 4% -> 4% of each run, Pallas kernels for 0% -> 0%
where the time goes in v5:
time: 91.8 us; the launch traced here: 91.1 us
  starting transfers between devices  34.7 us (38%)
  waiting for transfers between devices  19.4 us (21%)
  blocking collectives  17.4 us (19%)
  Pallas kernels  10.3 us (11%)
  local copies, waits for them, and re-layouts  6.62 us (7%)
  between operations  1.53 us (2%)
    ppermute x10, starting transfers between devices, shifted(): lax.ppermute(value, axis, [(source, source + steps) for source in range(i...  34.7 us
    ppermute x10, waiting for transfers between devices, shifted(): lax.ppermute(value, axis, [(source, source + steps) for source in range(i...  19.4 us
    all_to_all x1, blocking collectives, per_device(): lax.all_to_all(outgoing_rows, 'crow', 0, 0, tiled=True)  17.4 us
    pallas_call x1, Pallas kernels, eliminate_panel(): pl.pallas_call(panel_kernel, out_shape=(jax.ShapeDtypeStruct((share, widt...  6.66 us
    pallas_call x1, Pallas kernels, local_apply(): pl.pallas_call(local_apply_kernel, out_shape=(jax.ShapeDtypeStruct((width...  3.61 us
  transfers between devices with their start and end apart: 10, of which 4 were waited for; matrix products, arithmetic and copies ran while one was open for 4% of the time, Pallas kernels for 0%

profile of v5, /device:TPU:416, one launch (start us, length us, event | category | flops | bytes accessed | tf_op | source)
XLA Modules:
  0.0 91.1 jit_solution(6862954985168034070)
XLA Ops:
  0.6 0.8 slice_bitcast_fusion.2
  1.4 1.3 %collective-permute-start.1 = (bf16[128,128]{1,0:T(8,128)(2,1)S(1)}, bf16[128,128]{1,0:T(8,128)(2,1)S(1)}, u32[]{:S(2)}, u32[]{:S(2)}) collective-permute-start(bf16[128,128]{1,0:T(8,128)(2,1)S(1)} %get-tuple-element.9), channel_id=1, source_target_pairs={{1,0},{2,1},{3,2},{5,4},{6,5},{7,6},{9,8},{10,9},{11,10},{13,12},{... | collective-permute-start | bytes 98312 | tf_op jit(solution)/shard_map/ppermute | solution.py:25
  2.7 0.8 slice_bitcast_fusion.3
  3.5 4.5 %collective-permute-start = (bf16[2,128,128]{2,1,0:T(8,128)(2,1)S(1)}, bf16[2,128,128]{2,1,0:T(8,128)(2,1)S(1)}, u32[]{:S(2)}, u32[]{:S(2)}) collective-permute-start(bf16[2,128,128]{2,1,0:T(8,128)(2,1)S(1)} %pad_maximum_fusion.2), channel_id=1, source_target_pairs={{0,1},{1,2},{2,3},{4,5},{5,6},{6,7},{8,9},{9,10},{10,11},{12,13},{... | collective-permute-start | bytes 196616 | tf_op jit(solution)/shard_map/ppermute | solution.py:25
  8.0 0.7 compare_convert_fusion
  8.8 0.6 reshape.48.live_ref
  9.4 0.5 collective-permute-done
  9.9 0.6 slice_bitcast_fusion
  10.5 0.0 collective-permute-done.1.zn_ref
  10.5 0.6 copy-done.1
  11.1 3.6 %shard_map.85 = (f32[128,128]{1,0:T(8,128)}, bf16[16,128,128]{2,1,0:T(8,128)(2,1)}, bf16[16,128,128]{2,1,0:T(8,128)(2,1)}) custom-call(s32[16]{0:T(128)} %bitcast.46, s32[16]{0:T(128)} %reshape.48.live_ref, bf16[3072,128]{1,0:T(8,128)(2,1)} %bitcast.41, bf16[128,128]{1,0:T(8,128)(2,1)} %get-tuple-element.20.zp_ref, bf16[128,128]{1,0:T(8,128)(2,1)} %copy-done.1, ...), custom_call_target="tpu_custom_call" | custom-call | tf_op jit(solution)/shard_map/pallas_call | solution.py:74
  14.7 1.2 %fusion = (bf16[2,128,128]{2,1,0:T(8,128)(2,1)S(1)}, bf16[2,128,128]{2,1,0:T(8,128)(2,1)S(1)}, bf16[2,128,128]{2,1,0:T(8,128)(2,1)S(1)}, bf16[2,128,128]{2,1,0:T...) fusion(bf16[16,128,128]{2,1,0:T(8,128)(2,1)} %get-tuple-element.7), kind=kLoop, calls=%fused_computation.19 | loop fusion | bytes 1048576 | tf_op jit(solution)/shard_map/slice | solution.py:174
  15.9 1.9 %collective-permute-start.2 = (bf16[2,128,128]{2,1,0:T(8,128)(2,1)S(1)}, bf16[2,128,128]{2,1,0:T(8,128)(2,1)S(1)}, u32[]{:S(2)}, u32[]{:S(2)}) collective-permute-start(bf16[2,128,128]{2,1,0:T(8,128)(2,1)S(1)} %get-tuple-element.18), channel_id=1, source_target_pairs={{0,68},{4,72},{8,76},{12,80},{16,84},{20,88},{24,92},{28,96},{32,1... | collective-permute-start | bytes 196616 | tf_op jit(solution)/shard_map/ppermute | solution.py:25
  18.5 0.9 %copy.14 = f32[128,1,128]{0,2,1:T(8,128)S(1)} copy(f32[128,1,128]{2,0,1:T(8,128)} %bitcast.45) | data formatting | bytes 131072 | tf_op jit(solution)/shard_map/broadcast_in_dim | solution.py:182
  19.4 8.8 %collective-permute-start.9 = (bf16[2,128,128]{2,1,0:T(8,128)(2,1)S(1)}, bf16[2,128,128]{2,1,0:T(8,128)(2,1)S(1)}, u32[]{:S(2)}, u32[]{:S(2)}) collective-permute-start(bf16[2,128,128]{2,1,0:T(8,128)(2,1)S(1)} %get-tuple-element.11), channel_id=1, source_target_pairs={{68,0},{72,4},{76,8},{80,12},{84,16},{88,20},{92,24},{96,28},{100,... | collective-permute-start | bytes 196616 | tf_op jit(solution)/shard_map/ppermute | solution.py:25
  28.2 3.4 %collective-permute-start.8 = (bf16[2,128,128]{2,1,0:T(8,128)(2,1)S(1)}, bf16[2,128,128]{2,1,0:T(8,128)(2,1)S(1)}, u32[]{:S(2)}, u32[]{:S(2)}) collective-permute-start(bf16[2,128,128]{2,1,0:T(8,128)(2,1)S(1)} %get-tuple-element.12), channel_id=1, source_target_pairs={{64,0},{68,4},{72,8},{76,12},{80,16},{84,20},{88,24},{92,28},{96,3... | collective-permute-start | bytes 196616 | tf_op jit(solution)/shard_map/ppermute | solution.py:25
  31.6 1.9 %collective-permute-start.7 = (bf16[2,128,128]{2,1,0:T(8,128)(2,1)S(1)}, bf16[2,128,128]{2,1,0:T(8,128)(2,1)S(1)}, u32[]{:S(2)}, u32[]{:S(2)}) collective-permute-start(bf16[2,128,128]{2,1,0:T(8,128)(2,1)S(1)} %get-tuple-element.13), channel_id=1, source_target_pairs={{60,0},{64,4},{68,8},{72,12},{76,16},{80,20},{84,24},{88,28},{92,3... | collective-permute-start | bytes 196616 | tf_op jit(solution)/shard_map/ppermute | solution.py:25
  33.5 7.0 %collective-permute-start.6 = (bf16[2,128,128]{2,1,0:T(8,128)(2,1)S(1)}, bf16[2,128,128]{2,1,0:T(8,128)(2,1)S(1)}, u32[]{:S(2)}, u32[]{:S(2)}) collective-permute-start(bf16[2,128,128]{2,1,0:T(8,128)(2,1)S(1)} %get-tuple-element.14), channel_id=1, source_target_pairs={{4,0},{8,4},{12,8},{16,12},{20,16},{24,20},{28,24},{32,28},{36,32}... | collective-permute-start | bytes 196616 | tf_op jit(solution)/shard_map/ppermute | solution.py:25
  40.5 2.2 %collective-permute-start.3 = (bf16[2,128,128]{2,1,0:T(8,128)(2,1)S(1)}, bf16[2,128,128]{2,1,0:T(8,128)(2,1)S(1)}, u32[]{:S(2)}, u32[]{:S(2)}) collective-permute-start(bf16[2,128,128]{2,1,0:T(8,128)(2,1)S(1)} %get-tuple-element.17), channel_id=1, source_target_pairs={{0,64},{4,68},{8,72},{12,76},{16,80},{20,84},{24,88},{28,92},{32,9... | collective-permute-start | bytes 196616 | tf_op jit(solution)/shard_map/ppermute | solution.py:25
  42.7 6.8 %collective-permute-done.3 = bf16[2,128,128]{2,1,0:T(8,128)(2,1)S(1)} collective-permute-done((bf16[2,128,128]{2,1,0:T(8,128)(2,1)S(1)}, bf16[2,128,128]{2,1,0:T(8,128)(2,1)S(1)}, u32[]{:S(2)}, u32[]{:S(2)}) %collective-permute-start.3) | collective-permute-done | bytes 65568 | tf_op jit(solution)/shard_map/ppermute | solution.py:25
  49.4 1.9 %collective-permute-start.4 = (bf16[2,128,128]{2,1,0:T(8,128)(2,1)S(1)}, bf16[2,128,128]{2,1,0:T(8,128)(2,1)S(1)}, u32[]{:S(2)}, u32[]{:S(2)}) collective-permute-start(bf16[2,128,128]{2,1,0:T(8,128)(2,1)S(1)} %get-tuple-element.16), channel_id=1, source_target_pairs={{0,60},{4,64},{8,68},{12,72},{16,76},{20,80},{24,84},{28,88},{32,9... | collective-permute-start | bytes 196616 | tf_op jit(solution)/shard_map/ppermute | solution.py:25
  51.4 6.3 %collective-permute-done.4 = bf16[2,128,128]{2,1,0:T(8,128)(2,1)S(1)} collective-permute-done((bf16[2,128,128]{2,1,0:T(8,128)(2,1)S(1)}, bf16[2,128,128]{2,1,0:T(8,128)(2,1)S(1)}, u32[]{:S(2)}, u32[]{:S(2)}) %collective-permute-start.4) | collective-permute-done | bytes 65568 | tf_op jit(solution)/shard_map/ppermute | solution.py:25
  57.7 1.9 %collective-permute-start.5 = (bf16[2,128,128]{2,1,0:T(8,128)(2,1)S(1)}, bf16[2,128,128]{2,1,0:T(8,128)(2,1)S(1)}, u32[]{:S(2)}, u32[]{:S(2)}) collective-permute-start(bf16[2,128,128]{2,1,0:T(8,128)(2,1)S(1)} %get-tuple-element.15), channel_id=1, source_target_pairs={{0,4},{4,8},{8,12},{12,16},{16,20},{20,24},{24,28},{28,32},{32,36}... | collective-permute-start | bytes 196616 | tf_op jit(solution)/shard_map/ppermute | solution.py:25
  59.6 5.7 %collective-permute-done.5 = bf16[2,128,128]{2,1,0:T(8,128)(2,1)S(1)} collective-permute-done((bf16[2,128,128]{2,1,0:T(8,128)(2,1)S(1)}, bf16[2,128,128]{2,1,0:T(8,128)(2,1)S(1)}, u32[]{:S(2)}, u32[]{:S(2)}) %collective-permute-start.5) | collective-permute-done | bytes 65568 | tf_op jit(solution)/shard_map/ppermute | solution.py:25
  65.5 0.3 convolution_bitcast_fusion
  65.9 0.5 copy.15
  66.4 0.2 constant_dynamic-slice_fusion
  66.6 0.2 copy.19
  66.8 0.1 reshape_reshape.3
  67.0 0.1 pad_maximum_fusion
  67.1 17.4 %all_to_all.5.pieces_ref = f32[4,64,1152]{2,1,0:T(8,128)} all-to-all(f32[4,64,1152]{2,1,0:T(8,128)S(1)} %pad_maximum_fusion), channel_id=1, replica_groups=mesh['sub'=128,'crow'=4] {'crow'}, dimensions={0} | all-to-all | bytes 2359296 | tf_op jit(solution)/shard_map/all_to_all | solution.py:193
  84.5 6.7 %shard_map.86 = (f32[32,128]{1,0:T(8,128)}, f32[32,1024]{1,0:T(8,128)}, f32[32,32]{1,0:T(8,128)}) custom-call(s32[1]{0:T(128)S(6)} %copy.27.owner_ref, f32[4,64,1152]{2,1,0:T(8,128)} %all_to_all.5.pieces_ref), custom_call_target="tpu_custom_call" | custom-call | tf_op jit(solution)/shard_map/pallas_call | solution.py:136
  (20 shorter events, 0.2 us)
Async XLA Ops:
  1.4 9.1 %collective-permute-start.1 = (bf16[128,128]{1,0:T(8,128)(2,1)S(1)}, bf16[128,128]{1,0:T(8,128)(2,1)S(1)}, u32[]{:S(2)}, u32[]{:S(2)}) collective-permute-start(bf16[128,128]{1,0:T(8,128)(2,1)S(1)} %get-tuple-element.9), channel_id=1, source_target_pairs={{1,0},{2,1},{3,2},{5,4},{6,5},{7,6},{9,8},{10,9},{11,10},{13,12},{... | collective-permute-start | bytes 98312 | tf_op jit(solution)/shard_map/ppermute | solution.py:25
  3.5 6.4 %collective-permute-start = (bf16[2,128,128]{2,1,0:T(8,128)(2,1)S(1)}, bf16[2,128,128]{2,1,0:T(8,128)(2,1)S(1)}, u32[]{:S(2)}, u32[]{:S(2)}) collective-permute-start(bf16[2,128,128]{2,1,0:T(8,128)(2,1)S(1)} %pad_maximum_fusion.2), channel_id=1, source_target_pairs={{0,1},{1,2},{2,3},{4,5},{5,6},{6,7},{8,9},{9,10},{10,11},{12,13},{... | collective-permute-start | bytes 196616 | tf_op jit(solution)/shard_map/ppermute | solution.py:25
  10.5 0.6 copy-start.1
  14.7 50.7 %copy-start = (bf16[16,128,128]{2,1,0:T(8,128)(2,1)S(1)}, bf16[16,128,128]{2,1,0:T(8,128)(2,1)}, u32[]{:S(2)}) copy-start(bf16[16,128,128]{2,1,0:T(8,128)(2,1)} %get-tuple-element.8) | copy-start | bytes 1572868
  15.9 24.5 %collective-permute-start.2 = (bf16[2,128,128]{2,1,0:T(8,128)(2,1)S(1)}, bf16[2,128,128]{2,1,0:T(8,128)(2,1)S(1)}, u32[]{:S(2)}, u32[]{:S(2)}) collective-permute-start(bf16[2,128,128]{2,1,0:T(8,128)(2,1)S(1)} %get-tuple-element.18), channel_id=1, source_target_pairs={{0,68},{4,72},{8,76},{12,80},{16,84},{20,88},{24,92},{28,96},{32,1... | collective-permute-start | bytes 196616 | tf_op jit(solution)/shard_map/ppermute | solution.py:25
  19.4 46.0 %collective-permute-start.9 = (bf16[2,128,128]{2,1,0:T(8,128)(2,1)S(1)}, bf16[2,128,128]{2,1,0:T(8,128)(2,1)S(1)}, u32[]{:S(2)}, u32[]{:S(2)}) collective-permute-start(bf16[2,128,128]{2,1,0:T(8,128)(2,1)S(1)} %get-tuple-element.11), channel_id=1, source_target_pairs={{68,0},{72,4},{76,8},{80,12},{84,16},{88,20},{92,24},{96,28},{100,... | collective-permute-start | bytes 196616 | tf_op jit(solution)/shard_map/ppermute | solution.py:25
  28.2 37.2 %collective-permute-start.8 = (bf16[2,128,128]{2,1,0:T(8,128)(2,1)S(1)}, bf16[2,128,128]{2,1,0:T(8,128)(2,1)S(1)}, u32[]{:S(2)}, u32[]{:S(2)}) collective-permute-start(bf16[2,128,128]{2,1,0:T(8,128)(2,1)S(1)} %get-tuple-element.12), channel_id=1, source_target_pairs={{64,0},{68,4},{72,8},{76,12},{80,16},{84,20},{88,24},{92,28},{96,3... | collective-permute-start | bytes 196616 | tf_op jit(solution)/shard_map/ppermute | solution.py:25
  31.6 33.8 %collective-permute-start.7 = (bf16[2,128,128]{2,1,0:T(8,128)(2,1)S(1)}, bf16[2,128,128]{2,1,0:T(8,128)(2,1)S(1)}, u32[]{:S(2)}, u32[]{:S(2)}) collective-permute-start(bf16[2,128,128]{2,1,0:T(8,128)(2,1)S(1)} %get-tuple-element.13), channel_id=1, source_target_pairs={{60,0},{64,4},{68,8},{72,12},{76,16},{80,20},{84,24},{88,28},{92,3... | collective-permute-start | bytes 196616 | tf_op jit(solution)/shard_map/ppermute | solution.py:25
  33.5 31.9 %collective-permute-start.6 = (bf16[2,128,128]{2,1,0:T(8,128)(2,1)S(1)}, bf16[2,128,128]{2,1,0:T(8,128)(2,1)S(1)}, u32[]{:S(2)}, u32[]{:S(2)}) collective-permute-start(bf16[2,128,128]{2,1,0:T(8,128)(2,1)S(1)} %get-tuple-element.14), channel_id=1, source_target_pairs={{4,0},{8,4},{12,8},{16,12},{20,16},{24,20},{28,24},{32,28},{36,32}... | collective-permute-start | bytes 196616 | tf_op jit(solution)/shard_map/ppermute | solution.py:25
  40.5 9.0 %collective-permute-start.3 = (bf16[2,128,128]{2,1,0:T(8,128)(2,1)S(1)}, bf16[2,128,128]{2,1,0:T(8,128)(2,1)S(1)}, u32[]{:S(2)}, u32[]{:S(2)}) collective-permute-start(bf16[2,128,128]{2,1,0:T(8,128)(2,1)S(1)} %get-tuple-element.17), channel_id=1, source_target_pairs={{0,64},{4,68},{8,72},{12,76},{16,80},{20,84},{24,88},{28,92},{32,9... | collective-permute-start | bytes 196616 | tf_op jit(solution)/shard_map/ppermute | solution.py:25
  49.4 8.2 %collective-permute-start.4 = (bf16[2,128,128]{2,1,0:T(8,128)(2,1)S(1)}, bf16[2,128,128]{2,1,0:T(8,128)(2,1)S(1)}, u32[]{:S(2)}, u32[]{:S(2)}) collective-permute-start(bf16[2,128,128]{2,1,0:T(8,128)(2,1)S(1)} %get-tuple-element.16), channel_id=1, source_target_pairs={{0,60},{4,64},{8,68},{12,72},{16,76},{20,80},{24,84},{28,88},{32,9... | collective-permute-start | bytes 196616 | tf_op jit(solution)/shard_map/ppermute | solution.py:25
  57.7 7.7 %collective-permute-start.5 = (bf16[2,128,128]{2,1,0:T(8,128)(2,1)S(1)}, bf16[2,128,128]{2,1,0:T(8,128)(2,1)S(1)}, u32[]{:S(2)}, u32[]{:S(2)}) collective-permute-start(bf16[2,128,128]{2,1,0:T(8,128)(2,1)S(1)} %get-tuple-element.15), channel_id=1, source_target_pairs={{0,4},{4,8},{8,12},{12,16},{16,20},{20,24},{24,28},{28,32},{32,36}... | collective-permute-start | bytes 196616 | tf_op jit(solution)/shard_map/ppermute | solution.py:25

commit v6 on v5

--- a/solution.py
+++ b/solution.py
@@ -168,12 +168,33 @@
     )
     outgoing = outgoing.reshape(slot_count, per_slot, tile_rows, coarse_width)
     own_masked = own_masked.reshape(slot_count, per_slot, tile_rows, coarse_width)
-    arrived = [None] * slot_count
-    for slot_index in range(slot_count):
-        arrived[slot_index] = shifted(
-            outgoing[slot_count - 1 - slot_index], "sub", -offsets[slot_index]
-        )
-    received = jnp.stack(arrived)
+    slot_of = {offset: index for index, offset in enumerate(offsets)}
+
+    def piece(offset):
+        return outgoing[slot_of[offset]]
+
+    sub_place = lax.axis_index("sub")
+    down = shifted(jnp.stack([piece(-across - 1), piece(-1), piece(across - 1)]), "sub", -1)
+    up = shifted(jnp.stack([piece(-across + 1), piece(1), piece(across + 1)]), "sub", 1)
+    corner = lax.ppermute(
+        jnp.where(sub_place == 0, piece(across - 1), piece(-across + 1)),
+        "sub",
+        [(0, across - 1), (sub_count - 1, sub_count - across)],
+    )
+    far_down = shifted(jnp.stack([piece(-across), down[0], up[0]]), "sub", -across)
+    far_up = shifted(jnp.stack([piece(across), down[2], up[2]]), "sub", across)
+    zero = jnp.zeros_like(corner)
+    arrival = {
+        -across - 1: far_up[2],
+        -across: far_up[0],
+        -across + 1: far_up[1] + jnp.where(sub_place == across - 1, corner, zero),
+        -1: up[1],
+        1: down[1],
+        across - 1: far_down[2] + jnp.where(sub_place == sub_count - across, corner, zero),
+        across: far_down[0],
+        across + 1: far_down[1],
+    }
+    received = jnp.stack([arrival[offset] for offset in offsets])
     row_share = coarse_width // crow_count
     owner_index = pivot_owner[0]
     coupling = jnp.einsum(

time: 91.8 us -> 85.4 us (0.930)
  the two profiles are of different devices: /device:TPU:416 before, /device:TPU:198 now
where the time goes in v6:
time: 85.4 us; the launch traced here: 84.8 us
  waiting for transfers between devices  24.7 us (29%)
  blocking collectives  21.9 us (26%)
  starting transfers between devices  19.3 us (23%)
  Pallas kernels  10.3 us (12%)
  local copies, waits for them, and re-layouts  4.6 us (5%)
  other arithmetic  2.14 us (3%)
  between operations  1.52 us (2%)
    ppermute x6, waiting for transfers between devices, shifted(): lax.ppermute(value, axis, [(source, source + steps) for source in range(i...  24.7 us
    all_to_all x1, blocking collectives, per_device(): lax.all_to_all(outgoing_rows, 'crow', 0, 0, tiled=True)  21.9 us
    ppermute x6, starting transfers between devices, shifted(): lax.ppermute(value, axis, [(source, source + steps) for source in range(i...  18.6 us
    pallas_call x1, Pallas kernels, eliminate_panel(): pl.pallas_call(panel_kernel, out_shape=(jax.ShapeDtypeStruct((share, widt...  6.66 us
    pallas_call x1, Pallas kernels, local_apply(): pl.pallas_call(local_apply_kernel, out_shape=(jax.ShapeDtypeStruct((width...  3.61 us
  transfers between devices with their start and end apart: 7, of which 5 were waited for; matrix products, arithmetic and copies ran while one was open for 3% of the time, Pallas kernels for 0%

profile of v6, /device:TPU:198, one launch (start us, length us, event | category | flops | bytes accessed | tf_op | source)
XLA Modules:
  0.0 84.8 jit_solution(16387420758600291677)
XLA Ops:
  0.6 0.8 slice_bitcast_fusion.12
  1.4 1.3 %collective-permute-start.1 = (bf16[128,128]{1,0:T(8,128)(2,1)S(1)}, bf16[128,128]{1,0:T(8,128)(2,1)S(1)}, u32[]{:S(2)}, u32[]{:S(2)}) collective-permute-start(bf16[128,128]{1,0:T(8,128)(2,1)S(1)} %get-tuple-element.9), channel_id=1, source_target_pairs={{1,0},{2,1},{3,2},{5,4},{6,5},{7,6},{9,8},{10,9},{11,10},{13,12},{... | collective-permute-start | bytes 98312 | tf_op jit(solution)/shard_map/ppermute | solution.py:25
  2.7 0.8 slice_bitcast_fusion.13
  3.5 4.5 %collective-permute-start = (bf16[2,128,128]{2,1,0:T(8,128)(2,1)S(1)}, bf16[2,128,128]{2,1,0:T(8,128)(2,1)S(1)}, u32[]{:S(2)}, u32[]{:S(2)}) collective-permute-start(bf16[2,128,128]{2,1,0:T(8,128)(2,1)S(1)} %pad_maximum_fusion.6), channel_id=1, source_target_pairs={{0,1},{1,2},{2,3},{4,5},{5,6},{6,7},{8,9},{9,10},{10,11},{12,13},{... | collective-permute-start | bytes 196616 | tf_op jit(solution)/shard_map/ppermute | solution.py:25
  8.0 0.7 compare_convert_fusion
  8.8 0.6 reshape.42.live_ref
  9.4 0.5 collective-permute-done
  9.9 0.6 slice_bitcast_fusion.10
  10.5 0.0 collective-permute-done.1.zn_ref
  10.5 0.6 copy-done.2
  11.1 3.6 %shard_map.85 = (f32[128,128]{1,0:T(8,128)}, bf16[16,128,128]{2,1,0:T(8,128)(2,1)}, bf16[16,128,128]{2,1,0:T(8,128)(2,1)}) custom-call(s32[16]{0:T(128)} %bitcast.70, s32[16]{0:T(128)} %reshape.42.live_ref, bf16[3072,128]{1,0:T(8,128)(2,1)} %bitcast.65, bf16[128,128]{1,0:T(8,128)(2,1)} %get-tuple-element.25.zp_ref, bf16[128,128]{1,0:T(8,128)(2,1)} %copy-done.2, ...), custom_call_target="tpu_custom_call" | custom-call | tf_op jit(solution)/shard_map/pallas_call | solution.py:74
  14.7 1.1 %slice_bitcast_fusion.2 = (bf16[1,2,128,128]{3,2,1,0:T(8,128)(2,1)S(1)}, bf16[2,128,128]{2,1,0:T(8,128)(2,1)S(1)}, bf16[1,2,128,128]{3,2,1,0:T(8,128)(2,1)S(1)},...) fusion(bf16[16,128,128]{2,1,0:T(8,128)(2,1)} %get-tuple-element, ...), kind=kLoop, calls=%fused_computation.21 | loop fusion | flops 32768 | bytes 1114113 | tf_op jit(solution)/shard_map/slice | solution.py:174
  15.9 1.9 %collective-permute-start.2 = (bf16[3,2,128,128]{3,2,1,0:T(8,128)(2,1)S(1)}, bf16[3,2,128,128]{3,2,1,0:T(8,128)(2,1)S(1)}, u32[]{:S(2)}, u32[]{:S(2)}) collective-permute-start(bf16[3,2,128,128]{3,2,1,0:T(8,128)(2,1)S(1)} %pad_maximum_fusion.2), channel_id=1, source_target_pairs={{4,0},{8,4},{12,8},{16,12},{20,16},{24,20},{28,24},{32,28},{36,32}... | collective-permute-start | bytes 589832 | tf_op jit(solution)/shard_map/ppermute | solution.py:25
  17.8 0.0 copy-start.1
  17.9 2.4 %collective-permute-start.3 = (bf16[3,2,128,128]{3,2,1,0:T(8,128)(2,1)S(1)}, bf16[3,2,128,128]{3,2,1,0:T(8,128)(2,1)S(1)}, u32[]{:S(2)}, u32[]{:S(2)}) collective-permute-start(bf16[3,2,128,128]{3,2,1,0:T(8,128)(2,1)S(1)} %pad_maximum_fusion.3), channel_id=1, source_target_pairs={{0,4},{4,8},{8,12},{12,16},{16,20},{20,24},{24,28},{28,32},{32,36}... | collective-permute-start | bytes 589832 | tf_op jit(solution)/shard_map/ppermute | solution.py:25
  20.3 0.7 collective-permute-done.2
  21.0 3.9 %collective-permute-done.3 = bf16[3,2,128,128]{3,2,1,0:T(8,128)(2,1)S(1)} collective-permute-done((bf16[3,2,128,128]{3,2,1,0:T(8,128)(2,1)S(1)}, bf16[3,2,128,128]{3,2,1,0:T(8,128)(2,1)S(1)}, u32[]{:S(2)}, u32[]{:S(2)}) %collective-permute-start.3) | collective-permute-done | bytes 196640 | tf_op jit(solution)/shard_map/ppermute | solution.py:25
  24.9 6.5 %collective-permute-start.4 = (bf16[3,2,128,128]{3,2,1,0:T(8,128)(2,1)S(1)}, bf16[3,2,128,128]{3,2,1,0:T(8,128)(2,1)S(1)}, u32[]{:S(2)}, u32[]{:S(2)}) collective-permute-start(bf16[3,2,128,128]{3,2,1,0:T(8,128)(2,1)S(1)} %pad_maximum_fusion.4), channel_id=1, source_target_pairs={{0,64},{4,68},{8,72},{12,76},{16,80},{20,84},{24,88},{28,92},{32,9... | collective-permute-start | bytes 589832 | tf_op jit(solution)/shard_map/ppermute | solution.py:25
  31.4 0.7 collective-permute-start.5
  32.1 7.8 %collective-permute-done.4 = bf16[3,2,128,128]{3,2,1,0:T(8,128)(2,1)S(1)} collective-permute-done((bf16[3,2,128,128]{3,2,1,0:T(8,128)(2,1)S(1)}, bf16[3,2,128,128]{3,2,1,0:T(8,128)(2,1)S(1)}, u32[]{:S(2)}, u32[]{:S(2)}) %collective-permute-start.4) | collective-permute-done | bytes 196640 | tf_op jit(solution)/shard_map/ppermute | solution.py:25
  40.0 0.0 collective-permute-done.5
  40.1 1.9 %collective-permute-start.6 = (bf16[3,2,128,128]{3,2,1,0:T(8,128)(2,1)S(1)}, bf16[3,2,128,128]{3,2,1,0:T(8,128)(2,1)S(1)}, u32[]{:S(2)}, u32[]{:S(2)}) collective-permute-start(bf16[3,2,128,128]{3,2,1,0:T(8,128)(2,1)S(1)} %pad_maximum_fusion.5), channel_id=1, source_target_pairs={{64,0},{68,4},{72,8},{76,12},{80,16},{84,20},{88,24},{92,28},{96,3... | collective-permute-start | bytes 589832 | tf_op jit(solution)/shard_map/ppermute | solution.py:25
  42.7 0.1 copy.14
  42.8 11.8 %collective-permute-done.6 = bf16[3,2,128,128]{3,2,1,0:T(8,128)(2,1)S(1)} collective-permute-done((bf16[3,2,128,128]{3,2,1,0:T(8,128)(2,1)S(1)}, bf16[3,2,128,128]{3,2,1,0:T(8,128)(2,1)S(1)}, u32[]{:S(2)}, u32[]{:S(2)}) %collective-permute-start.6) | collective-permute-done | bytes 196640 | tf_op jit(solution)/shard_map/ppermute | solution.py:25
  54.6 0.3 convolution_bitcast_fusion
  55.0 0.5 copy.15
  55.5 0.2 constant_dynamic-slice_fusion
  55.7 0.2 copy.19
  55.9 0.1 reshape_reshape.3
  56.1 0.1 pad_maximum_fusion
  56.2 21.9 %all_to_all.5.pieces_ref = f32[4,64,1152]{2,1,0:T(8,128)} all-to-all(f32[4,64,1152]{2,1,0:T(8,128)S(1)} %pad_maximum_fusion), channel_id=1, replica_groups=mesh['sub'=128,'crow'=4] {'crow'}, dimensions={0} | all-to-all | bytes 2359296 | tf_op jit(solution)/shard_map/all_to_all | solution.py:214
  78.1 6.7 %shard_map.86 = (f32[32,128]{1,0:T(8,128)}, f32[32,1024]{1,0:T(8,128)}, f32[32,32]{1,0:T(8,128)}) custom-call(s32[1]{0:T(128)S(6)} %copy.26.owner_ref, f32[4,64,1152]{2,1,0:T(8,128)} %all_to_all.5.pieces_ref), custom_call_target="tpu_custom_call" | custom-call | tf_op jit(solution)/shard_map/pallas_call | solution.py:136
  (21 shorter events, 0.4 us)
Async XLA Ops:
  1.4 9.1 %collective-permute-start.1 = (bf16[128,128]{1,0:T(8,128)(2,1)S(1)}, bf16[128,128]{1,0:T(8,128)(2,1)S(1)}, u32[]{:S(2)}, u32[]{:S(2)}) collective-permute-start(bf16[128,128]{1,0:T(8,128)(2,1)S(1)} %get-tuple-element.9), channel_id=1, source_target_pairs={{1,0},{2,1},{3,2},{5,4},{6,5},{7,6},{9,8},{10,9},{11,10},{13,12},{... | collective-permute-start | bytes 98312 | tf_op jit(solution)/shard_map/ppermute | solution.py:25
  3.5 6.4 %collective-permute-start = (bf16[2,128,128]{2,1,0:T(8,128)(2,1)S(1)}, bf16[2,128,128]{2,1,0:T(8,128)(2,1)S(1)}, u32[]{:S(2)}, u32[]{:S(2)}) collective-permute-start(bf16[2,128,128]{2,1,0:T(8,128)(2,1)S(1)} %pad_maximum_fusion.6), channel_id=1, source_target_pairs={{0,1},{1,2},{2,3},{4,5},{5,6},{6,7},{8,9},{9,10},{10,11},{12,13},{... | collective-permute-start | bytes 196616 | tf_op jit(solution)/shard_map/ppermute | solution.py:25
  10.5 0.6 copy-start.2
  15.9 5.1 %collective-permute-start.2 = (bf16[3,2,128,128]{3,2,1,0:T(8,128)(2,1)S(1)}, bf16[3,2,128,128]{3,2,1,0:T(8,128)(2,1)S(1)}, u32[]{:S(2)}, u32[]{:S(2)}) collective-permute-start(bf16[3,2,128,128]{3,2,1,0:T(8,128)(2,1)S(1)} %pad_maximum_fusion.2), channel_id=1, source_target_pairs={{4,0},{8,4},{12,8},{16,12},{20,16},{24,20},{28,24},{32,28},{36,32}... | collective-permute-start | bytes 589832 | tf_op jit(solution)/shard_map/ppermute | solution.py:25
  17.8 24.9 %copy-start.1 = (f32[128,128]{1,0:T(8,128)S(1)}, f32[128,128]{1,0:T(8,128)}, u32[]{:S(2)}) copy-start(f32[128,128]{1,0:T(8,128)} %get-tuple-element.6) | copy-start | bytes 196612
  17.9 7.0 %collective-permute-start.3 = (bf16[3,2,128,128]{3,2,1,0:T(8,128)(2,1)S(1)}, bf16[3,2,128,128]{3,2,1,0:T(8,128)(2,1)S(1)}, u32[]{:S(2)}, u32[]{:S(2)}) collective-permute-start(bf16[3,2,128,128]{3,2,1,0:T(8,128)(2,1)S(1)} %pad_maximum_fusion.3), channel_id=1, source_target_pairs={{0,4},{4,8},{8,12},{12,16},{16,20},{20,24},{24,28},{28,32},{32,36}... | collective-permute-start | bytes 589832 | tf_op jit(solution)/shard_map/ppermute | solution.py:25
  24.9 29.8 %copy-start = (bf16[16,128,128]{2,1,0:T(8,128)(2,1)S(1)}, bf16[16,128,128]{2,1,0:T(8,128)(2,1)}, u32[]{:S(2)}) copy-start(bf16[16,128,128]{2,1,0:T(8,128)(2,1)} %get-tuple-element.8) | copy-start | bytes 1572868
  24.9 15.1 %collective-permute-start.4 = (bf16[3,2,128,128]{3,2,1,0:T(8,128)(2,1)S(1)}, bf16[3,2,128,128]{3,2,1,0:T(8,128)(2,1)S(1)}, u32[]{:S(2)}, u32[]{:S(2)}) collective-permute-start(bf16[3,2,128,128]{3,2,1,0:T(8,128)(2,1)S(1)} %pad_maximum_fusion.4), channel_id=1, source_target_pairs={{0,64},{4,68},{8,72},{12,76},{16,80},{20,84},{24,88},{28,92},{32,9... | collective-permute-start | bytes 589832 | tf_op jit(solution)/shard_map/ppermute | solution.py:25
  31.4 8.5 %collective-permute-start.5 = (bf16[2,128,128]{2,1,0:T(8,128)(2,1)S(1)}, bf16[2,128,128]{2,1,0:T(8,128)(2,1)S(1)}, u32[]{:S(2)}, u32[]{:S(2)}) collective-permute-start(bf16[2,128,128]{2,1,0:T(8,128)(2,1)S(1)} %get-tuple-element.12), channel_id=1, source_target_pairs={{0,60},{508,448},{1,61},{509,449},{2,62},{510,450},{3,63},{511,451}} | collective-permute-start | bytes 196616 | tf_op jit(solution)/shard_map/ppermute | solution.py:179
  40.1 14.4 %collective-permute-start.6 = (bf16[3,2,128,128]{3,2,1,0:T(8,128)(2,1)S(1)}, bf16[3,2,128,128]{3,2,1,0:T(8,128)(2,1)S(1)}, u32[]{:S(2)}, u32[]{:S(2)}) collective-permute-start(bf16[3,2,128,128]{3,2,1,0:T(8,128)(2,1)S(1)} %pad_maximum_fusion.5), channel_id=1, source_target_pairs={{64,0},{68,4},{72,8},{76,12},{80,16},{84,20},{88,24},{92,28},{96,3... | collective-permute-start | bytes 589832 | tf_op jit(solution)/shard_map/ppermute | solution.py:25

commit v7 on v6

--- a/solution.py
+++ b/solution.py
@@ -107,20 +107,14 @@
 
     pivot = pick(lead)
     pivot = (pivot + pivot.T) * 0.5
-    row_id = lax.broadcasted_iota(jnp.int32, (share, 2 * share), 0)
-    col_id = lax.broadcasted_iota(jnp.int32, (share, 2 * share), 1)
+    row_id = lax.broadcasted_iota(jnp.int32, (share, 1), 0)
     work = jnp.concatenate([pivot, jnp.eye(share, dtype=jnp.float32)], 1)
-
-    def step(k, work):
-        row = jnp.sum(jnp.where(row_id == k, work, 0.0), axis=0, keepdims=True)
-        col = jnp.sum(jnp.where(col_id == k, work, 0.0), axis=1, keepdims=True)
-        diag = jnp.sum(jnp.where(col_id[:1] == k, row, 0.0), axis=1, keepdims=True)
-        scale = 1.0 / jnp.sqrt(diag)
+    for k in range(share):
+        row = work[k:k + 1, :]
+        scale = 1.0 / jnp.sqrt(row[:, k:k + 1])
         unit_row = row * scale
-        below = jnp.where(row_id[:, :1] > k, col * scale, 0.0)
-        return jnp.where(row_id == k, unit_row, work - below * unit_row)
-
-    work = lax.fori_loop(0, share, step, work)
+        below = jnp.where(row_id > k, work[:, k:k + 1] * scale, 0.0)
+        work = jnp.where(row_id == k, unit_row, work - below * unit_row)
     inverse = work[:, share:]
     solved = _exact(inverse, lead, ((1,), (0,)))
     panel = _exact(pick(own), inverse, ((1,), (1,)))
@@ -173,24 +167,34 @@
     def piece(offset):
         return outgoing[slot_of[offset]]
 
-    sub_place = lax.axis_index("sub")
-    down = shifted(jnp.stack([piece(-across - 1), piece(-1), piece(across - 1)]), "sub", -1)
-    up = shifted(jnp.stack([piece(-across + 1), piece(1), piece(across + 1)]), "sub", 1)
-    corner = lax.ppermute(
-        jnp.where(sub_place == 0, piece(across - 1), piece(-across + 1)),
-        "sub",
-        [(0, across - 1), (sub_count - 1, sub_count - across)],
-    )
-    far_down = shifted(jnp.stack([piece(-across), down[0], up[0]]), "sub", -across)
-    far_up = shifted(jnp.stack([piece(across), down[2], up[2]]), "sub", across)
-    zero = jnp.zeros_like(corner)
+    last = sub_count - 1
+    down = lax.ppermute(
+        jnp.stack([piece(-across - 1), piece(-1), piece(across - 1)]),
+        "sub",
+        [(t, t - 1) for t in range(1, sub_count)] + [(0, last)],
+    )
+    up = lax.ppermute(
+        jnp.stack([piece(-across + 1), piece(1), piece(across + 1)]),
+        "sub",
+        [(t, t + 1) for t in range(last)] + [(last, 0)],
+    )
+    far_down = lax.ppermute(
+        jnp.stack([piece(-across), down[0], up[0]]),
+        "sub",
+        [(u, u - across) for u in range(across, sub_count)] + [(0, sub_count - across)],
+    )
+    far_up = lax.ppermute(
+        jnp.stack([piece(across), down[2], up[2]]),
+        "sub",
+        [(u, u + across) for u in range(sub_count - across)] + [(last, across - 1)],
+    )
     arrival = {
         -across - 1: far_up[2],
         -across: far_up[0],
-        -across + 1: far_up[1] + jnp.where(sub_place == across - 1, corner, zero),
+        -across + 1: far_up[1],
         -1: up[1],
         1: down[1],
-        across - 1: far_down[2] + jnp.where(sub_place == sub_count - across, corner, zero),
+        across - 1: far_down[2],
         across: far_down[0],
         across + 1: far_down[1],
     }

time: 85.4 us -> 84.7 us (level)
  other arithmetic: 2.14 us -> 0.96 us
  local copies, waits for them, and re-layouts: 4.6 us -> 5.73 us
    ppermute x1 -> x4, waiting for transfers between devices: 0.01 us -> 24.9 us  [the longest x1 11.8 us: per_device(): lax.ppermute(jnp.stack([piece(-across), down[0], up[0]]), 'sub', [(u, u -...]
    ppermute x6 -> x2, waiting for transfers between devices: 24.7 us -> 0.55 us  [shifted(): lax.ppermute(value, axis, [(source, source + steps) for source in range(i...]
    ppermute x6 -> x2, starting transfers between devices: 18.6 us -> 5.83 us  [shifted(): lax.ppermute(value, axis, [(source, source + steps) for source in range(i...]
    ppermute x1 -> x4, starting transfers between devices: 0.66 us -> 12.6 us  [the longest x1 6.39 us: per_device(): lax.ppermute(jnp.stack([piece(across), down[2], up[2]]), 'sub', [(u, u +...]
    slice x1 -> x0, other arithmetic: 1.1 us -> none  [piece(): return outgoing[slot_of[offset]]]
    slice x2 -> x3, local copies, waits for them, and re-layouts: 0.01 us -> 1.11 us  [the longest x1 1.1 us: piece(): return outgoing[slot_of[offset]]]
  transfers between devices with their start and end apart: 7 -> 6, of which waited for: 5 -> 5; matrix products, arithmetic and copies ran while one was open for 3% -> 3% of each run, Pallas kernels for 0% -> 0%
where the time goes in v7:
time: 84.7 us; the launch traced here: 84.2 us
  waiting for transfers between devices  25.4 us (30%)
  blocking collectives  22 us (26%)
  starting transfers between devices  18.5 us (22%)
  Pallas kernels  9.79 us (12%)
  local copies, waits for them, and re-layouts  5.73 us (7%)
  between operations  1.49 us (2%)
  other arithmetic  0.96 us (1%)
    all_to_all x1, blocking collectives, per_device(): lax.all_to_all(outgoing_rows, 'crow', 0, 0, tiled=True)  22 us
    ppermute x1, waiting for transfers between devices, per_device(): lax.ppermute(jnp.stack([piece(-across), down[0], up[0]]), 'sub', [(u, u -...  11.8 us
    ppermute x1, waiting for transfers between devices, per_device(): lax.ppermute(jnp.stack([piece(across), down[2], up[2]]), 'sub', [(u, u +...  8.53 us
    ppermute x1, starting transfers between devices, per_device(): lax.ppermute(jnp.stack([piece(across), down[2], up[2]]), 'sub', [(u, u +...  6.39 us
    pallas_call x1, Pallas kernels, eliminate_panel(): pl.pallas_call(panel_kernel, out_shape=(jax.ShapeDtypeStruct((share, widt...  6.18 us
    ppermute x2, starting transfers between devices, shifted(): lax.ppermute(value, axis, [(source, source + steps) for source in range(i...  5.83 us
    ppermute x1, waiting for transfers between devices, per_device(): lax.ppermute(jnp.stack([piece(-across + 1), piece(1), piece(across + 1)])...  3.86 us
    pallas_call x1, Pallas kernels, local_apply(): pl.pallas_call(local_apply_kernel, out_shape=(jax.ShapeDtypeStruct((width...  3.61 us
  transfers between devices with their start and end apart: 6, of which 5 were waited for; matrix products, arithmetic and copies ran while one was open for 3% of the time, Pallas kernels for 0%

profile of v7, /device:TPU:198, one launch (start us, length us, event | category | flops | bytes accessed | tf_op | source)
XLA Modules:
  0.0 84.2 jit_solution(1351332886900857114)
XLA Ops:
  0.6 0.8 slice_bitcast_fusion.10
  1.4 1.3 %collective-permute-start.1 = (bf16[128,128]{1,0:T(8,128)(2,1)S(1)}, bf16[128,128]{1,0:T(8,128)(2,1)S(1)}, u32[]{:S(2)}, u32[]{:S(2)}) collective-permute-start(bf16[128,128]{1,0:T(8,128)(2,1)S(1)} %get-tuple-element.9), channel_id=1, source_target_pairs={{1,0},{2,1},{3,2},{5,4},{6,5},{7,6},{9,8},{10,9},{11,10},{13,12},{... | collective-permute-start | bytes 98312 | tf_op jit(solution)/shard_map/ppermute | solution.py:25
  2.7 0.8 slice_bitcast_fusion.11
  3.5 4.5 %collective-permute-start = (bf16[2,128,128]{2,1,0:T(8,128)(2,1)S(1)}, bf16[2,128,128]{2,1,0:T(8,128)(2,1)S(1)}, u32[]{:S(2)}, u32[]{:S(2)}) collective-permute-start(bf16[2,128,128]{2,1,0:T(8,128)(2,1)S(1)} %pad_maximum_fusion.6), channel_id=1, source_target_pairs={{0,1},{1,2},{2,3},{4,5},{5,6},{6,7},{8,9},{9,10},{10,11},{12,13},{... | collective-permute-start | bytes 196616 | tf_op jit(solution)/shard_map/ppermute | solution.py:25
  8.0 0.7 compare_convert_fusion
  8.8 0.6 reshape.40.live_ref
  9.4 0.5 collective-permute-done
  9.9 0.6 slice_bitcast_fusion.8
  10.5 0.0 collective-permute-done.1.zn_ref
  10.5 0.6 copy-done.2
  11.2 3.6 %shard_map.85 = (f32[128,128]{1,0:T(8,128)}, bf16[16,128,128]{2,1,0:T(8,128)(2,1)}, bf16[16,128,128]{2,1,0:T(8,128)(2,1)}) custom-call(s32[16]{0:T(128)} %bitcast.46, s32[16]{0:T(128)} %reshape.40.live_ref, bf16[3072,128]{1,0:T(8,128)(2,1)} %bitcast.41, bf16[128,128]{1,0:T(8,128)(2,1)} %get-tuple-element.24.zp_ref, bf16[128,128]{1,0:T(8,128)(2,1)} %copy-done.2, ...), custom_call_target="tpu_custom_call" | custom-call | tf_op jit(solution)/shard_map/pallas_call | solution.py:74
  14.8 1.1 %slice_bitcast_fusion = (bf16[1,2,128,128]{3,2,1,0:T(8,128)(2,1)S(1)}, bf16[1,2,128,128]{3,2,1,0:T(8,128)(2,1)S(1)}, bf16[1,2,128,128]{3,2,1,0:T(8,128)(2,1)S(1)...) fusion(bf16[16,128,128]{2,1,0:T(8,128)(2,1)} %get-tuple-element.7), kind=kLoop, calls=%fused_computation.14 | loop fusion | bytes 1048576 | tf_op jit(solution)/shard_map/slice | solution.py:168
  15.9 1.9 %collective-permute-start.2 = (bf16[3,2,128,128]{3,2,1,0:T(8,128)(2,1)S(1)}, bf16[3,2,128,128]{3,2,1,0:T(8,128)(2,1)S(1)}, u32[]{:S(2)}, u32[]{:S(2)}) collective-permute-start(bf16[3,2,128,128]{3,2,1,0:T(8,128)(2,1)S(1)} %pad_maximum_fusion.2), channel_id=1, source_target_pairs={{4,0},{8,4},{12,8},{16,12},{20,16},{24,20},{28,24},{32,28},{36,32}... | collective-permute-start | bytes 589832 | tf_op jit(solution)/shard_map/ppermute | solution.py:171
  17.8 0.0 copy-start.1
  17.9 2.4 %collective-permute-start.3 = (bf16[3,2,128,128]{3,2,1,0:T(8,128)(2,1)S(1)}, bf16[3,2,128,128]{3,2,1,0:T(8,128)(2,1)S(1)}, u32[]{:S(2)}, u32[]{:S(2)}) collective-permute-start(bf16[3,2,128,128]{3,2,1,0:T(8,128)(2,1)S(1)} %pad_maximum_fusion.3), channel_id=1, source_target_pairs={{0,4},{4,8},{8,12},{12,16},{16,20},{20,24},{24,28},{28,32},{32,36}... | collective-permute-start | bytes 589832 | tf_op jit(solution)/shard_map/ppermute | solution.py:176
  20.3 0.7 collective-permute-done.2
  21.0 3.9 %collective-permute-done.3 = bf16[3,2,128,128]{3,2,1,0:T(8,128)(2,1)S(1)} collective-permute-done((bf16[3,2,128,128]{3,2,1,0:T(8,128)(2,1)S(1)}, bf16[3,2,128,128]{3,2,1,0:T(8,128)(2,1)S(1)}, u32[]{:S(2)}, u32[]{:S(2)}) %collective-permute-start.3) | collective-permute-done | bytes 196640 | tf_op jit(solution)/shard_map/ppermute | solution.py:176
  24.9 6.4 %collective-permute-start.4 = (bf16[3,2,128,128]{3,2,1,0:T(8,128)(2,1)S(1)}, bf16[3,2,128,128]{3,2,1,0:T(8,128)(2,1)S(1)}, u32[]{:S(2)}, u32[]{:S(2)}) collective-permute-start(bf16[3,2,128,128]{3,2,1,0:T(8,128)(2,1)S(1)} %pad_maximum_fusion.4), channel_id=1, source_target_pairs={{0,64},{4,68},{8,72},{12,76},{16,80},{20,84},{24,88},{28,92},{32,9... | collective-permute-start | bytes 589832 | tf_op jit(solution)/shard_map/ppermute | solution.py:186
  31.3 8.5 %collective-permute-done.4 = bf16[3,2,128,128]{3,2,1,0:T(8,128)(2,1)S(1)} collective-permute-done((bf16[3,2,128,128]{3,2,1,0:T(8,128)(2,1)S(1)}, bf16[3,2,128,128]{3,2,1,0:T(8,128)(2,1)S(1)}, u32[]{:S(2)}, u32[]{:S(2)}) %collective-permute-start.4) | collective-permute-done | bytes 196640 | tf_op jit(solution)/shard_map/ppermute | solution.py:186
  39.9 1.9 %collective-permute-start.5 = (bf16[3,2,128,128]{3,2,1,0:T(8,128)(2,1)S(1)}, bf16[3,2,128,128]{3,2,1,0:T(8,128)(2,1)S(1)}, u32[]{:S(2)}, u32[]{:S(2)}) collective-permute-start(bf16[3,2,128,128]{3,2,1,0:T(8,128)(2,1)S(1)} %pad_maximum_fusion.5), channel_id=1, source_target_pairs={{64,0},{68,4},{72,8},{76,12},{80,16},{84,20},{88,24},{92,28},{96,3... | collective-permute-start | bytes 589832 | tf_op jit(solution)/shard_map/ppermute | solution.py:181
  42.5 0.0 copy-done.1
  42.5 0.1 copy.14
  42.6 11.8 %collective-permute-done.5 = bf16[3,2,128,128]{3,2,1,0:T(8,128)(2,1)S(1)} collective-permute-done((bf16[3,2,128,128]{3,2,1,0:T(8,128)(2,1)S(1)}, bf16[3,2,128,128]{3,2,1,0:T(8,128)(2,1)S(1)}, u32[]{:S(2)}, u32[]{:S(2)}) %collective-permute-start.5) | collective-permute-done | bytes 196640 | tf_op jit(solution)/shard_map/ppermute | solution.py:181
  54.4 0.0 copy-done
  54.4 0.3 convolution_bitcast_fusion
  54.8 0.5 copy.15
  55.3 0.2 constant_dynamic-slice_fusion
  55.6 0.2 copy.19
  55.8 0.1 reshape_reshape.3
  55.9 0.1 pad_maximum_fusion
  56.0 22.0 %all_to_all.5.pieces_ref = f32[4,64,1152]{2,1,0:T(8,128)} all-to-all(f32[4,64,1152]{2,1,0:T(8,128)S(1)} %pad_maximum_fusion), channel_id=1, replica_groups=mesh['sub'=128,'crow'=4] {'crow'}, dimensions={0} | all-to-all | bytes 2359296 | tf_op jit(solution)/shard_map/all_to_all | solution.py:218
  78.0 6.2 %shard_map.86 = (f32[32,128]{1,0:T(8,128)}, f32[32,1024]{1,0:T(8,128)}, f32[32,32]{1,0:T(8,128)}) custom-call(s32[1]{0:T(128)S(6)} %copy.25.owner_ref, f32[4,64,1152]{2,1,0:T(8,128)} %all_to_all.5.pieces_ref), custom_call_target="tpu_custom_call" | custom-call | tf_op jit(solution)/shard_map/pallas_call | solution.py:130
  (18 shorter events, 0.3 us)
Async XLA Ops:
  1.4 9.1 %collective-permute-start.1 = (bf16[128,128]{1,0:T(8,128)(2,1)S(1)}, bf16[128,128]{1,0:T(8,128)(2,1)S(1)}, u32[]{:S(2)}, u32[]{:S(2)}) collective-permute-start(bf16[128,128]{1,0:T(8,128)(2,1)S(1)} %get-tuple-element.9), channel_id=1, source_target_pairs={{1,0},{2,1},{3,2},{5,4},{6,5},{7,6},{9,8},{10,9},{11,10},{13,12},{... | collective-permute-start | bytes 98312 | tf_op jit(solution)/shard_map/ppermute | solution.py:25
  3.5 6.4 %collective-permute-start = (bf16[2,128,128]{2,1,0:T(8,128)(2,1)S(1)}, bf16[2,128,128]{2,1,0:T(8,128)(2,1)S(1)}, u32[]{:S(2)}, u32[]{:S(2)}) collective-permute-start(bf16[2,128,128]{2,1,0:T(8,128)(2,1)S(1)} %pad_maximum_fusion.6), channel_id=1, source_target_pairs={{0,1},{1,2},{2,3},{4,5},{5,6},{6,7},{8,9},{9,10},{10,11},{12,13},{... | collective-permute-start | bytes 196616 | tf_op jit(solution)/shard_map/ppermute | solution.py:25
  10.5 0.6 copy-start.2
  15.9 5.1 %collective-permute-start.2 = (bf16[3,2,128,128]{3,2,1,0:T(8,128)(2,1)S(1)}, bf16[3,2,128,128]{3,2,1,0:T(8,128)(2,1)S(1)}, u32[]{:S(2)}, u32[]{:S(2)}) collective-permute-start(bf16[3,2,128,128]{3,2,1,0:T(8,128)(2,1)S(1)} %pad_maximum_fusion.2), channel_id=1, source_target_pairs={{4,0},{8,4},{12,8},{16,12},{20,16},{24,20},{28,24},{32,28},{36,32}... | collective-permute-start | bytes 589832 | tf_op jit(solution)/shard_map/ppermute | solution.py:171
  17.8 24.7 %copy-start.1 = (f32[128,128]{1,0:T(8,128)S(1)}, f32[128,128]{1,0:T(8,128)}, u32[]{:S(2)}) copy-start(f32[128,128]{1,0:T(8,128)} %get-tuple-element.6) | copy-start | bytes 196612
  17.9 7.0 %collective-permute-start.3 = (bf16[3,2,128,128]{3,2,1,0:T(8,128)(2,1)S(1)}, bf16[3,2,128,128]{3,2,1,0:T(8,128)(2,1)S(1)}, u32[]{:S(2)}, u32[]{:S(2)}) collective-permute-start(bf16[3,2,128,128]{3,2,1,0:T(8,128)(2,1)S(1)} %pad_maximum_fusion.3), channel_id=1, source_target_pairs={{0,4},{4,8},{8,12},{12,16},{16,20},{20,24},{24,28},{28,32},{32,36}... | collective-permute-start | bytes 589832 | tf_op jit(solution)/shard_map/ppermute | solution.py:176
  21.0 33.4 %copy-start = (bf16[16,128,128]{2,1,0:T(8,128)(2,1)S(1)}, bf16[16,128,128]{2,1,0:T(8,128)(2,1)}, u32[]{:S(2)}) copy-start(bf16[16,128,128]{2,1,0:T(8,128)(2,1)} %get-tuple-element.8) | copy-start | bytes 1572868
  24.9 14.9 %collective-permute-start.4 = (bf16[3,2,128,128]{3,2,1,0:T(8,128)(2,1)S(1)}, bf16[3,2,128,128]{3,2,1,0:T(8,128)(2,1)S(1)}, u32[]{:S(2)}, u32[]{:S(2)}) collective-permute-start(bf16[3,2,128,128]{3,2,1,0:T(8,128)(2,1)S(1)} %pad_maximum_fusion.4), channel_id=1, source_target_pairs={{0,64},{4,68},{8,72},{12,76},{16,80},{20,84},{24,88},{28,92},{32,9... | collective-permute-start | bytes 589832 | tf_op jit(solution)/shard_map/ppermute | solution.py:186
  39.9 14.4 %collective-permute-start.5 = (bf16[3,2,128,128]{3,2,1,0:T(8,128)(2,1)S(1)}, bf16[3,2,128,128]{3,2,1,0:T(8,128)(2,1)S(1)}, u32[]{:S(2)}, u32[]{:S(2)}) collective-permute-start(bf16[3,2,128,128]{3,2,1,0:T(8,128)(2,1)S(1)} %pad_maximum_fusion.5), channel_id=1, source_target_pairs={{64,0},{68,4},{72,8},{76,12},{80,16},{84,20},{88,24},{92,28},{96,3... | collective-permute-start | bytes 589832 | tf_op jit(solution)/shard_map/ppermute | solution.py:181

commit v8 on v7

--- a/solution.py
+++ b/solution.py
@@ -1,3 +1,4 @@
+import functools
 import jax
 import jax.numpy as jnp
 from jax import lax
@@ -43,45 +44,54 @@
 
 
 def local_apply_kernel(
-    chosen_ref, live_ref, z_ref, zp_ref, zn_ref, d_ref, u_ref, up_ref,
-    gram_ref, out_ref, own_ref, app_ref,
+    groups, blocks_ref, counts_ref, z_ref, fp_ref, zn_ref, d_ref, u_ref, *refs
 ):
-    count, rows = d_ref.shape[0], d_ref.shape[1]
+    group_refs, own_ref, gram_ref, app_ref = refs[:len(groups)], refs[-3], refs[-2], refs[-1]
+    count, rows = d_ref.shape[1], d_ref.shape[2]
+    per_slot = own_ref.shape[1]
+    crow = lax.axis_index("crow")
 
     def rows_of(b):
-        return z_ref[pl.ds(b * rows, rows), :]
+        return z_ref[0, pl.ds(b * rows, rows), :]
 
     for b in range(count):
-        below = zp_ref[...] if b == 0 else rows_of(b - 1)
-        lower = up_ref[...] if b == 0 else u_ref[b - 1]
+        below = fp_ref[0] if b == 0 else rows_of(b - 1)
+        lower = fp_ref[1] if b == 0 else u_ref[0, b - 1]
         above = zn_ref[...] if b == count - 1 else rows_of(b + 1)
-        total = (_ab(d_ref[b], rows_of(b)) + _ab(u_ref[b], above)) + _atb(lower, below)
+        total = (_ab(d_ref[0, b], rows_of(b)) + _ab(u_ref[0, b], above)) + _atb(lower, below)
         app_ref[pl.ds(b * rows, rows), :] = total.astype(app_ref.dtype)
-    gram_ref[...] = _atb(z_ref[...], app_ref[...])
-    for i in range(out_ref.shape[0]):
-        start = pl.multiple_of(chosen_ref[i] * rows, rows)
-        out_ref[i] = app_ref[pl.ds(start, rows), :]
-        tile = z_ref[pl.ds(start, rows), :]
-        own_ref[i] = jnp.where(live_ref[i] > 0, tile, jnp.zeros_like(tile))
-
-
-def local_apply(chosen, live, centre, prev_rows, next_rows, diagonal, upper, prev_upper):
-    tiles = chosen.shape[0]
-    blocks, rows = diagonal.shape[0], diagonal.shape[1]
-    width = centre.shape[1]
+    gram_ref[...] = _atb(z_ref[0], app_ref[...])
+    for slot in range(own_ref.shape[0]):
+        for unit in range(per_slot):
+            start = pl.multiple_of(blocks_ref[0, 0, slot * per_slot + unit] * rows, rows)
+            tile = z_ref[0, pl.ds(start, rows), :]
+            live = crow * per_slot + unit < counts_ref[0, slot]
+            own_ref[slot, unit] = jnp.where(live, tile, jnp.zeros_like(tile))
+    for group, out_ref in zip(groups, group_refs):
+        for place, slot in enumerate(group):
+            for unit in range(per_slot):
+                start = pl.multiple_of(blocks_ref[0, 0, slot * per_slot + unit] * rows, rows)
+                out_ref[place, unit] = app_ref[pl.ds(start, rows), :]
+
+
+def local_apply(groups, tile_blocks, pair_counts, deflation, forward_pair, next_rows, diag_op, upper_op):
+    slots = pair_counts.shape[1]
+    per_slot = tile_blocks.shape[2] // slots
+    blocks, rows = diag_op.shape[1], diag_op.shape[2]
+    width = deflation.shape[2]
     vmem = pl.BlockSpec(memory_space=pltpu.VMEM)
     smem = pl.BlockSpec(memory_space=pltpu.SMEM)
+    tile = lambda n: jax.ShapeDtypeStruct((n, per_slot, rows, width), deflation.dtype)
     return pl.pallas_call(
-        local_apply_kernel,
-        out_shape=(
+        functools.partial(local_apply_kernel, groups),
+        out_shape=tuple(tile(len(g)) for g in groups) + (
+            tile(slots),
             jax.ShapeDtypeStruct((width, width), jnp.float32),
-            jax.ShapeDtypeStruct((tiles, rows, width), centre.dtype),
-            jax.ShapeDtypeStruct((tiles, rows, width), centre.dtype),
         ),
-        in_specs=[smem, smem] + [vmem] * 6,
-        out_specs=(vmem, vmem, vmem),
-        scratch_shapes=[pltpu.VMEM((blocks * rows, width), centre.dtype)],
-    )(chosen, live, centre, prev_rows, next_rows, diagonal, upper, prev_upper)
+        in_specs=[smem, smem] + [vmem] * 5,
+        out_specs=tuple(vmem for _ in range(len(groups) + 2)),
+        scratch_shapes=[pltpu.VMEM((blocks * rows, width), deflation.dtype)],
+    )(tile_blocks, pair_counts, deflation, forward_pair, next_rows, diag_op, upper_op)
 
 
 def _exact(a, b, dims):
@@ -154,37 +164,28 @@
         jnp.stack([local_rows[-tile_rows:], upper_op[0, blocks_here - 1]]), "crow", 1
     )
     next_rows = shifted(local_rows[:tile_rows], "crow", -1)
-    chosen = tile_blocks[0, 0]
-    position = crow_place * per_slot + jnp.arange(per_slot, dtype=jnp.int32)
-    live = (position[None, :] < pair_counts[0][:, None]).astype(jnp.int32).reshape(-1)
-    gram_part, outgoing, own_masked = local_apply(
-        chosen, live, local_rows, forward_pair[0], next_rows, diag_op[0], upper_op[0], forward_pair[1]
-    )
-    outgoing = outgoing.reshape(slot_count, per_slot, tile_rows, coarse_width)
-    own_masked = own_masked.reshape(slot_count, per_slot, tile_rows, coarse_width)
     slot_of = {offset: index for index, offset in enumerate(offsets)}
-
-    def piece(offset):
-        return outgoing[slot_of[offset]]
-
+    groups = (
+        (slot_of[-across - 1], slot_of[-1], slot_of[across - 1]),
+        (slot_of[-across + 1], slot_of[1], slot_of[across + 1]),
+        (slot_of[-across],),
+        (slot_of[across],),
+    )
+    down_out, up_out, near_down, near_up, own_masked, gram_part = local_apply(
+        groups, tile_blocks, pair_counts, deflation, forward_pair, next_rows, diag_op, upper_op
+    )
     last = sub_count - 1
     down = lax.ppermute(
-        jnp.stack([piece(-across - 1), piece(-1), piece(across - 1)]),
-        "sub",
-        [(t, t - 1) for t in range(1, sub_count)] + [(0, last)],
-    )
-    up = lax.ppermute(
-        jnp.stack([piece(-across + 1), piece(1), piece(across + 1)]),
-        "sub",
-        [(t, t + 1) for t in range(last)] + [(last, 0)],
-    )
+        down_out, "sub", [(t, t - 1) for t in range(1, sub_count)] + [(0, last)]
+    )
+    up = lax.ppermute(up_out, "sub", [(t, t + 1) for t in range(last)] + [(last, 0)])
     far_down = lax.ppermute(
-        jnp.stack([piece(-across), down[0], up[0]]),
+        jnp.concatenate([near_down, down[:1], up[:1]]),
         "sub",
         [(u, u - across) for u in range(across, sub_count)] + [(0, sub_count - across)],
     )
     far_up = lax.ppermute(
-        jnp.stack([piece(across), down[2], up[2]]),
+        jnp.concatenate([near_up, down[2:], up[2:]]),
         "sub",
         [(u, u + across) for u in range(sub_count - across)] + [(last, across - 1)],
     )

time: 84.7 us -> 85.4 us (level)
  waiting for transfers between devices: 25.4 us -> 29.9 us
  local copies, waits for them, and re-layouts: 5.73 us -> 4.05 us
  blocking collectives: 22 us -> 20.7 us
  starting transfers between devices: 18.5 us -> 17.5 us
    ppermute x2, waiting for transfers between devices: 0.55 us -> 4.51 us  [shifted(): lax.ppermute(value, axis, [(source, source + steps) for source in range(i...]
    all_to_all x1, blocking collectives: 22 us -> 20.7 us  [per_device(): lax.all_to_all(outgoing_rows, 'crow', 0, 0, tiled=True)]
    slice x5 -> x4, local copies, waits for them, and re-layouts: 1.14 us -> 0.05 us  [the longest x1 0.02 us: per_device(): up[:1]]
    ppermute x2, starting transfers between devices: 5.83 us -> 4.78 us  [shifted(): lax.ppermute(value, axis, [(source, source + steps) for source in range(i...]
    concatenate x0 -> x2, other arithmetic: none -> 0.89 us  [the longest x1 0.86 us: per_device(): jnp.concatenate([near_up, down[2:], up[2:]])]
  transfers between devices with their start and end apart: 6 -> 6, of which waited for: 5 -> 5; matrix products, arithmetic and copies ran while one was open for 3% -> 0% of each run, Pallas kernels for 0% -> 0%
where the time goes in v8:
time: 85.4 us; the launch traced here: 84.8 us
  waiting for transfers between devices  29.9 us (35%)
  blocking collectives  20.7 us (24%)
  starting transfers between devices  17.5 us (20%)
  Pallas kernels  9.77 us (11%)
  local copies, waits for them, and re-layouts  4.05 us (5%)
  between operations  1.46 us (2%)
  other arithmetic  1.02 us (1%)
    all_to_all x1, blocking collectives, per_device(): lax.all_to_all(outgoing_rows, 'crow', 0, 0, tiled=True)  20.7 us
    ppermute x1, waiting for transfers between devices, per_device(): lax.ppermute(jnp.concatenate([near_down, down[:1], up[:1]]), 'sub', [(u,...  12.3 us
    ppermute x1, waiting for transfers between devices, per_device(): lax.ppermute(jnp.concatenate([near_up, down[2:], up[2:]]), 'sub', [(u, u...  8.33 us
    ppermute x1, starting transfers between devices, per_device(): lax.ppermute(jnp.concatenate([near_up, down[2:], up[2:]]), 'sub', [(u, u...  6.39 us
    pallas_call x1, Pallas kernels, eliminate_panel(): pl.pallas_call(panel_kernel, out_shape=(jax.ShapeDtypeStruct((share, widt...  6.16 us
    ppermute x2, starting transfers between devices, shifted(): lax.ppermute(value, axis, [(source, source + steps) for source in range(i...  4.78 us
    ppermute x2, waiting for transfers between devices, shifted(): lax.ppermute(value, axis, [(source, source + steps) for source in range(i...  4.51 us
    ppermute x1, waiting for transfers between devices, per_device(): lax.ppermute(up_out, 'sub', [(t, t + 1) for t in range(last)] + [(last, 0)])  3.71 us
  transfers between devices with their start and end apart: 6, of which 5 were waited for; matrix products, arithmetic and copies ran while one was open for 0% of the time, Pallas kernels for 0%

profile of v8, /device:TPU:198, one launch (start us, length us, event | category | flops | bytes accessed | tf_op | source)
XLA Modules:
  0.0 84.8 jit_solution(16249418856201423312)
XLA Ops:
  0.6 0.8 slice_bitcast_fusion.1
  1.4 0.8 slice_bitcast_fusion
  2.2 3.5 %collective-permute-start = (bf16[2,128,128]{2,1,0:T(8,128)(2,1)S(1)}, bf16[2,128,128]{2,1,0:T(8,128)(2,1)S(1)}, u32[]{:S(2)}, u32[]{:S(2)}) collective-permute-start(bf16[2,128,128]{2,1,0:T(8,128)(2,1)S(1)} %pad_maximum_fusion.4), channel_id=1, source_target_pairs={{0,1},{1,2},{2,3},{4,5},{5,6},{6,7},{8,9},{9,10},{10,11},{12,13},{... | collective-permute-start | bytes 196616 | tf_op jit(solution)/shard_map/ppermute | solution.py:26
  5.7 1.3 %collective-permute-start.1 = (bf16[128,128]{1,0:T(8,128)(2,1)S(1)}, bf16[128,128]{1,0:T(8,128)(2,1)S(1)}, u32[]{:S(2)}, u32[]{:S(2)}) collective-permute-start(bf16[128,128]{1,0:T(8,128)(2,1)S(1)} %get-tuple-element.15), channel_id=1, source_target_pairs={{1,0},{2,1},{3,2},{5,4},{6,5},{7,6},{9,8},{10,9},{11,10},{13,12},{... | collective-permute-start | bytes 98312 | tf_op jit(solution)/shard_map/ppermute | solution.py:26
  7.0 4.5 %collective-permute-done.1.zn_ref = bf16[128,128]{1,0:T(8,128)(2,1)S(1)} collective-permute-done((bf16[128,128]{1,0:T(8,128)(2,1)S(1)}, bf16[128,128]{1,0:T(8,128)(2,1)S(1)}, u32[]{:S(2)}, u32[]{:S(2)}) %collective-permute-start.1) | collective-permute-done | bytes 32800 | tf_op jit(solution)/shard_map/ppermute | solution.py:26
  11.5 0.0 copy-start.4
  11.5 0.0 collective-permute-done.fp_ref
  11.5 0.6 copy-done.4
  12.1 0.0 copy-start.1
  12.1 0.6 copy-done.1
  12.7 3.6 %shard_map.85 = (bf16[3,2,128,128]{3,2,1,0:T(8,128)(2,1)}, bf16[3,2,128,128]{3,2,1,0:T(8,128)(2,1)}, bf16[1,2,128,128]{3,2,1,0:T(8,128)(2,1)}, bf16[1,2,128,128]...) custom-call(s32[1,1,16]{2,1,0:T(1,128)} %blocks_ref.1, s32[1,8]{1,0:T(1,128)} %counts_ref.1, ...), custom_call_target="tpu_custom_call" | custom-call | tf_op jit(solution)/shard_map/pallas_call | solution.py:85
  16.3 2.1 %collective-permute-start.2 = (bf16[3,2,128,128]{3,2,1,0:T(8,128)(2,1)}, bf16[3,2,128,128]{3,2,1,0:T(8,128)(2,1)S(1)}, u32[]{:S(2)}, u32[]{:S(2)}) collective-permute-start(bf16[3,2,128,128]{3,2,1,0:T(8,128)(2,1)} %get-tuple-element.11), channel_id=1, source_target_pairs={{4,0},{8,4},{12,8},{16,12},{20,16},{24,20},{28,24},{32,28},{36,32}... | collective-permute-start | bytes 589832 | tf_op jit(solution)/shard_map/ppermute | solution.py:178
  18.4 2.4 %collective-permute-start.3 = (bf16[3,2,128,128]{3,2,1,0:T(8,128)(2,1)}, bf16[3,2,128,128]{3,2,1,0:T(8,128)(2,1)S(1)}, u32[]{:S(2)}, u32[]{:S(2)}) collective-permute-start(bf16[3,2,128,128]{3,2,1,0:T(8,128)(2,1)} %get-tuple-element.12), channel_id=1, source_target_pairs={{0,4},{4,8},{8,12},{12,16},{16,20},{20,24},{24,28},{28,32},{32,36}... | collective-permute-start | bytes 589832 | tf_op jit(solution)/shard_map/ppermute | solution.py:181
  20.8 1.1 %collective-permute-done.2 = bf16[3,2,128,128]{3,2,1,0:T(8,128)(2,1)S(1)} collective-permute-done((bf16[3,2,128,128]{3,2,1,0:T(8,128)(2,1)}, bf16[3,2,128,128]{3,2,1,0:T(8,128)(2,1)S(1)}, u32[]{:S(2)}, u32[]{:S(2)}) %collective-permute-start.2) | collective-permute-done | bytes 196640 | tf_op jit(solution)/shard_map/ppermute | solution.py:178
  21.9 3.7 %collective-permute-done.3 = bf16[3,2,128,128]{3,2,1,0:T(8,128)(2,1)S(1)} collective-permute-done((bf16[3,2,128,128]{3,2,1,0:T(8,128)(2,1)}, bf16[3,2,128,128]{3,2,1,0:T(8,128)(2,1)S(1)}, u32[]{:S(2)}, u32[]{:S(2)}) %collective-permute-start.3) | collective-permute-done | bytes 196640 | tf_op jit(solution)/shard_map/ppermute | solution.py:181
  25.6 0.9 %pad_maximum_fusion.2 = bf16[3,2,128,128]{3,2,1,0:T(8,128)(2,1)S(1)} fusion(bf16[1,2,128,128]{3,2,1,0:T(8,128)(2,1)S(1)} %slice.62, bf16[1,2,128,128]{3,2,1,0:T(8,128)(2,1)S(1)} %slice.61, bf16[1,2,128,128]{3,2,1,0:T(8,128)(2,1)} %get-tuple-element.10), kind=kLoop, calls=%fused_computation.3 | loop fusion | flops 196608 | bytes 393216 | tf_op jit(solution)/shard_map/concatenate | solution.py:188
  26.5 6.4 %collective-permute-start.4 = (bf16[3,2,128,128]{3,2,1,0:T(8,128)(2,1)S(1)}, bf16[3,2,128,128]{3,2,1,0:T(8,128)(2,1)S(1)}, u32[]{:S(2)}, u32[]{:S(2)}) collective-permute-start(bf16[3,2,128,128]{3,2,1,0:T(8,128)(2,1)S(1)} %pad_maximum_fusion.2), channel_id=1, source_target_pairs={{0,64},{4,68},{8,72},{12,76},{16,80},{20,84},{24,88},{28,92},{32,9... | collective-permute-start | bytes 589832 | tf_op jit(solution)/shard_map/ppermute | solution.py:187
  32.9 8.3 %collective-permute-done.4 = bf16[3,2,128,128]{3,2,1,0:T(8,128)(2,1)S(1)} collective-permute-done((bf16[3,2,128,128]{3,2,1,0:T(8,128)(2,1)S(1)}, bf16[3,2,128,128]{3,2,1,0:T(8,128)(2,1)S(1)}, u32[]{:S(2)}, u32[]{:S(2)}) %collective-permute-start.4) | collective-permute-done | bytes 196640 | tf_op jit(solution)/shard_map/ppermute | solution.py:187
  41.3 0.0 copy-done.3
  41.3 1.9 %collective-permute-start.5 = (bf16[3,2,128,128]{3,2,1,0:T(8,128)(2,1)S(1)}, bf16[3,2,128,128]{3,2,1,0:T(8,128)(2,1)S(1)}, u32[]{:S(2)}, u32[]{:S(2)}) collective-permute-start(bf16[3,2,128,128]{3,2,1,0:T(8,128)(2,1)S(1)} %pad_maximum_fusion.3), channel_id=1, source_target_pairs={{64,0},{68,4},{72,8},{76,12},{80,16},{84,20},{88,24},{92,28},{96,3... | collective-permute-start | bytes 589832 | tf_op jit(solution)/shard_map/ppermute | solution.py:182
  43.9 0.0 copy-done.2
  43.9 0.1 copy.14
  44.0 12.3 %collective-permute-done.5 = bf16[3,2,128,128]{3,2,1,0:T(8,128)(2,1)S(1)} collective-permute-done((bf16[3,2,128,128]{3,2,1,0:T(8,128)(2,1)S(1)}, bf16[3,2,128,128]{3,2,1,0:T(8,128)(2,1)S(1)}, u32[]{:S(2)}, u32[]{:S(2)}) %collective-permute-start.5) | collective-permute-done | bytes 196640 | tf_op jit(solution)/shard_map/ppermute | solution.py:182
  56.3 0.0 copy-done
  56.3 0.3 convolution_bitcast_fusion
  56.7 0.5 copy.15
  57.2 0.2 constant_dynamic-slice_fusion
  57.5 0.2 copy.19
  57.7 0.1 reshape_reshape.3
  57.8 0.1 pad_maximum_fusion
  57.9 20.7 %all_to_all.5.pieces_ref = f32[4,64,1152]{2,1,0:T(8,128)} all-to-all(f32[4,64,1152]{2,1,0:T(8,128)S(1)} %pad_maximum_fusion), channel_id=1, replica_groups=mesh['sub'=128,'crow'=4] {'crow'}, dimensions={0} | all-to-all | bytes 2359296 | tf_op jit(solution)/shard_map/all_to_all | solution.py:219
  78.7 6.2 %shard_map.86 = (f32[32,128]{1,0:T(8,128)}, f32[32,1024]{1,0:T(8,128)}, f32[32,32]{1,0:T(8,128)}) custom-call(s32[1]{0:T(128)S(6)} %copy.25.owner_ref, f32[4,64,1152]{2,1,0:T(8,128)} %all_to_all.5.pieces_ref), custom_call_target="tpu_custom_call" | custom-call | tf_op jit(solution)/shard_map/pallas_call | solution.py:140
  (15 shorter events, 0.2 us)
Async XLA Ops:
  2.2 9.3 %collective-permute-start = (bf16[2,128,128]{2,1,0:T(8,128)(2,1)S(1)}, bf16[2,128,128]{2,1,0:T(8,128)(2,1)S(1)}, u32[]{:S(2)}, u32[]{:S(2)}) collective-permute-start(bf16[2,128,128]{2,1,0:T(8,128)(2,1)S(1)} %pad_maximum_fusion.4), channel_id=1, source_target_pairs={{0,1},{1,2},{2,3},{4,5},{5,6},{6,7},{8,9},{9,10},{10,11},{12,13},{... | collective-permute-start | bytes 196616 | tf_op jit(solution)/shard_map/ppermute | solution.py:26
  5.7 5.8 %collective-permute-start.1 = (bf16[128,128]{1,0:T(8,128)(2,1)S(1)}, bf16[128,128]{1,0:T(8,128)(2,1)S(1)}, u32[]{:S(2)}, u32[]{:S(2)}) collective-permute-start(bf16[128,128]{1,0:T(8,128)(2,1)S(1)} %get-tuple-element.15), channel_id=1, source_target_pairs={{1,0},{2,1},{3,2},{5,4},{6,5},{7,6},{9,8},{10,9},{11,10},{13,12},{... | collective-permute-start | bytes 98312 | tf_op jit(solution)/shard_map/ppermute | solution.py:26
  11.5 0.6 copy-start.4
  12.1 0.6 copy-start.1
  16.3 24.9 %copy-start.3 = (bf16[1,2,128,128]{3,2,1,0:T(8,128)(2,1)S(1)}, bf16[1,2,128,128]{3,2,1,0:T(8,128)(2,1)}, u32[]{:S(2)}) copy-start(bf16[1,2,128,128]{3,2,1,0:T(8,128)(2,1)} %get-tuple-element.13) | copy-start | bytes 196612
  16.3 27.6 %copy-start.2 = (f32[128,128]{1,0:T(8,128)S(1)}, f32[128,128]{1,0:T(8,128)}, u32[]{:S(2)}) copy-start(f32[128,128]{1,0:T(8,128)} %get-tuple-element.9) | copy-start | bytes 196612
  16.3 5.5 %collective-permute-start.2 = (bf16[3,2,128,128]{3,2,1,0:T(8,128)(2,1)}, bf16[3,2,128,128]{3,2,1,0:T(8,128)(2,1)S(1)}, u32[]{:S(2)}, u32[]{:S(2)}) collective-permute-start(bf16[3,2,128,128]{3,2,1,0:T(8,128)(2,1)} %get-tuple-element.11), channel_id=1, source_target_pairs={{4,0},{8,4},{12,8},{16,12},{20,16},{24,20},{28,24},{32,28},{36,32}... | collective-permute-start | bytes 589832 | tf_op jit(solution)/shard_map/ppermute | solution.py:178
  18.4 7.2 %collective-permute-start.3 = (bf16[3,2,128,128]{3,2,1,0:T(8,128)(2,1)}, bf16[3,2,128,128]{3,2,1,0:T(8,128)(2,1)S(1)}, u32[]{:S(2)}, u32[]{:S(2)}) collective-permute-start(bf16[3,2,128,128]{3,2,1,0:T(8,128)(2,1)} %get-tuple-element.12), channel_id=1, source_target_pairs={{0,4},{4,8},{8,12},{12,16},{16,20},{20,24},{24,28},{28,32},{32,36}... | collective-permute-start | bytes 589832 | tf_op jit(solution)/shard_map/ppermute | solution.py:181
  21.9 34.4 %copy-start = (bf16[8,2,128,128]{3,2,1,0:T(8,128)(2,1)S(1)}, bf16[8,2,128,128]{3,2,1,0:T(8,128)(2,1)}, u32[]{:S(2)}) copy-start(bf16[8,2,128,128]{3,2,1,0:T(8,128)(2,1)} %get-tuple-element.14) | copy-start | bytes 1572868
  26.5 14.7 %collective-permute-start.4 = (bf16[3,2,128,128]{3,2,1,0:T(8,128)(2,1)S(1)}, bf16[3,2,128,128]{3,2,1,0:T(8,128)(2,1)S(1)}, u32[]{:S(2)}, u32[]{:S(2)}) collective-permute-start(bf16[3,2,128,128]{3,2,1,0:T(8,128)(2,1)S(1)} %pad_maximum_fusion.2), channel_id=1, source_target_pairs={{0,64},{4,68},{8,72},{12,76},{16,80},{20,84},{24,88},{28,92},{32,9... | collective-permute-start | bytes 589832 | tf_op jit(solution)/shard_map/ppermute | solution.py:187
  41.3 15.0 %collective-permute-start.5 = (bf16[3,2,128,128]{3,2,1,0:T(8,128)(2,1)S(1)}, bf16[3,2,128,128]{3,2,1,0:T(8,128)(2,1)S(1)}, u32[]{:S(2)}, u32[]{:S(2)}) collective-permute-start(bf16[3,2,128,128]{3,2,1,0:T(8,128)(2,1)S(1)} %pad_maximum_fusion.3), channel_id=1, source_target_pairs={{64,0},{68,4},{72,8},{76,12},{80,16},{84,20},{88,24},{92,28},{96,3... | collective-permute-start | bytes 589832 | tf_op jit(solution)/shard_map/ppermute | solution.py:182

commit v9 on v8

--- a/solution.py
+++ b/solution.py
@@ -121,7 +121,7 @@
     work = jnp.concatenate([pivot, jnp.eye(share, dtype=jnp.float32)], 1)
     for k in range(share):
         row = work[k:k + 1, :]
-        scale = 1.0 / jnp.sqrt(row[:, k:k + 1])
+        scale = lax.rsqrt(row[:, k:k + 1])
         unit_row = row * scale
         below = jnp.where(row_id > k, work[:, k:k + 1] * scale, 0.0)
         work = jnp.where(row_id == k, unit_row, work - below * unit_row)
@@ -149,6 +149,41 @@
     )(owner, pieces)
 
 
+def coarse_rows_kernel(owner_ref, gram_ref, own_ref, down_ref, up_ref, fdn_ref, fup_ref, out_ref, whole_ref):
+    width = gram_ref.shape[0]
+    share = out_ref.shape[1] // 2
+    sources = {
+        0: (fup_ref, 2), 1: (fup_ref, 0), 2: (fup_ref, 1), 3: (up_ref, 1),
+        4: (down_ref, 1), 5: (fdn_ref, 2), 6: (fdn_ref, 0), 7: (fdn_ref, 1),
+    }
+    whole_ref[:, :width] = gram_ref[...]
+    for slot in range(own_ref.shape[0]):
+        ref, place = sources[slot]
+        block = _atb(own_ref[slot, 0], ref[place, 0])
+        for unit in range(1, own_ref.shape[1]):
+            block = block + _atb(own_ref[slot, unit], ref[place, unit])
+        whole_ref[:, (slot + 1) * width:(slot + 2) * width] = block
+    start = pl.multiple_of(owner_ref[0] * share, share)
+    pivot = whole_ref[pl.ds(start, share), :]
+    for target in range(out_ref.shape[0]):
+        out_ref[target, :share] = whole_ref[target * share:(target + 1) * share, :]
+        out_ref[target, share:] = pivot
+
+
+def coarse_rows(owner, gram, own, down, up, far_down, far_up, crow_count):
+    width = gram.shape[0]
+    share = width // crow_count
+    columns = width * (own.shape[0] + 1)
+    vmem = pl.BlockSpec(memory_space=pltpu.VMEM)
+    return pl.pallas_call(
+        coarse_rows_kernel,
+        out_shape=jax.ShapeDtypeStruct((crow_count, 2 * share, columns), jnp.float32),
+        in_specs=[pl.BlockSpec(memory_space=pltpu.SMEM)] + [vmem] * 6,
+        out_specs=vmem,
+        scratch_shapes=[pltpu.VMEM((width, columns), jnp.float32)],
+    )(owner, gram, own, down, up, far_down, far_up)
+
+
 def per_device(deflation, diag_op, upper_op, tile_blocks, pair_counts, pivot_owner):
     crow_count = lax.axis_size("crow")
     crow_place = lax.axis_index("crow")
@@ -189,36 +224,11 @@
         "sub",
         [(u, u + across) for u in range(sub_count - across)] + [(last, across - 1)],
     )
-    arrival = {
-        -across - 1: far_up[2],
-        -across: far_up[0],
-        -across + 1: far_up[1],
-        -1: up[1],
-        1: down[1],
-        across - 1: far_down[2],
-        across: far_down[0],
-        across + 1: far_down[1],
-    }
-    received = jnp.stack([arrival[offset] for offset in offsets])
-    row_share = coarse_width // crow_count
-    owner_index = pivot_owner[0]
-    coupling = jnp.einsum(
-        "jutr,jutk->rjk", own_masked, received, preferred_element_type=jnp.float32
-    )
-    whole = jnp.concatenate([gram_part[:, None, :], coupling], 1).reshape(
-        coarse_width, (slot_count + 1) * coarse_width
-    )
-    pivot_partial = lax.dynamic_slice_in_dim(whole, owner_index * row_share, row_share, 0)
-    outgoing_rows = jnp.concatenate(
-        [
-            whole.reshape(crow_count, row_share, whole.shape[1]),
-            jnp.broadcast_to(pivot_partial[None], (crow_count,) + pivot_partial.shape),
-        ],
-        1,
-    )
-    pieces = lax.all_to_all(outgoing_rows, "crow", 0, 0, tiled=True).reshape(
-        crow_count, 2 * row_share, whole.shape[1]
-    )
+    assert offsets == [-across - 1, -across, -across + 1, -1, 1, across - 1, across, across + 1]
+    outgoing_rows = coarse_rows(
+        pivot_owner, gram_part, own_masked, down, up, far_down, far_up, crow_count
+    )
+    pieces = lax.all_to_all(outgoing_rows, "crow", 0, 0, tiled=True)
     return eliminate_panel(pivot_owner, pieces, coarse_width)
 
 

time: 85.4 us -> 78.1 us (0.915)
  the two profiles are of different devices: /device:TPU:198 before, /device:TPU:422 now
where the time goes in v9:
time: 78.1 us; the launch traced here: 77.4 us
  waiting for transfers between devices  21.5 us (28%)
  blocking collectives  21.4 us (27%)
  starting transfers between devices  15.8 us (20%)
  Pallas kernels  12.1 us (15%)
  local copies, waits for them, and re-layouts  3.46 us (4%)
  other arithmetic  1.81 us (2%)
  between operations  1.36 us (2%)
    all_to_all x1, blocking collectives, per_device(): pieces = lax.all_to_all(outgoing_rows, 'crow', 0, 0, tiled=True)  21.4 us
    ppermute x1, waiting for transfers between devices, per_device(): lax.ppermute(jnp.concatenate([near_up, down[2:], up[2:]]), 'sub', [(u, u...  7.06 us
    pallas_call x1, Pallas kernels, eliminate_panel(): pl.pallas_call(panel_kernel, out_shape=(jax.ShapeDtypeStruct((share, widt...  5.8 us
    ppermute x1, waiting for transfers between devices, per_device(): lax.ppermute(jnp.concatenate([near_down, down[:1], up[:1]]), 'sub', [(u,...  5.16 us
    ppermute x2, starting transfers between devices, shifted(): lax.ppermute(value, axis, [(source, source + steps) for source in range(i...  4.78 us
    ppermute x1, starting transfers between devices, per_device(): lax.ppermute(jnp.concatenate([near_down, down[:1], up[:1]]), 'sub', [(u,...  4.57 us
    ppermute x2, waiting for transfers between devices, shifted(): lax.ppermute(value, axis, [(source, source + steps) for source in range(i...  4.51 us
    ppermute x1, waiting for transfers between devices, per_device(): lax.ppermute(up_out, 'sub', [(t, t + 1) for t in range(last)] + [(last, 0)])  3.7 us
  transfers between devices with their start and end apart: 6, of which 5 were waited for; matrix products, arithmetic and copies ran while one was open for 1% of the time, Pallas kernels for 0%

profile of v9, /device:TPU:422, one launch (start us, length us, event | category | flops | bytes accessed | tf_op | source)
XLA Modules:
  0.0 77.4 jit_solution(1674004034920163508)
XLA Ops:
  0.6 0.8 slice_bitcast_fusion.1
  1.4 0.8 %slice_bitcast_fusion = (bf16[128,128]{1,0:T(8,128)(2,1)S(1)}, bf16[1,128,128]{2,1,0:T(8,128)(2,1)S(1)}) fusion(bf16[1,3072,128]{2,1,0:T(8,128)(2,1)} %z_ref.1), kind=kLoop, calls=%fused_computation.3 | loop fusion | bytes 131072 | tf_op jit(solution)/shard_map/slice | solution.py:201
  2.2 3.5 %collective-permute-start = (bf16[2,128,128]{2,1,0:T(8,128)(2,1)S(1)}, bf16[2,128,128]{2,1,0:T(8,128)(2,1)S(1)}, u32[]{:S(2)}, u32[]{:S(2)}) collective-permute-start(bf16[2,128,128]{2,1,0:T(8,128)(2,1)S(1)} %pad_maximum_fusion.2), channel_id=1, source_target_pairs={{0,1},{1,2},{2,3},{4,5},{5,6},{6,7},{8,9},{9,10},{10,11},{12,13},{... | collective-permute-start | bytes 196616 | tf_op jit(solution)/shard_map/ppermute | solution.py:26
  5.7 1.3 %collective-permute-start.1 = (bf16[128,128]{1,0:T(8,128)(2,1)S(1)}, bf16[128,128]{1,0:T(8,128)(2,1)S(1)}, u32[]{:S(2)}, u32[]{:S(2)}) collective-permute-start(bf16[128,128]{1,0:T(8,128)(2,1)S(1)} %get-tuple-element.15), channel_id=1, source_target_pairs={{1,0},{2,1},{3,2},{5,4},{6,5},{7,6},{9,8},{10,9},{11,10},{13,12},{... | collective-permute-start | bytes 98312 | tf_op jit(solution)/shard_map/ppermute | solution.py:26
  7.0 4.5 %collective-permute-done.1.zn_ref = bf16[128,128]{1,0:T(8,128)(2,1)S(1)} collective-permute-done((bf16[128,128]{1,0:T(8,128)(2,1)S(1)}, bf16[128,128]{1,0:T(8,128)(2,1)S(1)}, u32[]{:S(2)}, u32[]{:S(2)}) %collective-permute-start.1) | collective-permute-done | bytes 32800 | tf_op jit(solution)/shard_map/ppermute | solution.py:26
  11.5 0.0 copy-start.5
  11.5 0.0 collective-permute-done.fp_ref
  11.5 0.6 copy-done.5
  12.1 0.0 copy-start.4
  12.1 0.6 copy-done.4
  12.7 3.6 %shard_map.85 = (bf16[3,2,128,128]{3,2,1,0:T(8,128)(2,1)}, bf16[3,2,128,128]{3,2,1,0:T(8,128)(2,1)}, bf16[1,2,128,128]{3,2,1,0:T(8,128)(2,1)}, bf16[1,2,128,128]...) custom-call(s32[1,1,16]{2,1,0:T(1,128)} %blocks_ref.1, s32[1,8]{1,0:T(1,128)} %counts_ref.1, ...), custom_call_target="tpu_custom_call" | custom-call | tf_op jit(solution)/shard_map/pallas_call | solution.py:85
  16.3 1.9 %collective-permute-start.2 = (bf16[3,2,128,128]{3,2,1,0:T(8,128)(2,1)}, bf16[3,2,128,128]{3,2,1,0:T(8,128)(2,1)S(1)}, u32[]{:S(2)}, u32[]{:S(2)}) collective-permute-start(bf16[3,2,128,128]{3,2,1,0:T(8,128)(2,1)} %get-tuple-element.11), channel_id=1, source_target_pairs={{4,0},{8,4},{12,8},{16,12},{20,16},{24,20},{28,24},{32,28},{36,32}... | collective-permute-start | bytes 589832 | tf_op jit(solution)/shard_map/ppermute | solution.py:213
  18.2 2.4 %collective-permute-start.3 = (bf16[3,2,128,128]{3,2,1,0:T(8,128)(2,1)}, bf16[3,2,128,128]{3,2,1,0:T(8,128)(2,1)S(1)}, u32[]{:S(2)}, u32[]{:S(2)}) collective-permute-start(bf16[3,2,128,128]{3,2,1,0:T(8,128)(2,1)} %get-tuple-element.12), channel_id=1, source_target_pairs={{0,4},{4,8},{8,12},{12,16},{16,20},{20,24},{24,28},{28,32},{32,36}... | collective-permute-start | bytes 589832 | tf_op jit(solution)/shard_map/ppermute | solution.py:216
  20.6 1.1 %collective-permute-done.2.down_ref = bf16[3,2,128,128]{3,2,1,0:T(8,128)(2,1)S(1)} collective-permute-done((bf16[3,2,128,128]{3,2,1,0:T(8,128)(2,1)}, bf16[3,2,128,128]{3,2,1,0:T(8,128)(2,1)S(1)}, u32[]{:S(2)}, u32[]{:S(2)}) %collective-permute-start.2) | collective-permute-done | bytes 196640 | tf_op jit(solution)/shard_map/ppermute | solution.py:213
  21.7 0.0 copy-start
  21.7 3.7 %collective-permute-done.3.up_ref = bf16[3,2,128,128]{3,2,1,0:T(8,128)(2,1)S(1)} collective-permute-done((bf16[3,2,128,128]{3,2,1,0:T(8,128)(2,1)}, bf16[3,2,128,128]{3,2,1,0:T(8,128)(2,1)S(1)}, u32[]{:S(2)}, u32[]{:S(2)}) %collective-permute-start.3) | collective-permute-done | bytes 196640 | tf_op jit(solution)/shard_map/ppermute | solution.py:216
  25.4 0.0 copy-start.1
  25.4 0.9 %pad_maximum_fusion = bf16[3,2,128,128]{3,2,1,0:T(8,128)(2,1)S(1)} fusion(bf16[1,2,128,128]{3,2,1,0:T(8,128)(2,1)S(1)} %get-tuple-element.20, bf16[1,2,128,128]{3,2,1,0:T(8,128)(2,1)S(1)} %get-tuple-element.18, bf16[1,2,128,128]{3,2,1,0:T(8,128)(2,1)} %get-tuple-element.13), kind=kLoop, calls=%fused_computation | loop fusion | flops 196608 | bytes 393216 | tf_op jit(solution)/shard_map/concatenate | solution.py:218
  26.4 4.6 %collective-permute-start.4 = (bf16[3,2,128,128]{3,2,1,0:T(8,128)(2,1)S(1)}, bf16[3,2,128,128]{3,2,1,0:T(8,128)(2,1)S(1)}, u32[]{:S(2)}, u32[]{:S(2)}) collective-permute-start(bf16[3,2,128,128]{3,2,1,0:T(8,128)(2,1)S(1)} %pad_maximum_fusion), channel_id=1, source_target_pairs={{64,0},{68,4},{72,8},{76,12},{80,16},{84,20},{88,24},{92,28},{96,3... | collective-permute-start | bytes 589832 | tf_op jit(solution)/shard_map/ppermute | solution.py:217
  31.0 0.9 %pad_maximum_fusion.1 = bf16[3,2,128,128]{3,2,1,0:T(8,128)(2,1)S(1)} fusion(bf16[1,2,128,128]{3,2,1,0:T(8,128)(2,1)S(1)} %get-tuple-element.19, bf16[1,2,128,128]{3,2,1,0:T(8,128)(2,1)S(1)} %get-tuple-element.17, bf16[1,2,128,128]{3,2,1,0:T(8,128)(2,1)} %get-tuple-element.14), kind=kLoop, calls=%fused_computation.1 | loop fusion | flops 196608 | bytes 393216 | tf_op jit(solution)/shard_map/concatenate | solution.py:223
  31.8 2.2 %collective-permute-start.5 = (bf16[3,2,128,128]{3,2,1,0:T(8,128)(2,1)S(1)}, bf16[3,2,128,128]{3,2,1,0:T(8,128)(2,1)S(1)}, u32[]{:S(2)}, u32[]{:S(2)}) collective-permute-start(bf16[3,2,128,128]{3,2,1,0:T(8,128)(2,1)S(1)} %pad_maximum_fusion.1), channel_id=1, source_target_pairs={{0,64},{4,68},{8,72},{12,76},{16,80},{20,84},{24,88},{28,92},{32,9... | collective-permute-start | bytes 589832 | tf_op jit(solution)/shard_map/ppermute | solution.py:222
  34.7 5.2 %collective-permute-done.4.fdn_ref = bf16[3,2,128,128]{3,2,1,0:T(8,128)(2,1)S(1)} collective-permute-done((bf16[3,2,128,128]{3,2,1,0:T(8,128)(2,1)S(1)}, bf16[3,2,128,128]{3,2,1,0:T(8,128)(2,1)S(1)}, u32[]{:S(2)}, u32[]{:S(2)}) %collective-permute-start.4) | collective-permute-done | bytes 196640 | tf_op jit(solution)/shard_map/ppermute | solution.py:217
  39.8 0.0 copy-start.2
  39.8 7.1 %collective-permute-done.5.fup_ref = bf16[3,2,128,128]{3,2,1,0:T(8,128)(2,1)S(1)} collective-permute-done((bf16[3,2,128,128]{3,2,1,0:T(8,128)(2,1)S(1)}, bf16[3,2,128,128]{3,2,1,0:T(8,128)(2,1)S(1)}, u32[]{:S(2)}, u32[]{:S(2)}) %collective-permute-start.5) | collective-permute-done | bytes 196640 | tf_op jit(solution)/shard_map/ppermute | solution.py:222
  46.9 0.0 copy-start.3
  46.9 0.0 copy-done
  46.9 0.0 copy-done.1
  46.9 0.0 copy-done.2
  46.9 0.7 copy-done.3
  47.6 2.7 %shard_map.86 = f32[4,64,1152]{2,1,0:T(8,128)} custom-call(s32[1]{0:T(128)S(6)} %copy.9.owner_ref, f32[128,128]{1,0:T(8,128)} %get-tuple-element.9.gram_ref, bf16[8,2,128,128]{3,2,1,0:T(8,128)(2,1)} %get-tuple-element.10.own_ref, bf16[3,2,128,128]{3,2,1,0:T(8,128)(2,1)} %copy-done, bf16[3,2,128,128]{3,2,1,0:T(8,128)(2,1)} %copy-done.1, ...), custom_call_target="tpu_custom_call" | custom-call | tf_op jit(solution)/shard_map/pallas_call | solution.py:178
  50.3 21.4 %all_to_all.5.pieces_ref = f32[4,64,1152]{2,1,0:T(8,128)} all-to-all(f32[4,64,1152]{2,1,0:T(8,128)} %shard_map.86), channel_id=1, replica_groups=mesh['sub'=128,'crow'=4] {'crow'}, dimensions={0} | all-to-all | bytes 2359296 | tf_op jit(solution)/shard_map/all_to_all | solution.py:231
  71.6 5.8 %shard_map.87 = (f32[32,128]{1,0:T(8,128)}, f32[32,1024]{1,0:T(8,128)}, f32[32,32]{1,0:T(8,128)}) custom-call(s32[1]{0:T(128)S(6)} %copy.9.owner_ref, f32[4,64,1152]{2,1,0:T(8,128)} %all_to_all.5.pieces_ref), custom_call_target="tpu_custom_call" | custom-call | tf_op jit(solution)/shard_map/pallas_call | solution.py:140
  (3 shorter events, 0.0 us)
Async XLA Ops:
  2.2 9.3 %collective-permute-start = (bf16[2,128,128]{2,1,0:T(8,128)(2,1)S(1)}, bf16[2,128,128]{2,1,0:T(8,128)(2,1)S(1)}, u32[]{:S(2)}, u32[]{:S(2)}) collective-permute-start(bf16[2,128,128]{2,1,0:T(8,128)(2,1)S(1)} %pad_maximum_fusion.2), channel_id=1, source_target_pairs={{0,1},{1,2},{2,3},{4,5},{5,6},{6,7},{8,9},{9,10},{10,11},{12,13},{... | collective-permute-start | bytes 196616 | tf_op jit(solution)/shard_map/ppermute | solution.py:26
  5.7 5.8 %collective-permute-start.1 = (bf16[128,128]{1,0:T(8,128)(2,1)S(1)}, bf16[128,128]{1,0:T(8,128)(2,1)S(1)}, u32[]{:S(2)}, u32[]{:S(2)}) collective-permute-start(bf16[128,128]{1,0:T(8,128)(2,1)S(1)} %get-tuple-element.15), channel_id=1, source_target_pairs={{1,0},{2,1},{3,2},{5,4},{6,5},{7,6},{9,8},{10,9},{11,10},{13,12},{... | collective-permute-start | bytes 98312 | tf_op jit(solution)/shard_map/ppermute | solution.py:26
  11.5 0.6 copy-start.5
  12.1 0.6 copy-start.4
  16.3 5.4 %collective-permute-start.2 = (bf16[3,2,128,128]{3,2,1,0:T(8,128)(2,1)}, bf16[3,2,128,128]{3,2,1,0:T(8,128)(2,1)S(1)}, u32[]{:S(2)}, u32[]{:S(2)}) collective-permute-start(bf16[3,2,128,128]{3,2,1,0:T(8,128)(2,1)} %get-tuple-element.11), channel_id=1, source_target_pairs={{4,0},{8,4},{12,8},{16,12},{20,16},{24,20},{28,24},{32,28},{36,32}... | collective-permute-start | bytes 589832 | tf_op jit(solution)/shard_map/ppermute | solution.py:213
  18.2 7.2 %collective-permute-start.3 = (bf16[3,2,128,128]{3,2,1,0:T(8,128)(2,1)}, bf16[3,2,128,128]{3,2,1,0:T(8,128)(2,1)S(1)}, u32[]{:S(2)}, u32[]{:S(2)}) collective-permute-start(bf16[3,2,128,128]{3,2,1,0:T(8,128)(2,1)} %get-tuple-element.12), channel_id=1, source_target_pairs={{0,4},{4,8},{8,12},{12,16},{16,20},{20,24},{24,28},{28,32},{32,36}... | collective-permute-start | bytes 589832 | tf_op jit(solution)/shard_map/ppermute | solution.py:216
  21.7 25.2 %copy-start = (bf16[3,2,128,128]{3,2,1,0:T(8,128)(2,1)}, bf16[3,2,128,128]{3,2,1,0:T(8,128)(2,1)S(1)}, u32[]{:S(2)}) copy-start(bf16[3,2,128,128]{3,2,1,0:T(8,128)(2,1)S(1)} %collective-permute-done.2.down_ref) | copy-start | bytes 589828
  25.4 21.5 %copy-start.1 = (bf16[3,2,128,128]{3,2,1,0:T(8,128)(2,1)}, bf16[3,2,128,128]{3,2,1,0:T(8,128)(2,1)S(1)}, u32[]{:S(2)}) copy-start(bf16[3,2,128,128]{3,2,1,0:T(8,128)(2,1)S(1)} %collective-permute-done.3.up_ref) | copy-start | bytes 589828
  26.4 13.4 %collective-permute-start.4 = (bf16[3,2,128,128]{3,2,1,0:T(8,128)(2,1)S(1)}, bf16[3,2,128,128]{3,2,1,0:T(8,128)(2,1)S(1)}, u32[]{:S(2)}, u32[]{:S(2)}) collective-permute-start(bf16[3,2,128,128]{3,2,1,0:T(8,128)(2,1)S(1)} %pad_maximum_fusion), channel_id=1, source_target_pairs={{64,0},{68,4},{72,8},{76,12},{80,16},{84,20},{88,24},{92,28},{96,3... | collective-permute-start | bytes 589832 | tf_op jit(solution)/shard_map/ppermute | solution.py:217
  31.8 15.1 %collective-permute-start.5 = (bf16[3,2,128,128]{3,2,1,0:T(8,128)(2,1)S(1)}, bf16[3,2,128,128]{3,2,1,0:T(8,128)(2,1)S(1)}, u32[]{:S(2)}, u32[]{:S(2)}) collective-permute-start(bf16[3,2,128,128]{3,2,1,0:T(8,128)(2,1)S(1)} %pad_maximum_fusion.1), channel_id=1, source_target_pairs={{0,64},{4,68},{8,72},{12,76},{16,80},{20,84},{24,88},{28,92},{32,9... | collective-permute-start | bytes 589832 | tf_op jit(solution)/shard_map/ppermute | solution.py:222
  39.8 7.1 %copy-start.2 = (bf16[3,2,128,128]{3,2,1,0:T(8,128)(2,1)}, bf16[3,2,128,128]{3,2,1,0:T(8,128)(2,1)S(1)}, u32[]{:S(2)}) copy-start(bf16[3,2,128,128]{3,2,1,0:T(8,128)(2,1)S(1)} %collective-permute-done.4.fdn_ref) | copy-start | bytes 589828
  46.9 0.7 copy-start.3

commit v10 on v9

--- a/solution.py
+++ b/solution.py
@@ -101,21 +101,9 @@
     )
 
 
-def panel_kernel(owner_ref, pieces_ref, self_ref, coupling_ref, panel_ref):
-    share = panel_ref.shape[0]
-    width = self_ref.shape[1]
-    total = (pieces_ref[0] + pieces_ref[1]) + (pieces_ref[2] + pieces_ref[3])
-    own = total[:share]
-    lead = total[share:]
-    owner = owner_ref[0]
-
-    def pick(rows):
-        block = jnp.zeros((share, share), jnp.float32)
-        for q in range(width // share):
-            block = jnp.where(owner == q, rows[:, q * share:(q + 1) * share], block)
-        return block
-
-    pivot = pick(lead)
+def pivot_inverse_kernel(blocks_ref, inverse_ref):
+    share = inverse_ref.shape[0]
+    pivot = (blocks_ref[0] + blocks_ref[1]) + (blocks_ref[2] + blocks_ref[3])
     pivot = (pivot + pivot.T) * 0.5
     row_id = lax.broadcasted_iota(jnp.int32, (share, 1), 0)
     work = jnp.concatenate([pivot, jnp.eye(share, dtype=jnp.float32)], 1)
@@ -125,16 +113,40 @@
         unit_row = row * scale
         below = jnp.where(row_id > k, work[:, k:k + 1] * scale, 0.0)
         work = jnp.where(row_id == k, unit_row, work - below * unit_row)
-    inverse = work[:, share:]
+    inverse_ref[...] = work[:, share:]
+
+
+def pivot_inverse(blocks):
+    share = blocks.shape[1]
+    vmem = pl.BlockSpec(memory_space=pltpu.VMEM)
+    return pl.pallas_call(
+        pivot_inverse_kernel,
+        out_shape=jax.ShapeDtypeStruct((share, share), jnp.float32),
+        in_specs=[vmem],
+        out_specs=vmem,
+    )(blocks)
+
+
+def panel_kernel(owner_ref, pieces_ref, inverse_ref, self_ref, coupling_ref, panel_ref):
+    share = panel_ref.shape[0]
+    width = self_ref.shape[1]
+    total = (pieces_ref[0] + pieces_ref[1]) + (pieces_ref[2] + pieces_ref[3])
+    own = total[:share]
+    lead = total[share:]
+    owner = owner_ref[0]
+    columns = jnp.zeros((share, share), jnp.float32)
+    for q in range(width // share):
+        columns = jnp.where(owner == q, own[:, q * share:(q + 1) * share], columns)
+    inverse = inverse_ref[...]
     solved = _exact(inverse, lead, ((1,), (0,)))
-    panel = _exact(pick(own), inverse, ((1,), (1,)))
+    panel = _exact(columns, inverse, ((1,), (1,)))
     updated = own - _exact(panel, solved, ((1,), (0,)))
     self_ref[...] = updated[:, :width]
     coupling_ref[...] = updated[:, width:]
     panel_ref[...] = panel
 
 
-def eliminate_panel(owner, pieces, width):
+def eliminate_panel(owner, pieces, inverse, width):
     share = pieces.shape[1] // 2
     vmem = pl.BlockSpec(memory_space=pltpu.VMEM)
     return pl.pallas_call(
@@ -144,9 +156,9 @@
             jax.ShapeDtypeStruct((share, pieces.shape[2] - width), jnp.float32),
             jax.ShapeDtypeStruct((share, share), jnp.float32),
         ),
-        in_specs=[pl.BlockSpec(memory_space=pltpu.SMEM), vmem],
+        in_specs=[pl.BlockSpec(memory_space=pltpu.SMEM), vmem, vmem],
         out_specs=(vmem, vmem, vmem),
-    )(owner, pieces)
+    )(owner, pieces, inverse)
 
 
 def coarse_rows_kernel(owner_ref, gram_ref, own_ref, down_ref, up_ref, fdn_ref, fup_ref, out_ref, whole_ref):
@@ -209,6 +221,14 @@
     down_out, up_out, near_down, near_up, own_masked, gram_part = local_apply(
         groups, tile_blocks, pair_counts, deflation, forward_pair, next_rows, diag_op, upper_op
     )
+    row_share = coarse_width // crow_count
+    corner = pivot_owner[0] * row_share
+    pivot_part = lax.dynamic_slice(gram_part, (corner, corner), (row_share, row_share))
+    pivot_parts = lax.all_to_all(
+        jnp.broadcast_to(pivot_part[None], (crow_count, row_share, row_share)),
+        "crow", 0, 0, tiled=True,
+    )
+    inverse = pivot_inverse(pivot_parts)
     last = sub_count - 1
     down = lax.ppermute(
         down_out, "sub", [(t, t - 1) for t in range(1, sub_count)] + [(0, last)]
@@ -229,7 +249,7 @@
         pivot_owner, gram_part, own_masked, down, up, far_down, far_up, crow_count
     )
     pieces = lax.all_to_all(outgoing_rows, "crow", 0, 0, tiled=True)
-    return eliminate_panel(pivot_owner, pieces, coarse_width)
+    return eliminate_panel(pivot_owner, pieces, inverse, coarse_width)
 
 
 def solution(mesh):

time: 78.1 us -> 75.8 us (0.971)
  the two profiles are of different devices: /device:TPU:422 before, /device:TPU:194 now
where the time goes in v10:
time: 75.8 us; the launch traced here: 75 us
  starting transfers between devices  25.7 us (34%)
  waiting for transfers between devices  24.9 us (33%)
  Pallas kernels  13.2 us (17%)
  local copies, waits for them, and re-layouts  7.27 us (10%)
  other arithmetic  2.5 us (3%)
  between operations  1.37 us (2%)
    all_to_all x1, waiting for transfers between devices, per_device(): pieces = lax.all_to_all(outgoing_rows, 'crow', 0, 0, tiled=True)  9.98 us
    ppermute x1, starting transfers between devices, per_device(): lax.ppermute(jnp.concatenate([near_up, down[2:], up[2:]]), 'sub', [(u, u...  6.38 us
    ppermute x1, waiting for transfers between devices, per_device(): lax.ppermute(jnp.concatenate([near_down, down[:1], up[:1]]), 'sub', [(u,...  5.58 us
    ppermute x2, starting transfers between devices, shifted(): lax.ppermute(value, axis, [(source, source + steps) for source in range(i...  4.78 us
    ppermute x2, waiting for transfers between devices, shifted(): lax.ppermute(value, axis, [(source, source + steps) for source in range(i...  4.51 us
    unnamed x16, local copies, waits for them, and re-layouts  4.39 us
    pallas_call x1, Pallas kernels, pivot_inverse(): pl.pallas_call(pivot_inverse_kernel, out_shape=jax.ShapeDtypeStruct((shar...  4.24 us
    all_to_all x1, starting transfers between devices, per_device(): pieces = lax.all_to_all(outgoing_rows, 'crow', 0, 0, tiled=True)  4.17 us
  transfers between devices with their start and end apart: 8, of which 5 were waited for; matrix products, arithmetic and copies ran while one was open for 6% of the time, Pallas kernels for 9%

profile of v10, /device:TPU:194, one launch (start us, length us, event | category | flops | bytes accessed | tf_op | source)
XLA Modules:
  0.0 75.0 jit_solution(5094872194143426403)
XLA Ops:
  0.6 0.8 %slice_bitcast_fusion = (bf16[128,128]{1,0:T(8,128)(2,1)S(1)}, bf16[1,128,128]{2,1,0:T(8,128)(2,1)S(1)}) fusion(bf16[1,3072,128]{2,1,0:T(8,128)(2,1)} %z_ref.1), kind=kLoop, calls=%fused_computation.3 | loop fusion | bytes 131072 | tf_op jit(solution)/shard_map/slice | solution.py:213
  1.4 0.8 %slice_bitcast_fusion.1 = bf16[1,128,128]{2,1,0:T(8,128)(2,1)S(1)} fusion(bf16[1,24,128,128]{3,2,1,0:T(8,128)(2,1)} %u_ref.1), kind=kLoop, calls=%fused_computation.4 | loop fusion | bytes 65536 | tf_op jit(solution)/shard_map/stack;squeeze | solution.py:211
  2.2 3.5 %collective-permute-start = (bf16[2,128,128]{2,1,0:T(8,128)(2,1)S(1)}, bf16[2,128,128]{2,1,0:T(8,128)(2,1)S(1)}, u32[]{:S(2)}, u32[]{:S(2)}) collective-permute-start(bf16[2,128,128]{2,1,0:T(8,128)(2,1)S(1)} %pad_maximum_fusion.2), channel_id=1, source_target_pairs={{0,1},{1,2},{2,3},{4,5},{5,6},{6,7},{8,9},{9,10},{10,11},{12,13},{... | collective-permute-start | bytes 196616 | tf_op jit(solution)/shard_map/ppermute | solution.py:26
  5.7 1.3 %collective-permute-start.1 = (bf16[128,128]{1,0:T(8,128)(2,1)S(1)}, bf16[128,128]{1,0:T(8,128)(2,1)S(1)}, u32[]{:S(2)}, u32[]{:S(2)}) collective-permute-start(bf16[128,128]{1,0:T(8,128)(2,1)S(1)} %get-tuple-element.15), channel_id=1, source_target_pairs={{1,0},{2,1},{3,2},{5,4},{6,5},{7,6},{9,8},{10,9},{11,10},{13,12},{... | collective-permute-start | bytes 98312 | tf_op jit(solution)/shard_map/ppermute | solution.py:26
  7.0 4.5 %collective-permute-done.1.zn_ref = bf16[128,128]{1,0:T(8,128)(2,1)S(1)} collective-permute-done((bf16[128,128]{1,0:T(8,128)(2,1)S(1)}, bf16[128,128]{1,0:T(8,128)(2,1)S(1)}, u32[]{:S(2)}, u32[]{:S(2)}) %collective-permute-start.1) | collective-permute-done | bytes 32800 | tf_op jit(solution)/shard_map/ppermute | solution.py:26
  11.5 0.0 collective-permute-done.fp_ref
  11.5 0.6 copy-done.6
  12.1 0.6 copy-done.5
  12.7 3.6 %shard_map.85 = (bf16[3,2,128,128]{3,2,1,0:T(8,128)(2,1)}, bf16[3,2,128,128]{3,2,1,0:T(8,128)(2,1)}, bf16[1,2,128,128]{3,2,1,0:T(8,128)(2,1)}, bf16[1,2,128,128]...) custom-call(s32[1,1,16]{2,1,0:T(1,128)} %blocks_ref.1, s32[1,8]{1,0:T(1,128)} %counts_ref.1, ...), custom_call_target="tpu_custom_call" | custom-call | tf_op jit(solution)/shard_map/pallas_call | solution.py:85
  16.3 1.9 %collective-permute-start.2 = (bf16[3,2,128,128]{3,2,1,0:T(8,128)(2,1)}, bf16[3,2,128,128]{3,2,1,0:T(8,128)(2,1)S(1)}, u32[]{:S(2)}, u32[]{:S(2)}) collective-permute-start(bf16[3,2,128,128]{3,2,1,0:T(8,128)(2,1)} %get-tuple-element.11), channel_id=1, source_target_pairs={{4,0},{8,4},{12,8},{16,12},{20,16},{24,20},{28,24},{32,28},{36,32}... | collective-permute-start | bytes 589832 | tf_op jit(solution)/shard_map/ppermute | solution.py:233
  18.3 2.4 %collective-permute-start.3 = (bf16[3,2,128,128]{3,2,1,0:T(8,128)(2,1)}, bf16[3,2,128,128]{3,2,1,0:T(8,128)(2,1)S(1)}, u32[]{:S(2)}, u32[]{:S(2)}) collective-permute-start(bf16[3,2,128,128]{3,2,1,0:T(8,128)(2,1)} %get-tuple-element.12), channel_id=1, source_target_pairs={{0,4},{4,8},{8,12},{12,16},{16,20},{20,24},{24,28},{28,32},{32,36}... | collective-permute-start | bytes 589832 | tf_op jit(solution)/shard_map/ppermute | solution.py:236
  20.7 1.1 %collective-permute-done.2.down_ref = bf16[3,2,128,128]{3,2,1,0:T(8,128)(2,1)S(1)} collective-permute-done((bf16[3,2,128,128]{3,2,1,0:T(8,128)(2,1)}, bf16[3,2,128,128]{3,2,1,0:T(8,128)(2,1)S(1)}, u32[]{:S(2)}, u32[]{:S(2)}) %collective-permute-start.2) | collective-permute-done | bytes 196640 | tf_op jit(solution)/shard_map/ppermute | solution.py:233
  21.8 3.7 %collective-permute-done.3.up_ref = bf16[3,2,128,128]{3,2,1,0:T(8,128)(2,1)S(1)} collective-permute-done((bf16[3,2,128,128]{3,2,1,0:T(8,128)(2,1)}, bf16[3,2,128,128]{3,2,1,0:T(8,128)(2,1)S(1)}, u32[]{:S(2)}, u32[]{:S(2)}) %collective-permute-start.3) | collective-permute-done | bytes 196640 | tf_op jit(solution)/shard_map/ppermute | solution.py:236
  25.5 0.9 %pad_maximum_fusion.1 = bf16[3,2,128,128]{3,2,1,0:T(8,128)(2,1)S(1)} fusion(bf16[1,2,128,128]{3,2,1,0:T(8,128)(2,1)S(1)} %get-tuple-element.19, bf16[1,2,128,128]{3,2,1,0:T(8,128)(2,1)S(1)} %get-tuple-element.17, bf16[1,2,128,128]{3,2,1,0:T(8,128)(2,1)} %get-tuple-element.14), kind=kLoop, calls=%fused_computation.1 | loop fusion | flops 196608 | bytes 393216 | tf_op jit(solution)/shard_map/concatenate | solution.py:243
  26.4 6.4 %collective-permute-start.5 = (bf16[3,2,128,128]{3,2,1,0:T(8,128)(2,1)S(1)}, bf16[3,2,128,128]{3,2,1,0:T(8,128)(2,1)S(1)}, u32[]{:S(2)}, u32[]{:S(2)}) collective-permute-start(bf16[3,2,128,128]{3,2,1,0:T(8,128)(2,1)S(1)} %pad_maximum_fusion.1), channel_id=1, source_target_pairs={{0,64},{4,68},{8,72},{12,76},{16,80},{20,84},{24,88},{28,92},{32,9... | collective-permute-start | bytes 589832 | tf_op jit(solution)/shard_map/ppermute | solution.py:242
  32.8 0.9 %pad_maximum_fusion = bf16[3,2,128,128]{3,2,1,0:T(8,128)(2,1)S(1)} fusion(bf16[1,2,128,128]{3,2,1,0:T(8,128)(2,1)S(1)} %get-tuple-element.20, bf16[1,2,128,128]{3,2,1,0:T(8,128)(2,1)S(1)} %get-tuple-element.18, bf16[1,2,128,128]{3,2,1,0:T(8,128)(2,1)} %get-tuple-element.13), kind=kLoop, calls=%fused_computation | loop fusion | flops 196608 | bytes 393216 | tf_op jit(solution)/shard_map/concatenate | solution.py:238
  33.7 1.9 %collective-permute-start.4 = (bf16[3,2,128,128]{3,2,1,0:T(8,128)(2,1)S(1)}, bf16[3,2,128,128]{3,2,1,0:T(8,128)(2,1)S(1)}, u32[]{:S(2)}, u32[]{:S(2)}) collective-permute-start(bf16[3,2,128,128]{3,2,1,0:T(8,128)(2,1)S(1)} %pad_maximum_fusion), channel_id=1, source_target_pairs={{64,0},{68,4},{72,8},{76,12},{80,16},{84,20},{88,24},{92,28},{96,3... | collective-permute-start | bytes 589832 | tf_op jit(solution)/shard_map/ppermute | solution.py:237
  36.3 0.8 %dynamic_slice.3 = f32[32,32]{1,0:T(8,128)S(1)} dynamic-slice(f32[128,128]{1,0:T(8,128)} %get-tuple-element.9.gram_ref, s32[]{:T(128)S(6)} %select_n.4, s32[]{:T(128)S(6)} %select_n.4), dynamic_slice_sizes={32,32} | dynamic-slice | bytes 8196 | tf_op jit(solution)/shard_map/dynamic_slice | solution.py:226
  37.1 0.7 reshape.12
  37.8 4.2 %all-to-all-start.1 = ((f32[4,1,1024]{2,1,0:T(1,128)}), f32[4,1,1024]{2,1,0:T(1,128)S(1)}, u32[]{:S(2)}, u32[]{:S(2)}) async-start(f32[4,1,1024]{2,1,0:T(1,128)} %reshape.12), calls=%async_computation.1 | async-start | bytes 32768 | tf_op jit(solution)/shard_map/all_to_all | solution.py:227
  41.9 0.0 collective-permute-done.5.fup_ref
  41.9 5.6 %collective-permute-done.4.fdn_ref = bf16[3,2,128,128]{3,2,1,0:T(8,128)(2,1)S(1)} collective-permute-done((bf16[3,2,128,128]{3,2,1,0:T(8,128)(2,1)S(1)}, bf16[3,2,128,128]{3,2,1,0:T(8,128)(2,1)S(1)}, u32[]{:S(2)}, u32[]{:S(2)}) %collective-permute-start.4) | collective-permute-done | bytes 196640 | tf_op jit(solution)/shard_map/ppermute | solution.py:237
  47.5 0.7 copy-done.4
  48.2 2.7 %shard_map.86 = f32[4,64,1152]{2,1,0:T(8,128)} custom-call(s32[1]{0:T(128)S(6)} %copy.9.owner_ref, f32[128,128]{1,0:T(8,128)} %get-tuple-element.9.gram_ref, bf16[8,2,128,128]{3,2,1,0:T(8,128)(2,1)} %get-tuple-element.10.own_ref, bf16[3,2,128,128]{3,2,1,0:T(8,128)(2,1)} %copy-done.1, bf16[3,2,128,128]{3,2,1,0:T(8,128)(2,1)} %copy-done.2, ...), custom_call_target="tpu_custom_call" | custom-call | tf_op jit(solution)/shard_map/pallas_call | solution.py:190
  50.9 4.2 %all-to-all-start = ((f32[4,64,1152]{2,1,0:T(8,128)}), f32[4,64,1152]{2,1,0:T(8,128)S(1)}, u32[]{:S(2)}, u32[]{:S(2)}) async-start(f32[4,64,1152]{2,1,0:T(8,128)} %shard_map.86), calls=%async_computation | async-start | bytes 2359296 | tf_op jit(solution)/shard_map/all_to_all | solution.py:251
  55.1 0.5 broadcast.1
  55.6 0.7 reduce
  56.3 0.7 reshape.13.blocks_ref
  57.0 4.2 %shard_map.87.inverse_ref = f32[32,32]{1,0:T(8,128)} custom-call(f32[4,32,32]{2,1,0:T(8,128)} %reshape.13.blocks_ref), custom_call_target="tpu_custom_call" | custom-call | tf_op jit(solution)/shard_map/pallas_call | solution.py:122
  61.3 10.0 %all-to-all-done.pieces_ref = f32[4,64,1152]{2,1,0:T(8,128)S(1)} async-done(((f32[4,64,1152]{2,1,0:T(8,128)}), f32[4,64,1152]{2,1,0:T(8,128)S(1)}, u32[]{:S(2)}, u32[]{:S(2)}) %all-to-all-start) | async-done | bytes 1179680 | tf_op jit(solution)/shard_map/all_to_all | solution.py:251
  71.2 1.1 %copy-done = f32[4,64,1152]{2,1,0:T(8,128)} copy-done((f32[4,64,1152]{2,1,0:T(8,128)}, f32[4,64,1152]{2,1,0:T(8,128)S(1)}, u32[]{:S(2)}) %copy-start) | copy-done | bytes 1179672
  72.3 2.7 %shard_map.88 = (f32[32,128]{1,0:T(8,128)}, f32[32,1024]{1,0:T(8,128)}, f32[32,32]{1,0:T(8,128)}) custom-call(s32[1]{0:T(128)S(6)} %copy.9.owner_ref, f32[4,64,1152]{2,1,0:T(8,128)} %copy-done, f32[32,32]{1,0:T(8,128)} %shard_map.87.inverse_ref), custom_call_target="tpu_custom_call" | custom-call | tf_op jit(solution)/shard_map/pallas_call | solution.py:152
  (15 shorter events, 0.1 us)
Async XLA Ops:
  2.2 9.3 %collective-permute-start = (bf16[2,128,128]{2,1,0:T(8,128)(2,1)S(1)}, bf16[2,128,128]{2,1,0:T(8,128)(2,1)S(1)}, u32[]{:S(2)}, u32[]{:S(2)}) collective-permute-start(bf16[2,128,128]{2,1,0:T(8,128)(2,1)S(1)} %pad_maximum_fusion.2), channel_id=1, source_target_pairs={{0,1},{1,2},{2,3},{4,5},{5,6},{6,7},{8,9},{9,10},{10,11},{12,13},{... | collective-permute-start | bytes 196616 | tf_op jit(solution)/shard_map/ppermute | solution.py:26
  5.7 5.8 %collective-permute-start.1 = (bf16[128,128]{1,0:T(8,128)(2,1)S(1)}, bf16[128,128]{1,0:T(8,128)(2,1)S(1)}, u32[]{:S(2)}, u32[]{:S(2)}) collective-permute-start(bf16[128,128]{1,0:T(8,128)(2,1)S(1)} %get-tuple-element.15), channel_id=1, source_target_pairs={{1,0},{2,1},{3,2},{5,4},{6,5},{7,6},{9,8},{10,9},{11,10},{13,12},{... | collective-permute-start | bytes 98312 | tf_op jit(solution)/shard_map/ppermute | solution.py:26
  11.5 0.6 copy-start.6
  12.1 0.6 copy-start.5
  16.3 5.4 %collective-permute-start.2 = (bf16[3,2,128,128]{3,2,1,0:T(8,128)(2,1)}, bf16[3,2,128,128]{3,2,1,0:T(8,128)(2,1)S(1)}, u32[]{:S(2)}, u32[]{:S(2)}) collective-permute-start(bf16[3,2,128,128]{3,2,1,0:T(8,128)(2,1)} %get-tuple-element.11), channel_id=1, source_target_pairs={{4,0},{8,4},{12,8},{16,12},{20,16},{24,20},{28,24},{32,28},{36,32}... | collective-permute-start | bytes 589832 | tf_op jit(solution)/shard_map/ppermute | solution.py:233
  18.3 7.2 %collective-permute-start.3 = (bf16[3,2,128,128]{3,2,1,0:T(8,128)(2,1)}, bf16[3,2,128,128]{3,2,1,0:T(8,128)(2,1)S(1)}, u32[]{:S(2)}, u32[]{:S(2)}) collective-permute-start(bf16[3,2,128,128]{3,2,1,0:T(8,128)(2,1)} %get-tuple-element.12), channel_id=1, source_target_pairs={{0,4},{4,8},{8,12},{12,16},{16,20},{20,24},{24,28},{28,32},{32,36}... | collective-permute-start | bytes 589832 | tf_op jit(solution)/shard_map/ppermute | solution.py:236
  21.7 25.8 %copy-start.1 = (bf16[3,2,128,128]{3,2,1,0:T(8,128)(2,1)}, bf16[3,2,128,128]{3,2,1,0:T(8,128)(2,1)S(1)}, u32[]{:S(2)}) copy-start(bf16[3,2,128,128]{3,2,1,0:T(8,128)(2,1)S(1)} %collective-permute-done.2.down_ref) | copy-start | bytes 589828
  25.5 22.1 %copy-start.2 = (bf16[3,2,128,128]{3,2,1,0:T(8,128)(2,1)}, bf16[3,2,128,128]{3,2,1,0:T(8,128)(2,1)S(1)}, u32[]{:S(2)}) copy-start(bf16[3,2,128,128]{3,2,1,0:T(8,128)(2,1)S(1)} %collective-permute-done.3.up_ref) | copy-start | bytes 589828
  26.4 15.5 %collective-permute-start.5 = (bf16[3,2,128,128]{3,2,1,0:T(8,128)(2,1)S(1)}, bf16[3,2,128,128]{3,2,1,0:T(8,128)(2,1)S(1)}, u32[]{:S(2)}, u32[]{:S(2)}) collective-permute-start(bf16[3,2,128,128]{3,2,1,0:T(8,128)(2,1)S(1)} %pad_maximum_fusion.1), channel_id=1, source_target_pairs={{0,64},{4,68},{8,72},{12,76},{16,80},{20,84},{24,88},{28,92},{32,9... | collective-permute-start | bytes 589832 | tf_op jit(solution)/shard_map/ppermute | solution.py:242
  33.7 13.9 %collective-permute-start.4 = (bf16[3,2,128,128]{3,2,1,0:T(8,128)(2,1)S(1)}, bf16[3,2,128,128]{3,2,1,0:T(8,128)(2,1)S(1)}, u32[]{:S(2)}, u32[]{:S(2)}) collective-permute-start(bf16[3,2,128,128]{3,2,1,0:T(8,128)(2,1)S(1)} %pad_maximum_fusion), channel_id=1, source_target_pairs={{64,0},{68,4},{72,8},{76,12},{80,16},{84,20},{88,24},{92,28},{96,3... | collective-permute-start | bytes 589832 | tf_op jit(solution)/shard_map/ppermute | solution.py:237
  37.8 13.2 %all-to-all-start.1 = ((f32[4,1,1024]{2,1,0:T(1,128)}), f32[4,1,1024]{2,1,0:T(1,128)S(1)}, u32[]{:S(2)}, u32[]{:S(2)}) async-start(f32[4,1,1024]{2,1,0:T(1,128)} %reshape.12), calls=%async_computation.1 | async-start | bytes 32768 | tf_op jit(solution)/shard_map/all_to_all | solution.py:227
  41.9 5.6 %copy-start.3 = (bf16[3,2,128,128]{3,2,1,0:T(8,128)(2,1)}, bf16[3,2,128,128]{3,2,1,0:T(8,128)(2,1)S(1)}, u32[]{:S(2)}) copy-start(bf16[3,2,128,128]{3,2,1,0:T(8,128)(2,1)S(1)} %collective-permute-done.5.fup_ref) | copy-start | bytes 589828
  47.5 0.7 copy-start.4
  50.9 20.3 %all-to-all-start = ((f32[4,64,1152]{2,1,0:T(8,128)}), f32[4,64,1152]{2,1,0:T(8,128)S(1)}, u32[]{:S(2)}, u32[]{:S(2)}) async-start(f32[4,64,1152]{2,1,0:T(8,128)} %shard_map.86), calls=%async_computation | async-start | bytes 2359296 | tf_op jit(solution)/shard_map/all_to_all | solution.py:251
  71.2 1.1 %copy-start = (f32[4,64,1152]{2,1,0:T(8,128)}, f32[4,64,1152]{2,1,0:T(8,128)S(1)}, u32[]{:S(2)}) copy-start(f32[4,64,1152]{2,1,0:T(8,128)S(1)} %all-to-all-done.pieces_ref) | copy-start | bytes 3538948

commit v11 on v10

--- a/solution.py
+++ b/solution.py
@@ -101,9 +101,15 @@
     )
 
 
-def pivot_inverse_kernel(blocks_ref, inverse_ref):
+def pivot_inverse_kernel(owner_ref, early_ref, inverse_ref):
     share = inverse_ref.shape[0]
-    pivot = (blocks_ref[0] + blocks_ref[1]) + (blocks_ref[2] + blocks_ref[3])
+    width = 4 * share
+    total = (early_ref[0] + early_ref[1]) + (early_ref[2] + early_ref[3])
+    lead = total[share:, :width]
+    owner = owner_ref[0]
+    pivot = jnp.zeros((share, share), jnp.float32)
+    for q in range(width // share):
+        pivot = jnp.where(owner == q, lead[:, q * share:(q + 1) * share], pivot)
     pivot = (pivot + pivot.T) * 0.5
     row_id = lax.broadcasted_iota(jnp.int32, (share, 1), 0)
     work = jnp.concatenate([pivot, jnp.eye(share, dtype=jnp.float32)], 1)
@@ -116,65 +122,70 @@
     inverse_ref[...] = work[:, share:]
 
 
-def pivot_inverse(blocks):
-    share = blocks.shape[1]
+def pivot_inverse(owner, early):
+    share = early.shape[1] // 2
     vmem = pl.BlockSpec(memory_space=pltpu.VMEM)
     return pl.pallas_call(
         pivot_inverse_kernel,
         out_shape=jax.ShapeDtypeStruct((share, share), jnp.float32),
-        in_specs=[vmem],
+        in_specs=[pl.BlockSpec(memory_space=pltpu.SMEM), vmem],
         out_specs=vmem,
-    )(blocks)
-
-
-def panel_kernel(owner_ref, pieces_ref, inverse_ref, self_ref, coupling_ref, panel_ref):
+    )(owner, early)
+
+
+def panel_kernel(layout, owner_ref, early_ref, late_ref, inverse_ref, self_ref, coupling_ref, panel_ref):
     share = panel_ref.shape[0]
     width = self_ref.shape[1]
-    total = (pieces_ref[0] + pieces_ref[1]) + (pieces_ref[2] + pieces_ref[3])
-    own = total[:share]
-    lead = total[share:]
+    inverse = inverse_ref[...]
+    early = (early_ref[0] + early_ref[1]) + (early_ref[2] + early_ref[3])
+    late = (late_ref[0] + late_ref[1]) + (late_ref[2] + late_ref[3])
     owner = owner_ref[0]
     columns = jnp.zeros((share, share), jnp.float32)
     for q in range(width // share):
-        columns = jnp.where(owner == q, own[:, q * share:(q + 1) * share], columns)
-    inverse = inverse_ref[...]
-    solved = _exact(inverse, lead, ((1,), (0,)))
+        columns = jnp.where(owner == q, early[:share, q * share:(q + 1) * share], columns)
     panel = _exact(columns, inverse, ((1,), (1,)))
-    updated = own - _exact(panel, solved, ((1,), (0,)))
-    self_ref[...] = updated[:, :width]
-    coupling_ref[...] = updated[:, width:]
     panel_ref[...] = panel
-
-
-def eliminate_panel(owner, pieces, inverse, width):
-    share = pieces.shape[1] // 2
-    vmem = pl.BlockSpec(memory_space=pltpu.VMEM)
-    return pl.pallas_call(
-        panel_kernel,
+    updated = []
+    for total in (early, late):
+        solved = _exact(inverse, total[share:], ((1,), (0,)))
+        updated.append(total[:share] - _exact(panel, solved, ((1,), (0,))))
+    for part, place, slot in layout:
+        block = updated[part][:, place * width:(place + 1) * width]
+        if slot < 0:
+            self_ref[...] = block
+        else:
+            coupling_ref[:, slot * width:(slot + 1) * width] = block
+
+
+def eliminate_panel(layout, owner, early, late, inverse, width):
+    share = early.shape[1] // 2
+    columns = early.shape[2] + late.shape[2] - width
+    vmem = pl.BlockSpec(memory_space=pltpu.VMEM)
+    return pl.pallas_call(
+        functools.partial(panel_kernel, layout),
         out_shape=(
             jax.ShapeDtypeStruct((share, width), jnp.float32),
-            jax.ShapeDtypeStruct((share, pieces.shape[2] - width), jnp.float32),
+            jax.ShapeDtypeStruct((share, columns), jnp.float32),
             jax.ShapeDtypeStruct((share, share), jnp.float32),
         ),
-        in_specs=[pl.BlockSpec(memory_space=pltpu.SMEM), vmem, vmem],
+        in_specs=[pl.BlockSpec(memory_space=pltpu.SMEM), vmem, vmem, vmem],
         out_specs=(vmem, vmem, vmem),
-    )(owner, pieces, inverse)
-
-
-def coarse_rows_kernel(owner_ref, gram_ref, own_ref, down_ref, up_ref, fdn_ref, fup_ref, out_ref, whole_ref):
+    )(owner, early, late, inverse)
+
+
+def coarse_rows_kernel(columns, owner_ref, gram_ref, own_ref, *refs):
+    sources, out_ref, whole_ref = refs[:-2], refs[-2], refs[-1]
     width = gram_ref.shape[0]
     share = out_ref.shape[1] // 2
-    sources = {
-        0: (fup_ref, 2), 1: (fup_ref, 0), 2: (fup_ref, 1), 3: (up_ref, 1),
-        4: (down_ref, 1), 5: (fdn_ref, 2), 6: (fdn_ref, 0), 7: (fdn_ref, 1),
-    }
-    whole_ref[:, :width] = gram_ref[...]
-    for slot in range(own_ref.shape[0]):
-        ref, place = sources[slot]
-        block = _atb(own_ref[slot, 0], ref[place, 0])
-        for unit in range(1, own_ref.shape[1]):
-            block = block + _atb(own_ref[slot, unit], ref[place, unit])
-        whole_ref[:, (slot + 1) * width:(slot + 2) * width] = block
+    for place, (slot, source, index) in enumerate(columns):
+        if slot < 0:
+            block = gram_ref[...]
+        else:
+            ref = sources[source]
+            block = _atb(own_ref[slot, 0], ref[index, 0])
+            for unit in range(1, own_ref.shape[1]):
+                block = block + _atb(own_ref[slot, unit], ref[index, unit])
+        whole_ref[:, place * width:(place + 1) * width] = block
     start = pl.multiple_of(owner_ref[0] * share, share)
     pivot = whole_ref[pl.ds(start, share), :]
     for target in range(out_ref.shape[0]):
@@ -182,18 +193,18 @@
         out_ref[target, share:] = pivot
 
 
-def coarse_rows(owner, gram, own, down, up, far_down, far_up, crow_count):
+def coarse_rows(columns, owner, gram, own, sources, crow_count):
     width = gram.shape[0]
     share = width // crow_count
-    columns = width * (own.shape[0] + 1)
-    vmem = pl.BlockSpec(memory_space=pltpu.VMEM)
-    return pl.pallas_call(
-        coarse_rows_kernel,
-        out_shape=jax.ShapeDtypeStruct((crow_count, 2 * share, columns), jnp.float32),
-        in_specs=[pl.BlockSpec(memory_space=pltpu.SMEM)] + [vmem] * 6,
+    total = width * len(columns)
+    vmem = pl.BlockSpec(memory_space=pltpu.VMEM)
+    return pl.pallas_call(
+        functools.partial(coarse_rows_kernel, columns),
+        out_shape=jax.ShapeDtypeStruct((crow_count, 2 * share, total), jnp.float32),
+        in_specs=[pl.BlockSpec(memory_space=pltpu.SMEM)] + [vmem] * (2 + len(sources)),
         out_specs=vmem,
-        scratch_shapes=[pltpu.VMEM((width, columns), jnp.float32)],
-    )(owner, gram, own, down, up, far_down, far_up)
+        scratch_shapes=[pltpu.VMEM((width, total), jnp.float32)],
+    )(owner, gram, own, *sources)
 
 
 def per_device(deflation, diag_op, upper_op, tile_blocks, pair_counts, pivot_owner):
@@ -221,14 +232,6 @@
     down_out, up_out, near_down, near_up, own_masked, gram_part = local_apply(
         groups, tile_blocks, pair_counts, deflation, forward_pair, next_rows, diag_op, upper_op
     )
-    row_share = coarse_width // crow_count
-    corner = pivot_owner[0] * row_share
-    pivot_part = lax.dynamic_slice(gram_part, (corner, corner), (row_share, row_share))
-    pivot_parts = lax.all_to_all(
-        jnp.broadcast_to(pivot_part[None], (crow_count, row_share, row_share)),
-        "crow", 0, 0, tiled=True,
-    )
-    inverse = pivot_inverse(pivot_parts)
     last = sub_count - 1
     down = lax.ppermute(
         down_out, "sub", [(t, t - 1) for t in range(1, sub_count)] + [(0, last)]
@@ -245,11 +248,17 @@
         [(u, u + across) for u in range(sub_count - across)] + [(last, across - 1)],
     )
     assert offsets == [-across - 1, -across, -across + 1, -1, 1, across - 1, across, across + 1]
-    outgoing_rows = coarse_rows(
-        pivot_owner, gram_part, own_masked, down, up, far_down, far_up, crow_count
-    )
-    pieces = lax.all_to_all(outgoing_rows, "crow", 0, 0, tiled=True)
-    return eliminate_panel(pivot_owner, pieces, inverse, coarse_width)
+    early_columns = ((-1, 0, 0), (3, 1, 1), (4, 0, 1))
+    late_columns = ((0, 1, 2), (1, 1, 0), (2, 1, 1), (5, 0, 2), (6, 0, 0), (7, 0, 1))
+    early_rows = coarse_rows(early_columns, pivot_owner, gram_part, own_masked, (down, up), crow_count)
+    early = lax.all_to_all(early_rows, "crow", 0, 0, tiled=True)
+    inverse = pivot_inverse(pivot_owner, early)
+    late_rows = coarse_rows(
+        late_columns, pivot_owner, gram_part, own_masked, (far_down, far_up), crow_count
+    )
+    late = lax.all_to_all(late_rows, "crow", 0, 0, tiled=True)
+    layout = ((0, 0, -1), (1, 0, 0), (1, 1, 1), (1, 2, 2), (0, 1, 3), (0, 2, 4), (1, 3, 5), (1, 4, 6), (1, 5, 7))
+    return eliminate_panel(layout, pivot_owner, early, late, inverse, coarse_width)
 
 
 def solution(mesh):

time: 75.8 us -> 80 us (1.055)
  the two profiles are of different devices: /device:TPU:194 before, /device:TPU:64 now
where the time goes in v11:
time: 80 us; the launch traced here: 79.3 us
  starting transfers between devices  32.3 us (40%)
  waiting for transfers between devices  22.3 us (28%)
  Pallas kernels  15.7 us (20%)
  local copies, waits for them, and re-layouts  7.53 us (9%)
  between operations  1.37 us (2%)
    ppermute x1, starting transfers between devices, per_device(): lax.ppermute(jnp.concatenate([near_down, down[:1], up[:1]]), 'sub', [(u,...  12.2 us
    unnamed x24, local copies, waits for them, and re-layouts  5.96 us
    ppermute x1, waiting for transfers between devices, per_device(): lax.ppermute(up_out, 'sub', [(t, t + 1) for t in range(last)] + [(last, 0)])  5.82 us
    ppermute x1, waiting for transfers between devices, per_device(): lax.ppermute(jnp.concatenate([near_up, down[2:], up[2:]]), 'sub', [(u, u...  5.34 us
    all_to_all x1, starting transfers between devices, per_device(): late = lax.all_to_all(late_rows, 'crow', 0, 0, tiled=True)  4.79 us
    pallas_call x1, Pallas kernels, pivot_inverse(): pl.pallas_call(pivot_inverse_kernel, out_shape=jax.ShapeDtypeStruct((shar...  4.78 us
    ppermute x2, starting transfers between devices, shifted(): lax.ppermute(value, axis, [(source, source + steps) for source in range(i...  4.78 us
    all_to_all x1, waiting for transfers between devices, per_device(): late = lax.all_to_all(late_rows, 'crow', 0, 0, tiled=True)  4.71 us
  transfers between devices with their start and end apart: 8, of which 6 were waited for; matrix products, arithmetic and copies ran while one was open for 0% of the time, Pallas kernels for 9%

profile of v11, /device:TPU:64, one launch (start us, length us, event | category | flops | bytes accessed | tf_op | source)
XLA Modules:
  0.0 79.3 jit_solution(10355945554954420393)
XLA Ops:
  0.6 0.8 slice_bitcast_fusion.1
  1.4 0.8 slice_bitcast_fusion
  2.2 3.5 %collective-permute-start = (bf16[2,128,128]{2,1,0:T(8,128)(2,1)S(1)}, bf16[2,128,128]{2,1,0:T(8,128)(2,1)S(1)}, u32[]{:S(2)}, u32[]{:S(2)}) collective-permute-start(bf16[2,128,128]{2,1,0:T(8,128)(2,1)S(1)} %pad_maximum_fusion.2), channel_id=1, source_target_pairs={{0,1},{1,2},{2,3},{4,5},{5,6},{6,7},{8,9},{9,10},{10,11},{12,13},{... | collective-permute-start | bytes 196616 | tf_op jit(solution)/shard_map/ppermute | solution.py:26
  5.7 1.3 %collective-permute-start.1 = (bf16[128,128]{1,0:T(8,128)(2,1)S(1)}, bf16[128,128]{1,0:T(8,128)(2,1)S(1)}, u32[]{:S(2)}, u32[]{:S(2)}) collective-permute-start(bf16[128,128]{1,0:T(8,128)(2,1)S(1)} %get-tuple-element.15), channel_id=1, source_target_pairs={{1,0},{2,1},{3,2},{5,4},{6,5},{7,6},{9,8},{10,9},{11,10},{13,12},{... | collective-permute-start | bytes 98312 | tf_op jit(solution)/shard_map/ppermute | solution.py:26
  7.0 4.5 %collective-permute-done.1.zn_ref = bf16[128,128]{1,0:T(8,128)(2,1)S(1)} collective-permute-done((bf16[128,128]{1,0:T(8,128)(2,1)S(1)}, bf16[128,128]{1,0:T(8,128)(2,1)S(1)}, u32[]{:S(2)}, u32[]{:S(2)}) %collective-permute-start.1) | collective-permute-done | bytes 32800 | tf_op jit(solution)/shard_map/ppermute | solution.py:26
  11.5 0.0 collective-permute-done.fp_ref
  11.5 0.6 copy-done.11
  12.1 0.6 copy-done.8
  12.7 3.6 %shard_map.85 = (bf16[3,2,128,128]{3,2,1,0:T(8,128)(2,1)}, bf16[3,2,128,128]{3,2,1,0:T(8,128)(2,1)}, bf16[1,2,128,128]{3,2,1,0:T(8,128)(2,1)}, bf16[1,2,128,128]...) custom-call(s32[1,1,16]{2,1,0:T(1,128)} %blocks_ref.1, s32[1,8]{1,0:T(1,128)} %counts_ref.1, ...), custom_call_target="tpu_custom_call" | custom-call | tf_op jit(solution)/shard_map/pallas_call | solution.py:85
  16.3 2.2 %collective-permute-start.2 = (bf16[3,2,128,128]{3,2,1,0:T(8,128)(2,1)}, bf16[3,2,128,128]{3,2,1,0:T(8,128)(2,1)S(1)}, u32[]{:S(2)}, u32[]{:S(2)}) collective-permute-start(bf16[3,2,128,128]{3,2,1,0:T(8,128)(2,1)} %get-tuple-element.11), channel_id=1, source_target_pairs={{4,0},{8,4},{12,8},{16,12},{20,16},{24,20},{28,24},{32,28},{36,32}... | collective-permute-start | bytes 589832 | tf_op jit(solution)/shard_map/ppermute | solution.py:236
  18.6 2.1 %collective-permute-start.3 = (bf16[3,2,128,128]{3,2,1,0:T(8,128)(2,1)}, bf16[3,2,128,128]{3,2,1,0:T(8,128)(2,1)S(1)}, u32[]{:S(2)}, u32[]{:S(2)}) collective-permute-start(bf16[3,2,128,128]{3,2,1,0:T(8,128)(2,1)} %get-tuple-element.12), channel_id=1, source_target_pairs={{0,4},{4,8},{8,12},{12,16},{16,20},{20,24},{24,28},{28,32},{32,36}... | collective-permute-start | bytes 589832 | tf_op jit(solution)/shard_map/ppermute | solution.py:239
  21.3 0.7 collective-permute-done.2.refs_0_
  22.0 5.8 %collective-permute-done.3.refs_1_ = bf16[3,2,128,128]{3,2,1,0:T(8,128)(2,1)S(1)} collective-permute-done((bf16[3,2,128,128]{3,2,1,0:T(8,128)(2,1)}, bf16[3,2,128,128]{3,2,1,0:T(8,128)(2,1)S(1)}, u32[]{:S(2)}, u32[]{:S(2)}) %collective-permute-start.3) | collective-permute-done | bytes 196640 | tf_op jit(solution)/shard_map/ppermute | solution.py:239
  27.9 0.7 copy-done.4
  28.5 2.1 %shard_map.86 = f32[4,64,384]{2,1,0:T(8,128)} custom-call(s32[1]{0:T(128)S(6)} %copy.9.owner_ref, f32[128,128]{1,0:T(8,128)} %get-tuple-element.9.gram_ref, bf16[8,2,128,128]{3,2,1,0:T(8,128)(2,1)} %get-tuple-element.10.own_ref, bf16[3,2,128,128]{3,2,1,0:T(8,128)(2,1)} %copy-done.2, bf16[3,2,128,128]{3,2,1,0:T(8,128)(2,1)} %copy-done.4), custom_call_target="tpu_custom_call" | custom-call | tf_op jit(solution)/shard_map/pallas_call | solution.py:201
  30.7 4.3 %all-to-all-start = ((f32[4,64,384]{2,1,0:T(8,128)}), f32[4,64,384]{2,1,0:T(8,128)S(1)}, u32[]{:S(2)}, u32[]{:S(2)}) async-start(f32[4,64,384]{2,1,0:T(8,128)} %shard_map.86), calls=%async_computation | async-start | bytes 786432 | tf_op jit(solution)/shard_map/all_to_all | solution.py:254
  35.0 0.0 copy-done.5
  35.0 0.9 %copy-done.3 = bf16[3,2,128,128]{3,2,1,0:T(8,128)(2,1)S(1)} copy-done((bf16[3,2,128,128]{3,2,1,0:T(8,128)(2,1)S(1)}, bf16[3,2,128,128]{3,2,1,0:T(8,128)(2,1)}, u32[]{:S(2)}) %copy-start.3) | copy-done | bytes 196632
  35.9 0.8 %copy-done.10 = bf16[1,2,128,128]{3,2,1,0:T(8,128)(2,1)S(1)} copy-done((bf16[1,2,128,128]{3,2,1,0:T(8,128)(2,1)S(1)}, bf16[1,2,128,128]{3,2,1,0:T(8,128)(2,1)}, u32[]{:S(2)}) %copy-start.10) | copy-done | bytes 65560
  36.8 12.2 %collective-permute-start.4 = (bf16[3,2,128,128]{3,2,1,0:T(8,128)(2,1)S(1)}, bf16[3,2,128,128]{3,2,1,0:T(8,128)(2,1)S(1)}, u32[]{:S(2)}, u32[]{:S(2)}) collective-permute-start(bf16[3,2,128,128]{3,2,1,0:T(8,128)(2,1)S(1)} %pad_maximum_fusion), channel_id=1, source_target_pairs={{64,0},{68,4},{72,8},{76,12},{80,16},{84,20},{88,24},{92,28},{96,3... | collective-permute-start | bytes 589832 | tf_op jit(solution)/shard_map/ppermute | solution.py:240
  49.0 1.9 %collective-permute-start.5 = (bf16[3,2,128,128]{3,2,1,0:T(8,128)(2,1)S(1)}, bf16[3,2,128,128]{3,2,1,0:T(8,128)(2,1)S(1)}, u32[]{:S(2)}, u32[]{:S(2)}) collective-permute-start(bf16[3,2,128,128]{3,2,1,0:T(8,128)(2,1)S(1)} %pad_maximum_fusion.1), channel_id=1, source_target_pairs={{0,64},{4,68},{8,72},{12,76},{16,80},{20,84},{24,88},{28,92},{32,9... | collective-permute-start | bytes 589832 | tf_op jit(solution)/shard_map/ppermute | solution.py:245
  50.9 1.2 %collective-permute-done.4.refs_0_ = bf16[3,2,128,128]{3,2,1,0:T(8,128)(2,1)S(1)} collective-permute-done((bf16[3,2,128,128]{3,2,1,0:T(8,128)(2,1)S(1)}, bf16[3,2,128,128]{3,2,1,0:T(8,128)(2,1)S(1)}, u32[]{:S(2)}, u32[]{:S(2)}) %collective-permute-start.4) | collective-permute-done | bytes 196640 | tf_op jit(solution)/shard_map/ppermute | solution.py:240
  52.1 5.3 %collective-permute-done.5.refs_1_ = bf16[3,2,128,128]{3,2,1,0:T(8,128)(2,1)S(1)} collective-permute-done((bf16[3,2,128,128]{3,2,1,0:T(8,128)(2,1)S(1)}, bf16[3,2,128,128]{3,2,1,0:T(8,128)(2,1)S(1)}, u32[]{:S(2)}, u32[]{:S(2)}) %collective-permute-start.5) | collective-permute-done | bytes 196640 | tf_op jit(solution)/shard_map/ppermute | solution.py:245
  57.5 0.7 copy-done.7
  58.1 2.4 %shard_map.87 = f32[4,64,768]{2,1,0:T(8,128)} custom-call(s32[1]{0:T(128)S(6)} %copy.9.owner_ref, f32[128,128]{1,0:T(8,128)} %get-tuple-element.9.gram_ref, bf16[8,2,128,128]{3,2,1,0:T(8,128)(2,1)} %get-tuple-element.10.own_ref, bf16[3,2,128,128]{3,2,1,0:T(8,128)(2,1)} %copy-done.6, bf16[3,2,128,128]{3,2,1,0:T(8,128)(2,1)} %copy-done.7), custom_call_target="tpu_custom_call" | custom-call | tf_op jit(solution)/shard_map/pallas_call | solution.py:201
  60.5 0.0 all-to-all-done.early_ref
  60.5 0.8 copy-done
  61.3 4.8 %all-to-all-start.1 = ((f32[4,64,768]{2,1,0:T(8,128)}), f32[4,64,768]{2,1,0:T(8,128)S(1)}, u32[]{:S(2)}, u32[]{:S(2)}) async-start(f32[4,64,768]{2,1,0:T(8,128)} %shard_map.87), calls=%async_computation.1 | async-start | bytes 1572864 | tf_op jit(solution)/shard_map/all_to_all | solution.py:259
  66.1 4.8 %shard_map.88.inverse_ref = f32[32,32]{1,0:T(8,128)} custom-call(s32[1]{0:T(128)S(6)} %copy.9.owner_ref, f32[4,64,384]{2,1,0:T(8,128)} %copy-done), custom_call_target="tpu_custom_call" | custom-call | tf_op jit(solution)/shard_map/pallas_call | solution.py:128
  70.8 4.7 %all-to-all-done.1.late_ref = f32[4,64,768]{2,1,0:T(8,128)S(1)} async-done(((f32[4,64,768]{2,1,0:T(8,128)}), f32[4,64,768]{2,1,0:T(8,128)S(1)}, u32[]{:S(2)}, u32[]{:S(2)}) %all-to-all-start.1) | async-done | bytes 786464 | tf_op jit(solution)/shard_map/all_to_all | solution.py:259
  75.6 0.9 %copy-done.1 = f32[4,64,768]{2,1,0:T(8,128)} copy-done((f32[4,64,768]{2,1,0:T(8,128)}, f32[4,64,768]{2,1,0:T(8,128)S(1)}, u32[]{:S(2)}) %copy-start.1) | copy-done | bytes 786456
  76.4 2.8 %shard_map.89 = (f32[32,128]{1,0:T(8,128)}, f32[32,1024]{1,0:T(8,128)}, f32[32,32]{1,0:T(8,128)}) custom-call(s32[1]{0:T(128)S(6)} %copy.9.owner_ref, f32[4,64,384]{2,1,0:T(8,128)} %copy-done, f32[4,64,768]{2,1,0:T(8,128)} %copy-done.1, f32[32,32]{1,0:T(8,128)} %shard_map.88.inverse_ref), custom_call_target="tpu_custom_call" | custom-call | tf_op jit(solution)/shard_map/pallas_call | solution.py:164
  (20 shorter events, 0.1 us)
Async XLA Ops:
  2.2 9.3 %collective-permute-start = (bf16[2,128,128]{2,1,0:T(8,128)(2,1)S(1)}, bf16[2,128,128]{2,1,0:T(8,128)(2,1)S(1)}, u32[]{:S(2)}, u32[]{:S(2)}) collective-permute-start(bf16[2,128,128]{2,1,0:T(8,128)(2,1)S(1)} %pad_maximum_fusion.2), channel_id=1, source_target_pairs={{0,1},{1,2},{2,3},{4,5},{5,6},{6,7},{8,9},{9,10},{10,11},{12,13},{... | collective-permute-start | bytes 196616 | tf_op jit(solution)/shard_map/ppermute | solution.py:26
  5.7 5.8 %collective-permute-start.1 = (bf16[128,128]{1,0:T(8,128)(2,1)S(1)}, bf16[128,128]{1,0:T(8,128)(2,1)S(1)}, u32[]{:S(2)}, u32[]{:S(2)}) collective-permute-start(bf16[128,128]{1,0:T(8,128)(2,1)S(1)} %get-tuple-element.15), channel_id=1, source_target_pairs={{1,0},{2,1},{3,2},{5,4},{6,5},{7,6},{9,8},{10,9},{11,10},{13,12},{... | collective-permute-start | bytes 98312 | tf_op jit(solution)/shard_map/ppermute | solution.py:26
  11.5 0.6 copy-start.11
  12.1 0.6 copy-start.8
  16.3 5.7 %collective-permute-start.2 = (bf16[3,2,128,128]{3,2,1,0:T(8,128)(2,1)}, bf16[3,2,128,128]{3,2,1,0:T(8,128)(2,1)S(1)}, u32[]{:S(2)}, u32[]{:S(2)}) collective-permute-start(bf16[3,2,128,128]{3,2,1,0:T(8,128)(2,1)} %get-tuple-element.11), channel_id=1, source_target_pairs={{4,0},{8,4},{12,8},{16,12},{20,16},{24,20},{28,24},{32,28},{36,32}... | collective-permute-start | bytes 589832 | tf_op jit(solution)/shard_map/ppermute | solution.py:236
  18.6 9.3 %collective-permute-start.3 = (bf16[3,2,128,128]{3,2,1,0:T(8,128)(2,1)}, bf16[3,2,128,128]{3,2,1,0:T(8,128)(2,1)S(1)}, u32[]{:S(2)}, u32[]{:S(2)}) collective-permute-start(bf16[3,2,128,128]{3,2,1,0:T(8,128)(2,1)} %get-tuple-element.12), channel_id=1, source_target_pairs={{0,4},{4,8},{8,12},{12,16},{16,20},{20,24},{24,28},{28,32},{32,36}... | collective-permute-start | bytes 589832 | tf_op jit(solution)/shard_map/ppermute | solution.py:239
  22.0 5.8 %copy-start.2 = (bf16[3,2,128,128]{3,2,1,0:T(8,128)(2,1)}, bf16[3,2,128,128]{3,2,1,0:T(8,128)(2,1)S(1)}, u32[]{:S(2)}) copy-start(bf16[3,2,128,128]{3,2,1,0:T(8,128)(2,1)S(1)} %collective-permute-done.2.refs_0_) | copy-start | bytes 589828
  27.9 0.7 copy-start.4
  30.7 4.3 %copy-start.5 = (bf16[3,2,128,128]{3,2,1,0:T(8,128)(2,1)S(1)}, bf16[3,2,128,128]{3,2,1,0:T(8,128)(2,1)}, u32[]{:S(2)}) copy-start(bf16[3,2,128,128]{3,2,1,0:T(8,128)(2,1)} %copy-done.4) | copy-start | bytes 589828
  30.7 29.8 %all-to-all-start = ((f32[4,64,384]{2,1,0:T(8,128)}), f32[4,64,384]{2,1,0:T(8,128)S(1)}, u32[]{:S(2)}, u32[]{:S(2)}) async-start(f32[4,64,384]{2,1,0:T(8,128)} %shard_map.86), calls=%async_computation | async-start | bytes 786432 | tf_op jit(solution)/shard_map/all_to_all | solution.py:254
  35.0 0.9 %copy-start.3 = (bf16[3,2,128,128]{3,2,1,0:T(8,128)(2,1)S(1)}, bf16[3,2,128,128]{3,2,1,0:T(8,128)(2,1)}, u32[]{:S(2)}) copy-start(bf16[3,2,128,128]{3,2,1,0:T(8,128)(2,1)} %copy-done.2) | copy-start | bytes 589828
  35.9 0.8 %copy-start.10 = (bf16[1,2,128,128]{3,2,1,0:T(8,128)(2,1)S(1)}, bf16[1,2,128,128]{3,2,1,0:T(8,128)(2,1)}, u32[]{:S(2)}) copy-start(bf16[1,2,128,128]{3,2,1,0:T(8,128)(2,1)} %get-tuple-element.13) | copy-start | bytes 196612
  36.8 12.2 %copy-start.9 = (bf16[1,2,128,128]{3,2,1,0:T(8,128)(2,1)S(1)}, bf16[1,2,128,128]{3,2,1,0:T(8,128)(2,1)}, u32[]{:S(2)}) copy-start(bf16[1,2,128,128]{3,2,1,0:T(8,128)(2,1)} %get-tuple-element.14) | copy-start | bytes 196612
  36.8 15.3 %collective-permute-start.4 = (bf16[3,2,128,128]{3,2,1,0:T(8,128)(2,1)S(1)}, bf16[3,2,128,128]{3,2,1,0:T(8,128)(2,1)S(1)}, u32[]{:S(2)}, u32[]{:S(2)}) collective-permute-start(bf16[3,2,128,128]{3,2,1,0:T(8,128)(2,1)S(1)} %pad_maximum_fusion), channel_id=1, source_target_pairs={{64,0},{68,4},{72,8},{76,12},{80,16},{84,20},{88,24},{92,28},{96,3... | collective-permute-start | bytes 589832 | tf_op jit(solution)/shard_map/ppermute | solution.py:240
  49.0 8.5 %collective-permute-start.5 = (bf16[3,2,128,128]{3,2,1,0:T(8,128)(2,1)S(1)}, bf16[3,2,128,128]{3,2,1,0:T(8,128)(2,1)S(1)}, u32[]{:S(2)}, u32[]{:S(2)}) collective-permute-start(bf16[3,2,128,128]{3,2,1,0:T(8,128)(2,1)S(1)} %pad_maximum_fusion.1), channel_id=1, source_target_pairs={{0,64},{4,68},{8,72},{12,76},{16,80},{20,84},{24,88},{28,92},{32,9... | collective-permute-start | bytes 589832 | tf_op jit(solution)/shard_map/ppermute | solution.py:245
  52.1 5.3 %copy-start.6 = (bf16[3,2,128,128]{3,2,1,0:T(8,128)(2,1)}, bf16[3,2,128,128]{3,2,1,0:T(8,128)(2,1)S(1)}, u32[]{:S(2)}) copy-start(bf16[3,2,128,128]{3,2,1,0:T(8,128)(2,1)S(1)} %collective-permute-done.4.refs_0_) | copy-start | bytes 589828
  57.5 0.7 copy-start.7
  60.5 0.8 copy-start
  61.3 14.3 %all-to-all-start.1 = ((f32[4,64,768]{2,1,0:T(8,128)}), f32[4,64,768]{2,1,0:T(8,128)S(1)}, u32[]{:S(2)}, u32[]{:S(2)}) async-start(f32[4,64,768]{2,1,0:T(8,128)} %shard_map.87), calls=%async_computation.1 | async-start | bytes 1572864 | tf_op jit(solution)/shard_map/all_to_all | solution.py:259
  75.6 0.9 %copy-start.1 = (f32[4,64,768]{2,1,0:T(8,128)}, f32[4,64,768]{2,1,0:T(8,128)S(1)}, u32[]{:S(2)}) copy-start(f32[4,64,768]{2,1,0:T(8,128)S(1)} %all-to-all-done.1.late_ref) | copy-start | bytes 2359300

commit v12 on v10

--- a/solution.py
+++ b/solution.py
@@ -43,10 +43,7 @@
     return lax.dot_general(a, b, (((0,), (0,)), ((), ())), preferred_element_type=jnp.float32)
 
 
-def local_apply_kernel(
-    groups, blocks_ref, counts_ref, z_ref, fp_ref, zn_ref, d_ref, u_ref, *refs
-):
-    group_refs, own_ref, gram_ref, app_ref = refs[:len(groups)], refs[-3], refs[-2], refs[-1]
+def interior_kernel(blocks_ref, counts_ref, z_ref, d_ref, u_ref, app_ref, edge_ref, own_ref):
     count, rows = d_ref.shape[1], d_ref.shape[2]
     per_slot = own_ref.shape[1]
     crow = lax.axis_index("crow")
@@ -54,19 +51,34 @@
     def rows_of(b):
         return z_ref[0, pl.ds(b * rows, rows), :]
 
-    for b in range(count):
-        below = fp_ref[0] if b == 0 else rows_of(b - 1)
-        lower = fp_ref[1] if b == 0 else u_ref[0, b - 1]
-        above = zn_ref[...] if b == count - 1 else rows_of(b + 1)
-        total = (_ab(d_ref[0, b], rows_of(b)) + _ab(u_ref[0, b], above)) + _atb(lower, below)
+    for b in range(1, count - 1):
+        total = (_ab(d_ref[0, b], rows_of(b)) + _ab(u_ref[0, b], rows_of(b + 1))) + _atb(
+            u_ref[0, b - 1], rows_of(b - 1)
+        )
         app_ref[pl.ds(b * rows, rows), :] = total.astype(app_ref.dtype)
-    gram_ref[...] = _atb(z_ref[0], app_ref[...])
+    last = count - 1
+    edge_ref[0] = _ab(d_ref[0, 0], rows_of(0)) + _ab(u_ref[0, 0], rows_of(1))
+    edge_ref[1] = _ab(d_ref[0, last], rows_of(last))
+    edge_ref[2] = _atb(u_ref[0, last - 1], rows_of(last - 1))
     for slot in range(own_ref.shape[0]):
         for unit in range(per_slot):
             start = pl.multiple_of(blocks_ref[0, 0, slot * per_slot + unit] * rows, rows)
             tile = z_ref[0, pl.ds(start, rows), :]
             live = crow * per_slot + unit < counts_ref[0, slot]
             own_ref[slot, unit] = jnp.where(live, tile, jnp.zeros_like(tile))
+
+
+def finish_kernel(groups, blocks_ref, z_ref, fp_ref, zn_ref, u_ref, app_in_ref, edge_ref, *refs):
+    group_refs, gram_ref, app_ref = refs[:len(groups)], refs[-2], refs[-1]
+    count, rows = u_ref.shape[1], u_ref.shape[2]
+    last = count - 1
+    app_ref[...] = app_in_ref[...]
+    first = edge_ref[0] + _atb(fp_ref[1], fp_ref[0])
+    app_ref[pl.ds(0, rows), :] = first.astype(app_ref.dtype)
+    final = (edge_ref[1] + _ab(u_ref[0, last], zn_ref[...])) + edge_ref[2]
+    app_ref[pl.ds(last * rows, rows), :] = final.astype(app_ref.dtype)
+    gram_ref[...] = _atb(z_ref[0], app_ref[...])
+    per_slot = group_refs[0].shape[1]
     for group, out_ref in zip(groups, group_refs):
         for place, slot in enumerate(group):
             for unit in range(per_slot):
@@ -82,16 +94,26 @@
     vmem = pl.BlockSpec(memory_space=pltpu.VMEM)
     smem = pl.BlockSpec(memory_space=pltpu.SMEM)
     tile = lambda n: jax.ShapeDtypeStruct((n, per_slot, rows, width), deflation.dtype)
-    return pl.pallas_call(
-        functools.partial(local_apply_kernel, groups),
+    app, edge, own = pl.pallas_call(
+        interior_kernel,
+        out_shape=(
+            jax.ShapeDtypeStruct((blocks * rows, width), deflation.dtype),
+            jax.ShapeDtypeStruct((3, rows, width), jnp.float32),
+            tile(slots),
+        ),
+        in_specs=[smem, smem] + [vmem] * 3,
+        out_specs=(vmem, vmem, vmem),
+    )(tile_blocks, pair_counts, deflation, diag_op, upper_op)
+    outs = pl.pallas_call(
+        functools.partial(finish_kernel, groups),
         out_shape=tuple(tile(len(g)) for g in groups) + (
-            tile(slots),
             jax.ShapeDtypeStruct((width, width), jnp.float32),
         ),
-        in_specs=[smem, smem] + [vmem] * 5,
-        out_specs=tuple(vmem for _ in range(len(groups) + 2)),
+        in_specs=[smem] + [vmem] * 6,
+        out_specs=tuple(vmem for _ in range(len(groups) + 1)),
         scratch_shapes=[pltpu.VMEM((blocks * rows, width), deflation.dtype)],
-    )(tile_blocks, pair_counts, deflation, forward_pair, next_rows, diag_op, upper_op)
+    )(tile_blocks, deflation, forward_pair, next_rows, upper_op, app, edge)
+    return outs[:-1] + (own, outs[-1])
 
 
 def _exact(a, b, dims):

time: 75.8 us -> 76.7 us (1.012)
  the two profiles are of different devices: /device:TPU:194 before, /device:TPU:198 now
where the time goes in v12:
time: 76.7 us; the launch traced here: 75.8 us
  starting transfers between devices  27.2 us (35%)
  waiting for transfers between devices  22.1 us (29%)
  Pallas kernels  16 us (21%)
  local copies, waits for them, and re-layouts  6.66 us (9%)
  other arithmetic  2.5 us (3%)
  between operations  1.37 us (2%)
    all_to_all x1, waiting for transfers between devices, per_device(): pieces = lax.all_to_all(outgoing_rows, 'crow', 0, 0, tiled=True)  10.2 us
    ppermute x1, starting transfers between devices, per_device(): lax.ppermute(jnp.concatenate([near_up, down[2:], up[2:]]), 'sub', [(u, u...  6.39 us
    ppermute x1, waiting for transfers between devices, per_device(): lax.ppermute(jnp.concatenate([near_down, down[:1], up[:1]]), 'sub', [(u,...  6.14 us
    all_to_all x1, starting transfers between devices, per_device(): pieces = lax.all_to_all(outgoing_rows, 'crow', 0, 0, tiled=True)  5.26 us
    ppermute x2, starting transfers between devices, shifted(): lax.ppermute(value, axis, [(source, source + steps) for source in range(i...  4.78 us
    all_to_all x1, starting transfers between devices, per_device(): lax.all_to_all(jnp.broadcast_to(pivot_part[None], (crow_count, row_share,...  4.51 us
    pallas_call x1, Pallas kernels, pivot_inverse(): pl.pallas_call(pivot_inverse_kernel, out_shape=jax.ShapeDtypeStruct((shar...  4.23 us
    unnamed x16, local copies, waits for them, and re-layouts  3.79 us
  transfers between devices with their start and end apart: 8, of which 5 were waited for; matrix products, arithmetic and copies ran while one was open for 6% of the time, Pallas kernels for 14%

profile of v12, /device:TPU:198, one launch (start us, length us, event | category | flops | bytes accessed | tf_op | source)
XLA Modules:
  0.0 75.8 jit_solution(5418740704654227432)
XLA Ops:
  0.6 0.8 %slice_bitcast_fusion = (bf16[128,128]{1,0:T(8,128)(2,1)S(1)}, bf16[1,128,128]{2,1,0:T(8,128)(2,1)S(1)}) fusion(bf16[1,3072,128]{2,1,0:T(8,128)(2,1)} %z_ref.3), kind=kLoop, calls=%fused_computation.3 | loop fusion | bytes 131072 | tf_op jit(solution)/shard_map/slice | solution.py:235
  1.4 0.8 %slice_bitcast_fusion.1 = bf16[1,128,128]{2,1,0:T(8,128)(2,1)S(1)} fusion(bf16[1,24,128,128]{3,2,1,0:T(8,128)(2,1)} %u_ref.3), kind=kLoop, calls=%fused_computation.4 | loop fusion | bytes 65536 | tf_op jit(solution)/shard_map/stack;squeeze | solution.py:233
  2.2 3.5 %collective-permute-start = (bf16[2,128,128]{2,1,0:T(8,128)(2,1)S(1)}, bf16[2,128,128]{2,1,0:T(8,128)(2,1)S(1)}, u32[]{:S(2)}, u32[]{:S(2)}) collective-permute-start(bf16[2,128,128]{2,1,0:T(8,128)(2,1)S(1)} %pad_maximum_fusion.2), channel_id=1, source_target_pairs={{0,1},{1,2},{2,3},{4,5},{5,6},{6,7},{8,9},{9,10},{10,11},{12,13},{... | collective-permute-start | bytes 196616 | tf_op jit(solution)/shard_map/ppermute | solution.py:26
  5.7 1.3 %collective-permute-start.1 = (bf16[128,128]{1,0:T(8,128)(2,1)S(1)}, bf16[128,128]{1,0:T(8,128)(2,1)S(1)}, u32[]{:S(2)}, u32[]{:S(2)}) collective-permute-start(bf16[128,128]{1,0:T(8,128)(2,1)S(1)} %get-tuple-element.19), channel_id=1, source_target_pairs={{1,0},{2,1},{3,2},{5,4},{6,5},{7,6},{9,8},{10,9},{11,10},{13,12},{... | collective-permute-start | bytes 98312 | tf_op jit(solution)/shard_map/ppermute | solution.py:26
  7.0 3.5 %shard_map.85 = (bf16[3072,128]{1,0:T(8,128)(2,1)}, f32[3,128,128]{2,1,0:T(8,128)}, bf16[8,2,128,128]{3,2,1,0:T(8,128)(2,1)}) custom-call(s32[1,1,16]{2,1,0:T(1,128)} %blocks_ref.3, s32[1,8]{1,0:T(1,128)} %counts_ref.1, bf16[1,3072,128]{2,1,0:T(8,128)(2,1)} %z_ref.3, bf16[1,24,128,128]{3,2,1,0:T(8,128)(2,1)} %d_ref.1, bf16[1,24,128,128]{3,2,1,0:T(8,128)(2,1)} %u_ref.3), custom_call_target="tpu_custom_call" | custom-call | tf_op jit(solution)/shard_map/pallas_call | solution.py:97
  10.5 1.0 %collective-permute-done.1.zn_ref = bf16[128,128]{1,0:T(8,128)(2,1)S(1)} collective-permute-done((bf16[128,128]{1,0:T(8,128)(2,1)S(1)}, bf16[128,128]{1,0:T(8,128)(2,1)S(1)}, u32[]{:S(2)}, u32[]{:S(2)}) %collective-permute-start.1) | collective-permute-done | bytes 32800 | tf_op jit(solution)/shard_map/ppermute | solution.py:26
  11.5 0.0 collective-permute-done.fp_ref
  11.5 0.6 copy-done.6
  12.1 0.0 copy-done.5
  12.1 2.9 %shard_map.86 = (bf16[3,2,128,128]{3,2,1,0:T(8,128)(2,1)}, bf16[3,2,128,128]{3,2,1,0:T(8,128)(2,1)}, bf16[1,2,128,128]{3,2,1,0:T(8,128)(2,1)}, bf16[1,2,128,128]{3,2,1,0:T(8,128)(2,1)}, f32[128,128]{1,0:T(8,128)}) custom-call(s32[1,1,16]{2,1,0:T(1,128)} %blocks_ref.3, bf16[1,3072,128]{2,1,0:T(8,128)(2,1)} %z_ref.3, bf16[2,128,128]{2,1,0:T(8,128)(2,1)} %copy-done.5, ...), custom_call_target="tpu_custom_call" | custom-call | tf_op jit(solution)/shard_map/pallas_call | solution.py:107
  15.0 1.9 %collective-permute-start.2 = (bf16[3,2,128,128]{3,2,1,0:T(8,128)(2,1)}, bf16[3,2,128,128]{3,2,1,0:T(8,128)(2,1)S(1)}, u32[]{:S(2)}, u32[]{:S(2)}) collective-permute-start(bf16[3,2,128,128]{3,2,1,0:T(8,128)(2,1)} %get-tuple-element.15), channel_id=1, source_target_pairs={{4,0},{8,4},{12,8},{16,12},{20,16},{24,20},{28,24},{32,28},{36,32}... | collective-permute-start | bytes 589832 | tf_op jit(solution)/shard_map/ppermute | solution.py:255
  16.9 2.4 %collective-permute-start.3 = (bf16[3,2,128,128]{3,2,1,0:T(8,128)(2,1)}, bf16[3,2,128,128]{3,2,1,0:T(8,128)(2,1)S(1)}, u32[]{:S(2)}, u32[]{:S(2)}) collective-permute-start(bf16[3,2,128,128]{3,2,1,0:T(8,128)(2,1)} %get-tuple-element.16), channel_id=1, source_target_pairs={{0,4},{4,8},{8,12},{12,16},{16,20},{20,24},{24,28},{28,32},{32,36}... | collective-permute-start | bytes 589832 | tf_op jit(solution)/shard_map/ppermute | solution.py:258
  19.4 1.1 %collective-permute-done.2.down_ref = bf16[3,2,128,128]{3,2,1,0:T(8,128)(2,1)S(1)} collective-permute-done((bf16[3,2,128,128]{3,2,1,0:T(8,128)(2,1)}, bf16[3,2,128,128]{3,2,1,0:T(8,128)(2,1)S(1)}, u32[]{:S(2)}, u32[]{:S(2)}) %collective-permute-start.2) | collective-permute-done | bytes 196640 | tf_op jit(solution)/shard_map/ppermute | solution.py:255
  20.4 3.7 %collective-permute-done.3.up_ref = bf16[3,2,128,128]{3,2,1,0:T(8,128)(2,1)S(1)} collective-permute-done((bf16[3,2,128,128]{3,2,1,0:T(8,128)(2,1)}, bf16[3,2,128,128]{3,2,1,0:T(8,128)(2,1)S(1)}, u32[]{:S(2)}, u32[]{:S(2)}) %collective-permute-start.3) | collective-permute-done | bytes 196640 | tf_op jit(solution)/shard_map/ppermute | solution.py:258
  24.2 0.9 %pad_maximum_fusion.1 = bf16[3,2,128,128]{3,2,1,0:T(8,128)(2,1)S(1)} fusion(bf16[1,2,128,128]{3,2,1,0:T(8,128)(2,1)S(1)} %get-tuple-element.23, bf16[1,2,128,128]{3,2,1,0:T(8,128)(2,1)S(1)} %get-tuple-element.21, bf16[1,2,128,128]{3,2,1,0:T(8,128)(2,1)} %get-tuple-element.18), kind=kLoop, calls=%fused_computation.1 | loop fusion | flops 196608 | bytes 393216 | tf_op jit(solution)/shard_map/concatenate | solution.py:265
  25.1 6.4 %collective-permute-start.5 = (bf16[3,2,128,128]{3,2,1,0:T(8,128)(2,1)S(1)}, bf16[3,2,128,128]{3,2,1,0:T(8,128)(2,1)S(1)}, u32[]{:S(2)}, u32[]{:S(2)}) collective-permute-start(bf16[3,2,128,128]{3,2,1,0:T(8,128)(2,1)S(1)} %pad_maximum_fusion.1), channel_id=1, source_target_pairs={{0,64},{4,68},{8,72},{12,76},{16,80},{20,84},{24,88},{28,92},{32,9... | collective-permute-start | bytes 589832 | tf_op jit(solution)/shard_map/ppermute | solution.py:264
  31.5 0.9 %pad_maximum_fusion = bf16[3,2,128,128]{3,2,1,0:T(8,128)(2,1)S(1)} fusion(bf16[1,2,128,128]{3,2,1,0:T(8,128)(2,1)S(1)} %get-tuple-element.24, bf16[1,2,128,128]{3,2,1,0:T(8,128)(2,1)S(1)} %get-tuple-element.22, bf16[1,2,128,128]{3,2,1,0:T(8,128)(2,1)} %get-tuple-element.17), kind=kLoop, calls=%fused_computation | loop fusion | flops 196608 | bytes 393216 | tf_op jit(solution)/shard_map/concatenate | solution.py:260
  32.4 1.9 %collective-permute-start.4 = (bf16[3,2,128,128]{3,2,1,0:T(8,128)(2,1)S(1)}, bf16[3,2,128,128]{3,2,1,0:T(8,128)(2,1)S(1)}, u32[]{:S(2)}, u32[]{:S(2)}) collective-permute-start(bf16[3,2,128,128]{3,2,1,0:T(8,128)(2,1)S(1)} %pad_maximum_fusion), channel_id=1, source_target_pairs={{64,0},{68,4},{72,8},{76,12},{80,16},{84,20},{88,24},{92,28},{96,3... | collective-permute-start | bytes 589832 | tf_op jit(solution)/shard_map/ppermute | solution.py:259
  34.9 0.8 %dynamic_slice.3 = f32[32,32]{1,0:T(8,128)S(1)} dynamic-slice(f32[128,128]{1,0:T(8,128)} %get-tuple-element.13.gram_ref, s32[]{:T(128)S(6)} %select_n.4, s32[]{:T(128)S(6)} %select_n.4), dynamic_slice_sizes={32,32} | dynamic-slice | bytes 8196 | tf_op jit(solution)/shard_map/dynamic_slice | solution.py:248
  35.8 0.7 reshape.12
  36.5 4.5 %all-to-all-start.1 = ((f32[4,1,1024]{2,1,0:T(1,128)}), f32[4,1,1024]{2,1,0:T(1,128)S(1)}, u32[]{:S(2)}, u32[]{:S(2)}) async-start(f32[4,1,1024]{2,1,0:T(1,128)} %reshape.12), calls=%async_computation.1 | async-start | bytes 32768 | tf_op jit(solution)/shard_map/all_to_all | solution.py:249
  41.0 6.1 %collective-permute-done.4.fdn_ref = bf16[3,2,128,128]{3,2,1,0:T(8,128)(2,1)S(1)} collective-permute-done((bf16[3,2,128,128]{3,2,1,0:T(8,128)(2,1)S(1)}, bf16[3,2,128,128]{3,2,1,0:T(8,128)(2,1)S(1)}, u32[]{:S(2)}, u32[]{:S(2)}) %collective-permute-start.4) | collective-permute-done | bytes 196640 | tf_op jit(solution)/shard_map/ppermute | solution.py:259
  47.1 0.7 copy-done.4
  47.8 2.7 %shard_map.87 = f32[4,64,1152]{2,1,0:T(8,128)} custom-call(s32[1]{0:T(128)S(6)} %copy.9.owner_ref, f32[128,128]{1,0:T(8,128)} %get-tuple-element.13.gram_ref, bf16[8,2,128,128]{3,2,1,0:T(8,128)(2,1)} %get-tuple-element.14.own_ref, bf16[3,2,128,128]{3,2,1,0:T(8,128)(2,1)} %copy-done.1, bf16[3,2,128,128]{3,2,1,0:T(8,128)(2,1)} %copy-done.2, ...), custom_call_target="tpu_custom_call" | custom-call | tf_op jit(solution)/shard_map/pallas_call | solution.py:212
  50.5 5.3 %all-to-all-start = ((f32[4,64,1152]{2,1,0:T(8,128)}), f32[4,64,1152]{2,1,0:T(8,128)S(1)}, u32[]{:S(2)}, u32[]{:S(2)}) async-start(f32[4,64,1152]{2,1,0:T(8,128)} %shard_map.87), calls=%async_computation | async-start | bytes 2359296 | tf_op jit(solution)/shard_map/all_to_all | solution.py:273
  55.8 0.5 broadcast.1
  56.3 0.7 reduce
  57.0 0.7 reshape.13.blocks_ref
  57.7 4.2 %shard_map.88.inverse_ref = f32[32,32]{1,0:T(8,128)} custom-call(f32[4,32,32]{2,1,0:T(8,128)} %reshape.13.blocks_ref), custom_call_target="tpu_custom_call" | custom-call | tf_op jit(solution)/shard_map/pallas_call | solution.py:144
  61.9 10.2 %all-to-all-done.pieces_ref = f32[4,64,1152]{2,1,0:T(8,128)S(1)} async-done(((f32[4,64,1152]{2,1,0:T(8,128)}), f32[4,64,1152]{2,1,0:T(8,128)S(1)}, u32[]{:S(2)}, u32[]{:S(2)}) %all-to-all-start) | async-done | bytes 1179680 | tf_op jit(solution)/shard_map/all_to_all | solution.py:273
  72.1 1.0 %copy-done = f32[4,64,1152]{2,1,0:T(8,128)} copy-done((f32[4,64,1152]{2,1,0:T(8,128)}, f32[4,64,1152]{2,1,0:T(8,128)S(1)}, u32[]{:S(2)}) %copy-start) | copy-done | bytes 1179672
  73.2 2.7 %shard_map.89 = (f32[32,128]{1,0:T(8,128)}, f32[32,1024]{1,0:T(8,128)}, f32[32,32]{1,0:T(8,128)}) custom-call(s32[1]{0:T(128)S(6)} %copy.9.owner_ref, f32[4,64,1152]{2,1,0:T(8,128)} %copy-done, f32[32,32]{1,0:T(8,128)} %shard_map.88.inverse_ref), custom_call_target="tpu_custom_call" | custom-call | tf_op jit(solution)/shard_map/pallas_call | solution.py:174
  (16 shorter events, 0.1 us)
Async XLA Ops:
  2.2 9.3 %collective-permute-start = (bf16[2,128,128]{2,1,0:T(8,128)(2,1)S(1)}, bf16[2,128,128]{2,1,0:T(8,128)(2,1)S(1)}, u32[]{:S(2)}, u32[]{:S(2)}) collective-permute-start(bf16[2,128,128]{2,1,0:T(8,128)(2,1)S(1)} %pad_maximum_fusion.2), channel_id=1, source_target_pairs={{0,1},{1,2},{2,3},{4,5},{5,6},{6,7},{8,9},{9,10},{10,11},{12,13},{... | collective-permute-start | bytes 196616 | tf_op jit(solution)/shard_map/ppermute | solution.py:26
  5.7 5.8 %collective-permute-start.1 = (bf16[128,128]{1,0:T(8,128)(2,1)S(1)}, bf16[128,128]{1,0:T(8,128)(2,1)S(1)}, u32[]{:S(2)}, u32[]{:S(2)}) collective-permute-start(bf16[128,128]{1,0:T(8,128)(2,1)S(1)} %get-tuple-element.19), channel_id=1, source_target_pairs={{1,0},{2,1},{3,2},{5,4},{6,5},{7,6},{9,8},{10,9},{11,10},{13,12},{... | collective-permute-start | bytes 98312 | tf_op jit(solution)/shard_map/ppermute | solution.py:26
  11.5 0.6 copy-start.6
  11.5 0.6 copy-start.5
  15.0 5.4 %collective-permute-start.2 = (bf16[3,2,128,128]{3,2,1,0:T(8,128)(2,1)}, bf16[3,2,128,128]{3,2,1,0:T(8,128)(2,1)S(1)}, u32[]{:S(2)}, u32[]{:S(2)}) collective-permute-start(bf16[3,2,128,128]{3,2,1,0:T(8,128)(2,1)} %get-tuple-element.15), channel_id=1, source_target_pairs={{4,0},{8,4},{12,8},{16,12},{20,16},{24,20},{28,24},{32,28},{36,32}... | collective-permute-start | bytes 589832 | tf_op jit(solution)/shard_map/ppermute | solution.py:255
  16.9 7.2 %collective-permute-start.3 = (bf16[3,2,128,128]{3,2,1,0:T(8,128)(2,1)}, bf16[3,2,128,128]{3,2,1,0:T(8,128)(2,1)S(1)}, u32[]{:S(2)}, u32[]{:S(2)}) collective-permute-start(bf16[3,2,128,128]{3,2,1,0:T(8,128)(2,1)} %get-tuple-element.16), channel_id=1, source_target_pairs={{0,4},{4,8},{8,12},{12,16},{16,20},{20,24},{24,28},{28,32},{32,36}... | collective-permute-start | bytes 589832 | tf_op jit(solution)/shard_map/ppermute | solution.py:258
  20.4 26.7 %copy-start.1 = (bf16[3,2,128,128]{3,2,1,0:T(8,128)(2,1)}, bf16[3,2,128,128]{3,2,1,0:T(8,128)(2,1)S(1)}, u32[]{:S(2)}) copy-start(bf16[3,2,128,128]{3,2,1,0:T(8,128)(2,1)S(1)} %collective-permute-done.2.down_ref) | copy-start | bytes 589828
  24.1 23.0 %copy-start.2 = (bf16[3,2,128,128]{3,2,1,0:T(8,128)(2,1)}, bf16[3,2,128,128]{3,2,1,0:T(8,128)(2,1)S(1)}, u32[]{:S(2)}) copy-start(bf16[3,2,128,128]{3,2,1,0:T(8,128)(2,1)S(1)} %collective-permute-done.3.up_ref) | copy-start | bytes 589828
  25.1 15.9 %collective-permute-start.5 = (bf16[3,2,128,128]{3,2,1,0:T(8,128)(2,1)S(1)}, bf16[3,2,128,128]{3,2,1,0:T(8,128)(2,1)S(1)}, u32[]{:S(2)}, u32[]{:S(2)}) collective-permute-start(bf16[3,2,128,128]{3,2,1,0:T(8,128)(2,1)S(1)} %pad_maximum_fusion.1), channel_id=1, source_target_pairs={{0,64},{4,68},{8,72},{12,76},{16,80},{20,84},{24,88},{28,92},{32,9... | collective-permute-start | bytes 589832 | tf_op jit(solution)/shard_map/ppermute | solution.py:264
  32.4 14.7 %collective-permute-start.4 = (bf16[3,2,128,128]{3,2,1,0:T(8,128)(2,1)S(1)}, bf16[3,2,128,128]{3,2,1,0:T(8,128)(2,1)S(1)}, u32[]{:S(2)}, u32[]{:S(2)}) collective-permute-start(bf16[3,2,128,128]{3,2,1,0:T(8,128)(2,1)S(1)} %pad_maximum_fusion), channel_id=1, source_target_pairs={{64,0},{68,4},{72,8},{76,12},{80,16},{84,20},{88,24},{92,28},{96,3... | collective-permute-start | bytes 589832 | tf_op jit(solution)/shard_map/ppermute | solution.py:259
  36.5 14.0 %all-to-all-start.1 = ((f32[4,1,1024]{2,1,0:T(1,128)}), f32[4,1,1024]{2,1,0:T(1,128)S(1)}, u32[]{:S(2)}, u32[]{:S(2)}) async-start(f32[4,1,1024]{2,1,0:T(1,128)} %reshape.12), calls=%async_computation.1 | async-start | bytes 32768 | tf_op jit(solution)/shard_map/all_to_all | solution.py:249
  41.0 6.1 %copy-start.3 = (bf16[3,2,128,128]{3,2,1,0:T(8,128)(2,1)}, bf16[3,2,128,128]{3,2,1,0:T(8,128)(2,1)S(1)}, u32[]{:S(2)}) copy-start(bf16[3,2,128,128]{3,2,1,0:T(8,128)(2,1)S(1)} %collective-permute-done.5.fup_ref) | copy-start | bytes 589828
  47.1 0.7 copy-start.4
  50.5 21.6 %all-to-all-start = ((f32[4,64,1152]{2,1,0:T(8,128)}), f32[4,64,1152]{2,1,0:T(8,128)S(1)}, u32[]{:S(2)}, u32[]{:S(2)}) async-start(f32[4,64,1152]{2,1,0:T(8,128)} %shard_map.87), calls=%async_computation | async-start | bytes 2359296 | tf_op jit(solution)/shard_map/all_to_all | solution.py:273
  72.1 1.1 %copy-start = (f32[4,64,1152]{2,1,0:T(8,128)}, f32[4,64,1152]{2,1,0:T(8,128)S(1)}, u32[]{:S(2)}) copy-start(f32[4,64,1152]{2,1,0:T(8,128)S(1)} %all-to-all-done.pieces_ref) | copy-start | bytes 3538948

commit v13 on v12

--- a/solution.py
+++ b/solution.py
@@ -43,7 +43,7 @@
     return lax.dot_general(a, b, (((0,), (0,)), ((), ())), preferred_element_type=jnp.float32)
 
 
-def interior_kernel(blocks_ref, counts_ref, z_ref, d_ref, u_ref, app_ref, edge_ref, own_ref):
+def interior_kernel(blocks_ref, counts_ref, z_ref, d_ref, u_ref, app_ref, edge_ref, own_ref, gram_ref):
     count, rows = d_ref.shape[1], d_ref.shape[2]
     per_slot = own_ref.shape[1]
     crow = lax.axis_index("crow")
@@ -51,15 +51,20 @@
     def rows_of(b):
         return z_ref[0, pl.ds(b * rows, rows), :]
 
-    for b in range(1, count - 1):
+    last = count - 1
+    for b in range(1, last):
         total = (_ab(d_ref[0, b], rows_of(b)) + _ab(u_ref[0, b], rows_of(b + 1))) + _atb(
             u_ref[0, b - 1], rows_of(b - 1)
         )
         app_ref[pl.ds(b * rows, rows), :] = total.astype(app_ref.dtype)
-    last = count - 1
     edge_ref[0] = _ab(d_ref[0, 0], rows_of(0)) + _ab(u_ref[0, 0], rows_of(1))
     edge_ref[1] = _ab(d_ref[0, last], rows_of(last))
     edge_ref[2] = _atb(u_ref[0, last - 1], rows_of(last - 1))
+    app_ref[pl.ds(0, rows), :] = jnp.zeros((rows, app_ref.shape[1]), app_ref.dtype)
+    app_ref[pl.ds(last * rows, rows), :] = jnp.zeros((rows, app_ref.shape[1]), app_ref.dtype)
+    gram_ref[...] = _atb(
+        z_ref[0, pl.ds(rows, (count - 2) * rows), :], app_ref[pl.ds(rows, (count - 2) * rows), :]
+    )
     for slot in range(own_ref.shape[0]):
         for unit in range(per_slot):
             start = pl.multiple_of(blocks_ref[0, 0, slot * per_slot + unit] * rows, rows)
@@ -68,22 +73,34 @@
             own_ref[slot, unit] = jnp.where(live, tile, jnp.zeros_like(tile))
 
 
-def finish_kernel(groups, blocks_ref, z_ref, fp_ref, zn_ref, u_ref, app_in_ref, edge_ref, *refs):
-    group_refs, gram_ref, app_ref = refs[:len(groups)], refs[-2], refs[-1]
-    count, rows = u_ref.shape[1], u_ref.shape[2]
-    last = count - 1
-    app_ref[...] = app_in_ref[...]
-    first = edge_ref[0] + _atb(fp_ref[1], fp_ref[0])
-    app_ref[pl.ds(0, rows), :] = first.astype(app_ref.dtype)
-    final = (edge_ref[1] + _ab(u_ref[0, last], zn_ref[...])) + edge_ref[2]
-    app_ref[pl.ds(last * rows, rows), :] = final.astype(app_ref.dtype)
-    gram_ref[...] = _atb(z_ref[0], app_ref[...])
+def finish_kernel(groups, blocks_ref, edge_z_ref, fp_ref, zn_ref, up_ref, app_hbm, edge_ref, part_ref, *refs):
+    group_refs, gram_ref, sems = refs[:len(groups)], refs[-2], refs[-1]
+    rows = up_ref.shape[0]
+    last = app_hbm.shape[0] // rows - 1
     per_slot = group_refs[0].shape[1]
+    copies = []
     for group, out_ref in zip(groups, group_refs):
         for place, slot in enumerate(group):
             for unit in range(per_slot):
                 start = pl.multiple_of(blocks_ref[0, 0, slot * per_slot + unit] * rows, rows)
-                out_ref[place, unit] = app_ref[pl.ds(start, rows), :]
+                copy = pltpu.make_async_copy(
+                    app_hbm.at[pl.ds(start, rows)], out_ref.at[place, unit], sems.at[len(copies)]
+                )
+                copy.start()
+                copies.append(copy)
+    first = (edge_ref[0] + _atb(fp_ref[1], fp_ref[0])).astype(app_hbm.dtype)
+    final = ((edge_ref[1] + _ab(up_ref[...], zn_ref[...])) + edge_ref[2]).astype(app_hbm.dtype)
+    gram_ref[...] = (part_ref[...] + _atb(edge_z_ref[0], first)) + _atb(edge_z_ref[1], final)
+    for copy in copies:
+        copy.wait()
+    for group, out_ref in zip(groups, group_refs):
+        for place, slot in enumerate(group):
+            for unit in range(per_slot):
+                block = blocks_ref[0, 0, slot * per_slot + unit]
+                fetched = out_ref[place, unit]
+                out_ref[place, unit] = jnp.where(
+                    block == 0, first, jnp.where(block == last, final, fetched)
+                )
 
 
 def local_apply(groups, tile_blocks, pair_counts, deflation, forward_pair, next_rows, diag_op, upper_op):
@@ -94,25 +111,28 @@
     vmem = pl.BlockSpec(memory_space=pltpu.VMEM)
     smem = pl.BlockSpec(memory_space=pltpu.SMEM)
     tile = lambda n: jax.ShapeDtypeStruct((n, per_slot, rows, width), deflation.dtype)
-    app, edge, own = pl.pallas_call(
+    app, edge, own, part = pl.pallas_call(
         interior_kernel,
         out_shape=(
             jax.ShapeDtypeStruct((blocks * rows, width), deflation.dtype),
             jax.ShapeDtypeStruct((3, rows, width), jnp.float32),
             tile(slots),
+            jax.ShapeDtypeStruct((width, width), jnp.float32),
         ),
         in_specs=[smem, smem] + [vmem] * 3,
-        out_specs=(vmem, vmem, vmem),
+        out_specs=(vmem, vmem, vmem, vmem),
     )(tile_blocks, pair_counts, deflation, diag_op, upper_op)
+    local_rows = deflation[0]
+    edge_rows = jnp.stack([local_rows[:rows], local_rows[-rows:]])
     outs = pl.pallas_call(
         functools.partial(finish_kernel, groups),
         out_shape=tuple(tile(len(g)) for g in groups) + (
             jax.ShapeDtypeStruct((width, width), jnp.float32),
         ),
-        in_specs=[smem] + [vmem] * 6,
+        in_specs=[smem] + [vmem] * 4 + [pl.BlockSpec(memory_space=pl.ANY)] + [vmem] * 2,
         out_specs=tuple(vmem for _ in range(len(groups) + 1)),
-        scratch_shapes=[pltpu.VMEM((blocks * rows, width), deflation.dtype)],
-    )(tile_blocks, deflation, forward_pair, next_rows, upper_op, app, edge)
+        scratch_shapes=[pltpu.SemaphoreType.DMA((tile_blocks.shape[2],))],
+    )(tile_blocks, edge_rows, forward_pair, next_rows, upper_op[0, blocks - 1], app, edge, part)
     return outs[:-1] + (own, outs[-1])
 
 

time: 76.7 us -> 78.3 us (1.021)
    squeeze x0 -> x1, local copies, waits for them, and re-layouts: none -> 1.38 us  [local_apply(): upper_op[0, blocks - 1]]
where the time goes in v13:
time: 78.3 us; the launch traced here: 77.3 us
  starting transfers between devices  27.3 us (35%)
  waiting for transfers between devices  22 us (28%)
  Pallas kernels  16.2 us (21%)
  local copies, waits for them, and re-layouts  7.28 us (9%)
  other arithmetic  3.13 us (4%)
  between operations  1.38 us (2%)
    all_to_all x1, waiting for transfers between devices, per_device(): pieces = lax.all_to_all(outgoing_rows, 'crow', 0, 0, tiled=True)  10.2 us
    ppermute x1, starting transfers between devices, per_device(): lax.ppermute(jnp.concatenate([near_up, down[2:], up[2:]]), 'sub', [(u, u...  6.39 us
    ppermute x1, waiting for transfers between devices, per_device(): lax.ppermute(jnp.concatenate([near_down, down[:1], up[:1]]), 'sub', [(u,...  6.14 us
    all_to_all x1, starting transfers between devices, per_device(): pieces = lax.all_to_all(outgoing_rows, 'crow', 0, 0, tiled=True)  5.27 us
    ppermute x2, starting transfers between devices, shifted(): lax.ppermute(value, axis, [(source, source + steps) for source in range(i...  4.76 us
    all_to_all x1, starting transfers between devices, per_device(): lax.all_to_all(jnp.broadcast_to(pivot_part[None], (crow_count, row_share,...  4.61 us
    pallas_call x1, Pallas kernels, pivot_inverse(): pl.pallas_call(pivot_inverse_kernel, out_shape=jax.ShapeDtypeStruct((shar...  4.24 us
    unnamed x16, local copies, waits for them, and re-layouts  3.78 us
  transfers between devices with their start and end apart: 8, of which 5 were waited for; matrix products, arithmetic and copies ran while one was open for 6% of the time, Pallas kernels for 14%

profile of v13, /device:TPU:198, one launch (start us, length us, event | category | flops | bytes accessed | tf_op | source)
XLA Modules:
  0.0 77.3 jit_solution(11204815324564719179)
XLA Ops:
  0.6 0.8 %slice_bitcast_fusion.2 = (bf16[128,128]{1,0:T(8,128)(2,1)S(1)}, bf16[1,128,128]{2,1,0:T(8,128)(2,1)S(1)}, bf16[1,128,128]{2,1,0:T(8,128)(2,1)S(1)}) fusion(bf16[1,3072,128]{2,1,0:T(8,128)(2,1)} %z_ref.1), kind=kLoop, calls=%fused_computation.6 | loop fusion | bytes 163840 | tf_op jit(solution)/shard_map/slice | solution.py:126
  1.4 1.4 %slice_bitcast_fusion = (bf16[128,128]{1,0:T(8,128)(2,1)}, bf16[1,128,128]{2,1,0:T(8,128)(2,1)S(1)}) fusion(bf16[1,24,128,128]{3,2,1,0:T(8,128)(2,1)} %u_ref.1), kind=kLoop, calls=%fused_computation.4 | loop fusion | bytes 98304 | tf_op jit(solution)/shard_map/squeeze | solution.py:135
  2.8 0.6 pad_maximum_fusion.3
  3.4 3.5 %collective-permute-start = (bf16[2,128,128]{2,1,0:T(8,128)(2,1)S(1)}, bf16[2,128,128]{2,1,0:T(8,128)(2,1)S(1)}, u32[]{:S(2)}, u32[]{:S(2)}) collective-permute-start(bf16[2,128,128]{2,1,0:T(8,128)(2,1)S(1)} %get-tuple-element.30), channel_id=1, source_target_pairs={{0,1},{1,2},{2,3},{4,5},{5,6},{6,7},{8,9},{9,10},{10,11},{12,13},{... | collective-permute-start | bytes 196616 | tf_op jit(solution)/shard_map/ppermute | solution.py:26
  6.9 1.3 %collective-permute-start.1 = (bf16[128,128]{1,0:T(8,128)(2,1)S(1)}, bf16[128,128]{1,0:T(8,128)(2,1)S(1)}, u32[]{:S(2)}, u32[]{:S(2)}) collective-permute-start(bf16[128,128]{1,0:T(8,128)(2,1)S(1)} %get-tuple-element.23), channel_id=1, source_target_pairs={{1,0},{2,1},{3,2},{5,4},{6,5},{7,6},{9,8},{10,9},{11,10},{13,12},{... | collective-permute-start | bytes 98312 | tf_op jit(solution)/shard_map/ppermute | solution.py:26
  8.2 3.6 %shard_map.85 = (bf16[3072,128]{1,0:T(8,128)(2,1)}, f32[3,128,128]{2,1,0:T(8,128)}, bf16[8,2,128,128]{3,2,1,0:T(8,128)(2,1)}, f32[128,128]{1,0:T(8,128)}) custom-call(s32[1,1,16]{2,1,0:T(1,128)} %blocks_ref.3, s32[1,8]{1,0:T(1,128)} %counts_ref.1, bf16[1,3072,128]{2,1,0:T(8,128)(2,1)} %z_ref.1, bf16[1,24,128,128]{3,2,1,0:T(8,128)(2,1)} %d_ref.1, ...), custom_call_target="tpu_custom_call" | custom-call | tf_op jit(solution)/shard_map/pallas_call | solution.py:114
  11.8 0.9 %collective-permute-done.1.zn_ref = bf16[128,128]{1,0:T(8,128)(2,1)S(1)} collective-permute-done((bf16[128,128]{1,0:T(8,128)(2,1)S(1)}, bf16[128,128]{1,0:T(8,128)(2,1)S(1)}, u32[]{:S(2)}, u32[]{:S(2)}) %collective-permute-start.1) | collective-permute-done | bytes 32800 | tf_op jit(solution)/shard_map/ppermute | solution.py:26
  12.7 0.6 copy-done.6
  13.3 0.0 copy-done.5
  13.4 3.1 %shard_map.86 = (bf16[3,2,128,128]{3,2,1,0:T(8,128)(2,1)}, bf16[3,2,128,128]{3,2,1,0:T(8,128)(2,1)}, bf16[1,2,128,128]{3,2,1,0:T(8,128)(2,1)}, bf16[1,2,128,128]{3,2,1,0:T(8,128)(2,1)}, f32[128,128]{1,0:T(8,128)}) custom-call(s32[1,1,16]{2,1,0:T(1,128)} %blocks_ref.3, bf16[2,128,128]{2,1,0:T(8,128)(2,1)} %get-tuple-element.31.edge_z_ref, ...), custom_call_target="tpu_custom_call" | custom-call | tf_op jit(solution)/shard_map/pallas_call | solution.py:127
  16.4 1.9 %collective-permute-start.2 = (bf16[3,2,128,128]{3,2,1,0:T(8,128)(2,1)}, bf16[3,2,128,128]{3,2,1,0:T(8,128)(2,1)S(1)}, u32[]{:S(2)}, u32[]{:S(2)}) collective-permute-start(bf16[3,2,128,128]{3,2,1,0:T(8,128)(2,1)} %get-tuple-element.17), channel_id=1, source_target_pairs={{4,0},{8,4},{12,8},{16,12},{20,16},{24,20},{28,24},{32,28},{36,32}... | collective-permute-start | bytes 589832 | tf_op jit(solution)/shard_map/ppermute | solution.py:275
  18.4 2.4 %collective-permute-start.3 = (bf16[3,2,128,128]{3,2,1,0:T(8,128)(2,1)}, bf16[3,2,128,128]{3,2,1,0:T(8,128)(2,1)S(1)}, u32[]{:S(2)}, u32[]{:S(2)}) collective-permute-start(bf16[3,2,128,128]{3,2,1,0:T(8,128)(2,1)} %get-tuple-element.18), channel_id=1, source_target_pairs={{0,4},{4,8},{8,12},{12,16},{16,20},{20,24},{24,28},{28,32},{32,36}... | collective-permute-start | bytes 589832 | tf_op jit(solution)/shard_map/ppermute | solution.py:278
  20.8 1.1 %collective-permute-done.2.down_ref = bf16[3,2,128,128]{3,2,1,0:T(8,128)(2,1)S(1)} collective-permute-done((bf16[3,2,128,128]{3,2,1,0:T(8,128)(2,1)}, bf16[3,2,128,128]{3,2,1,0:T(8,128)(2,1)S(1)}, u32[]{:S(2)}, u32[]{:S(2)}) %collective-permute-start.2) | collective-permute-done | bytes 196640 | tf_op jit(solution)/shard_map/ppermute | solution.py:275
  21.9 3.7 %collective-permute-done.3.up_ref = bf16[3,2,128,128]{3,2,1,0:T(8,128)(2,1)S(1)} collective-permute-done((bf16[3,2,128,128]{3,2,1,0:T(8,128)(2,1)}, bf16[3,2,128,128]{3,2,1,0:T(8,128)(2,1)S(1)}, u32[]{:S(2)}, u32[]{:S(2)}) %collective-permute-start.3) | collective-permute-done | bytes 196640 | tf_op jit(solution)/shard_map/ppermute | solution.py:278
  25.6 0.9 %pad_maximum_fusion.1 = bf16[3,2,128,128]{3,2,1,0:T(8,128)(2,1)S(1)} fusion(bf16[1,2,128,128]{3,2,1,0:T(8,128)(2,1)S(1)} %get-tuple-element.28, bf16[1,2,128,128]{3,2,1,0:T(8,128)(2,1)S(1)} %get-tuple-element.26, bf16[1,2,128,128]{3,2,1,0:T(8,128)(2,1)} %get-tuple-element.20), kind=kLoop, calls=%fused_computation.1 | loop fusion | flops 196608 | bytes 393216 | tf_op jit(solution)/shard_map/concatenate | solution.py:285
  26.5 6.4 %collective-permute-start.5 = (bf16[3,2,128,128]{3,2,1,0:T(8,128)(2,1)S(1)}, bf16[3,2,128,128]{3,2,1,0:T(8,128)(2,1)S(1)}, u32[]{:S(2)}, u32[]{:S(2)}) collective-permute-start(bf16[3,2,128,128]{3,2,1,0:T(8,128)(2,1)S(1)} %pad_maximum_fusion.1), channel_id=1, source_target_pairs={{0,64},{4,68},{8,72},{12,76},{16,80},{20,84},{24,88},{28,92},{32,9... | collective-permute-start | bytes 589832 | tf_op jit(solution)/shard_map/ppermute | solution.py:284
  32.9 0.9 %pad_maximum_fusion = bf16[3,2,128,128]{3,2,1,0:T(8,128)(2,1)S(1)} fusion(bf16[1,2,128,128]{3,2,1,0:T(8,128)(2,1)S(1)} %get-tuple-element.29, bf16[1,2,128,128]{3,2,1,0:T(8,128)(2,1)S(1)} %get-tuple-element.27, bf16[1,2,128,128]{3,2,1,0:T(8,128)(2,1)} %get-tuple-element.19), kind=kLoop, calls=%fused_computation | loop fusion | flops 196608 | bytes 393216 | tf_op jit(solution)/shard_map/concatenate | solution.py:280
  33.8 1.9 %collective-permute-start.4 = (bf16[3,2,128,128]{3,2,1,0:T(8,128)(2,1)S(1)}, bf16[3,2,128,128]{3,2,1,0:T(8,128)(2,1)S(1)}, u32[]{:S(2)}, u32[]{:S(2)}) collective-permute-start(bf16[3,2,128,128]{3,2,1,0:T(8,128)(2,1)S(1)} %pad_maximum_fusion), channel_id=1, source_target_pairs={{64,0},{68,4},{72,8},{76,12},{80,16},{84,20},{88,24},{92,28},{96,3... | collective-permute-start | bytes 589832 | tf_op jit(solution)/shard_map/ppermute | solution.py:279
  36.4 0.8 %dynamic_slice.3 = f32[32,32]{1,0:T(8,128)S(1)} dynamic-slice(f32[128,128]{1,0:T(8,128)} %get-tuple-element.15.gram_ref, s32[]{:T(128)S(6)} %select_n.4, s32[]{:T(128)S(6)} %select_n.4), dynamic_slice_sizes={32,32} | dynamic-slice | bytes 8196 | tf_op jit(solution)/shard_map/dynamic_slice | solution.py:268
  37.2 0.7 reshape.13
  37.9 4.6 %all-to-all-start.1 = ((f32[4,1,1024]{2,1,0:T(1,128)}), f32[4,1,1024]{2,1,0:T(1,128)S(1)}, u32[]{:S(2)}, u32[]{:S(2)}) async-start(f32[4,1,1024]{2,1,0:T(1,128)} %reshape.13), calls=%async_computation.1 | async-start | bytes 32768 | tf_op jit(solution)/shard_map/all_to_all | solution.py:269
  42.5 6.1 %collective-permute-done.4.fdn_ref = bf16[3,2,128,128]{3,2,1,0:T(8,128)(2,1)S(1)} collective-permute-done((bf16[3,2,128,128]{3,2,1,0:T(8,128)(2,1)S(1)}, bf16[3,2,128,128]{3,2,1,0:T(8,128)(2,1)S(1)}, u32[]{:S(2)}, u32[]{:S(2)}) %collective-permute-start.4) | collective-permute-done | bytes 196640 | tf_op jit(solution)/shard_map/ppermute | solution.py:279
  48.6 0.7 copy-done.4
  49.3 2.7 %shard_map.87 = f32[4,64,1152]{2,1,0:T(8,128)} custom-call(s32[1]{0:T(128)S(6)} %copy.9.owner_ref, f32[128,128]{1,0:T(8,128)} %get-tuple-element.15.gram_ref, bf16[8,2,128,128]{3,2,1,0:T(8,128)(2,1)} %get-tuple-element.16.own_ref, bf16[3,2,128,128]{3,2,1,0:T(8,128)(2,1)} %copy-done.1, bf16[3,2,128,128]{3,2,1,0:T(8,128)(2,1)} %copy-done.2, ...), custom_call_target="tpu_custom_call" | custom-call | tf_op jit(solution)/shard_map/pallas_call | solution.py:232
  52.0 5.3 %all-to-all-start = ((f32[4,64,1152]{2,1,0:T(8,128)}), f32[4,64,1152]{2,1,0:T(8,128)S(1)}, u32[]{:S(2)}, u32[]{:S(2)}) async-start(f32[4,64,1152]{2,1,0:T(8,128)} %shard_map.87), calls=%async_computation | async-start | bytes 2359296 | tf_op jit(solution)/shard_map/all_to_all | solution.py:293
  57.3 0.5 broadcast.1
  57.8 0.7 reduce
  58.5 0.7 reshape.14.blocks_ref
  59.2 4.2 %shard_map.88.inverse_ref = f32[32,32]{1,0:T(8,128)} custom-call(f32[4,32,32]{2,1,0:T(8,128)} %reshape.14.blocks_ref), custom_call_target="tpu_custom_call" | custom-call | tf_op jit(solution)/shard_map/pallas_call | solution.py:164
  63.4 10.2 %all-to-all-done.pieces_ref = f32[4,64,1152]{2,1,0:T(8,128)S(1)} async-done(((f32[4,64,1152]{2,1,0:T(8,128)}), f32[4,64,1152]{2,1,0:T(8,128)S(1)}, u32[]{:S(2)}, u32[]{:S(2)}) %all-to-all-start) | async-done | bytes 1179680 | tf_op jit(solution)/shard_map/all_to_all | solution.py:293
  73.6 1.0 %copy-done = f32[4,64,1152]{2,1,0:T(8,128)} copy-done((f32[4,64,1152]{2,1,0:T(8,128)}, f32[4,64,1152]{2,1,0:T(8,128)S(1)}, u32[]{:S(2)}) %copy-start) | copy-done | bytes 1179672
  74.7 2.7 %shard_map.89 = (f32[32,128]{1,0:T(8,128)}, f32[32,1024]{1,0:T(8,128)}, f32[32,32]{1,0:T(8,128)}) custom-call(s32[1]{0:T(128)S(6)} %copy.9.owner_ref, f32[4,64,1152]{2,1,0:T(8,128)} %copy-done, f32[32,32]{1,0:T(8,128)} %shard_map.88.inverse_ref), custom_call_target="tpu_custom_call" | custom-call | tf_op jit(solution)/shard_map/pallas_call | solution.py:194
  (16 shorter events, 0.1 us)
Async XLA Ops:
  3.4 9.3 %collective-permute-start = (bf16[2,128,128]{2,1,0:T(8,128)(2,1)S(1)}, bf16[2,128,128]{2,1,0:T(8,128)(2,1)S(1)}, u32[]{:S(2)}, u32[]{:S(2)}) collective-permute-start(bf16[2,128,128]{2,1,0:T(8,128)(2,1)S(1)} %get-tuple-element.30), channel_id=1, source_target_pairs={{0,1},{1,2},{2,3},{4,5},{5,6},{6,7},{8,9},{9,10},{10,11},{12,13},{... | collective-permute-start | bytes 196616 | tf_op jit(solution)/shard_map/ppermute | solution.py:26
  6.9 5.8 %collective-permute-start.1 = (bf16[128,128]{1,0:T(8,128)(2,1)S(1)}, bf16[128,128]{1,0:T(8,128)(2,1)S(1)}, u32[]{:S(2)}, u32[]{:S(2)}) collective-permute-start(bf16[128,128]{1,0:T(8,128)(2,1)S(1)} %get-tuple-element.23), channel_id=1, source_target_pairs={{1,0},{2,1},{3,2},{5,4},{6,5},{7,6},{9,8},{10,9},{11,10},{13,12},{... | collective-permute-start | bytes 98312 | tf_op jit(solution)/shard_map/ppermute | solution.py:26
  12.7 0.6 copy-start.6
  12.7 0.6 copy-start.5
  16.4 5.4 %collective-permute-start.2 = (bf16[3,2,128,128]{3,2,1,0:T(8,128)(2,1)}, bf16[3,2,128,128]{3,2,1,0:T(8,128)(2,1)S(1)}, u32[]{:S(2)}, u32[]{:S(2)}) collective-permute-start(bf16[3,2,128,128]{3,2,1,0:T(8,128)(2,1)} %get-tuple-element.17), channel_id=1, source_target_pairs={{4,0},{8,4},{12,8},{16,12},{20,16},{24,20},{28,24},{32,28},{36,32}... | collective-permute-start | bytes 589832 | tf_op jit(solution)/shard_map/ppermute | solution.py:275
  18.4 7.2 %collective-permute-start.3 = (bf16[3,2,128,128]{3,2,1,0:T(8,128)(2,1)}, bf16[3,2,128,128]{3,2,1,0:T(8,128)(2,1)S(1)}, u32[]{:S(2)}, u32[]{:S(2)}) collective-permute-start(bf16[3,2,128,128]{3,2,1,0:T(8,128)(2,1)} %get-tuple-element.18), channel_id=1, source_target_pairs={{0,4},{4,8},{8,12},{12,16},{16,20},{20,24},{24,28},{28,32},{32,36}... | collective-permute-start | bytes 589832 | tf_op jit(solution)/shard_map/ppermute | solution.py:278
  21.8 26.8 %copy-start.1 = (bf16[3,2,128,128]{3,2,1,0:T(8,128)(2,1)}, bf16[3,2,128,128]{3,2,1,0:T(8,128)(2,1)S(1)}, u32[]{:S(2)}) copy-start(bf16[3,2,128,128]{3,2,1,0:T(8,128)(2,1)S(1)} %collective-permute-done.2.down_ref) | copy-start | bytes 589828
  25.6 23.1 %copy-start.2 = (bf16[3,2,128,128]{3,2,1,0:T(8,128)(2,1)}, bf16[3,2,128,128]{3,2,1,0:T(8,128)(2,1)S(1)}, u32[]{:S(2)}) copy-start(bf16[3,2,128,128]{3,2,1,0:T(8,128)(2,1)S(1)} %collective-permute-done.3.up_ref) | copy-start | bytes 589828
  26.5 16.0 %collective-permute-start.5 = (bf16[3,2,128,128]{3,2,1,0:T(8,128)(2,1)S(1)}, bf16[3,2,128,128]{3,2,1,0:T(8,128)(2,1)S(1)}, u32[]{:S(2)}, u32[]{:S(2)}) collective-permute-start(bf16[3,2,128,128]{3,2,1,0:T(8,128)(2,1)S(1)} %pad_maximum_fusion.1), channel_id=1, source_target_pairs={{0,64},{4,68},{8,72},{12,76},{16,80},{20,84},{24,88},{28,92},{32,9... | collective-permute-start | bytes 589832 | tf_op jit(solution)/shard_map/ppermute | solution.py:284
  33.8 14.8 %collective-permute-start.4 = (bf16[3,2,128,128]{3,2,1,0:T(8,128)(2,1)S(1)}, bf16[3,2,128,128]{3,2,1,0:T(8,128)(2,1)S(1)}, u32[]{:S(2)}, u32[]{:S(2)}) collective-permute-start(bf16[3,2,128,128]{3,2,1,0:T(8,128)(2,1)S(1)} %pad_maximum_fusion), channel_id=1, source_target_pairs={{64,0},{68,4},{72,8},{76,12},{80,16},{84,20},{88,24},{92,28},{96,3... | collective-permute-start | bytes 589832 | tf_op jit(solution)/shard_map/ppermute | solution.py:279
  37.9 14.1 %all-to-all-start.1 = ((f32[4,1,1024]{2,1,0:T(1,128)}), f32[4,1,1024]{2,1,0:T(1,128)S(1)}, u32[]{:S(2)}, u32[]{:S(2)}) async-start(f32[4,1,1024]{2,1,0:T(1,128)} %reshape.13), calls=%async_computation.1 | async-start | bytes 32768 | tf_op jit(solution)/shard_map/all_to_all | solution.py:269
  42.5 6.1 %copy-start.3 = (bf16[3,2,128,128]{3,2,1,0:T(8,128)(2,1)}, bf16[3,2,128,128]{3,2,1,0:T(8,128)(2,1)S(1)}, u32[]{:S(2)}) copy-start(bf16[3,2,128,128]{3,2,1,0:T(8,128)(2,1)S(1)} %collective-permute-done.5.fup_ref) | copy-start | bytes 589828
  48.6 0.7 copy-start.4
  52.0 21.6 %all-to-all-start = ((f32[4,64,1152]{2,1,0:T(8,128)}), f32[4,64,1152]{2,1,0:T(8,128)S(1)}, u32[]{:S(2)}, u32[]{:S(2)}) async-start(f32[4,64,1152]{2,1,0:T(8,128)} %shard_map.87), calls=%async_computation | async-start | bytes 2359296 | tf_op jit(solution)/shard_map/all_to_all | solution.py:293
  73.6 1.0 %copy-start = (f32[4,64,1152]{2,1,0:T(8,128)}, f32[4,64,1152]{2,1,0:T(8,128)S(1)}, u32[]{:S(2)}) copy-start(f32[4,64,1152]{2,1,0:T(8,128)S(1)} %all-to-all-done.pieces_ref) | copy-start | bytes 3538948

commit v14 on v10

--- a/solution.py
+++ b/solution.py
@@ -57,7 +57,7 @@
     for b in range(count):
         below = fp_ref[0] if b == 0 else rows_of(b - 1)
         lower = fp_ref[1] if b == 0 else u_ref[0, b - 1]
-        above = zn_ref[...] if b == count - 1 else rows_of(b + 1)
+        above = zn_ref[2] if b == count - 1 else rows_of(b + 1)
         total = (_ab(d_ref[0, b], rows_of(b)) + _ab(u_ref[0, b], above)) + _atb(lower, below)
         app_ref[pl.ds(b * rows, rows), :] = total.astype(app_ref.dtype)
     gram_ref[...] = _atb(z_ref[0], app_ref[...])
@@ -207,10 +207,9 @@
     coarse_width = local_rows.shape[1]
     slot_count = pair_counts.shape[1]
     per_slot = tile_blocks.shape[2] // slot_count
-    forward_pair = shifted(
-        jnp.stack([local_rows[-tile_rows:], upper_op[0, blocks_here - 1]]), "crow", 1
-    )
-    next_rows = shifted(local_rows[:tile_rows], "crow", -1)
+    halo = jnp.stack([local_rows[-tile_rows:], upper_op[0, blocks_here - 1], local_rows[:tile_rows]])
+    forward_pair = shifted(halo, "crow", 1)
+    next_rows = shifted(halo, "crow", -1)
     slot_of = {offset: index for index, offset in enumerate(offsets)}
     groups = (
         (slot_of[-across - 1], slot_of[-1], slot_of[across - 1]),

time: 75.8 us -> 75.9 us (level)
  transfers between devices with their start and end apart: 8 -> 8, of which waited for: 5 -> 6; matrix products, arithmetic and copies ran while one was open for 6% -> 6% of each run, Pallas kernels for 9% -> 9%
where the time goes in v14:
time: 75.9 us; the launch traced here: 75.1 us
  starting transfers between devices  25.7 us (34%)
  waiting for transfers between devices  25.5 us (34%)
  Pallas kernels  13.3 us (18%)
  local copies, waits for them, and re-layouts  6.68 us (9%)
  other arithmetic  2.5 us (3%)
  between operations  1.37 us (2%)
    all_to_all x1, waiting for transfers between devices, per_device(): pieces = lax.all_to_all(outgoing_rows, 'crow', 0, 0, tiled=True)  9.98 us
    ppermute x1, starting transfers between devices, per_device(): lax.ppermute(jnp.concatenate([near_up, down[2:], up[2:]]), 'sub', [(u, u...  6.39 us
    ppermute x1, waiting for transfers between devices, per_device(): lax.ppermute(jnp.concatenate([near_down, down[:1], up[:1]]), 'sub', [(u,...  5.58 us
    ppermute x2, waiting for transfers between devices, shifted(): lax.ppermute(value, axis, [(source, source + steps) for source in range(i...  5.21 us
    ppermute x2, starting transfers between devices, shifted(): lax.ppermute(value, axis, [(source, source + steps) for source in range(i...  4.78 us
    pallas_call x1, Pallas kernels, pivot_inverse(): pl.pallas_call(pivot_inverse_kernel, out_shape=jax.ShapeDtypeStruct((shar...  4.24 us
    all_to_all x1, starting transfers between devices, per_device(): pieces = lax.all_to_all(outgoing_rows, 'crow', 0, 0, tiled=True)  4.18 us
    all_to_all x1, starting transfers between devices, per_device(): lax.all_to_all(jnp.broadcast_to(pivot_part[None], (crow_count, row_share,...  4.16 us
  transfers between devices with their start and end apart: 8, of which 6 were waited for; matrix products, arithmetic and copies ran while one was open for 6% of the time, Pallas kernels for 9%

profile of v14, /device:TPU:194, one launch (start us, length us, event | category | flops | bytes accessed | tf_op | source)
XLA Modules:
  0.0 75.1 jit_solution(274307022041263208)
XLA Ops:
  0.6 0.8 %fusion = (bf16[1,128,128]{2,1,0:T(8,128)(2,1)S(1)}, bf16[1,128,128]{2,1,0:T(8,128)(2,1)S(1)}) fusion(bf16[1,3072,128]{2,1,0:T(8,128)(2,1)} %z_ref.1), kind=kLoop, calls=%fused_computation.4 | loop fusion | bytes 131072 | tf_op jit(solution)/shard_map/slice | solution.py:210
  1.4 0.8 %slice_bitcast_fusion = bf16[1,128,128]{2,1,0:T(8,128)(2,1)S(1)} fusion(bf16[1,24,128,128]{3,2,1,0:T(8,128)(2,1)} %u_ref.1), kind=kLoop, calls=%fused_computation.3 | loop fusion | bytes 65536 | tf_op jit(solution)/shard_map/stack;squeeze | solution.py:210
  2.2 3.5 %collective-permute-start = (bf16[3,128,128]{2,1,0:T(8,128)(2,1)S(1)}, bf16[3,128,128]{2,1,0:T(8,128)(2,1)S(1)}, u32[]{:S(2)}, u32[]{:S(2)}) collective-permute-start(bf16[3,128,128]{2,1,0:T(8,128)(2,1)S(1)} %pad_maximum_fusion.2), channel_id=1, source_target_pairs={{0,1},{1,2},{2,3},{4,5},{5,6},{6,7},{8,9},{9,10},{10,11},{12,13},{... | collective-permute-start | bytes 294920 | tf_op jit(solution)/shard_map/ppermute | solution.py:26
  5.7 1.3 %collective-permute-start.1 = (bf16[3,128,128]{2,1,0:T(8,128)(2,1)S(1)}, bf16[3,128,128]{2,1,0:T(8,128)(2,1)S(1)}, u32[]{:S(2)}, u32[]{:S(2)}) collective-permute-start(bf16[3,128,128]{2,1,0:T(8,128)(2,1)S(1)} %pad_maximum_fusion.2), channel_id=1, source_target_pairs={{1,0},{2,1},{3,2},{5,4},{6,5},{7,6},{9,8},{10,9},{11,10},{13,12},{... | collective-permute-start | bytes 294920 | tf_op jit(solution)/shard_map/ppermute | solution.py:26
  7.0 0.9 %collective-permute-done.fp_ref = bf16[3,128,128]{2,1,0:T(8,128)(2,1)S(1)} collective-permute-done((bf16[3,128,128]{2,1,0:T(8,128)(2,1)S(1)}, bf16[3,128,128]{2,1,0:T(8,128)(2,1)S(1)}, u32[]{:S(2)}, u32[]{:S(2)}) %collective-permute-start) | collective-permute-done | bytes 98336 | tf_op jit(solution)/shard_map/ppermute | solution.py:26
  7.9 4.3 %collective-permute-done.1.zn_ref = bf16[3,128,128]{2,1,0:T(8,128)(2,1)S(1)} collective-permute-done((bf16[3,128,128]{2,1,0:T(8,128)(2,1)S(1)}, bf16[3,128,128]{2,1,0:T(8,128)(2,1)S(1)}, u32[]{:S(2)}, u32[]{:S(2)}) %collective-permute-start.1) | collective-permute-done | bytes 98336 | tf_op jit(solution)/shard_map/ppermute | solution.py:26
  12.2 0.6 copy-done.6
  12.8 3.6 %shard_map.85 = (bf16[3,2,128,128]{3,2,1,0:T(8,128)(2,1)}, bf16[3,2,128,128]{3,2,1,0:T(8,128)(2,1)}, bf16[1,2,128,128]{3,2,1,0:T(8,128)(2,1)}, bf16[1,2,128,128]...) custom-call(s32[1,1,16]{2,1,0:T(1,128)} %blocks_ref.1, s32[1,8]{1,0:T(1,128)} %counts_ref.1, ...), custom_call_target="tpu_custom_call" | custom-call | tf_op jit(solution)/shard_map/pallas_call | solution.py:85
  16.5 1.9 %collective-permute-start.2 = (bf16[3,2,128,128]{3,2,1,0:T(8,128)(2,1)}, bf16[3,2,128,128]{3,2,1,0:T(8,128)(2,1)S(1)}, u32[]{:S(2)}, u32[]{:S(2)}) collective-permute-start(bf16[3,2,128,128]{3,2,1,0:T(8,128)(2,1)} %get-tuple-element.11), channel_id=1, source_target_pairs={{4,0},{8,4},{12,8},{16,12},{20,16},{24,20},{28,24},{32,28},{36,32}... | collective-permute-start | bytes 589832 | tf_op jit(solution)/shard_map/ppermute | solution.py:232
  18.4 2.4 %collective-permute-start.3 = (bf16[3,2,128,128]{3,2,1,0:T(8,128)(2,1)}, bf16[3,2,128,128]{3,2,1,0:T(8,128)(2,1)S(1)}, u32[]{:S(2)}, u32[]{:S(2)}) collective-permute-start(bf16[3,2,128,128]{3,2,1,0:T(8,128)(2,1)} %get-tuple-element.12), channel_id=1, source_target_pairs={{0,4},{4,8},{8,12},{12,16},{16,20},{20,24},{24,28},{28,32},{32,36}... | collective-permute-start | bytes 589832 | tf_op jit(solution)/shard_map/ppermute | solution.py:235
  20.8 1.1 %collective-permute-done.2.down_ref = bf16[3,2,128,128]{3,2,1,0:T(8,128)(2,1)S(1)} collective-permute-done((bf16[3,2,128,128]{3,2,1,0:T(8,128)(2,1)}, bf16[3,2,128,128]{3,2,1,0:T(8,128)(2,1)S(1)}, u32[]{:S(2)}, u32[]{:S(2)}) %collective-permute-start.2) | collective-permute-done | bytes 196640 | tf_op jit(solution)/shard_map/ppermute | solution.py:232
  21.9 3.7 %collective-permute-done.3.up_ref = bf16[3,2,128,128]{3,2,1,0:T(8,128)(2,1)S(1)} collective-permute-done((bf16[3,2,128,128]{3,2,1,0:T(8,128)(2,1)}, bf16[3,2,128,128]{3,2,1,0:T(8,128)(2,1)S(1)}, u32[]{:S(2)}, u32[]{:S(2)}) %collective-permute-start.3) | collective-permute-done | bytes 196640 | tf_op jit(solution)/shard_map/ppermute | solution.py:235
  25.6 0.9 %pad_maximum_fusion.1 = bf16[3,2,128,128]{3,2,1,0:T(8,128)(2,1)S(1)} fusion(bf16[1,2,128,128]{3,2,1,0:T(8,128)(2,1)S(1)} %get-tuple-element.19, bf16[1,2,128,128]{3,2,1,0:T(8,128)(2,1)S(1)} %get-tuple-element.17, bf16[1,2,128,128]{3,2,1,0:T(8,128)(2,1)} %get-tuple-element.14), kind=kLoop, calls=%fused_computation.1 | loop fusion | flops 196608 | bytes 393216 | tf_op jit(solution)/shard_map/concatenate | solution.py:242
  26.6 6.4 %collective-permute-start.5 = (bf16[3,2,128,128]{3,2,1,0:T(8,128)(2,1)S(1)}, bf16[3,2,128,128]{3,2,1,0:T(8,128)(2,1)S(1)}, u32[]{:S(2)}, u32[]{:S(2)}) collective-permute-start(bf16[3,2,128,128]{3,2,1,0:T(8,128)(2,1)S(1)} %pad_maximum_fusion.1), channel_id=1, source_target_pairs={{0,64},{4,68},{8,72},{12,76},{16,80},{20,84},{24,88},{28,92},{32,9... | collective-permute-start | bytes 589832 | tf_op jit(solution)/shard_map/ppermute | solution.py:241
  33.0 0.9 %pad_maximum_fusion = bf16[3,2,128,128]{3,2,1,0:T(8,128)(2,1)S(1)} fusion(bf16[1,2,128,128]{3,2,1,0:T(8,128)(2,1)S(1)} %get-tuple-element.20, bf16[1,2,128,128]{3,2,1,0:T(8,128)(2,1)S(1)} %get-tuple-element.18, bf16[1,2,128,128]{3,2,1,0:T(8,128)(2,1)} %get-tuple-element.13), kind=kLoop, calls=%fused_computation | loop fusion | flops 196608 | bytes 393216 | tf_op jit(solution)/shard_map/concatenate | solution.py:237
  33.8 1.9 %collective-permute-start.4 = (bf16[3,2,128,128]{3,2,1,0:T(8,128)(2,1)S(1)}, bf16[3,2,128,128]{3,2,1,0:T(8,128)(2,1)S(1)}, u32[]{:S(2)}, u32[]{:S(2)}) collective-permute-start(bf16[3,2,128,128]{3,2,1,0:T(8,128)(2,1)S(1)} %pad_maximum_fusion), channel_id=1, source_target_pairs={{64,0},{68,4},{72,8},{76,12},{80,16},{84,20},{88,24},{92,28},{96,3... | collective-permute-start | bytes 589832 | tf_op jit(solution)/shard_map/ppermute | solution.py:236
  36.4 0.8 %dynamic_slice.3 = f32[32,32]{1,0:T(8,128)S(1)} dynamic-slice(f32[128,128]{1,0:T(8,128)} %get-tuple-element.9.gram_ref, s32[]{:T(128)S(6)} %select_n.4, s32[]{:T(128)S(6)} %select_n.4), dynamic_slice_sizes={32,32} | dynamic-slice | bytes 8196 | tf_op jit(solution)/shard_map/dynamic_slice | solution.py:225
  37.2 0.7 reshape.13
  37.9 4.2 %all-to-all-start.1 = ((f32[4,1,1024]{2,1,0:T(1,128)}), f32[4,1,1024]{2,1,0:T(1,128)S(1)}, u32[]{:S(2)}, u32[]{:S(2)}) async-start(f32[4,1,1024]{2,1,0:T(1,128)} %reshape.13), calls=%async_computation.1 | async-start | bytes 32768 | tf_op jit(solution)/shard_map/all_to_all | solution.py:226
  42.1 0.0 collective-permute-done.5.fup_ref
  42.1 5.6 %collective-permute-done.4.fdn_ref = bf16[3,2,128,128]{3,2,1,0:T(8,128)(2,1)S(1)} collective-permute-done((bf16[3,2,128,128]{3,2,1,0:T(8,128)(2,1)S(1)}, bf16[3,2,128,128]{3,2,1,0:T(8,128)(2,1)S(1)}, u32[]{:S(2)}, u32[]{:S(2)}) %collective-permute-start.4) | collective-permute-done | bytes 196640 | tf_op jit(solution)/shard_map/ppermute | solution.py:236
  47.7 0.7 copy-done.4
  48.3 2.7 %shard_map.86 = f32[4,64,1152]{2,1,0:T(8,128)} custom-call(s32[1]{0:T(128)S(6)} %copy.9.owner_ref, f32[128,128]{1,0:T(8,128)} %get-tuple-element.9.gram_ref, bf16[8,2,128,128]{3,2,1,0:T(8,128)(2,1)} %get-tuple-element.10.own_ref, bf16[3,2,128,128]{3,2,1,0:T(8,128)(2,1)} %copy-done.1, bf16[3,2,128,128]{3,2,1,0:T(8,128)(2,1)} %copy-done.2, ...), custom_call_target="tpu_custom_call" | custom-call | tf_op jit(solution)/shard_map/pallas_call | solution.py:190
  51.0 0.0 all-to-all-done.1
  51.1 4.2 %all-to-all-start = ((f32[4,64,1152]{2,1,0:T(8,128)}), f32[4,64,1152]{2,1,0:T(8,128)S(1)}, u32[]{:S(2)}, u32[]{:S(2)}) async-start(f32[4,64,1152]{2,1,0:T(8,128)} %shard_map.86), calls=%async_computation | async-start | bytes 2359296 | tf_op jit(solution)/shard_map/all_to_all | solution.py:250
  55.2 0.5 broadcast.1
  55.7 0.7 reduce
  56.4 0.7 reshape.14.blocks_ref
  57.2 4.2 %shard_map.87.inverse_ref = f32[32,32]{1,0:T(8,128)} custom-call(f32[4,32,32]{2,1,0:T(8,128)} %reshape.14.blocks_ref), custom_call_target="tpu_custom_call" | custom-call | tf_op jit(solution)/shard_map/pallas_call | solution.py:122
  61.4 10.0 %all-to-all-done.pieces_ref = f32[4,64,1152]{2,1,0:T(8,128)S(1)} async-done(((f32[4,64,1152]{2,1,0:T(8,128)}), f32[4,64,1152]{2,1,0:T(8,128)S(1)}, u32[]{:S(2)}, u32[]{:S(2)}) %all-to-all-start) | async-done | bytes 1179680 | tf_op jit(solution)/shard_map/all_to_all | solution.py:250
  71.4 1.1 %copy-done = f32[4,64,1152]{2,1,0:T(8,128)} copy-done((f32[4,64,1152]{2,1,0:T(8,128)}, f32[4,64,1152]{2,1,0:T(8,128)S(1)}, u32[]{:S(2)}) %copy-start) | copy-done | bytes 1179672
  72.4 2.7 %shard_map.88 = (f32[32,128]{1,0:T(8,128)}, f32[32,1024]{1,0:T(8,128)}, f32[32,32]{1,0:T(8,128)}) custom-call(s32[1]{0:T(128)S(6)} %copy.9.owner_ref, f32[4,64,1152]{2,1,0:T(8,128)} %copy-done, f32[32,32]{1,0:T(8,128)} %shard_map.87.inverse_ref), custom_call_target="tpu_custom_call" | custom-call | tf_op jit(solution)/shard_map/pallas_call | solution.py:152
  (15 shorter events, 0.1 us)
Async XLA Ops:
  2.2 5.7 %collective-permute-start = (bf16[3,128,128]{2,1,0:T(8,128)(2,1)S(1)}, bf16[3,128,128]{2,1,0:T(8,128)(2,1)S(1)}, u32[]{:S(2)}, u32[]{:S(2)}) collective-permute-start(bf16[3,128,128]{2,1,0:T(8,128)(2,1)S(1)} %pad_maximum_fusion.2), channel_id=1, source_target_pairs={{0,1},{1,2},{2,3},{4,5},{5,6},{6,7},{8,9},{9,10},{10,11},{12,13},{... | collective-permute-start | bytes 294920 | tf_op jit(solution)/shard_map/ppermute | solution.py:26
  5.7 6.5 %collective-permute-start.1 = (bf16[3,128,128]{2,1,0:T(8,128)(2,1)S(1)}, bf16[3,128,128]{2,1,0:T(8,128)(2,1)S(1)}, u32[]{:S(2)}, u32[]{:S(2)}) collective-permute-start(bf16[3,128,128]{2,1,0:T(8,128)(2,1)S(1)} %pad_maximum_fusion.2), channel_id=1, source_target_pairs={{1,0},{2,1},{3,2},{5,4},{6,5},{7,6},{9,8},{10,9},{11,10},{13,12},{... | collective-permute-start | bytes 294920 | tf_op jit(solution)/shard_map/ppermute | solution.py:26
  7.9 4.3 %copy-start.5 = (bf16[3,128,128]{2,1,0:T(8,128)(2,1)}, bf16[3,128,128]{2,1,0:T(8,128)(2,1)S(1)}, u32[]{:S(2)}) copy-start(bf16[3,128,128]{2,1,0:T(8,128)(2,1)S(1)} %collective-permute-done.fp_ref) | copy-start | bytes 294916
  12.2 0.6 copy-start.6
  16.5 5.4 %collective-permute-start.2 = (bf16[3,2,128,128]{3,2,1,0:T(8,128)(2,1)}, bf16[3,2,128,128]{3,2,1,0:T(8,128)(2,1)S(1)}, u32[]{:S(2)}, u32[]{:S(2)}) collective-permute-start(bf16[3,2,128,128]{3,2,1,0:T(8,128)(2,1)} %get-tuple-element.11), channel_id=1, source_target_pairs={{4,0},{8,4},{12,8},{16,12},{20,16},{24,20},{28,24},{32,28},{36,32}... | collective-permute-start | bytes 589832 | tf_op jit(solution)/shard_map/ppermute | solution.py:232
  18.4 7.2 %collective-permute-start.3 = (bf16[3,2,128,128]{3,2,1,0:T(8,128)(2,1)}, bf16[3,2,128,128]{3,2,1,0:T(8,128)(2,1)S(1)}, u32[]{:S(2)}, u32[]{:S(2)}) collective-permute-start(bf16[3,2,128,128]{3,2,1,0:T(8,128)(2,1)} %get-tuple-element.12), channel_id=1, source_target_pairs={{0,4},{4,8},{8,12},{12,16},{16,20},{20,24},{24,28},{28,32},{32,36}... | collective-permute-start | bytes 589832 | tf_op jit(solution)/shard_map/ppermute | solution.py:235
  21.9 25.8 %copy-start.1 = (bf16[3,2,128,128]{3,2,1,0:T(8,128)(2,1)}, bf16[3,2,128,128]{3,2,1,0:T(8,128)(2,1)S(1)}, u32[]{:S(2)}) copy-start(bf16[3,2,128,128]{3,2,1,0:T(8,128)(2,1)S(1)} %collective-permute-done.2.down_ref) | copy-start | bytes 589828
  25.6 22.1 %copy-start.2 = (bf16[3,2,128,128]{3,2,1,0:T(8,128)(2,1)}, bf16[3,2,128,128]{3,2,1,0:T(8,128)(2,1)S(1)}, u32[]{:S(2)}) copy-start(bf16[3,2,128,128]{3,2,1,0:T(8,128)(2,1)S(1)} %collective-permute-done.3.up_ref) | copy-start | bytes 589828
  26.6 15.5 %collective-permute-start.5 = (bf16[3,2,128,128]{3,2,1,0:T(8,128)(2,1)S(1)}, bf16[3,2,128,128]{3,2,1,0:T(8,128)(2,1)S(1)}, u32[]{:S(2)}, u32[]{:S(2)}) collective-permute-start(bf16[3,2,128,128]{3,2,1,0:T(8,128)(2,1)S(1)} %pad_maximum_fusion.1), channel_id=1, source_target_pairs={{0,64},{4,68},{8,72},{12,76},{16,80},{20,84},{24,88},{28,92},{32,9... | collective-permute-start | bytes 589832 | tf_op jit(solution)/shard_map/ppermute | solution.py:241
  33.8 13.8 %collective-permute-start.4 = (bf16[3,2,128,128]{3,2,1,0:T(8,128)(2,1)S(1)}, bf16[3,2,128,128]{3,2,1,0:T(8,128)(2,1)S(1)}, u32[]{:S(2)}, u32[]{:S(2)}) collective-permute-start(bf16[3,2,128,128]{3,2,1,0:T(8,128)(2,1)S(1)} %pad_maximum_fusion), channel_id=1, source_target_pairs={{64,0},{68,4},{72,8},{76,12},{80,16},{84,20},{88,24},{92,28},{96,3... | collective-permute-start | bytes 589832 | tf_op jit(solution)/shard_map/ppermute | solution.py:236
  37.9 13.1 %all-to-all-start.1 = ((f32[4,1,1024]{2,1,0:T(1,128)}), f32[4,1,1024]{2,1,0:T(1,128)S(1)}, u32[]{:S(2)}, u32[]{:S(2)}) async-start(f32[4,1,1024]{2,1,0:T(1,128)} %reshape.13), calls=%async_computation.1 | async-start | bytes 32768 | tf_op jit(solution)/shard_map/all_to_all | solution.py:226
  42.1 5.6 %copy-start.3 = (bf16[3,2,128,128]{3,2,1,0:T(8,128)(2,1)}, bf16[3,2,128,128]{3,2,1,0:T(8,128)(2,1)S(1)}, u32[]{:S(2)}) copy-start(bf16[3,2,128,128]{3,2,1,0:T(8,128)(2,1)S(1)} %collective-permute-done.5.fup_ref) | copy-start | bytes 589828
  47.7 0.7 copy-start.4
  51.1 20.3 %all-to-all-start = ((f32[4,64,1152]{2,1,0:T(8,128)}), f32[4,64,1152]{2,1,0:T(8,128)S(1)}, u32[]{:S(2)}, u32[]{:S(2)}) async-start(f32[4,64,1152]{2,1,0:T(8,128)} %shard_map.86), calls=%async_computation | async-start | bytes 2359296 | tf_op jit(solution)/shard_map/all_to_all | solution.py:250
  71.4 1.1 %copy-start = (f32[4,64,1152]{2,1,0:T(8,128)}, f32[4,64,1152]{2,1,0:T(8,128)S(1)}, u32[]{:S(2)}) copy-start(f32[4,64,1152]{2,1,0:T(8,128)S(1)} %all-to-all-done.pieces_ref) | copy-start | bytes 3538948

commit v15 on v10

--- a/solution.py
+++ b/solution.py
@@ -234,6 +234,7 @@
         down_out, "sub", [(t, t - 1) for t in range(1, sub_count)] + [(0, last)]
     )
     up = lax.ppermute(up_out, "sub", [(t, t + 1) for t in range(last)] + [(last, 0)])
+    down, up, pivot_parts = lax.optimization_barrier((down, up, pivot_parts))
     far_down = lax.ppermute(
         jnp.concatenate([near_down, down[:1], up[:1]]),
         "sub",

time: 75.8 us -> 83.1 us (1.096)
  the two profiles are of different devices: /device:TPU:194 before, /device:TPU:422 now
where the time goes in v15:
time: 83.1 us; the launch traced here: 82.3 us
  waiting for transfers between devices  30.6 us (37%)
  starting transfers between devices  19.5 us (23%)
  Pallas kernels  13.2 us (16%)
  blocking collectives  9.33 us (11%)
  local copies, waits for them, and re-layouts  6.62 us (8%)
  other arithmetic  1.68 us (2%)
  between operations  1.41 us (2%)
    all_to_all x1, waiting for transfers between devices, per_device(): pieces = lax.all_to_all(outgoing_rows, 'crow', 0, 0, tiled=True)  12.8 us
    ppermute x1, waiting for transfers between devices, per_device(): lax.ppermute(jnp.concatenate([near_up, down[2:], up[2:]]), 'sub', [(u, u...  10.1 us
    all_to_all x1, blocking collectives, per_device(): lax.all_to_all(jnp.broadcast_to(pivot_part[None], (crow_count, row_share,...  9.33 us
    ppermute x2, starting transfers between devices, shifted(): lax.ppermute(value, axis, [(source, source + steps) for source in range(i...  4.78 us
    ppermute x1, starting transfers between devices, per_device(): lax.ppermute(jnp.concatenate([near_down, down[:1], up[:1]]), 'sub', [(u,...  4.57 us
    ppermute x2, waiting for transfers between devices, shifted(): lax.ppermute(value, axis, [(source, source + steps) for source in range(i...  4.51 us
    pallas_call x1, Pallas kernels, pivot_inverse(): pl.pallas_call(pivot_inverse_kernel, out_shape=jax.ShapeDtypeStruct((shar...  4.23 us
    unnamed x18, local copies, waits for them, and re-layouts  3.74 us
  transfers between devices with their start and end apart: 7, of which 4 were waited for; matrix products, arithmetic and copies ran while one was open for 3% of the time, Pallas kernels for 5%

profile of v15, /device:TPU:422, one launch (start us, length us, event | category | flops | bytes accessed | tf_op | source)
XLA Modules:
  0.0 82.3 jit_solution(15379341054540488408)
XLA Ops:
  0.6 0.8 slice_bitcast_fusion.1
  1.4 0.8 slice_bitcast_fusion
  2.2 3.5 %collective-permute-start = (bf16[2,128,128]{2,1,0:T(8,128)(2,1)S(1)}, bf16[2,128,128]{2,1,0:T(8,128)(2,1)S(1)}, u32[]{:S(2)}, u32[]{:S(2)}) collective-permute-start(bf16[2,128,128]{2,1,0:T(8,128)(2,1)S(1)} %pad_maximum_fusion.2), channel_id=1, source_target_pairs={{0,1},{1,2},{2,3},{4,5},{5,6},{6,7},{8,9},{9,10},{10,11},{12,13},{... | collective-permute-start | bytes 196616 | tf_op jit(solution)/shard_map/ppermute | solution.py:26
  5.7 1.3 %collective-permute-start.1 = (bf16[128,128]{1,0:T(8,128)(2,1)S(1)}, bf16[128,128]{1,0:T(8,128)(2,1)S(1)}, u32[]{:S(2)}, u32[]{:S(2)}) collective-permute-start(bf16[128,128]{1,0:T(8,128)(2,1)S(1)} %get-tuple-element.19), channel_id=1, source_target_pairs={{1,0},{2,1},{3,2},{5,4},{6,5},{7,6},{9,8},{10,9},{11,10},{13,12},{... | collective-permute-start | bytes 98312 | tf_op jit(solution)/shard_map/ppermute | solution.py:26
  7.0 4.5 %collective-permute-done.1.zn_ref = bf16[128,128]{1,0:T(8,128)(2,1)S(1)} collective-permute-done((bf16[128,128]{1,0:T(8,128)(2,1)S(1)}, bf16[128,128]{1,0:T(8,128)(2,1)S(1)}, u32[]{:S(2)}, u32[]{:S(2)}) %collective-permute-start.1) | collective-permute-done | bytes 32800 | tf_op jit(solution)/shard_map/ppermute | solution.py:26
  11.5 0.0 collective-permute-done.fp_ref
  11.5 0.6 copy-done.7
  12.1 0.6 copy-done.5
  12.7 3.6 %shard_map.85 = (bf16[3,2,128,128]{3,2,1,0:T(8,128)(2,1)}, bf16[3,2,128,128]{3,2,1,0:T(8,128)(2,1)}, bf16[1,2,128,128]{3,2,1,0:T(8,128)(2,1)}, bf16[1,2,128,128]...) custom-call(s32[1,1,16]{2,1,0:T(1,128)} %blocks_ref.1, s32[1,8]{1,0:T(1,128)} %counts_ref.1, ...), custom_call_target="tpu_custom_call" | custom-call | tf_op jit(solution)/shard_map/pallas_call | solution.py:85
  16.3 2.0 %collective-permute-start.2 = (bf16[3,2,128,128]{3,2,1,0:T(8,128)(2,1)}, bf16[3,2,128,128]{3,2,1,0:T(8,128)(2,1)S(1)}, u32[]{:S(2)}, u32[]{:S(2)}) collective-permute-start(bf16[3,2,128,128]{3,2,1,0:T(8,128)(2,1)} %get-tuple-element.13), channel_id=1, source_target_pairs={{4,0},{8,4},{12,8},{16,12},{20,16},{24,20},{28,24},{32,28},{36,32}... | collective-permute-start | bytes 589832 | tf_op jit(solution)/shard_map/ppermute | solution.py:233
  18.4 2.4 %collective-permute-start.3 = (bf16[3,2,128,128]{3,2,1,0:T(8,128)(2,1)}, bf16[3,2,128,128]{3,2,1,0:T(8,128)(2,1)S(1)}, u32[]{:S(2)}, u32[]{:S(2)}) collective-permute-start(bf16[3,2,128,128]{3,2,1,0:T(8,128)(2,1)} %get-tuple-element.14), channel_id=1, source_target_pairs={{0,4},{4,8},{8,12},{12,16},{16,20},{20,24},{24,28},{28,32},{32,36}... | collective-permute-start | bytes 589832 | tf_op jit(solution)/shard_map/ppermute | solution.py:236
  21.5 0.8 dynamic_slice.3
  22.3 0.1 reshape.12
  22.4 9.3 %all_to_all.10 = f32[4,1,1024]{2,1,0:T(1,128)S(1)} all-to-all(f32[4,1,1024]{2,1,0:T(1,128)S(1)} %reshape.12), channel_id=1, replica_groups=mesh['sub'=128,'crow'=4] {'crow'}, dimensions={0} | all-to-all | bytes 32768 | tf_op jit(solution)/shard_map/all_to_all | solution.py:227
  31.7 0.5 broadcast.1
  32.2 0.7 reduce
  32.9 0.7 reshape.13.blocks_ref
  33.6 0.0 collective-permute-done.2.down_ref
  33.6 0.0 collective-permute-done.3.up_ref
  33.6 0.0 copy-start.2
  33.7 1.0 %pad_maximum_fusion = bf16[3,2,128,128]{3,2,1,0:T(8,128)(2,1)S(1)} fusion(bf16[1,2,128,128]{3,2,1,0:T(8,128)(2,1)S(1)} %get-tuple-element.25, bf16[1,2,128,128]{3,2,1,0:T(8,128)(2,1)S(1)} %get-tuple-element.22, bf16[1,2,128,128]{3,2,1,0:T(8,128)(2,1)} %get-tuple-element.17), kind=kLoop, calls=%fused_computation | loop fusion | flops 196608 | bytes 393216 | tf_op jit(solution)/shard_map/concatenate | solution.py:239
  34.6 4.6 %collective-permute-start.4 = (bf16[3,2,128,128]{3,2,1,0:T(8,128)(2,1)S(1)}, bf16[3,2,128,128]{3,2,1,0:T(8,128)(2,1)S(1)}, u32[]{:S(2)}, u32[]{:S(2)}) collective-permute-start(bf16[3,2,128,128]{3,2,1,0:T(8,128)(2,1)S(1)} %pad_maximum_fusion), channel_id=1, source_target_pairs={{64,0},{68,4},{72,8},{76,12},{80,16},{84,20},{88,24},{92,28},{96,3... | collective-permute-start | bytes 589832 | tf_op jit(solution)/shard_map/ppermute | solution.py:238
  39.3 2.2 %collective-permute-start.5 = (bf16[3,2,128,128]{3,2,1,0:T(8,128)(2,1)S(1)}, bf16[3,2,128,128]{3,2,1,0:T(8,128)(2,1)S(1)}, u32[]{:S(2)}, u32[]{:S(2)}) collective-permute-start(bf16[3,2,128,128]{3,2,1,0:T(8,128)(2,1)S(1)} %pad_maximum_fusion.1), channel_id=1, source_target_pairs={{0,64},{4,68},{8,72},{12,76},{16,80},{20,84},{24,88},{28,92},{32,9... | collective-permute-start | bytes 589832 | tf_op jit(solution)/shard_map/ppermute | solution.py:243
  41.4 3.2 %collective-permute-done.4.fdn_ref = bf16[3,2,128,128]{3,2,1,0:T(8,128)(2,1)S(1)} collective-permute-done((bf16[3,2,128,128]{3,2,1,0:T(8,128)(2,1)S(1)}, bf16[3,2,128,128]{3,2,1,0:T(8,128)(2,1)S(1)}, u32[]{:S(2)}, u32[]{:S(2)}) %collective-permute-start.4) | collective-permute-done | bytes 196640 | tf_op jit(solution)/shard_map/ppermute | solution.py:238
  44.7 10.1 %collective-permute-done.5.fup_ref = bf16[3,2,128,128]{3,2,1,0:T(8,128)(2,1)S(1)} collective-permute-done((bf16[3,2,128,128]{3,2,1,0:T(8,128)(2,1)S(1)}, bf16[3,2,128,128]{3,2,1,0:T(8,128)(2,1)S(1)}, u32[]{:S(2)}, u32[]{:S(2)}) %collective-permute-start.5) | collective-permute-done | bytes 196640 | tf_op jit(solution)/shard_map/ppermute | solution.py:243
  54.8 0.7 copy-done.4
  55.4 2.7 %shard_map.86 = f32[4,64,1152]{2,1,0:T(8,128)} custom-call(s32[1]{0:T(128)S(6)} %copy.9.owner_ref, f32[128,128]{1,0:T(8,128)} %get-tuple-element.11.gram_ref, bf16[8,2,128,128]{3,2,1,0:T(8,128)(2,1)} %get-tuple-element.12.own_ref, bf16[3,2,128,128]{3,2,1,0:T(8,128)(2,1)} %copy-done.1, bf16[3,2,128,128]{3,2,1,0:T(8,128)(2,1)} %copy-done.2, ...), custom_call_target="tpu_custom_call" | custom-call | tf_op jit(solution)/shard_map/pallas_call | solution.py:190
  58.1 3.5 %all-to-all-start.1 = ((f32[4,64,1152]{2,1,0:T(8,128)}), f32[4,64,1152]{2,1,0:T(8,128)S(1)}, u32[]{:S(2)}, u32[]{:S(2)}) async-start(f32[4,64,1152]{2,1,0:T(8,128)} %shard_map.86), calls=%async_computation.1 | async-start | bytes 2359296 | tf_op jit(solution)/shard_map/all_to_all | solution.py:252
  61.6 4.2 %shard_map.87.inverse_ref = f32[32,32]{1,0:T(8,128)} custom-call(f32[4,32,32]{2,1,0:T(8,128)} %reshape.13.blocks_ref), custom_call_target="tpu_custom_call" | custom-call | tf_op jit(solution)/shard_map/pallas_call | solution.py:122
  65.9 12.8 %all-to-all-done.1.pieces_ref = f32[4,64,1152]{2,1,0:T(8,128)S(1)} async-done(((f32[4,64,1152]{2,1,0:T(8,128)}), f32[4,64,1152]{2,1,0:T(8,128)S(1)}, u32[]{:S(2)}, u32[]{:S(2)}) %all-to-all-start.1) | async-done | bytes 1179680 | tf_op jit(solution)/shard_map/all_to_all | solution.py:252
  78.7 1.0 %copy-done = f32[4,64,1152]{2,1,0:T(8,128)} copy-done((f32[4,64,1152]{2,1,0:T(8,128)}, f32[4,64,1152]{2,1,0:T(8,128)S(1)}, u32[]{:S(2)}) %copy-start) | copy-done | bytes 1179672
  79.7 2.7 %shard_map.88 = (f32[32,128]{1,0:T(8,128)}, f32[32,1024]{1,0:T(8,128)}, f32[32,32]{1,0:T(8,128)}) custom-call(s32[1]{0:T(128)S(6)} %copy.9.owner_ref, f32[4,64,1152]{2,1,0:T(8,128)} %copy-done, f32[32,32]{1,0:T(8,128)} %shard_map.87.inverse_ref), custom_call_target="tpu_custom_call" | custom-call | tf_op jit(solution)/shard_map/pallas_call | solution.py:152
  (15 shorter events, 0.1 us)
Async XLA Ops:
  2.2 9.3 %collective-permute-start = (bf16[2,128,128]{2,1,0:T(8,128)(2,1)S(1)}, bf16[2,128,128]{2,1,0:T(8,128)(2,1)S(1)}, u32[]{:S(2)}, u32[]{:S(2)}) collective-permute-start(bf16[2,128,128]{2,1,0:T(8,128)(2,1)S(1)} %pad_maximum_fusion.2), channel_id=1, source_target_pairs={{0,1},{1,2},{2,3},{4,5},{5,6},{6,7},{8,9},{9,10},{10,11},{12,13},{... | collective-permute-start | bytes 196616 | tf_op jit(solution)/shard_map/ppermute | solution.py:26
  5.7 5.8 %collective-permute-start.1 = (bf16[128,128]{1,0:T(8,128)(2,1)S(1)}, bf16[128,128]{1,0:T(8,128)(2,1)S(1)}, u32[]{:S(2)}, u32[]{:S(2)}) collective-permute-start(bf16[128,128]{1,0:T(8,128)(2,1)S(1)} %get-tuple-element.19), channel_id=1, source_target_pairs={{1,0},{2,1},{3,2},{5,4},{6,5},{7,6},{9,8},{10,9},{11,10},{13,12},{... | collective-permute-start | bytes 98312 | tf_op jit(solution)/shard_map/ppermute | solution.py:26
  11.5 0.6 copy-start.7
  12.1 0.6 copy-start.5
  16.3 22.9 %copy-start.6 = (bf16[1,2,128,128]{3,2,1,0:T(8,128)(2,1)S(1)}, bf16[1,2,128,128]{3,2,1,0:T(8,128)(2,1)}, u32[]{:S(2)}) copy-start(bf16[1,2,128,128]{3,2,1,0:T(8,128)(2,1)} %get-tuple-element.18) | copy-start | bytes 196612
  16.3 17.3 %collective-permute-start.2 = (bf16[3,2,128,128]{3,2,1,0:T(8,128)(2,1)}, bf16[3,2,128,128]{3,2,1,0:T(8,128)(2,1)S(1)}, u32[]{:S(2)}, u32[]{:S(2)}) collective-permute-start(bf16[3,2,128,128]{3,2,1,0:T(8,128)(2,1)} %get-tuple-element.13), channel_id=1, source_target_pairs={{4,0},{8,4},{12,8},{16,12},{20,16},{24,20},{28,24},{32,28},{36,32}... | collective-permute-start | bytes 589832 | tf_op jit(solution)/shard_map/ppermute | solution.py:233
  18.4 15.2 %collective-permute-start.3 = (bf16[3,2,128,128]{3,2,1,0:T(8,128)(2,1)}, bf16[3,2,128,128]{3,2,1,0:T(8,128)(2,1)S(1)}, u32[]{:S(2)}, u32[]{:S(2)}) collective-permute-start(bf16[3,2,128,128]{3,2,1,0:T(8,128)(2,1)} %get-tuple-element.14), channel_id=1, source_target_pairs={{0,4},{4,8},{8,12},{12,16},{16,20},{20,24},{24,28},{28,32},{32,36}... | collective-permute-start | bytes 589832 | tf_op jit(solution)/shard_map/ppermute | solution.py:236
  33.6 21.1 %copy-start.1 = (bf16[3,2,128,128]{3,2,1,0:T(8,128)(2,1)}, bf16[3,2,128,128]{3,2,1,0:T(8,128)(2,1)S(1)}, u32[]{:S(2)}) copy-start(bf16[3,2,128,128]{3,2,1,0:T(8,128)(2,1)S(1)} %collective-permute-done.2.down_ref) | copy-start | bytes 589828
  33.6 21.1 %copy-start.2 = (bf16[3,2,128,128]{3,2,1,0:T(8,128)(2,1)}, bf16[3,2,128,128]{3,2,1,0:T(8,128)(2,1)S(1)}, u32[]{:S(2)}) copy-start(bf16[3,2,128,128]{3,2,1,0:T(8,128)(2,1)S(1)} %collective-permute-done.3.up_ref) | copy-start | bytes 589828
  34.6 10.0 %collective-permute-start.4 = (bf16[3,2,128,128]{3,2,1,0:T(8,128)(2,1)S(1)}, bf16[3,2,128,128]{3,2,1,0:T(8,128)(2,1)S(1)}, u32[]{:S(2)}, u32[]{:S(2)}) collective-permute-start(bf16[3,2,128,128]{3,2,1,0:T(8,128)(2,1)S(1)} %pad_maximum_fusion), channel_id=1, source_target_pairs={{64,0},{68,4},{72,8},{76,12},{80,16},{84,20},{88,24},{92,28},{96,3... | collective-permute-start | bytes 589832 | tf_op jit(solution)/shard_map/ppermute | solution.py:238
  39.3 15.5 %collective-permute-start.5 = (bf16[3,2,128,128]{3,2,1,0:T(8,128)(2,1)S(1)}, bf16[3,2,128,128]{3,2,1,0:T(8,128)(2,1)S(1)}, u32[]{:S(2)}, u32[]{:S(2)}) collective-permute-start(bf16[3,2,128,128]{3,2,1,0:T(8,128)(2,1)S(1)} %pad_maximum_fusion.1), channel_id=1, source_target_pairs={{0,64},{4,68},{8,72},{12,76},{16,80},{20,84},{24,88},{28,92},{32,9... | collective-permute-start | bytes 589832 | tf_op jit(solution)/shard_map/ppermute | solution.py:243
  44.7 10.1 %copy-start.3 = (bf16[3,2,128,128]{3,2,1,0:T(8,128)(2,1)}, bf16[3,2,128,128]{3,2,1,0:T(8,128)(2,1)S(1)}, u32[]{:S(2)}) copy-start(bf16[3,2,128,128]{3,2,1,0:T(8,128)(2,1)S(1)} %collective-permute-done.4.fdn_ref) | copy-start | bytes 589828
  54.7 0.7 copy-start.4
  58.1 20.6 %all-to-all-start.1 = ((f32[4,64,1152]{2,1,0:T(8,128)}), f32[4,64,1152]{2,1,0:T(8,128)S(1)}, u32[]{:S(2)}, u32[]{:S(2)}) async-start(f32[4,64,1152]{2,1,0:T(8,128)} %shard_map.86), calls=%async_computation.1 | async-start | bytes 2359296 | tf_op jit(solution)/shard_map/all_to_all | solution.py:252
  78.7 1.0 %copy-start = (f32[4,64,1152]{2,1,0:T(8,128)}, f32[4,64,1152]{2,1,0:T(8,128)S(1)}, u32[]{:S(2)}) copy-start(f32[4,64,1152]{2,1,0:T(8,128)S(1)} %all-to-all-done.1.pieces_ref) | copy-start | bytes 3538948

commit v16 on v10

--- a/solution.py
+++ b/solution.py
@@ -59,8 +59,11 @@
         lower = fp_ref[1] if b == 0 else u_ref[0, b - 1]
         above = zn_ref[...] if b == count - 1 else rows_of(b + 1)
         total = (_ab(d_ref[0, b], rows_of(b)) + _ab(u_ref[0, b], above)) + _atb(lower, below)
-        app_ref[pl.ds(b * rows, rows), :] = total.astype(app_ref.dtype)
-    gram_ref[...] = _atb(z_ref[0], app_ref[...])
+        app = total.astype(app_ref.dtype)
+        app_ref[pl.ds(b * rows, rows), :] = app
+        part = _atb(rows_of(b), app)
+        gram = part if b == 0 else gram + part
+    gram_ref[...] = gram
     for slot in range(own_ref.shape[0]):
         for unit in range(per_slot):
             start = pl.multiple_of(blocks_ref[0, 0, slot * per_slot + unit] * rows, rows)

time: 75.8 us -> 76.7 us (1.012)
  Pallas kernels: 13.2 us -> 14.1 us
    pallas_call x1, Pallas kernels: 3.61 us -> 4.51 us  [local_apply(): pl.pallas_call(functools.partial(local_apply_kernel, groups), out_shape=t...]
where the time goes in v16:
time: 76.7 us; the launch traced here: 75.8 us
  starting transfers between devices  25.7 us (34%)
  waiting for transfers between devices  24.8 us (32%)
  Pallas kernels  14.1 us (18%)
  local copies, waits for them, and re-layouts  7.27 us (9%)
  other arithmetic  2.5 us (3%)
  between operations  1.37 us (2%)
    all_to_all x1, waiting for transfers between devices, per_device(): pieces = lax.all_to_all(outgoing_rows, 'crow', 0, 0, tiled=True)  9.98 us
    ppermute x1, starting transfers between devices, per_device(): lax.ppermute(jnp.concatenate([near_up, down[2:], up[2:]]), 'sub', [(u, u...  6.39 us
    ppermute x1, waiting for transfers between devices, per_device(): lax.ppermute(jnp.concatenate([near_down, down[:1], up[:1]]), 'sub', [(u,...  5.57 us
    ppermute x2, starting transfers between devices, shifted(): lax.ppermute(value, axis, [(source, source + steps) for source in range(i...  4.78 us
    pallas_call x1, Pallas kernels, local_apply(): pl.pallas_call(functools.partial(local_apply_kernel, groups), out_shape=t...  4.51 us
    ppermute x2, waiting for transfers between devices, shifted(): lax.ppermute(value, axis, [(source, source + steps) for source in range(i...  4.51 us
    unnamed x16, local copies, waits for them, and re-layouts  4.39 us
    pallas_call x1, Pallas kernels, pivot_inverse(): pl.pallas_call(pivot_inverse_kernel, out_shape=jax.ShapeDtypeStruct((shar...  4.24 us
  transfers between devices with their start and end apart: 8, of which 5 were waited for; matrix products, arithmetic and copies ran while one was open for 6% of the time, Pallas kernels for 9%

profile of v16, /device:TPU:194, one launch (start us, length us, event | category | flops | bytes accessed | tf_op | source)
XLA Modules:
  0.0 75.8 jit_solution(7180149898926475944)
XLA Ops:
  0.6 0.8 %slice_bitcast_fusion = (bf16[128,128]{1,0:T(8,128)(2,1)S(1)}, bf16[1,128,128]{2,1,0:T(8,128)(2,1)S(1)}) fusion(bf16[1,3072,128]{2,1,0:T(8,128)(2,1)} %z_ref.1), kind=kLoop, calls=%fused_computation.3 | loop fusion | bytes 131072 | tf_op jit(solution)/shard_map/slice | solution.py:216
  1.4 0.8 %slice_bitcast_fusion.1 = bf16[1,128,128]{2,1,0:T(8,128)(2,1)S(1)} fusion(bf16[1,24,128,128]{3,2,1,0:T(8,128)(2,1)} %u_ref.1), kind=kLoop, calls=%fused_computation.4 | loop fusion | bytes 65536 | tf_op jit(solution)/shard_map/stack;squeeze | solution.py:214
  2.2 3.5 %collective-permute-start = (bf16[2,128,128]{2,1,0:T(8,128)(2,1)S(1)}, bf16[2,128,128]{2,1,0:T(8,128)(2,1)S(1)}, u32[]{:S(2)}, u32[]{:S(2)}) collective-permute-start(bf16[2,128,128]{2,1,0:T(8,128)(2,1)S(1)} %pad_maximum_fusion.2), channel_id=1, source_target_pairs={{0,1},{1,2},{2,3},{4,5},{5,6},{6,7},{8,9},{9,10},{10,11},{12,13},{... | collective-permute-start | bytes 196616 | tf_op jit(solution)/shard_map/ppermute | solution.py:26
  5.7 1.3 %collective-permute-start.1 = (bf16[128,128]{1,0:T(8,128)(2,1)S(1)}, bf16[128,128]{1,0:T(8,128)(2,1)S(1)}, u32[]{:S(2)}, u32[]{:S(2)}) collective-permute-start(bf16[128,128]{1,0:T(8,128)(2,1)S(1)} %get-tuple-element.15), channel_id=1, source_target_pairs={{1,0},{2,1},{3,2},{5,4},{6,5},{7,6},{9,8},{10,9},{11,10},{13,12},{... | collective-permute-start | bytes 98312 | tf_op jit(solution)/shard_map/ppermute | solution.py:26
  7.0 4.5 %collective-permute-done.1.zn_ref = bf16[128,128]{1,0:T(8,128)(2,1)S(1)} collective-permute-done((bf16[128,128]{1,0:T(8,128)(2,1)S(1)}, bf16[128,128]{1,0:T(8,128)(2,1)S(1)}, u32[]{:S(2)}, u32[]{:S(2)}) %collective-permute-start.1) | collective-permute-done | bytes 32800 | tf_op jit(solution)/shard_map/ppermute | solution.py:26
  11.5 0.0 collective-permute-done.fp_ref
  11.5 0.6 copy-done.6
  12.1 0.6 copy-done.5
  12.7 4.5 %shard_map.85 = (bf16[3,2,128,128]{3,2,1,0:T(8,128)(2,1)}, bf16[3,2,128,128]{3,2,1,0:T(8,128)(2,1)}, bf16[1,2,128,128]{3,2,1,0:T(8,128)(2,1)}, bf16[1,2,128,128]...) custom-call(s32[1,1,16]{2,1,0:T(1,128)} %blocks_ref.1, s32[1,8]{1,0:T(1,128)} %counts_ref.1, ...), custom_call_target="tpu_custom_call" | custom-call | tf_op jit(solution)/shard_map/pallas_call | solution.py:88
  17.2 1.9 %collective-permute-start.2 = (bf16[3,2,128,128]{3,2,1,0:T(8,128)(2,1)}, bf16[3,2,128,128]{3,2,1,0:T(8,128)(2,1)S(1)}, u32[]{:S(2)}, u32[]{:S(2)}) collective-permute-start(bf16[3,2,128,128]{3,2,1,0:T(8,128)(2,1)} %get-tuple-element.11), channel_id=1, source_target_pairs={{4,0},{8,4},{12,8},{16,12},{20,16},{24,20},{28,24},{32,28},{36,32}... | collective-permute-start | bytes 589832 | tf_op jit(solution)/shard_map/ppermute | solution.py:236
  19.2 2.4 %collective-permute-start.3 = (bf16[3,2,128,128]{3,2,1,0:T(8,128)(2,1)}, bf16[3,2,128,128]{3,2,1,0:T(8,128)(2,1)S(1)}, u32[]{:S(2)}, u32[]{:S(2)}) collective-permute-start(bf16[3,2,128,128]{3,2,1,0:T(8,128)(2,1)} %get-tuple-element.12), channel_id=1, source_target_pairs={{0,4},{4,8},{8,12},{12,16},{16,20},{20,24},{24,28},{28,32},{32,36}... | collective-permute-start | bytes 589832 | tf_op jit(solution)/shard_map/ppermute | solution.py:239
  21.6 1.1 %collective-permute-done.2.down_ref = bf16[3,2,128,128]{3,2,1,0:T(8,128)(2,1)S(1)} collective-permute-done((bf16[3,2,128,128]{3,2,1,0:T(8,128)(2,1)}, bf16[3,2,128,128]{3,2,1,0:T(8,128)(2,1)S(1)}, u32[]{:S(2)}, u32[]{:S(2)}) %collective-permute-start.2) | collective-permute-done | bytes 196640 | tf_op jit(solution)/shard_map/ppermute | solution.py:236
  22.7 3.7 %collective-permute-done.3.up_ref = bf16[3,2,128,128]{3,2,1,0:T(8,128)(2,1)S(1)} collective-permute-done((bf16[3,2,128,128]{3,2,1,0:T(8,128)(2,1)}, bf16[3,2,128,128]{3,2,1,0:T(8,128)(2,1)S(1)}, u32[]{:S(2)}, u32[]{:S(2)}) %collective-permute-start.3) | collective-permute-done | bytes 196640 | tf_op jit(solution)/shard_map/ppermute | solution.py:239
  26.4 0.9 %pad_maximum_fusion.1 = bf16[3,2,128,128]{3,2,1,0:T(8,128)(2,1)S(1)} fusion(bf16[1,2,128,128]{3,2,1,0:T(8,128)(2,1)S(1)} %get-tuple-element.19, bf16[1,2,128,128]{3,2,1,0:T(8,128)(2,1)S(1)} %get-tuple-element.17, bf16[1,2,128,128]{3,2,1,0:T(8,128)(2,1)} %get-tuple-element.14), kind=kLoop, calls=%fused_computation.1 | loop fusion | flops 196608 | bytes 393216 | tf_op jit(solution)/shard_map/concatenate | solution.py:246
  27.3 6.4 %collective-permute-start.5 = (bf16[3,2,128,128]{3,2,1,0:T(8,128)(2,1)S(1)}, bf16[3,2,128,128]{3,2,1,0:T(8,128)(2,1)S(1)}, u32[]{:S(2)}, u32[]{:S(2)}) collective-permute-start(bf16[3,2,128,128]{3,2,1,0:T(8,128)(2,1)S(1)} %pad_maximum_fusion.1), channel_id=1, source_target_pairs={{0,64},{4,68},{8,72},{12,76},{16,80},{20,84},{24,88},{28,92},{32,9... | collective-permute-start | bytes 589832 | tf_op jit(solution)/shard_map/ppermute | solution.py:245
  33.7 0.9 %pad_maximum_fusion = bf16[3,2,128,128]{3,2,1,0:T(8,128)(2,1)S(1)} fusion(bf16[1,2,128,128]{3,2,1,0:T(8,128)(2,1)S(1)} %get-tuple-element.20, bf16[1,2,128,128]{3,2,1,0:T(8,128)(2,1)S(1)} %get-tuple-element.18, bf16[1,2,128,128]{3,2,1,0:T(8,128)(2,1)} %get-tuple-element.13), kind=kLoop, calls=%fused_computation | loop fusion | flops 196608 | bytes 393216 | tf_op jit(solution)/shard_map/concatenate | solution.py:241
  34.6 1.9 %collective-permute-start.4 = (bf16[3,2,128,128]{3,2,1,0:T(8,128)(2,1)S(1)}, bf16[3,2,128,128]{3,2,1,0:T(8,128)(2,1)S(1)}, u32[]{:S(2)}, u32[]{:S(2)}) collective-permute-start(bf16[3,2,128,128]{3,2,1,0:T(8,128)(2,1)S(1)} %pad_maximum_fusion), channel_id=1, source_target_pairs={{64,0},{68,4},{72,8},{76,12},{80,16},{84,20},{88,24},{92,28},{96,3... | collective-permute-start | bytes 589832 | tf_op jit(solution)/shard_map/ppermute | solution.py:240
  37.2 0.8 %dynamic_slice.3 = f32[32,32]{1,0:T(8,128)S(1)} dynamic-slice(f32[128,128]{1,0:T(8,128)} %get-tuple-element.9.gram_ref, s32[]{:T(128)S(6)} %select_n.4, s32[]{:T(128)S(6)} %select_n.4), dynamic_slice_sizes={32,32} | dynamic-slice | bytes 8196 | tf_op jit(solution)/shard_map/dynamic_slice | solution.py:229
  38.0 0.7 reshape.12
  38.7 4.2 %all-to-all-start.1 = ((f32[4,1,1024]{2,1,0:T(1,128)}), f32[4,1,1024]{2,1,0:T(1,128)S(1)}, u32[]{:S(2)}, u32[]{:S(2)}) async-start(f32[4,1,1024]{2,1,0:T(1,128)} %reshape.12), calls=%async_computation.1 | async-start | bytes 32768 | tf_op jit(solution)/shard_map/all_to_all | solution.py:230
  42.8 0.0 collective-permute-done.5.fup_ref
  42.8 5.6 %collective-permute-done.4.fdn_ref = bf16[3,2,128,128]{3,2,1,0:T(8,128)(2,1)S(1)} collective-permute-done((bf16[3,2,128,128]{3,2,1,0:T(8,128)(2,1)S(1)}, bf16[3,2,128,128]{3,2,1,0:T(8,128)(2,1)S(1)}, u32[]{:S(2)}, u32[]{:S(2)}) %collective-permute-start.4) | collective-permute-done | bytes 196640 | tf_op jit(solution)/shard_map/ppermute | solution.py:240
  48.4 0.7 copy-done.4
  49.1 2.7 %shard_map.86 = f32[4,64,1152]{2,1,0:T(8,128)} custom-call(s32[1]{0:T(128)S(6)} %copy.9.owner_ref, f32[128,128]{1,0:T(8,128)} %get-tuple-element.9.gram_ref, bf16[8,2,128,128]{3,2,1,0:T(8,128)(2,1)} %get-tuple-element.10.own_ref, bf16[3,2,128,128]{3,2,1,0:T(8,128)(2,1)} %copy-done.1, bf16[3,2,128,128]{3,2,1,0:T(8,128)(2,1)} %copy-done.2, ...), custom_call_target="tpu_custom_call" | custom-call | tf_op jit(solution)/shard_map/pallas_call | solution.py:193
  51.8 4.2 %all-to-all-start = ((f32[4,64,1152]{2,1,0:T(8,128)}), f32[4,64,1152]{2,1,0:T(8,128)S(1)}, u32[]{:S(2)}, u32[]{:S(2)}) async-start(f32[4,64,1152]{2,1,0:T(8,128)} %shard_map.86), calls=%async_computation | async-start | bytes 2359296 | tf_op jit(solution)/shard_map/all_to_all | solution.py:254
  56.0 0.5 broadcast.1
  56.5 0.7 reduce
  57.2 0.7 reshape.13.blocks_ref
  57.9 4.2 %shard_map.87.inverse_ref = f32[32,32]{1,0:T(8,128)} custom-call(f32[4,32,32]{2,1,0:T(8,128)} %reshape.13.blocks_ref), custom_call_target="tpu_custom_call" | custom-call | tf_op jit(solution)/shard_map/pallas_call | solution.py:125
  62.1 10.0 %all-to-all-done.pieces_ref = f32[4,64,1152]{2,1,0:T(8,128)S(1)} async-done(((f32[4,64,1152]{2,1,0:T(8,128)}), f32[4,64,1152]{2,1,0:T(8,128)S(1)}, u32[]{:S(2)}, u32[]{:S(2)}) %all-to-all-start) | async-done | bytes 1179680 | tf_op jit(solution)/shard_map/all_to_all | solution.py:254
  72.1 1.1 %copy-done = f32[4,64,1152]{2,1,0:T(8,128)} copy-done((f32[4,64,1152]{2,1,0:T(8,128)}, f32[4,64,1152]{2,1,0:T(8,128)S(1)}, u32[]{:S(2)}) %copy-start) | copy-done | bytes 1179672
  73.2 2.7 %shard_map.88 = (f32[32,128]{1,0:T(8,128)}, f32[32,1024]{1,0:T(8,128)}, f32[32,32]{1,0:T(8,128)}) custom-call(s32[1]{0:T(128)S(6)} %copy.9.owner_ref, f32[4,64,1152]{2,1,0:T(8,128)} %copy-done, f32[32,32]{1,0:T(8,128)} %shard_map.87.inverse_ref), custom_call_target="tpu_custom_call" | custom-call | tf_op jit(solution)/shard_map/pallas_call | solution.py:155
  (15 shorter events, 0.1 us)
Async XLA Ops:
  2.2 9.3 %collective-permute-start = (bf16[2,128,128]{2,1,0:T(8,128)(2,1)S(1)}, bf16[2,128,128]{2,1,0:T(8,128)(2,1)S(1)}, u32[]{:S(2)}, u32[]{:S(2)}) collective-permute-start(bf16[2,128,128]{2,1,0:T(8,128)(2,1)S(1)} %pad_maximum_fusion.2), channel_id=1, source_target_pairs={{0,1},{1,2},{2,3},{4,5},{5,6},{6,7},{8,9},{9,10},{10,11},{12,13},{... | collective-permute-start | bytes 196616 | tf_op jit(solution)/shard_map/ppermute | solution.py:26
  5.7 5.8 %collective-permute-start.1 = (bf16[128,128]{1,0:T(8,128)(2,1)S(1)}, bf16[128,128]{1,0:T(8,128)(2,1)S(1)}, u32[]{:S(2)}, u32[]{:S(2)}) collective-permute-start(bf16[128,128]{1,0:T(8,128)(2,1)S(1)} %get-tuple-element.15), channel_id=1, source_target_pairs={{1,0},{2,1},{3,2},{5,4},{6,5},{7,6},{9,8},{10,9},{11,10},{13,12},{... | collective-permute-start | bytes 98312 | tf_op jit(solution)/shard_map/ppermute | solution.py:26
  11.5 0.6 copy-start.6
  12.1 0.6 copy-start.5
  17.2 5.4 %collective-permute-start.2 = (bf16[3,2,128,128]{3,2,1,0:T(8,128)(2,1)}, bf16[3,2,128,128]{3,2,1,0:T(8,128)(2,1)S(1)}, u32[]{:S(2)}, u32[]{:S(2)}) collective-permute-start(bf16[3,2,128,128]{3,2,1,0:T(8,128)(2,1)} %get-tuple-element.11), channel_id=1, source_target_pairs={{4,0},{8,4},{12,8},{16,12},{20,16},{24,20},{28,24},{32,28},{36,32}... | collective-permute-start | bytes 589832 | tf_op jit(solution)/shard_map/ppermute | solution.py:236
  19.2 7.2 %collective-permute-start.3 = (bf16[3,2,128,128]{3,2,1,0:T(8,128)(2,1)}, bf16[3,2,128,128]{3,2,1,0:T(8,128)(2,1)S(1)}, u32[]{:S(2)}, u32[]{:S(2)}) collective-permute-start(bf16[3,2,128,128]{3,2,1,0:T(8,128)(2,1)} %get-tuple-element.12), channel_id=1, source_target_pairs={{0,4},{4,8},{8,12},{12,16},{16,20},{20,24},{24,28},{28,32},{32,36}... | collective-permute-start | bytes 589832 | tf_op jit(solution)/shard_map/ppermute | solution.py:239
  22.6 25.8 %copy-start.1 = (bf16[3,2,128,128]{3,2,1,0:T(8,128)(2,1)}, bf16[3,2,128,128]{3,2,1,0:T(8,128)(2,1)S(1)}, u32[]{:S(2)}) copy-start(bf16[3,2,128,128]{3,2,1,0:T(8,128)(2,1)S(1)} %collective-permute-done.2.down_ref) | copy-start | bytes 589828
  26.4 22.1 %copy-start.2 = (bf16[3,2,128,128]{3,2,1,0:T(8,128)(2,1)}, bf16[3,2,128,128]{3,2,1,0:T(8,128)(2,1)S(1)}, u32[]{:S(2)}) copy-start(bf16[3,2,128,128]{3,2,1,0:T(8,128)(2,1)S(1)} %collective-permute-done.3.up_ref) | copy-start | bytes 589828
  27.3 15.5 %collective-permute-start.5 = (bf16[3,2,128,128]{3,2,1,0:T(8,128)(2,1)S(1)}, bf16[3,2,128,128]{3,2,1,0:T(8,128)(2,1)S(1)}, u32[]{:S(2)}, u32[]{:S(2)}) collective-permute-start(bf16[3,2,128,128]{3,2,1,0:T(8,128)(2,1)S(1)} %pad_maximum_fusion.1), channel_id=1, source_target_pairs={{0,64},{4,68},{8,72},{12,76},{16,80},{20,84},{24,88},{28,92},{32,9... | collective-permute-start | bytes 589832 | tf_op jit(solution)/shard_map/ppermute | solution.py:245
  34.6 13.8 %collective-permute-start.4 = (bf16[3,2,128,128]{3,2,1,0:T(8,128)(2,1)S(1)}, bf16[3,2,128,128]{3,2,1,0:T(8,128)(2,1)S(1)}, u32[]{:S(2)}, u32[]{:S(2)}) collective-permute-start(bf16[3,2,128,128]{3,2,1,0:T(8,128)(2,1)S(1)} %pad_maximum_fusion), channel_id=1, source_target_pairs={{64,0},{68,4},{72,8},{76,12},{80,16},{84,20},{88,24},{92,28},{96,3... | collective-permute-start | bytes 589832 | tf_op jit(solution)/shard_map/ppermute | solution.py:240
  38.7 13.1 %all-to-all-start.1 = ((f32[4,1,1024]{2,1,0:T(1,128)}), f32[4,1,1024]{2,1,0:T(1,128)S(1)}, u32[]{:S(2)}, u32[]{:S(2)}) async-start(f32[4,1,1024]{2,1,0:T(1,128)} %reshape.12), calls=%async_computation.1 | async-start | bytes 32768 | tf_op jit(solution)/shard_map/all_to_all | solution.py:230
  42.8 5.6 %copy-start.3 = (bf16[3,2,128,128]{3,2,1,0:T(8,128)(2,1)}, bf16[3,2,128,128]{3,2,1,0:T(8,128)(2,1)S(1)}, u32[]{:S(2)}) copy-start(bf16[3,2,128,128]{3,2,1,0:T(8,128)(2,1)S(1)} %collective-permute-done.5.fup_ref) | copy-start | bytes 589828
  48.4 0.7 copy-start.4
  51.8 20.3 %all-to-all-start = ((f32[4,64,1152]{2,1,0:T(8,128)}), f32[4,64,1152]{2,1,0:T(8,128)S(1)}, u32[]{:S(2)}, u32[]{:S(2)}) async-start(f32[4,64,1152]{2,1,0:T(8,128)} %shard_map.86), calls=%async_computation | async-start | bytes 2359296 | tf_op jit(solution)/shard_map/all_to_all | solution.py:254
  72.1 1.1 %copy-start = (f32[4,64,1152]{2,1,0:T(8,128)}, f32[4,64,1152]{2,1,0:T(8,128)S(1)}, u32[]{:S(2)}) copy-start(f32[4,64,1152]{2,1,0:T(8,128)S(1)} %all-to-all-done.pieces_ref) | copy-start | bytes 3538948

commit v17 on v10

--- a/solution.py
+++ b/solution.py
@@ -55,10 +55,14 @@
         return z_ref[0, pl.ds(b * rows, rows), :]
 
     for b in range(count):
-        below = fp_ref[0] if b == 0 else rows_of(b - 1)
-        lower = fp_ref[1] if b == 0 else u_ref[0, b - 1]
-        above = zn_ref[...] if b == count - 1 else rows_of(b + 1)
-        total = (_ab(d_ref[0, b], rows_of(b)) + _ab(u_ref[0, b], above)) + _atb(lower, below)
+        if 0 < b < count - 1:
+            left = jnp.concatenate([u_ref[0, b - 1].T, d_ref[0, b], u_ref[0, b]], 1)
+            total = _ab(left, z_ref[0, pl.ds((b - 1) * rows, 3 * rows), :])
+        else:
+            below = fp_ref[0] if b == 0 else rows_of(b - 1)
+            lower = fp_ref[1] if b == 0 else u_ref[0, b - 1]
+            above = zn_ref[...] if b == count - 1 else rows_of(b + 1)
+            total = (_ab(d_ref[0, b], rows_of(b)) + _ab(u_ref[0, b], above)) + _atb(lower, below)
         app_ref[pl.ds(b * rows, rows), :] = total.astype(app_ref.dtype)
     gram_ref[...] = _atb(z_ref[0], app_ref[...])
     for slot in range(own_ref.shape[0]):

time: 75.8 us -> 75.8 us (level)
  no operation moved by 1% of the time
where the time goes in v17:
time: 75.8 us; the launch traced here: 75 us
  starting transfers between devices  25.7 us (34%)
  waiting for transfers between devices  24.8 us (33%)
  Pallas kernels  13.2 us (17%)
  local copies, waits for them, and re-layouts  7.27 us (10%)
  other arithmetic  2.5 us (3%)
  between operations  1.37 us (2%)
    all_to_all x1, waiting for transfers between devices, per_device(): pieces = lax.all_to_all(outgoing_rows, 'crow', 0, 0, tiled=True)  9.98 us
    ppermute x1, starting transfers between devices, per_device(): lax.ppermute(jnp.concatenate([near_up, down[2:], up[2:]]), 'sub', [(u, u...  6.4 us
    ppermute x1, waiting for transfers between devices, per_device(): lax.ppermute(jnp.concatenate([near_down, down[:1], up[:1]]), 'sub', [(u,...  5.56 us
    ppermute x2, starting transfers between devices, shifted(): lax.ppermute(value, axis, [(source, source + steps) for source in range(i...  4.78 us
    ppermute x2, waiting for transfers between devices, shifted(): lax.ppermute(value, axis, [(source, source + steps) for source in range(i...  4.51 us
    unnamed x16, local copies, waits for them, and re-layouts  4.39 us
    pallas_call x1, Pallas kernels, pivot_inverse(): pl.pallas_call(pivot_inverse_kernel, out_shape=jax.ShapeDtypeStruct((shar...  4.24 us
    all_to_all x1, starting transfers between devices, per_device(): pieces = lax.all_to_all(outgoing_rows, 'crow', 0, 0, tiled=True)  4.17 us
  transfers between devices with their start and end apart: 8, of which 5 were waited for; matrix products, arithmetic and copies ran while one was open for 6% of the time, Pallas kernels for 9%

profile of v17, /device:TPU:194, one launch (start us, length us, event | category | flops | bytes accessed | tf_op | source)
XLA Modules:
  0.0 75.0 jit_solution(11197413647639163632)
XLA Ops:
  0.6 0.8 %slice_bitcast_fusion = (bf16[128,128]{1,0:T(8,128)(2,1)S(1)}, bf16[1,128,128]{2,1,0:T(8,128)(2,1)S(1)}) fusion(bf16[1,3072,128]{2,1,0:T(8,128)(2,1)} %z_ref.1), kind=kLoop, calls=%fused_computation.3 | loop fusion | bytes 131072 | tf_op jit(solution)/shard_map/slice | solution.py:217
  1.4 0.8 %slice_bitcast_fusion.1 = bf16[1,128,128]{2,1,0:T(8,128)(2,1)S(1)} fusion(bf16[1,24,128,128]{3,2,1,0:T(8,128)(2,1)} %u_ref.1), kind=kLoop, calls=%fused_computation.4 | loop fusion | bytes 65536 | tf_op jit(solution)/shard_map/stack;squeeze | solution.py:215
  2.2 3.5 %collective-permute-start = (bf16[2,128,128]{2,1,0:T(8,128)(2,1)S(1)}, bf16[2,128,128]{2,1,0:T(8,128)(2,1)S(1)}, u32[]{:S(2)}, u32[]{:S(2)}) collective-permute-start(bf16[2,128,128]{2,1,0:T(8,128)(2,1)S(1)} %pad_maximum_fusion.2), channel_id=1, source_target_pairs={{0,1},{1,2},{2,3},{4,5},{5,6},{6,7},{8,9},{9,10},{10,11},{12,13},{... | collective-permute-start | bytes 196616 | tf_op jit(solution)/shard_map/ppermute | solution.py:26
  5.7 1.3 %collective-permute-start.1 = (bf16[128,128]{1,0:T(8,128)(2,1)S(1)}, bf16[128,128]{1,0:T(8,128)(2,1)S(1)}, u32[]{:S(2)}, u32[]{:S(2)}) collective-permute-start(bf16[128,128]{1,0:T(8,128)(2,1)S(1)} %get-tuple-element.15), channel_id=1, source_target_pairs={{1,0},{2,1},{3,2},{5,4},{6,5},{7,6},{9,8},{10,9},{11,10},{13,12},{... | collective-permute-start | bytes 98312 | tf_op jit(solution)/shard_map/ppermute | solution.py:26
  7.0 4.5 %collective-permute-done.1.zn_ref = bf16[128,128]{1,0:T(8,128)(2,1)S(1)} collective-permute-done((bf16[128,128]{1,0:T(8,128)(2,1)S(1)}, bf16[128,128]{1,0:T(8,128)(2,1)S(1)}, u32[]{:S(2)}, u32[]{:S(2)}) %collective-permute-start.1) | collective-permute-done | bytes 32800 | tf_op jit(solution)/shard_map/ppermute | solution.py:26
  11.5 0.0 collective-permute-done.fp_ref
  11.5 0.6 copy-done.6
  12.1 0.6 copy-done.5
  12.7 3.6 %shard_map.85 = (bf16[3,2,128,128]{3,2,1,0:T(8,128)(2,1)}, bf16[3,2,128,128]{3,2,1,0:T(8,128)(2,1)}, bf16[1,2,128,128]{3,2,1,0:T(8,128)(2,1)}, bf16[1,2,128,128]...) custom-call(s32[1,1,16]{2,1,0:T(1,128)} %blocks_ref.1, s32[1,8]{1,0:T(1,128)} %counts_ref.1, ...), custom_call_target="tpu_custom_call" | custom-call | tf_op jit(solution)/shard_map/pallas_call | solution.py:89
  16.3 1.9 %collective-permute-start.2 = (bf16[3,2,128,128]{3,2,1,0:T(8,128)(2,1)}, bf16[3,2,128,128]{3,2,1,0:T(8,128)(2,1)S(1)}, u32[]{:S(2)}, u32[]{:S(2)}) collective-permute-start(bf16[3,2,128,128]{3,2,1,0:T(8,128)(2,1)} %get-tuple-element.11), channel_id=1, source_target_pairs={{4,0},{8,4},{12,8},{16,12},{20,16},{24,20},{28,24},{32,28},{36,32}... | collective-permute-start | bytes 589832 | tf_op jit(solution)/shard_map/ppermute | solution.py:237
  18.3 2.4 %collective-permute-start.3 = (bf16[3,2,128,128]{3,2,1,0:T(8,128)(2,1)}, bf16[3,2,128,128]{3,2,1,0:T(8,128)(2,1)S(1)}, u32[]{:S(2)}, u32[]{:S(2)}) collective-permute-start(bf16[3,2,128,128]{3,2,1,0:T(8,128)(2,1)} %get-tuple-element.12), channel_id=1, source_target_pairs={{0,4},{4,8},{8,12},{12,16},{16,20},{20,24},{24,28},{28,32},{32,36}... | collective-permute-start | bytes 589832 | tf_op jit(solution)/shard_map/ppermute | solution.py:240
  20.7 1.1 %collective-permute-done.2.down_ref = bf16[3,2,128,128]{3,2,1,0:T(8,128)(2,1)S(1)} collective-permute-done((bf16[3,2,128,128]{3,2,1,0:T(8,128)(2,1)}, bf16[3,2,128,128]{3,2,1,0:T(8,128)(2,1)S(1)}, u32[]{:S(2)}, u32[]{:S(2)}) %collective-permute-start.2) | collective-permute-done | bytes 196640 | tf_op jit(solution)/shard_map/ppermute | solution.py:237
  21.8 3.7 %collective-permute-done.3.up_ref = bf16[3,2,128,128]{3,2,1,0:T(8,128)(2,1)S(1)} collective-permute-done((bf16[3,2,128,128]{3,2,1,0:T(8,128)(2,1)}, bf16[3,2,128,128]{3,2,1,0:T(8,128)(2,1)S(1)}, u32[]{:S(2)}, u32[]{:S(2)}) %collective-permute-start.3) | collective-permute-done | bytes 196640 | tf_op jit(solution)/shard_map/ppermute | solution.py:240
  25.5 0.9 %pad_maximum_fusion.1 = bf16[3,2,128,128]{3,2,1,0:T(8,128)(2,1)S(1)} fusion(bf16[1,2,128,128]{3,2,1,0:T(8,128)(2,1)S(1)} %get-tuple-element.19, bf16[1,2,128,128]{3,2,1,0:T(8,128)(2,1)S(1)} %get-tuple-element.17, bf16[1,2,128,128]{3,2,1,0:T(8,128)(2,1)} %get-tuple-element.14), kind=kLoop, calls=%fused_computation.1 | loop fusion | flops 196608 | bytes 393216 | tf_op jit(solution)/shard_map/concatenate | solution.py:247
  26.4 6.4 %collective-permute-start.5 = (bf16[3,2,128,128]{3,2,1,0:T(8,128)(2,1)S(1)}, bf16[3,2,128,128]{3,2,1,0:T(8,128)(2,1)S(1)}, u32[]{:S(2)}, u32[]{:S(2)}) collective-permute-start(bf16[3,2,128,128]{3,2,1,0:T(8,128)(2,1)S(1)} %pad_maximum_fusion.1), channel_id=1, source_target_pairs={{0,64},{4,68},{8,72},{12,76},{16,80},{20,84},{24,88},{28,92},{32,9... | collective-permute-start | bytes 589832 | tf_op jit(solution)/shard_map/ppermute | solution.py:246
  32.8 0.9 %pad_maximum_fusion = bf16[3,2,128,128]{3,2,1,0:T(8,128)(2,1)S(1)} fusion(bf16[1,2,128,128]{3,2,1,0:T(8,128)(2,1)S(1)} %get-tuple-element.20, bf16[1,2,128,128]{3,2,1,0:T(8,128)(2,1)S(1)} %get-tuple-element.18, bf16[1,2,128,128]{3,2,1,0:T(8,128)(2,1)} %get-tuple-element.13), kind=kLoop, calls=%fused_computation | loop fusion | flops 196608 | bytes 393216 | tf_op jit(solution)/shard_map/concatenate | solution.py:242
  33.7 1.9 %collective-permute-start.4 = (bf16[3,2,128,128]{3,2,1,0:T(8,128)(2,1)S(1)}, bf16[3,2,128,128]{3,2,1,0:T(8,128)(2,1)S(1)}, u32[]{:S(2)}, u32[]{:S(2)}) collective-permute-start(bf16[3,2,128,128]{3,2,1,0:T(8,128)(2,1)S(1)} %pad_maximum_fusion), channel_id=1, source_target_pairs={{64,0},{68,4},{72,8},{76,12},{80,16},{84,20},{88,24},{92,28},{96,3... | collective-permute-start | bytes 589832 | tf_op jit(solution)/shard_map/ppermute | solution.py:241
  36.3 0.8 %dynamic_slice.3 = f32[32,32]{1,0:T(8,128)S(1)} dynamic-slice(f32[128,128]{1,0:T(8,128)} %get-tuple-element.9.gram_ref, s32[]{:T(128)S(6)} %select_n.4, s32[]{:T(128)S(6)} %select_n.4), dynamic_slice_sizes={32,32} | dynamic-slice | bytes 8196 | tf_op jit(solution)/shard_map/dynamic_slice | solution.py:230
  37.1 0.7 reshape.12
  37.8 4.2 %all-to-all-start.1 = ((f32[4,1,1024]{2,1,0:T(1,128)}), f32[4,1,1024]{2,1,0:T(1,128)S(1)}, u32[]{:S(2)}, u32[]{:S(2)}) async-start(f32[4,1,1024]{2,1,0:T(1,128)} %reshape.12), calls=%async_computation.1 | async-start | bytes 32768 | tf_op jit(solution)/shard_map/all_to_all | solution.py:231
  42.0 0.0 collective-permute-done.5.fup_ref
  42.0 5.6 %collective-permute-done.4.fdn_ref = bf16[3,2,128,128]{3,2,1,0:T(8,128)(2,1)S(1)} collective-permute-done((bf16[3,2,128,128]{3,2,1,0:T(8,128)(2,1)S(1)}, bf16[3,2,128,128]{3,2,1,0:T(8,128)(2,1)S(1)}, u32[]{:S(2)}, u32[]{:S(2)}) %collective-permute-start.4) | collective-permute-done | bytes 196640 | tf_op jit(solution)/shard_map/ppermute | solution.py:241
  47.5 0.7 copy-done.4
  48.2 2.7 %shard_map.86 = f32[4,64,1152]{2,1,0:T(8,128)} custom-call(s32[1]{0:T(128)S(6)} %copy.9.owner_ref, f32[128,128]{1,0:T(8,128)} %get-tuple-element.9.gram_ref, bf16[8,2,128,128]{3,2,1,0:T(8,128)(2,1)} %get-tuple-element.10.own_ref, bf16[3,2,128,128]{3,2,1,0:T(8,128)(2,1)} %copy-done.1, bf16[3,2,128,128]{3,2,1,0:T(8,128)(2,1)} %copy-done.2, ...), custom_call_target="tpu_custom_call" | custom-call | tf_op jit(solution)/shard_map/pallas_call | solution.py:194
  50.9 4.2 %all-to-all-start = ((f32[4,64,1152]{2,1,0:T(8,128)}), f32[4,64,1152]{2,1,0:T(8,128)S(1)}, u32[]{:S(2)}, u32[]{:S(2)}) async-start(f32[4,64,1152]{2,1,0:T(8,128)} %shard_map.86), calls=%async_computation | async-start | bytes 2359296 | tf_op jit(solution)/shard_map/all_to_all | solution.py:255
  55.1 0.5 broadcast.1
  55.6 0.7 reduce
  56.3 0.7 reshape.13.blocks_ref
  57.0 4.2 %shard_map.87.inverse_ref = f32[32,32]{1,0:T(8,128)} custom-call(f32[4,32,32]{2,1,0:T(8,128)} %reshape.13.blocks_ref), custom_call_target="tpu_custom_call" | custom-call | tf_op jit(solution)/shard_map/pallas_call | solution.py:126
  61.3 10.0 %all-to-all-done.pieces_ref = f32[4,64,1152]{2,1,0:T(8,128)S(1)} async-done(((f32[4,64,1152]{2,1,0:T(8,128)}), f32[4,64,1152]{2,1,0:T(8,128)S(1)}, u32[]{:S(2)}, u32[]{:S(2)}) %all-to-all-start) | async-done | bytes 1179680 | tf_op jit(solution)/shard_map/all_to_all | solution.py:255
  71.2 1.1 %copy-done = f32[4,64,1152]{2,1,0:T(8,128)} copy-done((f32[4,64,1152]{2,1,0:T(8,128)}, f32[4,64,1152]{2,1,0:T(8,128)S(1)}, u32[]{:S(2)}) %copy-start) | copy-done | bytes 1179672
  72.3 2.7 %shard_map.88 = (f32[32,128]{1,0:T(8,128)}, f32[32,1024]{1,0:T(8,128)}, f32[32,32]{1,0:T(8,128)}) custom-call(s32[1]{0:T(128)S(6)} %copy.9.owner_ref, f32[4,64,1152]{2,1,0:T(8,128)} %copy-done, f32[32,32]{1,0:T(8,128)} %shard_map.87.inverse_ref), custom_call_target="tpu_custom_call" | custom-call | tf_op jit(solution)/shard_map/pallas_call | solution.py:156
  (15 shorter events, 0.1 us)
Async XLA Ops:
  2.2 9.3 %collective-permute-start = (bf16[2,128,128]{2,1,0:T(8,128)(2,1)S(1)}, bf16[2,128,128]{2,1,0:T(8,128)(2,1)S(1)}, u32[]{:S(2)}, u32[]{:S(2)}) collective-permute-start(bf16[2,128,128]{2,1,0:T(8,128)(2,1)S(1)} %pad_maximum_fusion.2), channel_id=1, source_target_pairs={{0,1},{1,2},{2,3},{4,5},{5,6},{6,7},{8,9},{9,10},{10,11},{12,13},{... | collective-permute-start | bytes 196616 | tf_op jit(solution)/shard_map/ppermute | solution.py:26
  5.7 5.8 %collective-permute-start.1 = (bf16[128,128]{1,0:T(8,128)(2,1)S(1)}, bf16[128,128]{1,0:T(8,128)(2,1)S(1)}, u32[]{:S(2)}, u32[]{:S(2)}) collective-permute-start(bf16[128,128]{1,0:T(8,128)(2,1)S(1)} %get-tuple-element.15), channel_id=1, source_target_pairs={{1,0},{2,1},{3,2},{5,4},{6,5},{7,6},{9,8},{10,9},{11,10},{13,12},{... | collective-permute-start | bytes 98312 | tf_op jit(solution)/shard_map/ppermute | solution.py:26
  11.5 0.6 copy-start.6
  12.1 0.6 copy-start.5
  16.3 5.4 %collective-permute-start.2 = (bf16[3,2,128,128]{3,2,1,0:T(8,128)(2,1)}, bf16[3,2,128,128]{3,2,1,0:T(8,128)(2,1)S(1)}, u32[]{:S(2)}, u32[]{:S(2)}) collective-permute-start(bf16[3,2,128,128]{3,2,1,0:T(8,128)(2,1)} %get-tuple-element.11), channel_id=1, source_target_pairs={{4,0},{8,4},{12,8},{16,12},{20,16},{24,20},{28,24},{32,28},{36,32}... | collective-permute-start | bytes 589832 | tf_op jit(solution)/shard_map/ppermute | solution.py:237
  18.3 7.2 %collective-permute-start.3 = (bf16[3,2,128,128]{3,2,1,0:T(8,128)(2,1)}, bf16[3,2,128,128]{3,2,1,0:T(8,128)(2,1)S(1)}, u32[]{:S(2)}, u32[]{:S(2)}) collective-permute-start(bf16[3,2,128,128]{3,2,1,0:T(8,128)(2,1)} %get-tuple-element.12), channel_id=1, source_target_pairs={{0,4},{4,8},{8,12},{12,16},{16,20},{20,24},{24,28},{28,32},{32,36}... | collective-permute-start | bytes 589832 | tf_op jit(solution)/shard_map/ppermute | solution.py:240
  21.7 25.8 %copy-start.1 = (bf16[3,2,128,128]{3,2,1,0:T(8,128)(2,1)}, bf16[3,2,128,128]{3,2,1,0:T(8,128)(2,1)S(1)}, u32[]{:S(2)}) copy-start(bf16[3,2,128,128]{3,2,1,0:T(8,128)(2,1)S(1)} %collective-permute-done.2.down_ref) | copy-start | bytes 589828
  25.5 22.1 %copy-start.2 = (bf16[3,2,128,128]{3,2,1,0:T(8,128)(2,1)}, bf16[3,2,128,128]{3,2,1,0:T(8,128)(2,1)S(1)}, u32[]{:S(2)}) copy-start(bf16[3,2,128,128]{3,2,1,0:T(8,128)(2,1)S(1)} %collective-permute-done.3.up_ref) | copy-start | bytes 589828
  26.4 15.5 %collective-permute-start.5 = (bf16[3,2,128,128]{3,2,1,0:T(8,128)(2,1)S(1)}, bf16[3,2,128,128]{3,2,1,0:T(8,128)(2,1)S(1)}, u32[]{:S(2)}, u32[]{:S(2)}) collective-permute-start(bf16[3,2,128,128]{3,2,1,0:T(8,128)(2,1)S(1)} %pad_maximum_fusion.1), channel_id=1, source_target_pairs={{0,64},{4,68},{8,72},{12,76},{16,80},{20,84},{24,88},{28,92},{32,9... | collective-permute-start | bytes 589832 | tf_op jit(solution)/shard_map/ppermute | solution.py:246
  33.7 13.8 %collective-permute-start.4 = (bf16[3,2,128,128]{3,2,1,0:T(8,128)(2,1)S(1)}, bf16[3,2,128,128]{3,2,1,0:T(8,128)(2,1)S(1)}, u32[]{:S(2)}, u32[]{:S(2)}) collective-permute-start(bf16[3,2,128,128]{3,2,1,0:T(8,128)(2,1)S(1)} %pad_maximum_fusion), channel_id=1, source_target_pairs={{64,0},{68,4},{72,8},{76,12},{80,16},{84,20},{88,24},{92,28},{96,3... | collective-permute-start | bytes 589832 | tf_op jit(solution)/shard_map/ppermute | solution.py:241
  37.8 13.1 %all-to-all-start.1 = ((f32[4,1,1024]{2,1,0:T(1,128)}), f32[4,1,1024]{2,1,0:T(1,128)S(1)}, u32[]{:S(2)}, u32[]{:S(2)}) async-start(f32[4,1,1024]{2,1,0:T(1,128)} %reshape.12), calls=%async_computation.1 | async-start | bytes 32768 | tf_op jit(solution)/shard_map/all_to_all | solution.py:231
  42.0 5.6 %copy-start.3 = (bf16[3,2,128,128]{3,2,1,0:T(8,128)(2,1)}, bf16[3,2,128,128]{3,2,1,0:T(8,128)(2,1)S(1)}, u32[]{:S(2)}) copy-start(bf16[3,2,128,128]{3,2,1,0:T(8,128)(2,1)S(1)} %collective-permute-done.5.fup_ref) | copy-start | bytes 589828
  47.5 0.7 copy-start.4
  50.9 20.3 %all-to-all-start = ((f32[4,64,1152]{2,1,0:T(8,128)}), f32[4,64,1152]{2,1,0:T(8,128)S(1)}, u32[]{:S(2)}, u32[]{:S(2)}) async-start(f32[4,64,1152]{2,1,0:T(8,128)} %shard_map.86), calls=%async_computation | async-start | bytes 2359296 | tf_op jit(solution)/shard_map/all_to_all | solution.py:255
  71.2 1.1 %copy-start = (f32[4,64,1152]{2,1,0:T(8,128)}, f32[4,64,1152]{2,1,0:T(8,128)S(1)}, u32[]{:S(2)}) copy-start(f32[4,64,1152]{2,1,0:T(8,128)S(1)} %all-to-all-done.pieces_ref) | copy-start | bytes 3538948

commit v18 on v10

--- a/solution.py
+++ b/solution.py
@@ -44,27 +44,47 @@
 
 
 def local_apply_kernel(
-    groups, blocks_ref, counts_ref, z_ref, fp_ref, zn_ref, d_ref, u_ref, *refs
+    groups, blocks_ref, counts_ref, z_hbm, fp_ref, zn_ref, d_hbm, u_hbm, *refs
 ):
-    group_refs, own_ref, gram_ref, app_ref = refs[:len(groups)], refs[-3], refs[-2], refs[-1]
-    count, rows = d_ref.shape[1], d_ref.shape[2]
+    group_refs = refs[:len(groups)]
+    own_ref, gram_ref, app_ref, z_ref, d_ref, u_ref, sems = refs[len(groups):]
+    count, rows = d_ref.shape[0], d_ref.shape[1]
     per_slot = own_ref.shape[1]
     crow = lax.axis_index("crow")
+    copies = {}
+    for b in range(count):
+        for kind, (src, dst) in enumerate((
+            (z_hbm.at[0, pl.ds(b * rows, rows)], z_ref.at[pl.ds(b * rows, rows)]),
+            (d_hbm.at[0, b], d_ref.at[b]),
+            (u_hbm.at[0, b], u_ref.at[b]),
+        )):
+            copy = pltpu.make_async_copy(src, dst, sems.at[kind, b])
+            copy.start()
+            copies[kind, b] = copy
+
+    def need(kind, b):
+        if (kind, b) in copies:
+            copies.pop((kind, b)).wait()
 
     def rows_of(b):
-        return z_ref[0, pl.ds(b * rows, rows), :]
+        return z_ref[pl.ds(b * rows, rows), :]
 
     for b in range(count):
+        for step in (b - 1, b, b + 1):
+            if 0 <= step < count:
+                need(0, step)
+        need(1, b)
+        need(2, b)
         below = fp_ref[0] if b == 0 else rows_of(b - 1)
-        lower = fp_ref[1] if b == 0 else u_ref[0, b - 1]
+        lower = fp_ref[1] if b == 0 else u_ref[b - 1]
         above = zn_ref[...] if b == count - 1 else rows_of(b + 1)
-        total = (_ab(d_ref[0, b], rows_of(b)) + _ab(u_ref[0, b], above)) + _atb(lower, below)
+        total = (_ab(d_ref[b], rows_of(b)) + _ab(u_ref[b], above)) + _atb(lower, below)
         app_ref[pl.ds(b * rows, rows), :] = total.astype(app_ref.dtype)
-    gram_ref[...] = _atb(z_ref[0], app_ref[...])
+    gram_ref[...] = _atb(z_ref[...], app_ref[...])
     for slot in range(own_ref.shape[0]):
         for unit in range(per_slot):
             start = pl.multiple_of(blocks_ref[0, 0, slot * per_slot + unit] * rows, rows)
-            tile = z_ref[0, pl.ds(start, rows), :]
+            tile = z_ref[pl.ds(start, rows), :]
             live = crow * per_slot + unit < counts_ref[0, slot]
             own_ref[slot, unit] = jnp.where(live, tile, jnp.zeros_like(tile))
     for group, out_ref in zip(groups, group_refs):
@@ -81,6 +101,7 @@
     width = deflation.shape[2]
     vmem = pl.BlockSpec(memory_space=pltpu.VMEM)
     smem = pl.BlockSpec(memory_space=pltpu.SMEM)
+    hbm = pl.BlockSpec(memory_space=pl.ANY)
     tile = lambda n: jax.ShapeDtypeStruct((n, per_slot, rows, width), deflation.dtype)
     return pl.pallas_call(
         functools.partial(local_apply_kernel, groups),
@@ -88,9 +109,15 @@
             tile(slots),
             jax.ShapeDtypeStruct((width, width), jnp.float32),
         ),
-        in_specs=[smem, smem] + [vmem] * 5,
+        in_specs=[smem, smem, hbm, vmem, vmem, hbm, hbm],
         out_specs=tuple(vmem for _ in range(len(groups) + 2)),
-        scratch_shapes=[pltpu.VMEM((blocks * rows, width), deflation.dtype)],
+        scratch_shapes=[
+            pltpu.VMEM((blocks * rows, width), deflation.dtype),
+            pltpu.VMEM((blocks * rows, width), deflation.dtype),
+            pltpu.VMEM((blocks, rows, rows), diag_op.dtype),
+            pltpu.VMEM((blocks, rows, rows), upper_op.dtype),
+            pltpu.SemaphoreType.DMA((3, blocks)),
+        ],
     )(tile_blocks, pair_counts, deflation, forward_pair, next_rows, diag_op, upper_op)
 
 

time: 75.8 us -> 80.3 us (1.059)
  Pallas kernels: 13.2 us -> 17.6 us
    pallas_call x1, Pallas kernels: 3.61 us -> 7.98 us  [local_apply(): pl.pallas_call(functools.partial(local_apply_kernel, groups), out_shape=t...]
  transfers between devices with their start and end apart: 8 -> 8, of which waited for: 5 -> 5; matrix products, arithmetic and copies ran while one was open for 6% -> 5% of each run, Pallas kernels for 9% -> 9%
where the time goes in v18:
time: 80.3 us; the launch traced here: 79.3 us
  starting transfers between devices  25.8 us (32%)
  waiting for transfers between devices  24.8 us (31%)
  Pallas kernels  17.6 us (22%)
  local copies, waits for them, and re-layouts  7.27 us (9%)
  other arithmetic  2.5 us (3%)
  between operations  1.38 us (2%)
    all_to_all x1, waiting for transfers between devices, per_device(): pieces = lax.all_to_all(outgoing_rows, 'crow', 0, 0, tiled=True)  9.98 us
    pallas_call x1, Pallas kernels, local_apply(): pl.pallas_call(functools.partial(local_apply_kernel, groups), out_shape=t...  7.98 us
    ppermute x1, starting transfers between devices, per_device(): lax.ppermute(jnp.concatenate([near_up, down[2:], up[2:]]), 'sub', [(u, u...  6.39 us
    ppermute x1, waiting for transfers between devices, per_device(): lax.ppermute(jnp.concatenate([near_down, down[:1], up[:1]]), 'sub', [(u,...  5.57 us
    ppermute x2, starting transfers between devices, shifted(): lax.ppermute(value, axis, [(source, source + steps) for source in range(i...  4.78 us
    ppermute x2, waiting for transfers between devices, shifted(): lax.ppermute(value, axis, [(source, source + steps) for source in range(i...  4.51 us
    unnamed x16, local copies, waits for them, and re-layouts  4.39 us
    pallas_call x1, Pallas kernels, pivot_inverse(): pl.pallas_call(pivot_inverse_kernel, out_shape=jax.ShapeDtypeStruct((shar...  4.24 us
  transfers between devices with their start and end apart: 8, of which 5 were waited for; matrix products, arithmetic and copies ran while one was open for 5% of the time, Pallas kernels for 9%

profile of v18, /device:TPU:194, one launch (start us, length us, event | category | flops | bytes accessed | tf_op | source)
XLA Modules:
  0.0 79.3 jit_solution(17429360391257963517)
XLA Ops:
  0.6 0.8 slice_bitcast_fusion
  1.4 0.8 slice_bitcast_fusion.1
  2.2 3.5 %collective-permute-start = (bf16[2,128,128]{2,1,0:T(8,128)(2,1)S(1)}, bf16[2,128,128]{2,1,0:T(8,128)(2,1)S(1)}, u32[]{:S(2)}, u32[]{:S(2)}) collective-permute-start(bf16[2,128,128]{2,1,0:T(8,128)(2,1)S(1)} %pad_maximum_fusion.2), channel_id=1, source_target_pairs={{0,1},{1,2},{2,3},{4,5},{5,6},{6,7},{8,9},{9,10},{10,11},{12,13},{... | collective-permute-start | bytes 196616 | tf_op jit(solution)/shard_map/ppermute | solution.py:26
  5.7 1.3 %collective-permute-start.1 = (bf16[128,128]{1,0:T(8,128)(2,1)S(1)}, bf16[128,128]{1,0:T(8,128)(2,1)S(1)}, u32[]{:S(2)}, u32[]{:S(2)}) collective-permute-start(bf16[128,128]{1,0:T(8,128)(2,1)S(1)} %get-tuple-element.15), channel_id=1, source_target_pairs={{1,0},{2,1},{3,2},{5,4},{6,5},{7,6},{9,8},{10,9},{11,10},{13,12},{... | collective-permute-start | bytes 98312 | tf_op jit(solution)/shard_map/ppermute | solution.py:26
  7.0 4.5 %collective-permute-done.1.zn_ref = bf16[128,128]{1,0:T(8,128)(2,1)S(1)} collective-permute-done((bf16[128,128]{1,0:T(8,128)(2,1)S(1)}, bf16[128,128]{1,0:T(8,128)(2,1)S(1)}, u32[]{:S(2)}, u32[]{:S(2)}) %collective-permute-start.1) | collective-permute-done | bytes 32800 | tf_op jit(solution)/shard_map/ppermute | solution.py:26
  11.5 0.0 collective-permute-done.fp_ref
  11.5 0.6 copy-done.6
  12.1 0.6 copy-done.5
  12.7 8.0 %shard_map.85 = (bf16[3,2,128,128]{3,2,1,0:T(8,128)(2,1)}, bf16[3,2,128,128]{3,2,1,0:T(8,128)(2,1)}, bf16[1,2,128,128]{3,2,1,0:T(8,128)(2,1)}, bf16[1,2,128,128]...) custom-call(s32[1,1,16]{2,1,0:T(1,128)} %blocks_ref.1, s32[1,8]{1,0:T(1,128)} %counts_ref.1, ...), custom_call_target="tpu_custom_call" | custom-call | tf_op jit(solution)/shard_map/pallas_call | solution.py:106
  20.7 1.9 %collective-permute-start.2 = (bf16[3,2,128,128]{3,2,1,0:T(8,128)(2,1)}, bf16[3,2,128,128]{3,2,1,0:T(8,128)(2,1)S(1)}, u32[]{:S(2)}, u32[]{:S(2)}) collective-permute-start(bf16[3,2,128,128]{3,2,1,0:T(8,128)(2,1)} %get-tuple-element.11), channel_id=1, source_target_pairs={{4,0},{8,4},{12,8},{16,12},{20,16},{24,20},{28,24},{32,28},{36,32}... | collective-permute-start | bytes 589832 | tf_op jit(solution)/shard_map/ppermute | solution.py:260
  22.6 2.4 %collective-permute-start.3 = (bf16[3,2,128,128]{3,2,1,0:T(8,128)(2,1)}, bf16[3,2,128,128]{3,2,1,0:T(8,128)(2,1)S(1)}, u32[]{:S(2)}, u32[]{:S(2)}) collective-permute-start(bf16[3,2,128,128]{3,2,1,0:T(8,128)(2,1)} %get-tuple-element.12), channel_id=1, source_target_pairs={{0,4},{4,8},{8,12},{12,16},{16,20},{20,24},{24,28},{28,32},{32,36}... | collective-permute-start | bytes 589832 | tf_op jit(solution)/shard_map/ppermute | solution.py:263
  25.1 1.1 %collective-permute-done.2.down_ref = bf16[3,2,128,128]{3,2,1,0:T(8,128)(2,1)S(1)} collective-permute-done((bf16[3,2,128,128]{3,2,1,0:T(8,128)(2,1)}, bf16[3,2,128,128]{3,2,1,0:T(8,128)(2,1)S(1)}, u32[]{:S(2)}, u32[]{:S(2)}) %collective-permute-start.2) | collective-permute-done | bytes 196640 | tf_op jit(solution)/shard_map/ppermute | solution.py:260
  26.1 3.7 %collective-permute-done.3.up_ref = bf16[3,2,128,128]{3,2,1,0:T(8,128)(2,1)S(1)} collective-permute-done((bf16[3,2,128,128]{3,2,1,0:T(8,128)(2,1)}, bf16[3,2,128,128]{3,2,1,0:T(8,128)(2,1)S(1)}, u32[]{:S(2)}, u32[]{:S(2)}) %collective-permute-start.3) | collective-permute-done | bytes 196640 | tf_op jit(solution)/shard_map/ppermute | solution.py:263
  29.9 0.9 %pad_maximum_fusion.1 = bf16[3,2,128,128]{3,2,1,0:T(8,128)(2,1)S(1)} fusion(bf16[1,2,128,128]{3,2,1,0:T(8,128)(2,1)S(1)} %get-tuple-element.19, bf16[1,2,128,128]{3,2,1,0:T(8,128)(2,1)S(1)} %get-tuple-element.17, bf16[1,2,128,128]{3,2,1,0:T(8,128)(2,1)} %get-tuple-element.14), kind=kLoop, calls=%fused_computation.1 | loop fusion | flops 196608 | bytes 393216 | tf_op jit(solution)/shard_map/concatenate | solution.py:270
  30.8 6.4 %collective-permute-start.5 = (bf16[3,2,128,128]{3,2,1,0:T(8,128)(2,1)S(1)}, bf16[3,2,128,128]{3,2,1,0:T(8,128)(2,1)S(1)}, u32[]{:S(2)}, u32[]{:S(2)}) collective-permute-start(bf16[3,2,128,128]{3,2,1,0:T(8,128)(2,1)S(1)} %pad_maximum_fusion.1), channel_id=1, source_target_pairs={{0,64},{4,68},{8,72},{12,76},{16,80},{20,84},{24,88},{28,92},{32,9... | collective-permute-start | bytes 589832 | tf_op jit(solution)/shard_map/ppermute | solution.py:269
  37.2 0.9 %pad_maximum_fusion = bf16[3,2,128,128]{3,2,1,0:T(8,128)(2,1)S(1)} fusion(bf16[1,2,128,128]{3,2,1,0:T(8,128)(2,1)S(1)} %get-tuple-element.20, bf16[1,2,128,128]{3,2,1,0:T(8,128)(2,1)S(1)} %get-tuple-element.18, bf16[1,2,128,128]{3,2,1,0:T(8,128)(2,1)} %get-tuple-element.13), kind=kLoop, calls=%fused_computation | loop fusion | flops 196608 | bytes 393216 | tf_op jit(solution)/shard_map/concatenate | solution.py:265
  38.1 1.9 %collective-permute-start.4 = (bf16[3,2,128,128]{3,2,1,0:T(8,128)(2,1)S(1)}, bf16[3,2,128,128]{3,2,1,0:T(8,128)(2,1)S(1)}, u32[]{:S(2)}, u32[]{:S(2)}) collective-permute-start(bf16[3,2,128,128]{3,2,1,0:T(8,128)(2,1)S(1)} %pad_maximum_fusion), channel_id=1, source_target_pairs={{64,0},{68,4},{72,8},{76,12},{80,16},{84,20},{88,24},{92,28},{96,3... | collective-permute-start | bytes 589832 | tf_op jit(solution)/shard_map/ppermute | solution.py:264
  40.6 0.8 %dynamic_slice.3 = f32[32,32]{1,0:T(8,128)S(1)} dynamic-slice(f32[128,128]{1,0:T(8,128)} %get-tuple-element.9.gram_ref, s32[]{:T(128)S(6)} %select_n.4, s32[]{:T(128)S(6)} %select_n.4), dynamic_slice_sizes={32,32} | dynamic-slice | bytes 8196 | tf_op jit(solution)/shard_map/dynamic_slice | solution.py:253
  41.4 0.7 reshape.12
  42.2 4.2 %all-to-all-start.1 = ((f32[4,1,1024]{2,1,0:T(1,128)}), f32[4,1,1024]{2,1,0:T(1,128)S(1)}, u32[]{:S(2)}, u32[]{:S(2)}) async-start(f32[4,1,1024]{2,1,0:T(1,128)} %reshape.12), calls=%async_computation.1 | async-start | bytes 32768 | tf_op jit(solution)/shard_map/all_to_all | solution.py:254
  46.3 0.0 collective-permute-done.5.fup_ref
  46.3 5.6 %collective-permute-done.4.fdn_ref = bf16[3,2,128,128]{3,2,1,0:T(8,128)(2,1)S(1)} collective-permute-done((bf16[3,2,128,128]{3,2,1,0:T(8,128)(2,1)S(1)}, bf16[3,2,128,128]{3,2,1,0:T(8,128)(2,1)S(1)}, u32[]{:S(2)}, u32[]{:S(2)}) %collective-permute-start.4) | collective-permute-done | bytes 196640 | tf_op jit(solution)/shard_map/ppermute | solution.py:264
  51.9 0.7 copy-done.4
  52.6 2.7 %shard_map.86 = f32[4,64,1152]{2,1,0:T(8,128)} custom-call(s32[1]{0:T(128)S(6)} %copy.9.owner_ref, f32[128,128]{1,0:T(8,128)} %get-tuple-element.9.gram_ref, bf16[8,2,128,128]{3,2,1,0:T(8,128)(2,1)} %get-tuple-element.10.own_ref, bf16[3,2,128,128]{3,2,1,0:T(8,128)(2,1)} %copy-done.1, bf16[3,2,128,128]{3,2,1,0:T(8,128)(2,1)} %copy-done.2, ...), custom_call_target="tpu_custom_call" | custom-call | tf_op jit(solution)/shard_map/pallas_call | solution.py:217
  55.3 4.2 %all-to-all-start = ((f32[4,64,1152]{2,1,0:T(8,128)}), f32[4,64,1152]{2,1,0:T(8,128)S(1)}, u32[]{:S(2)}, u32[]{:S(2)}) async-start(f32[4,64,1152]{2,1,0:T(8,128)} %shard_map.86), calls=%async_computation | async-start | bytes 2359296 | tf_op jit(solution)/shard_map/all_to_all | solution.py:278
  59.5 0.5 broadcast.1
  60.0 0.7 reduce
  60.7 0.7 reshape.13.blocks_ref
  61.4 4.2 %shard_map.87.inverse_ref = f32[32,32]{1,0:T(8,128)} custom-call(f32[4,32,32]{2,1,0:T(8,128)} %reshape.13.blocks_ref), custom_call_target="tpu_custom_call" | custom-call | tf_op jit(solution)/shard_map/pallas_call | solution.py:149
  65.6 10.0 %all-to-all-done.pieces_ref = f32[4,64,1152]{2,1,0:T(8,128)S(1)} async-done(((f32[4,64,1152]{2,1,0:T(8,128)}), f32[4,64,1152]{2,1,0:T(8,128)S(1)}, u32[]{:S(2)}, u32[]{:S(2)}) %all-to-all-start) | async-done | bytes 1179680 | tf_op jit(solution)/shard_map/all_to_all | solution.py:278
  75.6 1.1 %copy-done = f32[4,64,1152]{2,1,0:T(8,128)} copy-done((f32[4,64,1152]{2,1,0:T(8,128)}, f32[4,64,1152]{2,1,0:T(8,128)S(1)}, u32[]{:S(2)}) %copy-start) | copy-done | bytes 1179672
  76.7 2.7 %shard_map.88 = (f32[32,128]{1,0:T(8,128)}, f32[32,1024]{1,0:T(8,128)}, f32[32,32]{1,0:T(8,128)}) custom-call(s32[1]{0:T(128)S(6)} %copy.9.owner_ref, f32[4,64,1152]{2,1,0:T(8,128)} %copy-done, f32[32,32]{1,0:T(8,128)} %shard_map.87.inverse_ref), custom_call_target="tpu_custom_call" | custom-call | tf_op jit(solution)/shard_map/pallas_call | solution.py:179
  (15 shorter events, 0.1 us)
Async XLA Ops:
  2.2 9.3 %collective-permute-start = (bf16[2,128,128]{2,1,0:T(8,128)(2,1)S(1)}, bf16[2,128,128]{2,1,0:T(8,128)(2,1)S(1)}, u32[]{:S(2)}, u32[]{:S(2)}) collective-permute-start(bf16[2,128,128]{2,1,0:T(8,128)(2,1)S(1)} %pad_maximum_fusion.2), channel_id=1, source_target_pairs={{0,1},{1,2},{2,3},{4,5},{5,6},{6,7},{8,9},{9,10},{10,11},{12,13},{... | collective-permute-start | bytes 196616 | tf_op jit(solution)/shard_map/ppermute | solution.py:26
  5.7 5.8 %collective-permute-start.1 = (bf16[128,128]{1,0:T(8,128)(2,1)S(1)}, bf16[128,128]{1,0:T(8,128)(2,1)S(1)}, u32[]{:S(2)}, u32[]{:S(2)}) collective-permute-start(bf16[128,128]{1,0:T(8,128)(2,1)S(1)} %get-tuple-element.15), channel_id=1, source_target_pairs={{1,0},{2,1},{3,2},{5,4},{6,5},{7,6},{9,8},{10,9},{11,10},{13,12},{... | collective-permute-start | bytes 98312 | tf_op jit(solution)/shard_map/ppermute | solution.py:26
  11.5 0.6 copy-start.6
  12.1 0.6 copy-start.5
  20.7 5.4 %collective-permute-start.2 = (bf16[3,2,128,128]{3,2,1,0:T(8,128)(2,1)}, bf16[3,2,128,128]{3,2,1,0:T(8,128)(2,1)S(1)}, u32[]{:S(2)}, u32[]{:S(2)}) collective-permute-start(bf16[3,2,128,128]{3,2,1,0:T(8,128)(2,1)} %get-tuple-element.11), channel_id=1, source_target_pairs={{4,0},{8,4},{12,8},{16,12},{20,16},{24,20},{28,24},{32,28},{36,32}... | collective-permute-start | bytes 589832 | tf_op jit(solution)/shard_map/ppermute | solution.py:260
  22.6 7.2 %collective-permute-start.3 = (bf16[3,2,128,128]{3,2,1,0:T(8,128)(2,1)}, bf16[3,2,128,128]{3,2,1,0:T(8,128)(2,1)S(1)}, u32[]{:S(2)}, u32[]{:S(2)}) collective-permute-start(bf16[3,2,128,128]{3,2,1,0:T(8,128)(2,1)} %get-tuple-element.12), channel_id=1, source_target_pairs={{0,4},{4,8},{8,12},{12,16},{16,20},{20,24},{24,28},{28,32},{32,36}... | collective-permute-start | bytes 589832 | tf_op jit(solution)/shard_map/ppermute | solution.py:263
  26.1 25.8 %copy-start.1 = (bf16[3,2,128,128]{3,2,1,0:T(8,128)(2,1)}, bf16[3,2,128,128]{3,2,1,0:T(8,128)(2,1)S(1)}, u32[]{:S(2)}) copy-start(bf16[3,2,128,128]{3,2,1,0:T(8,128)(2,1)S(1)} %collective-permute-done.2.down_ref) | copy-start | bytes 589828
  29.8 22.1 %copy-start.2 = (bf16[3,2,128,128]{3,2,1,0:T(8,128)(2,1)}, bf16[3,2,128,128]{3,2,1,0:T(8,128)(2,1)S(1)}, u32[]{:S(2)}) copy-start(bf16[3,2,128,128]{3,2,1,0:T(8,128)(2,1)S(1)} %collective-permute-done.3.up_ref) | copy-start | bytes 589828
  30.8 15.5 %collective-permute-start.5 = (bf16[3,2,128,128]{3,2,1,0:T(8,128)(2,1)S(1)}, bf16[3,2,128,128]{3,2,1,0:T(8,128)(2,1)S(1)}, u32[]{:S(2)}, u32[]{:S(2)}) collective-permute-start(bf16[3,2,128,128]{3,2,1,0:T(8,128)(2,1)S(1)} %pad_maximum_fusion.1), channel_id=1, source_target_pairs={{0,64},{4,68},{8,72},{12,76},{16,80},{20,84},{24,88},{28,92},{32,9... | collective-permute-start | bytes 589832 | tf_op jit(solution)/shard_map/ppermute | solution.py:269
  38.1 13.8 %collective-permute-start.4 = (bf16[3,2,128,128]{3,2,1,0:T(8,128)(2,1)S(1)}, bf16[3,2,128,128]{3,2,1,0:T(8,128)(2,1)S(1)}, u32[]{:S(2)}, u32[]{:S(2)}) collective-permute-start(bf16[3,2,128,128]{3,2,1,0:T(8,128)(2,1)S(1)} %pad_maximum_fusion), channel_id=1, source_target_pairs={{64,0},{68,4},{72,8},{76,12},{80,16},{84,20},{88,24},{92,28},{96,3... | collective-permute-start | bytes 589832 | tf_op jit(solution)/shard_map/ppermute | solution.py:264
  42.2 13.1 %all-to-all-start.1 = ((f32[4,1,1024]{2,1,0:T(1,128)}), f32[4,1,1024]{2,1,0:T(1,128)S(1)}, u32[]{:S(2)}, u32[]{:S(2)}) async-start(f32[4,1,1024]{2,1,0:T(1,128)} %reshape.12), calls=%async_computation.1 | async-start | bytes 32768 | tf_op jit(solution)/shard_map/all_to_all | solution.py:254
  46.3 5.6 %copy-start.3 = (bf16[3,2,128,128]{3,2,1,0:T(8,128)(2,1)}, bf16[3,2,128,128]{3,2,1,0:T(8,128)(2,1)S(1)}, u32[]{:S(2)}) copy-start(bf16[3,2,128,128]{3,2,1,0:T(8,128)(2,1)S(1)} %collective-permute-done.5.fup_ref) | copy-start | bytes 589828
  51.9 0.7 copy-start.4
  55.3 20.3 %all-to-all-start = ((f32[4,64,1152]{2,1,0:T(8,128)}), f32[4,64,1152]{2,1,0:T(8,128)S(1)}, u32[]{:S(2)}, u32[]{:S(2)}) async-start(f32[4,64,1152]{2,1,0:T(8,128)} %shard_map.86), calls=%async_computation | async-start | bytes 2359296 | tf_op jit(solution)/shard_map/all_to_all | solution.py:278
  75.6 1.1 %copy-start = (f32[4,64,1152]{2,1,0:T(8,128)}, f32[4,64,1152]{2,1,0:T(8,128)S(1)}, u32[]{:S(2)}) copy-start(f32[4,64,1152]{2,1,0:T(8,128)S(1)} %all-to-all-done.pieces_ref) | copy-start | bytes 3538948

commit v19 on v18

--- a/solution.py
+++ b/solution.py
@@ -51,20 +51,23 @@
     count, rows = d_ref.shape[0], d_ref.shape[1]
     per_slot = own_ref.shape[1]
     crow = lax.axis_index("crow")
+    half = count // 2
+    spans = ((0, half), (half, count - half))
     copies = {}
-    for b in range(count):
+    for part, (first, size) in enumerate(spans):
         for kind, (src, dst) in enumerate((
-            (z_hbm.at[0, pl.ds(b * rows, rows)], z_ref.at[pl.ds(b * rows, rows)]),
-            (d_hbm.at[0, b], d_ref.at[b]),
-            (u_hbm.at[0, b], u_ref.at[b]),
+            (z_hbm.at[0, pl.ds(first * rows, size * rows)], z_ref.at[pl.ds(first * rows, size * rows)]),
+            (d_hbm.at[0, pl.ds(first, size)], d_ref.at[pl.ds(first, size)]),
+            (u_hbm.at[0, pl.ds(first, size)], u_ref.at[pl.ds(first, size)]),
         )):
-            copy = pltpu.make_async_copy(src, dst, sems.at[kind, b])
+            copy = pltpu.make_async_copy(src, dst, sems.at[kind, part])
             copy.start()
-            copies[kind, b] = copy
+            copies[kind, part] = copy
 
     def need(kind, b):
-        if (kind, b) in copies:
-            copies.pop((kind, b)).wait()
+        part = 0 if b < half else 1
+        if (kind, part) in copies:
+            copies.pop((kind, part)).wait()
 
     def rows_of(b):
         return z_ref[pl.ds(b * rows, rows), :]
@@ -116,7 +119,7 @@
             pltpu.VMEM((blocks * rows, width), deflation.dtype),
             pltpu.VMEM((blocks, rows, rows), diag_op.dtype),
             pltpu.VMEM((blocks, rows, rows), upper_op.dtype),
-            pltpu.SemaphoreType.DMA((3, blocks)),
+            pltpu.SemaphoreType.DMA((3, 2)),
         ],
     )(tile_blocks, pair_counts, deflation, forward_pair, next_rows, diag_op, upper_op)
 

time: 80.3 us -> 76.6 us (0.954)
  Pallas kernels: 17.6 us -> 14 us
    pallas_call x1, Pallas kernels: 7.98 us -> 4.41 us  [local_apply(): pl.pallas_call(functools.partial(local_apply_kernel, groups), out_shape=t...]
  transfers between devices with their start and end apart: 8 -> 8, of which waited for: 5 -> 5; matrix products, arithmetic and copies ran while one was open for 5% -> 6% of each run, Pallas kernels for 9% -> 9%
where the time goes in v19:
time: 76.6 us; the launch traced here: 75.8 us
  starting transfers between devices  25.8 us (34%)
  waiting for transfers between devices  24.8 us (32%)
  Pallas kernels  14 us (18%)
  local copies, waits for them, and re-layouts  7.27 us (9%)
  other arithmetic  2.5 us (3%)
  between operations  1.38 us (2%)
    all_to_all x1, waiting for transfers between devices, per_device(): pieces = lax.all_to_all(outgoing_rows, 'crow', 0, 0, tiled=True)  9.98 us
    ppermute x1, starting transfers between devices, per_device(): lax.ppermute(jnp.concatenate([near_up, down[2:], up[2:]]), 'sub', [(u, u...  6.39 us
    ppermute x1, waiting for transfers between devices, per_device(): lax.ppermute(jnp.concatenate([near_down, down[:1], up[:1]]), 'sub', [(u,...  5.58 us
    ppermute x2, starting transfers between devices, shifted(): lax.ppermute(value, axis, [(source, source + steps) for source in range(i...  4.78 us
    ppermute x2, waiting for transfers between devices, shifted(): lax.ppermute(value, axis, [(source, source + steps) for source in range(i...  4.51 us
    pallas_call x1, Pallas kernels, local_apply(): pl.pallas_call(functools.partial(local_apply_kernel, groups), out_shape=t...  4.41 us
    unnamed x16, local copies, waits for them, and re-layouts  4.39 us
    pallas_call x1, Pallas kernels, pivot_inverse(): pl.pallas_call(pivot_inverse_kernel, out_shape=jax.ShapeDtypeStruct((shar...  4.24 us
  transfers between devices with their start and end apart: 8, of which 5 were waited for; matrix products, arithmetic and copies ran while one was open for 6% of the time, Pallas kernels for 9%

profile of v19, /device:TPU:194, one launch (start us, length us, event | category | flops | bytes accessed | tf_op | source)
XLA Modules:
  0.0 75.8 jit_solution(15254923103916164641)
XLA Ops:
  0.6 0.8 %slice_bitcast_fusion = (bf16[128,128]{1,0:T(8,128)(2,1)S(1)}, bf16[1,128,128]{2,1,0:T(8,128)(2,1)S(1)}) fusion(bf16[1,3072,128]{2,1,0:T(8,128)(2,1)} %z_hbm.1), kind=kLoop, calls=%fused_computation.3 | loop fusion | bytes 131072 | tf_op jit(solution)/shard_map/slice | solution.py:243
  1.4 0.8 %slice_bitcast_fusion.1 = bf16[1,128,128]{2,1,0:T(8,128)(2,1)S(1)} fusion(bf16[1,24,128,128]{3,2,1,0:T(8,128)(2,1)} %u_hbm.1), kind=kLoop, calls=%fused_computation.4 | loop fusion | bytes 65536 | tf_op jit(solution)/shard_map/stack;squeeze | solution.py:241
  2.2 3.5 %collective-permute-start = (bf16[2,128,128]{2,1,0:T(8,128)(2,1)S(1)}, bf16[2,128,128]{2,1,0:T(8,128)(2,1)S(1)}, u32[]{:S(2)}, u32[]{:S(2)}) collective-permute-start(bf16[2,128,128]{2,1,0:T(8,128)(2,1)S(1)} %pad_maximum_fusion.2), channel_id=1, source_target_pairs={{0,1},{1,2},{2,3},{4,5},{5,6},{6,7},{8,9},{9,10},{10,11},{12,13},{... | collective-permute-start | bytes 196616 | tf_op jit(solution)/shard_map/ppermute | solution.py:26
  5.7 1.3 %collective-permute-start.1 = (bf16[128,128]{1,0:T(8,128)(2,1)S(1)}, bf16[128,128]{1,0:T(8,128)(2,1)S(1)}, u32[]{:S(2)}, u32[]{:S(2)}) collective-permute-start(bf16[128,128]{1,0:T(8,128)(2,1)S(1)} %get-tuple-element.15), channel_id=1, source_target_pairs={{1,0},{2,1},{3,2},{5,4},{6,5},{7,6},{9,8},{10,9},{11,10},{13,12},{... | collective-permute-start | bytes 98312 | tf_op jit(solution)/shard_map/ppermute | solution.py:26
  7.0 4.5 %collective-permute-done.1.zn_ref = bf16[128,128]{1,0:T(8,128)(2,1)S(1)} collective-permute-done((bf16[128,128]{1,0:T(8,128)(2,1)S(1)}, bf16[128,128]{1,0:T(8,128)(2,1)S(1)}, u32[]{:S(2)}, u32[]{:S(2)}) %collective-permute-start.1) | collective-permute-done | bytes 32800 | tf_op jit(solution)/shard_map/ppermute | solution.py:26
  11.5 0.0 collective-permute-done.fp_ref
  11.5 0.6 copy-done.6
  12.1 0.6 copy-done.5
  12.7 4.4 %shard_map.85 = (bf16[3,2,128,128]{3,2,1,0:T(8,128)(2,1)}, bf16[3,2,128,128]{3,2,1,0:T(8,128)(2,1)}, bf16[1,2,128,128]{3,2,1,0:T(8,128)(2,1)}, bf16[1,2,128,128]...) custom-call(s32[1,1,16]{2,1,0:T(1,128)} %blocks_ref.1, s32[1,8]{1,0:T(1,128)} %counts_ref.1, ...), custom_call_target="tpu_custom_call" | custom-call | tf_op jit(solution)/shard_map/pallas_call | solution.py:109
  17.1 1.9 %collective-permute-start.2 = (bf16[3,2,128,128]{3,2,1,0:T(8,128)(2,1)}, bf16[3,2,128,128]{3,2,1,0:T(8,128)(2,1)S(1)}, u32[]{:S(2)}, u32[]{:S(2)}) collective-permute-start(bf16[3,2,128,128]{3,2,1,0:T(8,128)(2,1)} %get-tuple-element.11), channel_id=1, source_target_pairs={{4,0},{8,4},{12,8},{16,12},{20,16},{24,20},{28,24},{32,28},{36,32}... | collective-permute-start | bytes 589832 | tf_op jit(solution)/shard_map/ppermute | solution.py:263
  19.1 2.4 %collective-permute-start.3 = (bf16[3,2,128,128]{3,2,1,0:T(8,128)(2,1)}, bf16[3,2,128,128]{3,2,1,0:T(8,128)(2,1)S(1)}, u32[]{:S(2)}, u32[]{:S(2)}) collective-permute-start(bf16[3,2,128,128]{3,2,1,0:T(8,128)(2,1)} %get-tuple-element.12), channel_id=1, source_target_pairs={{0,4},{4,8},{8,12},{12,16},{16,20},{20,24},{24,28},{28,32},{32,36}... | collective-permute-start | bytes 589832 | tf_op jit(solution)/shard_map/ppermute | solution.py:266
  21.5 1.1 %collective-permute-done.2.down_ref = bf16[3,2,128,128]{3,2,1,0:T(8,128)(2,1)S(1)} collective-permute-done((bf16[3,2,128,128]{3,2,1,0:T(8,128)(2,1)}, bf16[3,2,128,128]{3,2,1,0:T(8,128)(2,1)S(1)}, u32[]{:S(2)}, u32[]{:S(2)}) %collective-permute-start.2) | collective-permute-done | bytes 196640 | tf_op jit(solution)/shard_map/ppermute | solution.py:263
  22.6 3.7 %collective-permute-done.3.up_ref = bf16[3,2,128,128]{3,2,1,0:T(8,128)(2,1)S(1)} collective-permute-done((bf16[3,2,128,128]{3,2,1,0:T(8,128)(2,1)}, bf16[3,2,128,128]{3,2,1,0:T(8,128)(2,1)S(1)}, u32[]{:S(2)}, u32[]{:S(2)}) %collective-permute-start.3) | collective-permute-done | bytes 196640 | tf_op jit(solution)/shard_map/ppermute | solution.py:266
  26.3 0.9 %pad_maximum_fusion.1 = bf16[3,2,128,128]{3,2,1,0:T(8,128)(2,1)S(1)} fusion(bf16[1,2,128,128]{3,2,1,0:T(8,128)(2,1)S(1)} %get-tuple-element.19, bf16[1,2,128,128]{3,2,1,0:T(8,128)(2,1)S(1)} %get-tuple-element.17, bf16[1,2,128,128]{3,2,1,0:T(8,128)(2,1)} %get-tuple-element.14), kind=kLoop, calls=%fused_computation.1 | loop fusion | flops 196608 | bytes 393216 | tf_op jit(solution)/shard_map/concatenate | solution.py:273
  27.2 6.4 %collective-permute-start.5 = (bf16[3,2,128,128]{3,2,1,0:T(8,128)(2,1)S(1)}, bf16[3,2,128,128]{3,2,1,0:T(8,128)(2,1)S(1)}, u32[]{:S(2)}, u32[]{:S(2)}) collective-permute-start(bf16[3,2,128,128]{3,2,1,0:T(8,128)(2,1)S(1)} %pad_maximum_fusion.1), channel_id=1, source_target_pairs={{0,64},{4,68},{8,72},{12,76},{16,80},{20,84},{24,88},{28,92},{32,9... | collective-permute-start | bytes 589832 | tf_op jit(solution)/shard_map/ppermute | solution.py:272
  33.6 0.9 %pad_maximum_fusion = bf16[3,2,128,128]{3,2,1,0:T(8,128)(2,1)S(1)} fusion(bf16[1,2,128,128]{3,2,1,0:T(8,128)(2,1)S(1)} %get-tuple-element.20, bf16[1,2,128,128]{3,2,1,0:T(8,128)(2,1)S(1)} %get-tuple-element.18, bf16[1,2,128,128]{3,2,1,0:T(8,128)(2,1)} %get-tuple-element.13), kind=kLoop, calls=%fused_computation | loop fusion | flops 196608 | bytes 393216 | tf_op jit(solution)/shard_map/concatenate | solution.py:268
  34.5 1.9 %collective-permute-start.4 = (bf16[3,2,128,128]{3,2,1,0:T(8,128)(2,1)S(1)}, bf16[3,2,128,128]{3,2,1,0:T(8,128)(2,1)S(1)}, u32[]{:S(2)}, u32[]{:S(2)}) collective-permute-start(bf16[3,2,128,128]{3,2,1,0:T(8,128)(2,1)S(1)} %pad_maximum_fusion), channel_id=1, source_target_pairs={{64,0},{68,4},{72,8},{76,12},{80,16},{84,20},{88,24},{92,28},{96,3... | collective-permute-start | bytes 589832 | tf_op jit(solution)/shard_map/ppermute | solution.py:267
  37.1 0.8 %dynamic_slice.3 = f32[32,32]{1,0:T(8,128)S(1)} dynamic-slice(f32[128,128]{1,0:T(8,128)} %get-tuple-element.9.gram_ref, s32[]{:T(128)S(6)} %select_n.4, s32[]{:T(128)S(6)} %select_n.4), dynamic_slice_sizes={32,32} | dynamic-slice | bytes 8196 | tf_op jit(solution)/shard_map/dynamic_slice | solution.py:256
  37.9 0.7 reshape.12
  38.6 4.2 %all-to-all-start.1 = ((f32[4,1,1024]{2,1,0:T(1,128)}), f32[4,1,1024]{2,1,0:T(1,128)S(1)}, u32[]{:S(2)}, u32[]{:S(2)}) async-start(f32[4,1,1024]{2,1,0:T(1,128)} %reshape.12), calls=%async_computation.1 | async-start | bytes 32768 | tf_op jit(solution)/shard_map/all_to_all | solution.py:257
  42.8 0.0 collective-permute-done.5.fup_ref
  42.8 5.6 %collective-permute-done.4.fdn_ref = bf16[3,2,128,128]{3,2,1,0:T(8,128)(2,1)S(1)} collective-permute-done((bf16[3,2,128,128]{3,2,1,0:T(8,128)(2,1)S(1)}, bf16[3,2,128,128]{3,2,1,0:T(8,128)(2,1)S(1)}, u32[]{:S(2)}, u32[]{:S(2)}) %collective-permute-start.4) | collective-permute-done | bytes 196640 | tf_op jit(solution)/shard_map/ppermute | solution.py:267
  48.4 0.7 copy-done.4
  49.0 2.7 %shard_map.86 = f32[4,64,1152]{2,1,0:T(8,128)} custom-call(s32[1]{0:T(128)S(6)} %copy.9.owner_ref, f32[128,128]{1,0:T(8,128)} %get-tuple-element.9.gram_ref, bf16[8,2,128,128]{3,2,1,0:T(8,128)(2,1)} %get-tuple-element.10.own_ref, bf16[3,2,128,128]{3,2,1,0:T(8,128)(2,1)} %copy-done.1, bf16[3,2,128,128]{3,2,1,0:T(8,128)(2,1)} %copy-done.2, ...), custom_call_target="tpu_custom_call" | custom-call | tf_op jit(solution)/shard_map/pallas_call | solution.py:220
  51.7 4.2 %all-to-all-start = ((f32[4,64,1152]{2,1,0:T(8,128)}), f32[4,64,1152]{2,1,0:T(8,128)S(1)}, u32[]{:S(2)}, u32[]{:S(2)}) async-start(f32[4,64,1152]{2,1,0:T(8,128)} %shard_map.86), calls=%async_computation | async-start | bytes 2359296 | tf_op jit(solution)/shard_map/all_to_all | solution.py:281
  55.9 0.5 broadcast.1
  56.4 0.7 reduce
  57.1 0.7 reshape.13.blocks_ref
  57.8 4.2 %shard_map.87.inverse_ref = f32[32,32]{1,0:T(8,128)} custom-call(f32[4,32,32]{2,1,0:T(8,128)} %reshape.13.blocks_ref), custom_call_target="tpu_custom_call" | custom-call | tf_op jit(solution)/shard_map/pallas_call | solution.py:152
  62.1 10.0 %all-to-all-done.pieces_ref = f32[4,64,1152]{2,1,0:T(8,128)S(1)} async-done(((f32[4,64,1152]{2,1,0:T(8,128)}), f32[4,64,1152]{2,1,0:T(8,128)S(1)}, u32[]{:S(2)}, u32[]{:S(2)}) %all-to-all-start) | async-done | bytes 1179680 | tf_op jit(solution)/shard_map/all_to_all | solution.py:281
  72.1 1.1 %copy-done = f32[4,64,1152]{2,1,0:T(8,128)} copy-done((f32[4,64,1152]{2,1,0:T(8,128)}, f32[4,64,1152]{2,1,0:T(8,128)S(1)}, u32[]{:S(2)}) %copy-start) | copy-done | bytes 1179672
  73.1 2.7 %shard_map.88 = (f32[32,128]{1,0:T(8,128)}, f32[32,1024]{1,0:T(8,128)}, f32[32,32]{1,0:T(8,128)}) custom-call(s32[1]{0:T(128)S(6)} %copy.9.owner_ref, f32[4,64,1152]{2,1,0:T(8,128)} %copy-done, f32[32,32]{1,0:T(8,128)} %shard_map.87.inverse_ref), custom_call_target="tpu_custom_call" | custom-call | tf_op jit(solution)/shard_map/pallas_call | solution.py:182
  (15 shorter events, 0.1 us)
Async XLA Ops:
  2.2 9.3 %collective-permute-start = (bf16[2,128,128]{2,1,0:T(8,128)(2,1)S(1)}, bf16[2,128,128]{2,1,0:T(8,128)(2,1)S(1)}, u32[]{:S(2)}, u32[]{:S(2)}) collective-permute-start(bf16[2,128,128]{2,1,0:T(8,128)(2,1)S(1)} %pad_maximum_fusion.2), channel_id=1, source_target_pairs={{0,1},{1,2},{2,3},{4,5},{5,6},{6,7},{8,9},{9,10},{10,11},{12,13},{... | collective-permute-start | bytes 196616 | tf_op jit(solution)/shard_map/ppermute | solution.py:26
  5.7 5.8 %collective-permute-start.1 = (bf16[128,128]{1,0:T(8,128)(2,1)S(1)}, bf16[128,128]{1,0:T(8,128)(2,1)S(1)}, u32[]{:S(2)}, u32[]{:S(2)}) collective-permute-start(bf16[128,128]{1,0:T(8,128)(2,1)S(1)} %get-tuple-element.15), channel_id=1, source_target_pairs={{1,0},{2,1},{3,2},{5,4},{6,5},{7,6},{9,8},{10,9},{11,10},{13,12},{... | collective-permute-start | bytes 98312 | tf_op jit(solution)/shard_map/ppermute | solution.py:26
  11.5 0.6 copy-start.6
  12.1 0.6 copy-start.5
  17.1 5.4 %collective-permute-start.2 = (bf16[3,2,128,128]{3,2,1,0:T(8,128)(2,1)}, bf16[3,2,128,128]{3,2,1,0:T(8,128)(2,1)S(1)}, u32[]{:S(2)}, u32[]{:S(2)}) collective-permute-start(bf16[3,2,128,128]{3,2,1,0:T(8,128)(2,1)} %get-tuple-element.11), channel_id=1, source_target_pairs={{4,0},{8,4},{12,8},{16,12},{20,16},{24,20},{28,24},{32,28},{36,32}... | collective-permute-start | bytes 589832 | tf_op jit(solution)/shard_map/ppermute | solution.py:263
  19.1 7.2 %collective-permute-start.3 = (bf16[3,2,128,128]{3,2,1,0:T(8,128)(2,1)}, bf16[3,2,128,128]{3,2,1,0:T(8,128)(2,1)S(1)}, u32[]{:S(2)}, u32[]{:S(2)}) collective-permute-start(bf16[3,2,128,128]{3,2,1,0:T(8,128)(2,1)} %get-tuple-element.12), channel_id=1, source_target_pairs={{0,4},{4,8},{8,12},{12,16},{16,20},{20,24},{24,28},{28,32},{32,36}... | collective-permute-start | bytes 589832 | tf_op jit(solution)/shard_map/ppermute | solution.py:266
  22.6 25.8 %copy-start.1 = (bf16[3,2,128,128]{3,2,1,0:T(8,128)(2,1)}, bf16[3,2,128,128]{3,2,1,0:T(8,128)(2,1)S(1)}, u32[]{:S(2)}) copy-start(bf16[3,2,128,128]{3,2,1,0:T(8,128)(2,1)S(1)} %collective-permute-done.2.down_ref) | copy-start | bytes 589828
  26.3 22.1 %copy-start.2 = (bf16[3,2,128,128]{3,2,1,0:T(8,128)(2,1)}, bf16[3,2,128,128]{3,2,1,0:T(8,128)(2,1)S(1)}, u32[]{:S(2)}) copy-start(bf16[3,2,128,128]{3,2,1,0:T(8,128)(2,1)S(1)} %collective-permute-done.3.up_ref) | copy-start | bytes 589828
  27.2 15.5 %collective-permute-start.5 = (bf16[3,2,128,128]{3,2,1,0:T(8,128)(2,1)S(1)}, bf16[3,2,128,128]{3,2,1,0:T(8,128)(2,1)S(1)}, u32[]{:S(2)}, u32[]{:S(2)}) collective-permute-start(bf16[3,2,128,128]{3,2,1,0:T(8,128)(2,1)S(1)} %pad_maximum_fusion.1), channel_id=1, source_target_pairs={{0,64},{4,68},{8,72},{12,76},{16,80},{20,84},{24,88},{28,92},{32,9... | collective-permute-start | bytes 589832 | tf_op jit(solution)/shard_map/ppermute | solution.py:272
  34.5 13.8 %collective-permute-start.4 = (bf16[3,2,128,128]{3,2,1,0:T(8,128)(2,1)S(1)}, bf16[3,2,128,128]{3,2,1,0:T(8,128)(2,1)S(1)}, u32[]{:S(2)}, u32[]{:S(2)}) collective-permute-start(bf16[3,2,128,128]{3,2,1,0:T(8,128)(2,1)S(1)} %pad_maximum_fusion), channel_id=1, source_target_pairs={{64,0},{68,4},{72,8},{76,12},{80,16},{84,20},{88,24},{92,28},{96,3... | collective-permute-start | bytes 589832 | tf_op jit(solution)/shard_map/ppermute | solution.py:267
  38.6 13.1 %all-to-all-start.1 = ((f32[4,1,1024]{2,1,0:T(1,128)}), f32[4,1,1024]{2,1,0:T(1,128)S(1)}, u32[]{:S(2)}, u32[]{:S(2)}) async-start(f32[4,1,1024]{2,1,0:T(1,128)} %reshape.12), calls=%async_computation.1 | async-start | bytes 32768 | tf_op jit(solution)/shard_map/all_to_all | solution.py:257
  42.8 5.6 %copy-start.3 = (bf16[3,2,128,128]{3,2,1,0:T(8,128)(2,1)}, bf16[3,2,128,128]{3,2,1,0:T(8,128)(2,1)S(1)}, u32[]{:S(2)}) copy-start(bf16[3,2,128,128]{3,2,1,0:T(8,128)(2,1)S(1)} %collective-permute-done.5.fup_ref) | copy-start | bytes 589828
  48.3 0.7 copy-start.4
  51.7 20.3 %all-to-all-start = ((f32[4,64,1152]{2,1,0:T(8,128)}), f32[4,64,1152]{2,1,0:T(8,128)S(1)}, u32[]{:S(2)}, u32[]{:S(2)}) async-start(f32[4,64,1152]{2,1,0:T(8,128)} %shard_map.86), calls=%async_computation | async-start | bytes 2359296 | tf_op jit(solution)/shard_map/all_to_all | solution.py:281
  72.1 1.1 %copy-start = (f32[4,64,1152]{2,1,0:T(8,128)}, f32[4,64,1152]{2,1,0:T(8,128)S(1)}, u32[]{:S(2)}) copy-start(f32[4,64,1152]{2,1,0:T(8,128)S(1)} %all-to-all-done.pieces_ref) | copy-start | bytes 3538948

commit v20 on v10

--- a/solution.py
+++ b/solution.py
@@ -138,9 +138,9 @@
     for q in range(width // share):
         columns = jnp.where(owner == q, own[:, q * share:(q + 1) * share], columns)
     inverse = inverse_ref[...]
-    solved = _exact(inverse, lead, ((1,), (0,)))
     panel = _exact(columns, inverse, ((1,), (1,)))
-    updated = own - _exact(panel, solved, ((1,), (0,)))
+    weights = _exact(panel, inverse, ((1,), (0,)))
+    updated = own - _exact(weights, lead, ((1,), (0,)))
     self_ref[...] = updated[:, :width]
     coupling_ref[...] = updated[:, width:]
     panel_ref[...] = panel

time: 75.8 us -> 75.9 us (level)
  no operation moved by 1% of the time
where the time goes in v20:
time: 75.9 us; the launch traced here: 75.1 us
  starting transfers between devices  25.7 us (34%)
  waiting for transfers between devices  24.9 us (33%)
  Pallas kernels  13.4 us (18%)
  local copies, waits for them, and re-layouts  7.27 us (10%)
  other arithmetic  2.5 us (3%)
  between operations  1.37 us (2%)
    all_to_all x1, waiting for transfers between devices, per_device(): pieces = lax.all_to_all(outgoing_rows, 'crow', 0, 0, tiled=True)  9.98 us
    ppermute x1, starting transfers between devices, per_device(): lax.ppermute(jnp.concatenate([near_up, down[2:], up[2:]]), 'sub', [(u, u...  6.38 us
    ppermute x1, waiting for transfers between devices, per_device(): lax.ppermute(jnp.concatenate([near_down, down[:1], up[:1]]), 'sub', [(u,...  5.58 us
    ppermute x2, starting transfers between devices, shifted(): lax.ppermute(value, axis, [(source, source + steps) for source in range(i...  4.78 us
    ppermute x2, waiting for transfers between devices, shifted(): lax.ppermute(value, axis, [(source, source + steps) for source in range(i...  4.51 us
    unnamed x16, local copies, waits for them, and re-layouts  4.39 us
    pallas_call x1, Pallas kernels, pivot_inverse(): pl.pallas_call(pivot_inverse_kernel, out_shape=jax.ShapeDtypeStruct((shar...  4.24 us
    all_to_all x1, starting transfers between devices, per_device(): pieces = lax.all_to_all(outgoing_rows, 'crow', 0, 0, tiled=True)  4.17 us
  transfers between devices with their start and end apart: 8, of which 5 were waited for; matrix products, arithmetic and copies ran while one was open for 6% of the time, Pallas kernels for 9%

profile of v20, /device:TPU:194, one launch (start us, length us, event | category | flops | bytes accessed | tf_op | source)
XLA Modules:
  0.0 75.1 jit_solution(8641641567559580933)
XLA Ops:
  0.6 0.8 %slice_bitcast_fusion = (bf16[128,128]{1,0:T(8,128)(2,1)S(1)}, bf16[1,128,128]{2,1,0:T(8,128)(2,1)S(1)}) fusion(bf16[1,3072,128]{2,1,0:T(8,128)(2,1)} %z_ref.1), kind=kLoop, calls=%fused_computation.3 | loop fusion | bytes 131072 | tf_op jit(solution)/shard_map/slice | solution.py:213
  1.4 0.8 %slice_bitcast_fusion.1 = bf16[1,128,128]{2,1,0:T(8,128)(2,1)S(1)} fusion(bf16[1,24,128,128]{3,2,1,0:T(8,128)(2,1)} %u_ref.1), kind=kLoop, calls=%fused_computation.4 | loop fusion | bytes 65536 | tf_op jit(solution)/shard_map/stack;squeeze | solution.py:211
  2.2 3.5 %collective-permute-start = (bf16[2,128,128]{2,1,0:T(8,128)(2,1)S(1)}, bf16[2,128,128]{2,1,0:T(8,128)(2,1)S(1)}, u32[]{:S(2)}, u32[]{:S(2)}) collective-permute-start(bf16[2,128,128]{2,1,0:T(8,128)(2,1)S(1)} %pad_maximum_fusion.2), channel_id=1, source_target_pairs={{0,1},{1,2},{2,3},{4,5},{5,6},{6,7},{8,9},{9,10},{10,11},{12,13},{... | collective-permute-start | bytes 196616 | tf_op jit(solution)/shard_map/ppermute | solution.py:26
  5.7 1.3 %collective-permute-start.1 = (bf16[128,128]{1,0:T(8,128)(2,1)S(1)}, bf16[128,128]{1,0:T(8,128)(2,1)S(1)}, u32[]{:S(2)}, u32[]{:S(2)}) collective-permute-start(bf16[128,128]{1,0:T(8,128)(2,1)S(1)} %get-tuple-element.15), channel_id=1, source_target_pairs={{1,0},{2,1},{3,2},{5,4},{6,5},{7,6},{9,8},{10,9},{11,10},{13,12},{... | collective-permute-start | bytes 98312 | tf_op jit(solution)/shard_map/ppermute | solution.py:26
  7.0 4.5 %collective-permute-done.1.zn_ref = bf16[128,128]{1,0:T(8,128)(2,1)S(1)} collective-permute-done((bf16[128,128]{1,0:T(8,128)(2,1)S(1)}, bf16[128,128]{1,0:T(8,128)(2,1)S(1)}, u32[]{:S(2)}, u32[]{:S(2)}) %collective-permute-start.1) | collective-permute-done | bytes 32800 | tf_op jit(solution)/shard_map/ppermute | solution.py:26
  11.5 0.0 collective-permute-done.fp_ref
  11.5 0.6 copy-done.6
  12.1 0.6 copy-done.5
  12.7 3.6 %shard_map.85 = (bf16[3,2,128,128]{3,2,1,0:T(8,128)(2,1)}, bf16[3,2,128,128]{3,2,1,0:T(8,128)(2,1)}, bf16[1,2,128,128]{3,2,1,0:T(8,128)(2,1)}, bf16[1,2,128,128]...) custom-call(s32[1,1,16]{2,1,0:T(1,128)} %blocks_ref.1, s32[1,8]{1,0:T(1,128)} %counts_ref.1, ...), custom_call_target="tpu_custom_call" | custom-call | tf_op jit(solution)/shard_map/pallas_call | solution.py:85
  16.3 1.9 %collective-permute-start.2 = (bf16[3,2,128,128]{3,2,1,0:T(8,128)(2,1)}, bf16[3,2,128,128]{3,2,1,0:T(8,128)(2,1)S(1)}, u32[]{:S(2)}, u32[]{:S(2)}) collective-permute-start(bf16[3,2,128,128]{3,2,1,0:T(8,128)(2,1)} %get-tuple-element.11), channel_id=1, source_target_pairs={{4,0},{8,4},{12,8},{16,12},{20,16},{24,20},{28,24},{32,28},{36,32}... | collective-permute-start | bytes 589832 | tf_op jit(solution)/shard_map/ppermute | solution.py:233
  18.3 2.4 %collective-permute-start.3 = (bf16[3,2,128,128]{3,2,1,0:T(8,128)(2,1)}, bf16[3,2,128,128]{3,2,1,0:T(8,128)(2,1)S(1)}, u32[]{:S(2)}, u32[]{:S(2)}) collective-permute-start(bf16[3,2,128,128]{3,2,1,0:T(8,128)(2,1)} %get-tuple-element.12), channel_id=1, source_target_pairs={{0,4},{4,8},{8,12},{12,16},{16,20},{20,24},{24,28},{28,32},{32,36}... | collective-permute-start | bytes 589832 | tf_op jit(solution)/shard_map/ppermute | solution.py:236
  20.7 1.1 %collective-permute-done.2.down_ref = bf16[3,2,128,128]{3,2,1,0:T(8,128)(2,1)S(1)} collective-permute-done((bf16[3,2,128,128]{3,2,1,0:T(8,128)(2,1)}, bf16[3,2,128,128]{3,2,1,0:T(8,128)(2,1)S(1)}, u32[]{:S(2)}, u32[]{:S(2)}) %collective-permute-start.2) | collective-permute-done | bytes 196640 | tf_op jit(solution)/shard_map/ppermute | solution.py:233
  21.8 3.7 %collective-permute-done.3.up_ref = bf16[3,2,128,128]{3,2,1,0:T(8,128)(2,1)S(1)} collective-permute-done((bf16[3,2,128,128]{3,2,1,0:T(8,128)(2,1)}, bf16[3,2,128,128]{3,2,1,0:T(8,128)(2,1)S(1)}, u32[]{:S(2)}, u32[]{:S(2)}) %collective-permute-start.3) | collective-permute-done | bytes 196640 | tf_op jit(solution)/shard_map/ppermute | solution.py:236
  25.5 0.9 %pad_maximum_fusion.1 = bf16[3,2,128,128]{3,2,1,0:T(8,128)(2,1)S(1)} fusion(bf16[1,2,128,128]{3,2,1,0:T(8,128)(2,1)S(1)} %get-tuple-element.19, bf16[1,2,128,128]{3,2,1,0:T(8,128)(2,1)S(1)} %get-tuple-element.17, bf16[1,2,128,128]{3,2,1,0:T(8,128)(2,1)} %get-tuple-element.14), kind=kLoop, calls=%fused_computation.1 | loop fusion | flops 196608 | bytes 393216 | tf_op jit(solution)/shard_map/concatenate | solution.py:243
  26.4 6.4 %collective-permute-start.5 = (bf16[3,2,128,128]{3,2,1,0:T(8,128)(2,1)S(1)}, bf16[3,2,128,128]{3,2,1,0:T(8,128)(2,1)S(1)}, u32[]{:S(2)}, u32[]{:S(2)}) collective-permute-start(bf16[3,2,128,128]{3,2,1,0:T(8,128)(2,1)S(1)} %pad_maximum_fusion.1), channel_id=1, source_target_pairs={{0,64},{4,68},{8,72},{12,76},{16,80},{20,84},{24,88},{28,92},{32,9... | collective-permute-start | bytes 589832 | tf_op jit(solution)/shard_map/ppermute | solution.py:242
  32.8 0.9 %pad_maximum_fusion = bf16[3,2,128,128]{3,2,1,0:T(8,128)(2,1)S(1)} fusion(bf16[1,2,128,128]{3,2,1,0:T(8,128)(2,1)S(1)} %get-tuple-element.20, bf16[1,2,128,128]{3,2,1,0:T(8,128)(2,1)S(1)} %get-tuple-element.18, bf16[1,2,128,128]{3,2,1,0:T(8,128)(2,1)} %get-tuple-element.13), kind=kLoop, calls=%fused_computation | loop fusion | flops 196608 | bytes 393216 | tf_op jit(solution)/shard_map/concatenate | solution.py:238
  33.7 1.9 %collective-permute-start.4 = (bf16[3,2,128,128]{3,2,1,0:T(8,128)(2,1)S(1)}, bf16[3,2,128,128]{3,2,1,0:T(8,128)(2,1)S(1)}, u32[]{:S(2)}, u32[]{:S(2)}) collective-permute-start(bf16[3,2,128,128]{3,2,1,0:T(8,128)(2,1)S(1)} %pad_maximum_fusion), channel_id=1, source_target_pairs={{64,0},{68,4},{72,8},{76,12},{80,16},{84,20},{88,24},{92,28},{96,3... | collective-permute-start | bytes 589832 | tf_op jit(solution)/shard_map/ppermute | solution.py:237
  36.3 0.8 %dynamic_slice.3 = f32[32,32]{1,0:T(8,128)S(1)} dynamic-slice(f32[128,128]{1,0:T(8,128)} %get-tuple-element.9.gram_ref, s32[]{:T(128)S(6)} %select_n.4, s32[]{:T(128)S(6)} %select_n.4), dynamic_slice_sizes={32,32} | dynamic-slice | bytes 8196 | tf_op jit(solution)/shard_map/dynamic_slice | solution.py:226
  37.1 0.7 reshape.12
  37.8 4.2 %all-to-all-start.1 = ((f32[4,1,1024]{2,1,0:T(1,128)}), f32[4,1,1024]{2,1,0:T(1,128)S(1)}, u32[]{:S(2)}, u32[]{:S(2)}) async-start(f32[4,1,1024]{2,1,0:T(1,128)} %reshape.12), calls=%async_computation.1 | async-start | bytes 32768 | tf_op jit(solution)/shard_map/all_to_all | solution.py:227
  41.9 0.0 collective-permute-done.5.fup_ref
  41.9 5.6 %collective-permute-done.4.fdn_ref = bf16[3,2,128,128]{3,2,1,0:T(8,128)(2,1)S(1)} collective-permute-done((bf16[3,2,128,128]{3,2,1,0:T(8,128)(2,1)S(1)}, bf16[3,2,128,128]{3,2,1,0:T(8,128)(2,1)S(1)}, u32[]{:S(2)}, u32[]{:S(2)}) %collective-permute-start.4) | collective-permute-done | bytes 196640 | tf_op jit(solution)/shard_map/ppermute | solution.py:237
  47.5 0.7 copy-done.4
  48.2 2.7 %shard_map.86 = f32[4,64,1152]{2,1,0:T(8,128)} custom-call(s32[1]{0:T(128)S(6)} %copy.9.owner_ref, f32[128,128]{1,0:T(8,128)} %get-tuple-element.9.gram_ref, bf16[8,2,128,128]{3,2,1,0:T(8,128)(2,1)} %get-tuple-element.10.own_ref, bf16[3,2,128,128]{3,2,1,0:T(8,128)(2,1)} %copy-done.1, bf16[3,2,128,128]{3,2,1,0:T(8,128)(2,1)} %copy-done.2, ...), custom_call_target="tpu_custom_call" | custom-call | tf_op jit(solution)/shard_map/pallas_call | solution.py:190
  50.9 4.2 %all-to-all-start = ((f32[4,64,1152]{2,1,0:T(8,128)}), f32[4,64,1152]{2,1,0:T(8,128)S(1)}, u32[]{:S(2)}, u32[]{:S(2)}) async-start(f32[4,64,1152]{2,1,0:T(8,128)} %shard_map.86), calls=%async_computation | async-start | bytes 2359296 | tf_op jit(solution)/shard_map/all_to_all | solution.py:251
  55.1 0.5 broadcast.1
  55.6 0.7 reduce
  56.3 0.7 reshape.13.blocks_ref
  57.0 4.2 %shard_map.87.inverse_ref = f32[32,32]{1,0:T(8,128)} custom-call(f32[4,32,32]{2,1,0:T(8,128)} %reshape.13.blocks_ref), custom_call_target="tpu_custom_call" | custom-call | tf_op jit(solution)/shard_map/pallas_call | solution.py:122
  61.3 10.0 %all-to-all-done.pieces_ref = f32[4,64,1152]{2,1,0:T(8,128)S(1)} async-done(((f32[4,64,1152]{2,1,0:T(8,128)}), f32[4,64,1152]{2,1,0:T(8,128)S(1)}, u32[]{:S(2)}, u32[]{:S(2)}) %all-to-all-start) | async-done | bytes 1179680 | tf_op jit(solution)/shard_map/all_to_all | solution.py:251
  71.2 1.1 %copy-done = f32[4,64,1152]{2,1,0:T(8,128)} copy-done((f32[4,64,1152]{2,1,0:T(8,128)}, f32[4,64,1152]{2,1,0:T(8,128)S(1)}, u32[]{:S(2)}) %copy-start) | copy-done | bytes 1179672
  72.3 2.8 %shard_map.88 = (f32[32,128]{1,0:T(8,128)}, f32[32,1024]{1,0:T(8,128)}, f32[32,32]{1,0:T(8,128)}) custom-call(s32[1]{0:T(128)S(6)} %copy.9.owner_ref, f32[4,64,1152]{2,1,0:T(8,128)} %copy-done, f32[32,32]{1,0:T(8,128)} %shard_map.87.inverse_ref), custom_call_target="tpu_custom_call" | custom-call | tf_op jit(solution)/shard_map/pallas_call | solution.py:152
  (15 shorter events, 0.1 us)
Async XLA Ops:
  2.2 9.3 %collective-permute-start = (bf16[2,128,128]{2,1,0:T(8,128)(2,1)S(1)}, bf16[2,128,128]{2,1,0:T(8,128)(2,1)S(1)}, u32[]{:S(2)}, u32[]{:S(2)}) collective-permute-start(bf16[2,128,128]{2,1,0:T(8,128)(2,1)S(1)} %pad_maximum_fusion.2), channel_id=1, source_target_pairs={{0,1},{1,2},{2,3},{4,5},{5,6},{6,7},{8,9},{9,10},{10,11},{12,13},{... | collective-permute-start | bytes 196616 | tf_op jit(solution)/shard_map/ppermute | solution.py:26
  5.7 5.8 %collective-permute-start.1 = (bf16[128,128]{1,0:T(8,128)(2,1)S(1)}, bf16[128,128]{1,0:T(8,128)(2,1)S(1)}, u32[]{:S(2)}, u32[]{:S(2)}) collective-permute-start(bf16[128,128]{1,0:T(8,128)(2,1)S(1)} %get-tuple-element.15), channel_id=1, source_target_pairs={{1,0},{2,1},{3,2},{5,4},{6,5},{7,6},{9,8},{10,9},{11,10},{13,12},{... | collective-permute-start | bytes 98312 | tf_op jit(solution)/shard_map/ppermute | solution.py:26
  11.5 0.6 copy-start.6
  12.1 0.6 copy-start.5
  16.3 5.4 %collective-permute-start.2 = (bf16[3,2,128,128]{3,2,1,0:T(8,128)(2,1)}, bf16[3,2,128,128]{3,2,1,0:T(8,128)(2,1)S(1)}, u32[]{:S(2)}, u32[]{:S(2)}) collective-permute-start(bf16[3,2,128,128]{3,2,1,0:T(8,128)(2,1)} %get-tuple-element.11), channel_id=1, source_target_pairs={{4,0},{8,4},{12,8},{16,12},{20,16},{24,20},{28,24},{32,28},{36,32}... | collective-permute-start | bytes 589832 | tf_op jit(solution)/shard_map/ppermute | solution.py:233
  18.3 7.2 %collective-permute-start.3 = (bf16[3,2,128,128]{3,2,1,0:T(8,128)(2,1)}, bf16[3,2,128,128]{3,2,1,0:T(8,128)(2,1)S(1)}, u32[]{:S(2)}, u32[]{:S(2)}) collective-permute-start(bf16[3,2,128,128]{3,2,1,0:T(8,128)(2,1)} %get-tuple-element.12), channel_id=1, source_target_pairs={{0,4},{4,8},{8,12},{12,16},{16,20},{20,24},{24,28},{28,32},{32,36}... | collective-permute-start | bytes 589832 | tf_op jit(solution)/shard_map/ppermute | solution.py:236
  21.7 25.8 %copy-start.1 = (bf16[3,2,128,128]{3,2,1,0:T(8,128)(2,1)}, bf16[3,2,128,128]{3,2,1,0:T(8,128)(2,1)S(1)}, u32[]{:S(2)}) copy-start(bf16[3,2,128,128]{3,2,1,0:T(8,128)(2,1)S(1)} %collective-permute-done.2.down_ref) | copy-start | bytes 589828
  25.5 22.1 %copy-start.2 = (bf16[3,2,128,128]{3,2,1,0:T(8,128)(2,1)}, bf16[3,2,128,128]{3,2,1,0:T(8,128)(2,1)S(1)}, u32[]{:S(2)}) copy-start(bf16[3,2,128,128]{3,2,1,0:T(8,128)(2,1)S(1)} %collective-permute-done.3.up_ref) | copy-start | bytes 589828
  26.4 15.5 %collective-permute-start.5 = (bf16[3,2,128,128]{3,2,1,0:T(8,128)(2,1)S(1)}, bf16[3,2,128,128]{3,2,1,0:T(8,128)(2,1)S(1)}, u32[]{:S(2)}, u32[]{:S(2)}) collective-permute-start(bf16[3,2,128,128]{3,2,1,0:T(8,128)(2,1)S(1)} %pad_maximum_fusion.1), channel_id=1, source_target_pairs={{0,64},{4,68},{8,72},{12,76},{16,80},{20,84},{24,88},{28,92},{32,9... | collective-permute-start | bytes 589832 | tf_op jit(solution)/shard_map/ppermute | solution.py:242
  33.7 13.9 %collective-permute-start.4 = (bf16[3,2,128,128]{3,2,1,0:T(8,128)(2,1)S(1)}, bf16[3,2,128,128]{3,2,1,0:T(8,128)(2,1)S(1)}, u32[]{:S(2)}, u32[]{:S(2)}) collective-permute-start(bf16[3,2,128,128]{3,2,1,0:T(8,128)(2,1)S(1)} %pad_maximum_fusion), channel_id=1, source_target_pairs={{64,0},{68,4},{72,8},{76,12},{80,16},{84,20},{88,24},{92,28},{96,3... | collective-permute-start | bytes 589832 | tf_op jit(solution)/shard_map/ppermute | solution.py:237
  37.8 13.2 %all-to-all-start.1 = ((f32[4,1,1024]{2,1,0:T(1,128)}), f32[4,1,1024]{2,1,0:T(1,128)S(1)}, u32[]{:S(2)}, u32[]{:S(2)}) async-start(f32[4,1,1024]{2,1,0:T(1,128)} %reshape.12), calls=%async_computation.1 | async-start | bytes 32768 | tf_op jit(solution)/shard_map/all_to_all | solution.py:227
  41.9 5.6 %copy-start.3 = (bf16[3,2,128,128]{3,2,1,0:T(8,128)(2,1)}, bf16[3,2,128,128]{3,2,1,0:T(8,128)(2,1)S(1)}, u32[]{:S(2)}) copy-start(bf16[3,2,128,128]{3,2,1,0:T(8,128)(2,1)S(1)} %collective-permute-done.5.fup_ref) | copy-start | bytes 589828
  47.5 0.7 copy-start.4
  50.9 20.3 %all-to-all-start = ((f32[4,64,1152]{2,1,0:T(8,128)}), f32[4,64,1152]{2,1,0:T(8,128)S(1)}, u32[]{:S(2)}, u32[]{:S(2)}) async-start(f32[4,64,1152]{2,1,0:T(8,128)} %shard_map.86), calls=%async_computation | async-start | bytes 2359296 | tf_op jit(solution)/shard_map/all_to_all | solution.py:251
  71.2 1.1 %copy-start = (f32[4,64,1152]{2,1,0:T(8,128)}, f32[4,64,1152]{2,1,0:T(8,128)S(1)}, u32[]{:S(2)}) copy-start(f32[4,64,1152]{2,1,0:T(8,128)S(1)} %all-to-all-done.pieces_ref) | copy-start | bytes 3538948
